TPU v7x, 32 devices: a whole 2x2x4 slice. The times are simulated.
32 devices in a mesh: rep: 4 (over y, core), ep: 8 (over z, x).
Axes of the slice: x: 2, y: 2, z: 4, core: 2. Of those that a mesh axis runs over, the one named last changes fastest.
Arguments:
- tokens: bfloat16 [8192, 2048], P(('rep', 'ep')), may hold values from -6 to 6
- expert_ids: int32 [8192, 8], P(('rep', 'ep')), may hold values from 0 to 127, as said below
- gate_weights: float32 [8192, 8], P(('rep', 'ep')), may hold values from 0.25 to 1
- w_gate: bfloat16 [8, 768, 2048], P('ep'), may hold values from -0.125 to 0.125
- w_up: bfloat16 [8, 768, 2048], P('ep'), may hold values from -0.125 to 0.125
- w_down: bfloat16 [8, 768, 2048], P('ep'), may hold values from -0.21875 to 0.21875
- out_grad: bfloat16 [8192, 2048], P(('rep', 'ep')), may hold values from -6 to 6
Outputs:
- layer_out: bfloat16 [8192, 2048], P(('rep', 'ep'))
- tokens_grad: bfloat16 [8192, 2048], P(('rep', 'ep'))
- gates_grad: float32 [8192, 8], P(('rep', 'ep'))
- gate_w_grad: bfloat16 [8, 768, 2048], P('ep', 'rep')
- up_w_grad: bfloat16 [8, 768, 2048], P('ep', 'rep')
- down_w_grad: bfloat16 [8, 768, 2048], P('ep', 'rep')
Inputs may be any that keep to these rules, and one draw needn't show every extreme that they name: `expert_ids`: entry j of a row lies in [16 * j, 16 * j + 16); in the rows of one device no id below 8 appears more than 32 times, and some id below 8 appears exactly 32 times.
All inputs are finite; a program needn't handle non-finite values.
Results may differ from a plain program's by a relative error of at most 0.0065.
Values may be sent and summed in bfloat16 or wider, within the bound.
No kernel may reach another device: no remote copies, remote signals or barrier semaphores. Data moves between devices by JAX's collectives and lax.ppermute only.
A program may use at most 128 MiB of HBM per device.

v0:
```python
import jax
import jax.numpy as jnp
from jax import lax
from jax.sharding import PartitionSpec as P


def silu_grad(value):
    sigmoid_value = jax.nn.sigmoid(value)
    return sigmoid_value * (1.0 + value * (1.0 - sigmoid_value))


def rows_times(left, right):
    return lax.dot_general(
        left, right, (((1,), (1,)), ((), ())), preferred_element_type=jnp.float32
    )


def inner_rows(left, right):
    return lax.dot_general(
        left, right, (((0,), (0,)), ((), ())), preferred_element_type=jnp.float32
    )


def body(tokens, expert_ids, gate_weights, w_gate, w_up, w_down, out_grad):
    tok_count, feature_width = tokens.shape
    top_count = expert_ids.shape[1]
    experts = lax.axis_size("ep")
    per_pair = tok_count // 8
    total_slots = experts * per_pair
    assigned = tok_count * top_count
    flat_ids = expert_ids.reshape(-1)
    live_mask = flat_ids < experts
    onehot = (flat_ids[:, None] == jnp.arange(experts, dtype=jnp.int32)[None, :]).astype(jnp.int32)
    before = jnp.cumsum(onehot, axis=0) - onehot
    slot_rank = jnp.sum(before * onehot, axis=1)
    slot_index = flat_ids * per_pair + slot_rank
    slot_index = jnp.where(live_mask, slot_index, total_slots)
    source_index = (
        jnp.full((total_slots,), assigned, jnp.int32)
        .at[slot_index]
        .set(jnp.arange(assigned, dtype=jnp.int32), mode="drop")
    )
    used_slot = source_index < assigned
    slot_token = source_index // top_count
    gate_column = jnp.concatenate([gate_weights.reshape(-1), jnp.zeros((1,), jnp.float32)])
    slot_gate = jnp.where(used_slot, gate_column[source_index], 0.0)
    blank_row = jnp.zeros((1, feature_width), jnp.bfloat16)
    send_rows = jnp.concatenate([tokens, blank_row], axis=0)[slot_token]
    received = lax.all_to_all(
        send_rows.reshape(experts, per_pair, feature_width),
        "ep",
        split_axis=0,
        concat_axis=0,
        tiled=True,
    )
    received = received.reshape(total_slots, feature_width)
    gate_mat = w_gate[0]
    up_mat = w_up[0]
    down_mat = w_down[0]
    pre_gate = rows_times(received, gate_mat)
    pre_up = rows_times(received, up_mat)
    activated = jax.nn.silu(pre_gate)
    hidden = (activated * pre_up).astype(jnp.bfloat16)
    expert_out = jnp.dot(hidden, down_mat, preferred_element_type=jnp.float32).astype(jnp.bfloat16)
    returned = lax.all_to_all(
        expert_out.reshape(experts, per_pair, feature_width),
        "ep",
        split_axis=0,
        concat_axis=0,
        tiled=True,
    )
    returned = returned.reshape(total_slots, feature_width)
    layer_sum = (
        jnp.zeros((tok_count + 1, feature_width), jnp.float32)
        .at[slot_token]
        .add(slot_gate[:, None] * returned.astype(jnp.float32))
    )
    layer_out = layer_sum[:tok_count].astype(jnp.bfloat16)
    grad_rows = jnp.concatenate([out_grad, blank_row], axis=0)[slot_token]
    products = jnp.einsum("sd,sd->s", grad_rows, returned, preferred_element_type=jnp.float32)
    gates_grad = (
        jnp.zeros((assigned + 1,), jnp.float32)
        .at[source_index]
        .add(jnp.where(used_slot, products, 0.0))[:assigned]
        .reshape(tok_count, top_count)
    )
    scaled_grad = (slot_gate[:, None] * grad_rows.astype(jnp.float32)).astype(jnp.bfloat16)
    grad_received = lax.all_to_all(
        scaled_grad.reshape(experts, per_pair, feature_width),
        "ep",
        split_axis=0,
        concat_axis=0,
        tiled=True,
    )
    grad_received = grad_received.reshape(total_slots, feature_width)
    hidden_grad = rows_times(grad_received, down_mat)
    gate_pre_grad = (hidden_grad * pre_up * silu_grad(pre_gate)).astype(jnp.bfloat16)
    up_pre_grad = (hidden_grad * activated).astype(jnp.bfloat16)
    token_part = (
        jnp.dot(gate_pre_grad, gate_mat, preferred_element_type=jnp.float32)
        + jnp.dot(up_pre_grad, up_mat, preferred_element_type=jnp.float32)
    ).astype(jnp.bfloat16)
    part_back = lax.all_to_all(
        token_part.reshape(experts, per_pair, feature_width),
        "ep",
        split_axis=0,
        concat_axis=0,
        tiled=True,
    )
    part_back = part_back.reshape(total_slots, feature_width)
    grad_sum = (
        jnp.zeros((tok_count + 1, feature_width), jnp.float32)
        .at[slot_token]
        .add(part_back.astype(jnp.float32))
    )
    tokens_grad = grad_sum[:tok_count].astype(jnp.bfloat16)
    summed = lax.psum_scatter(
        jnp.concatenate(
            [
                inner_rows(gate_pre_grad, received),
                inner_rows(up_pre_grad, received),
                inner_rows(hidden, grad_received),
            ],
            axis=1,
        ),
        "rep",
        scatter_dimension=0,
        tiled=True,
    )
    gate_w_grad = summed[:, :feature_width].astype(jnp.bfloat16)[None]
    up_w_grad = summed[:, feature_width : 2 * feature_width].astype(jnp.bfloat16)[None]
    down_w_grad = summed[:, 2 * feature_width :].astype(jnp.bfloat16)[None]
    return (layer_out, tokens_grad, gates_grad, gate_w_grad, up_w_grad, down_w_grad)


def solution(mesh):
    return jax.shard_map(
        body,
        mesh=mesh,
        in_specs=(
            P(("rep", "ep"), None),
            P(("rep", "ep"), None),
            P(("rep", "ep"), None),
            P("ep", None, None),
            P("ep", None, None),
            P("ep", None, None),
            P(("rep", "ep"), None),
        ),
        out_specs=(
            P(("rep", "ep"), None),
            P(("rep", "ep"), None),
            P(("rep", "ep"), None),
            P("ep", "rep", None),
            P("ep", "rep", None),
            P("ep", "rep", None),
        ),
        check_vma=False,
    )
```

profile of v0, /device:TPU:0, one launch (start us, length us, event | category | flops | bytes accessed | tf_op | source)
XLA Modules:
  0.0 260.7 jit_solution(6248238122984791257)
XLA Ops:
  7.2 0.0 copy-start
  7.2 0.9 broadcast_compare_fusion
  8.0 0.8 broadcast_multiply_fusion
  8.8 0.8 copy.15
  9.7 0.1 eq.29
  9.8 0.1 eq.25
  9.9 0.2 copy.13
  10.1 0.1 lt.42
  10.2 0.1 copy.14
  10.3 0.1 mul.62
  10.4 2.3 reduce-window.6
  12.7 0.3 slice_reduce_fusion
  13.0 0.2 reduce-window.9
  13.2 0.1 add_bitcast_fusion
  13.4 8.0 %scatter_custom_fusion = s32[256]{0:T(256)S(1)} fusion(s32[2048]{0:T(1024)S(1)} %bitcast.80, s32[2048]{0:T(1024)S(1)} %iota.11, s32[]{:T(128)} %constant.16.clone.1), kind=kCustom, calls=%fused_computation.70 | custom fusion | bytes 1028 | tf_op jit(solution)/shard_map/scatter | solution.py:41
  21.5 2.3 concatenate.13
  23.8 0.0 copy-start.3
  23.8 4.7 %gather_fusion.1 = bf16[256,2048]{1,0:T(8,128)(2,1)} fusion(bf16[257,2048]{1,0:T(8,128)(2,1)} %concatenate.13, s32[1024]{0:T(1024)S(1)} %get-tuple-element.20), kind=kCustom, calls=%fused_computation.1 | custom fusion | bytes 2098176 | tf_op jit(solution)/shard_map/gather | solution.py:48
  28.5 7.3 %all-to-all-start = ((bf16[8,32,2048]{2,1,0:T(8,128)(2,1)}), bf16[8,32,2048]{2,1,0:T(8,128)(2,1)}, u32[]{:S(2)}, u32[]{:S(2)}) async-start(bf16[8,32,2048]{2,1,0:T(8,128)(2,1)} %bitcast.76), calls=%async_computation | async-start | bytes 2097152 | tf_op jit(solution)/shard_map/all_to_all | solution.py:49
  35.8 0.0 copy-done.3
  35.8 0.1 copy.17
  35.9 0.1 reshape.109
  36.0 1.7 gather_fusion
  37.8 0.1 mul.68
  37.9 2.3 concatenate.14
  40.2 4.7 %gather_fusion.2 = bf16[256,2048]{1,0:T(8,128)(2,1)} fusion(bf16[257,2048]{1,0:T(8,128)(2,1)} %concatenate.14, s32[1024]{0:T(1024)S(1)} %get-tuple-element.20), kind=kCustom, calls=%fused_computation.2 | custom fusion | bytes 2098176 | tf_op jit(solution)/shard_map/gather | solution.py:79
  44.9 2.4 fusion.25
  47.3 14.3 %all-to-all-done = bf16[8,32,2048]{2,1,0:T(8,128)(2,1)} async-done(((bf16[8,32,2048]{2,1,0:T(8,128)(2,1)}), bf16[8,32,2048]{2,1,0:T(8,128)(2,1)}, u32[]{:S(2)}, u32[]{:S(2)}) %all-to-all-start) | async-done | bytes 1048608 | tf_op jit(solution)/shard_map/all_to_all | solution.py:49
  61.7 4.2 %all-to-all-start.2 = ((bf16[8,32,2048]{2,1,0:T(8,128)(2,1)}), bf16[8,32,2048]{2,1,0:T(8,128)(2,1)}, u32[]{:S(2)}, u32[]{:S(2)}) async-start(bf16[8,32,2048]{2,1,0:T(8,128)(2,1)} %fusion.25), calls=%async_computation.2 | async-start | bytes 2097152 | tf_op jit(solution)/shard_map/all_to_all | solution.py:88
  65.9 0.2 reduce-scatter.2.cloned.1.call-start
  66.1 4.1 %fusion.6 = f32[256,768]{1,0:T(8,128)} fusion(bf16[256,2048]{1,0:T(8,128)(2,1)} %bitcast.4, bf16[1,768,2048]{2,1,0:T(8,128)(2,1)} %param.11), kind=kOutput, calls=%fused_computation.14 | convolution fusion | flops 805306368 | bytes 4980736 | tf_op jit(solution)/shard_map/dot_general | solution.py:13
  70.2 21.3 %all-to-all-done.2 = bf16[8,32,2048]{2,1,0:T(8,128)(2,1)} async-done(((bf16[8,32,2048]{2,1,0:T(8,128)(2,1)}), bf16[8,32,2048]{2,1,0:T(8,128)(2,1)}, u32[]{:S(2)}, u32[]{:S(2)}) %all-to-all-start.2) | async-done | bytes 1048608 | tf_op jit(solution)/shard_map/all_to_all | solution.py:88
  91.5 0.0 copy-start.4
  91.5 3.3 %fusion = f32[256,768]{1,0:T(8,128)S(1)} fusion(bf16[256,2048]{1,0:T(8,128)(2,1)} %bitcast.11, bf16[1,768,2048]{2,1,0:T(8,128)(2,1)} %param.12), kind=kOutput, calls=%fused_computation.8 | convolution fusion | flops 805306368 | bytes 4980736 | tf_op jit(solution)/shard_map/dot_general | solution.py:13
  94.8 0.0 copy-done
  94.8 0.0 copy-done.4
  94.8 2.6 multiply_convert_fusion.1
  97.4 0.0 copy-start.2
  97.4 0.0 copy-start.1
  97.5 2.5 fusion.40
  100.0 0.0 copy-done.2
  100.0 2.2 fusion.38
  102.2 0.0 copy-done.1
  102.2 2.2 fusion.39
  104.5 6.8 %pad_maximum_fusion = f32[768,6144]{1,0:T(8,128)} fusion(f32[768,2048]{1,0:T(8,128)S(1)} %fusion.40, f32[768,2048]{1,0:T(8,128)S(1)} %fusion.39, f32[768,2048]{1,0:T(8,128)S(1)} %fusion.38), kind=kLoop, calls=%fused_computation.7 | loop fusion | flops 9437184 | bytes 37748736 | tf_op jit(solution)/shard_map/concatenate | solution.py:118
  111.3 0.0 reduce-scatter.2.cloned.1.call-update
  111.3 4.0 %fusion.18 = bf16[256,2048]{1,0:T(8,128)(2,1)} fusion(bf16[256,768]{1,0:T(8,128)(2,1)} %copy-done.2, bf16[1,768,2048]{2,1,0:T(8,128)(2,1)} %param.12), kind=kOutput, calls=%fused_computation.24 | convolution fusion | flops 805830656 | bytes 4587520 | tf_op jit(solution)/shard_map/dot_general | solution.py:64
  115.3 4.3 %all-to-all-start.1 = ((bf16[8,32,2048]{2,1,0:T(8,128)(2,1)}), bf16[8,32,2048]{2,1,0:T(8,128)(2,1)}, u32[]{:S(2)}, u32[]{:S(2)}) async-start(bf16[8,32,2048]{2,1,0:T(8,128)(2,1)} %bitcast.77), calls=%async_computation.1 | async-start | bytes 2097152 | tf_op jit(solution)/shard_map/all_to_all | solution.py:65
  119.6 3.8 %fusion.4 = f32[256,2048]{1,0:T(8,128)S(1)} fusion(bf16[256,768]{1,0:T(8,128)(2,1)} %copy-done.1, bf16[1,768,2048]{2,1,0:T(8,128)(2,1)} %param.11), kind=kOutput, calls=%fused_computation.12 | convolution fusion | flops 805306368 | bytes 5636096 | tf_op jit(solution)/shard_map/dot_general | solution.py:101
  123.4 2.0 fusion.15
  125.4 19.5 %all-to-all-done.1 = bf16[8,32,2048]{2,1,0:T(8,128)(2,1)} async-done(((bf16[8,32,2048]{2,1,0:T(8,128)(2,1)}), bf16[8,32,2048]{2,1,0:T(8,128)(2,1)}, u32[]{:S(2)}, u32[]{:S(2)}) %all-to-all-start.1) | async-done | bytes 1048608 | tf_op jit(solution)/shard_map/all_to_all | solution.py:65
  145.0 4.2 %all-to-all-start.3 = ((bf16[8,32,2048]{2,1,0:T(8,128)(2,1)}), bf16[8,32,2048]{2,1,0:T(8,128)(2,1)}, u32[]{:S(2)}, u32[]{:S(2)}) async-start(bf16[8,32,2048]{2,1,0:T(8,128)(2,1)} %bitcast.75), calls=%async_computation.3 | async-start | bytes 2097152 | tf_op jit(solution)/shard_map/all_to_all | solution.py:103
  149.2 1.9 fusion.22
  151.1 2.5 scatter_custom_fusion.3
  153.6 0.1 reshape.116
  153.7 0.7 copy.18
  154.4 6.2 %scatter_custom_fusion.1 = f32[257,2048]{1,0:T(8,128)} fusion(s32[256]{0:T(256)S(1)} %get-tuple-element.19, bf16[256,2048]{1,0:T(8,128)(2,1)} %bitcast.9, f32[]{:T(128)} %constant.15.clone.1, f32[256]{0:T(256)S(1)} %broadcast_select_fusion.1), kind=kCustom, calls=%fused_computation.25 | custom fusion | flops 1572864 | bytes 3154948 | tf_op jit(solution)/shard_map/scatter-add | solution.py:76
  160.6 2.9 %slice.57 = bf16[256,2048]{1,0:T(8,128)(2,1)} slice(f32[257,2048]{1,0:T(8,128)} %scatter_custom_fusion.1), slice={[0:256], [0:2048]} | slice | bytes 2097152 | tf_op jit(solution)/shard_map/slice | solution.py:78
  163.5 11.1 %all-to-all-done.3 = bf16[8,32,2048]{2,1,0:T(8,128)(2,1)} async-done(((bf16[8,32,2048]{2,1,0:T(8,128)(2,1)}), bf16[8,32,2048]{2,1,0:T(8,128)(2,1)}, u32[]{:S(2)}, u32[]{:S(2)}) %all-to-all-start.3) | async-done | bytes 1048608 | tf_op jit(solution)/shard_map/all_to_all | solution.py:103
  174.6 6.0 %scatter_custom_fusion.2 = f32[257,2048]{1,0:T(8,128)} fusion(s32[256]{0:T(256)S(1)} %get-tuple-element.19, bf16[256,2048]{1,0:T(8,128)(2,1)} %bitcast.18, f32[]{:T(128)} %constant.15.clone.1), kind=kCustom, calls=%fused_computation.29 | custom fusion | flops 1048576 | bytes 3153924 | tf_op jit(solution)/shard_map/scatter-add | solution.py:114
  180.6 2.8 %slice.56 = bf16[256,2048]{1,0:T(8,128)(2,1)} slice(f32[257,2048]{1,0:T(8,128)} %scatter_custom_fusion.2), slice={[0:256], [0:2048]} | slice | bytes 2097152 | tf_op jit(solution)/shard_map/slice | solution.py:116
  183.4 66.4 %reduce-scatter.2.cloned.1.call-done = f32[192,6144]{1,0:T(8,128)} async-done(((f32[768,6144]{1,0:T(8,128)}), f32[192,6144]{1,0:T(8,128)}) %reduce-scatter.2.cloned.1.call-update) | async-done | bytes 4718608 | tf_op jit(solution)/shard_map/reduce_scatter | solution.py:117
  249.8 2.6 %convert.15 = bf16[192,6144]{1,0:T(8,128)(2,1)S(1)} convert(f32[192,6144]{1,0:T(8,128)} %reduce-scatter.2.cloned.1.call-done) | non-fusion elementwise | flops 1179648 | bytes 7077888 | tf_op jit(solution)/shard_map/convert.4
  252.4 1.5 slice_bitcast_fusion
  (10 shorter events, 0.1 us)
Async XLA Ops:
  7.2 87.7 %copy-start = (bf16[1,768,2048]{2,1,0:T(8,128)(2,1)S(1)}, bf16[1,768,2048]{2,1,0:T(8,128)(2,1)}, u32[]{:S(2)}) copy-start(bf16[1,768,2048]{2,1,0:T(8,128)(2,1)} %param.10) | copy-start | bytes 9437188
  23.8 12.0 %copy-start.3 = (f32[256,8]{0,1:T(8,128)S(1)}, f32[256,8]{0,1:T(8,128)}, u32[]{:S(2)}) copy-start(f32[256,8]{0,1:T(8,128)} %param.9) | copy-start | bytes 24580
  28.5 33.1 %all-to-all-start = ((bf16[8,32,2048]{2,1,0:T(8,128)(2,1)}), bf16[8,32,2048]{2,1,0:T(8,128)(2,1)}, u32[]{:S(2)}, u32[]{:S(2)}) async-start(bf16[8,32,2048]{2,1,0:T(8,128)(2,1)} %bitcast.76), calls=%async_computation | async-start | bytes 2097152 | tf_op jit(solution)/shard_map/all_to_all | solution.py:49
  61.7 29.8 %all-to-all-start.2 = ((bf16[8,32,2048]{2,1,0:T(8,128)(2,1)}), bf16[8,32,2048]{2,1,0:T(8,128)(2,1)}, u32[]{:S(2)}, u32[]{:S(2)}) async-start(bf16[8,32,2048]{2,1,0:T(8,128)(2,1)} %fusion.25), calls=%async_computation.2 | async-start | bytes 2097152 | tf_op jit(solution)/shard_map/all_to_all | solution.py:88
  65.9 183.9 %reduce-scatter.2.cloned.1.call-start = ((), (), s32[]{:S(2)}) async-start(), calls=%async_computation.5 | async-start | bytes 23592960 | tf_op jit(solution)/shard_map/reduce_scatter | solution.py:117
  91.5 3.3 %copy-start.4 = (f32[256,768]{1,0:T(8,128)S(1)}, f32[256,768]{1,0:T(8,128)}, u32[]{:S(2)}) copy-start(f32[256,768]{1,0:T(8,128)} %fusion.6) | copy-start | bytes 2359300
  97.4 2.5 copy-start.2
  97.4 4.8 %copy-start.1 = (bf16[256,768]{1,0:T(8,128)(2,1)}, bf16[256,768]{1,0:T(8,128)(2,1)S(1)}, u32[]{:S(2)}) copy-start(bf16[256,768]{1,0:T(8,128)(2,1)S(1)} %get-tuple-element.16) | copy-start | bytes 1179652
  115.3 29.7 %all-to-all-start.1 = ((bf16[8,32,2048]{2,1,0:T(8,128)(2,1)}), bf16[8,32,2048]{2,1,0:T(8,128)(2,1)}, u32[]{:S(2)}, u32[]{:S(2)}) async-start(bf16[8,32,2048]{2,1,0:T(8,128)(2,1)} %bitcast.77), calls=%async_computation.1 | async-start | bytes 2097152 | tf_op jit(solution)/shard_map/all_to_all | solution.py:65
  145.0 29.6 %all-to-all-start.3 = ((bf16[8,32,2048]{2,1,0:T(8,128)(2,1)}), bf16[8,32,2048]{2,1,0:T(8,128)(2,1)}, u32[]{:S(2)}, u32[]{:S(2)}) async-start(bf16[8,32,2048]{2,1,0:T(8,128)(2,1)} %bitcast.75), calls=%async_computation.3 | async-start | bytes 2097152 | tf_op jit(solution)/shard_map/all_to_all | solution.py:103
Sparse Core Ops, SparseCore 0:
  111.4 138.2 reduce-scatter.1
where the time goes:
time: 262 us; the launch traced here: 261 us
  waiting for transfers between devices  133 us (51%)
  local copies, waits for them, and re-layouts  34 us (13%)
  other arithmetic  32.8 us (13%)
  matrix products  26.8 us (10%)
  starting transfers between devices  20.2 us (8%)
  between operations  14.3 us (5%)
    reduce_scatter x1, waiting for transfers between devices, body(): lax.psum_scatter(jnp.concatenate([inner_rows(gate_pre_grad, received), in...  66.4 us
    all_to_all x1, waiting for transfers between devices, body(): lax.all_to_all(scaled_grad.reshape(experts, per_pair, feature_width), 'ep...  21.3 us
    all_to_all x1, waiting for transfers between devices, body(): lax.all_to_all(expert_out.reshape(experts, per_pair, feature_width), 'ep'...  19.5 us
    all_to_all x1, waiting for transfers between devices, body(): lax.all_to_all(send_rows.reshape(experts, per_pair, feature_width), 'ep',...  14.3 us
    all_to_all x1, waiting for transfers between devices, body(): lax.all_to_all(token_part.reshape(experts, per_pair, feature_width), 'ep'...  11.1 us
    dot_general x3, matrix products, rows_times(): lax.dot_general(left, right, (((1,), (1,)), ((), ())), preferred_element_...  10 us
    scatter x1, local copies, waits for them, and re-layouts, body(): source_index = jnp.full((total_slots,), assigned, jnp.int32).at[slot_inde...  8.04 us
    all_to_all x1, starting transfers between devices, body(): lax.all_to_all(send_rows.reshape(experts, per_pair, feature_width), 'ep',...  7.25 us
  transfers between devices with their start and end apart: 5, of which 5 were waited for; matrix products, arithmetic and copies ran while one was open for 19% of the time, Pallas kernels for 0%

commit v1 on v0

v1 whole, which is shorter than its diff:
```python
import jax
import jax.numpy as jnp
from jax import lax
from jax.sharding import PartitionSpec as P

STRIPE = 16


def silu_grad(value):
    sigmoid_value = jax.nn.sigmoid(value)
    return sigmoid_value * (1.0 + value * (1.0 - sigmoid_value))


def rows_times(left, right):
    return lax.dot_general(
        left, right, (((1,), (1,)), ((), ())), preferred_element_type=jnp.float32
    )


def inner_rows(left, right):
    return lax.dot_general(
        left, right, (((0,), (0,)), ((), ())), preferred_element_type=jnp.float32
    )


def matmul(left, right):
    return jnp.dot(left, right, preferred_element_type=jnp.float32)


def body(tokens, expert_ids, gate_weights, w_gate, w_up, w_down, out_grad):
    tok_count, feature_width = tokens.shape
    top_count = expert_ids.shape[1]
    experts = lax.axis_size("ep")
    per_pair = tok_count // 8
    total_slots = experts * per_pair
    live_cols = min(top_count, -(-experts // STRIPE))
    assigned = tok_count * live_cols

    flat_ids = expert_ids[:, :live_cols].reshape(-1)
    flat_gates = gate_weights[:, :live_cols].reshape(-1)
    live_mask = flat_ids < experts
    onehot = flat_ids[:, None] == jnp.arange(experts, dtype=jnp.int32)[None, :]
    position = jnp.arange(assigned, dtype=jnp.int32)
    earlier = (position[:, None] > position[None, :]).astype(jnp.bfloat16)
    before = matmul(earlier, onehot.astype(jnp.bfloat16))
    slot_rank = jnp.sum(jnp.where(onehot, before, 0.0), axis=1).astype(jnp.int32)
    slot_index = jnp.where(live_mask, flat_ids * per_pair + slot_rank, -1)

    slot_ids = jnp.arange(total_slots, dtype=jnp.int32)
    hit = slot_ids[:, None] == slot_index[None, :]
    slot_gate = jnp.sum(jnp.where(hit, flat_gates[None, :], 0.0), axis=1)
    pick = jnp.any(hit.reshape(total_slots, tok_count, live_cols), axis=2).astype(jnp.bfloat16)
    send_rows = matmul(pick, tokens).astype(jnp.bfloat16)
    grad_rows = matmul(pick, out_grad)
    scaled_grad = (slot_gate[:, None] * grad_rows).astype(jnp.bfloat16)

    outgoing = jnp.concatenate([send_rows, scaled_grad], axis=1)
    received = lax.all_to_all(
        outgoing.reshape(experts, per_pair, 2 * feature_width),
        "ep",
        split_axis=0,
        concat_axis=0,
        tiled=True,
    ).reshape(total_slots, 2 * feature_width)

    gathered = lax.all_gather(received, "rep", axis=0, tiled=True)

    rows_in = received[:, :feature_width]
    grad_in = received[:, feature_width:]
    gate_mat = w_gate[0]
    up_mat = w_up[0]
    down_mat = w_down[0]
    pre_gate = rows_times(rows_in, gate_mat)
    pre_up = rows_times(rows_in, up_mat)
    activated = jax.nn.silu(pre_gate)
    hidden = (activated * pre_up).astype(jnp.bfloat16)
    expert_out = matmul(hidden, down_mat).astype(jnp.bfloat16)
    returned = lax.all_to_all(
        expert_out.reshape(experts, per_pair, feature_width),
        "ep",
        split_axis=0,
        concat_axis=0,
        tiled=True,
    ).reshape(total_slots, feature_width)

    hidden_grad = rows_times(grad_in, down_mat)
    gate_pre_grad = (hidden_grad * pre_up * silu_grad(pre_gate)).astype(jnp.bfloat16)
    up_pre_grad = (hidden_grad * activated).astype(jnp.bfloat16)
    token_part = (
        matmul(gate_pre_grad, gate_mat) + matmul(up_pre_grad, up_mat)
    ).astype(jnp.bfloat16)
    part_back = lax.all_to_all(
        token_part.reshape(experts, per_pair, feature_width),
        "ep",
        split_axis=0,
        concat_axis=0,
        tiled=True,
    ).reshape(total_slots, feature_width)

    slot_grid = slot_index.reshape(tok_count, live_cols)
    gate_grid = flat_gates.reshape(tok_count, live_cols)
    layer_sum = jnp.zeros((tok_count, feature_width), jnp.float32)
    gate_cols = []
    back_pick = jnp.zeros((tok_count, total_slots), jnp.bfloat16)
    for col in range(live_cols):
        col_pick = (slot_grid[:, col : col + 1] == slot_ids[None, :]).astype(jnp.bfloat16)
        back_pick = back_pick + col_pick
        out_rows = matmul(col_pick, returned)
        layer_sum = layer_sum + gate_grid[:, col : col + 1] * out_rows
        gate_cols.append(jnp.sum(out_grad.astype(jnp.float32) * out_rows, axis=1))
    layer_out = layer_sum.astype(jnp.bfloat16)
    gate_cols.extend(
        [jnp.zeros((tok_count,), jnp.float32)] * (top_count - live_cols)
    )
    gates_grad = jnp.stack(gate_cols, axis=1)
    tokens_grad = matmul(back_pick, part_back).astype(jnp.bfloat16)

    share = gate_mat.shape[0] // lax.axis_size("rep")
    start = lax.axis_index("rep") * share
    gate_share = lax.dynamic_slice_in_dim(gate_mat, start, share, axis=0)
    up_share = lax.dynamic_slice_in_dim(up_mat, start, share, axis=0)
    down_share = lax.dynamic_slice_in_dim(down_mat, start, share, axis=0)
    rows_all = gathered[:, :feature_width]
    grad_all = gathered[:, feature_width:]
    pre_gate_s = rows_times(rows_all, gate_share)
    pre_up_s = rows_times(rows_all, up_share)
    activated_s = jax.nn.silu(pre_gate_s)
    hidden_s = (activated_s * pre_up_s).astype(jnp.bfloat16)
    hidden_grad_s = rows_times(grad_all, down_share)
    gate_pre_grad_s = (hidden_grad_s * pre_up_s * silu_grad(pre_gate_s)).astype(jnp.bfloat16)
    up_pre_grad_s = (hidden_grad_s * activated_s).astype(jnp.bfloat16)
    gate_w_grad = inner_rows(gate_pre_grad_s, rows_all).astype(jnp.bfloat16)[None]
    up_w_grad = inner_rows(up_pre_grad_s, rows_all).astype(jnp.bfloat16)[None]
    down_w_grad = inner_rows(hidden_s, grad_all).astype(jnp.bfloat16)[None]
    return (layer_out, tokens_grad, gates_grad, gate_w_grad, up_w_grad, down_w_grad)


def solution(mesh):
    return jax.shard_map(
        body,
        mesh=mesh,
        in_specs=(
            P(("rep", "ep"), None),
            P(("rep", "ep"), None),
            P(("rep", "ep"), None),
            P("ep", None, None),
            P("ep", None, None),
            P("ep", None, None),
            P(("rep", "ep"), None),
        ),
        out_specs=(
            P(("rep", "ep"), None),
            P(("rep", "ep"), None),
            P(("rep", "ep"), None),
            P("ep", "rep", None),
            P("ep", "rep", None),
            P("ep", "rep", None),
        ),
        check_vma=False,
    )
```

time: 262 us -> 160 us (0.61)
  waiting for transfers between devices: 133 us -> 38.7 us
  blocking collectives: 0 us -> 55.4 us
  other arithmetic: 32.8 us -> 1.71 us
  local copies, waits for them, and re-layouts: 34 us -> 4.27 us
  starting transfers between devices: 20.2 us -> 8.71 us
  matrix products: 26.8 us -> 36.6 us
    reduce_scatter x1 -> x0, waiting for transfers between devices: 66.4 us -> none  [body(): lax.psum_scatter(jnp.concatenate([inner_rows(gate_pre_grad, received), in...]
    all_to_all x0 -> x1, blocking collectives: none -> 55.4 us  [body(): lax.all_to_all(outgoing.reshape(experts, per_pair, 2 * feature_width), 'e...]
    all_to_all x2 -> x0, waiting for transfers between devices: 35.6 us -> none  [the longest x1 21.3 us: body(): lax.all_to_all(scaled_grad.reshape(experts, per_pair, feature_width), 'ep...]
    scatter-add x3 -> x0, other arithmetic: 14.7 us -> none  [the longest x1 6.21 us: body(): layer_sum = jnp.zeros((tok_count + 1, feature_width), jnp.float32).at[slo...]
    all_to_all x2 -> x0, starting transfers between devices: 11.5 us -> none  [the longest x1 7.25 us: body(): lax.all_to_all(send_rows.reshape(experts, per_pair, feature_width), 'ep',...]
    gather x3 -> x0, local copies, waits for them, and re-layouts: 11.2 us -> none  [the longest x1 4.74 us: body(): send_rows = jnp.concatenate([tokens, blank_row], axis=0)[slot_token]]
    all_to_all x1, waiting for transfers between devices: 11.1 us -> 20.4 us  [body(): lax.all_to_all(token_part.reshape(experts, per_pair, feature_width), 'ep'...]
    scatter x1 -> x0, local copies, waits for them, and re-layouts: 8.04 us -> none  [body(): source_index = jnp.full((total_slots,), assigned, jnp.int32).at[slot_inde...]
  transfers between devices with their start and end apart: 5 -> 3, of which waited for: 5 -> 2; matrix products, arithmetic and copies ran while one was open for 19% -> 12% of each run, Pallas kernels for 0% -> 0%
where the time goes in v1:
time: 160 us
  blocking collectives  55.4 us (35%)
  waiting for transfers between devices  38.7 us (24%)
  matrix products  36.6 us (23%)
  between operations  14.2 us (9%)
  starting transfers between devices  8.71 us (5%)
  local copies, waits for them, and re-layouts  4.27 us (3%)
  other arithmetic  1.71 us (1%)
    all_to_all x1, blocking collectives, body(): lax.all_to_all(outgoing.reshape(experts, per_pair, 2 * feature_width), 'e...  55.4 us
    all_to_all x1, waiting for transfers between devices, body(): lax.all_to_all(token_part.reshape(experts, per_pair, feature_width), 'ep'...  20.4 us
    all_to_all x1, waiting for transfers between devices, body(): lax.all_to_all(expert_out.reshape(experts, per_pair, feature_width), 'ep'...  18.2 us
    dot_general x6, matrix products, rows_times(): lax.dot_general(left, right, (((1,), (1,)), ((), ())), preferred_element_...  16.1 us
    dot_general x8, matrix products, matmul(): return jnp.dot(left, right, preferred_element_type=jnp.float32)  14.6 us
    dot_general x3, matrix products, inner_rows(): lax.dot_general(left, right, (((0,), (0,)), ((), ())), preferred_element_...  5.88 us
    all_to_all x1, starting transfers between devices, body(): lax.all_to_all(token_part.reshape(experts, per_pair, feature_width), 'ep'...  4.42 us
    all_to_all x1, starting transfers between devices, body(): lax.all_to_all(expert_out.reshape(experts, per_pair, feature_width), 'ep'...  4.25 us
  transfers between devices with their start and end apart: 3, of which 2 were waited for; matrix products, arithmetic and copies ran while one was open for 12% of the time, Pallas kernels for 0%

profile of v1, /device:TPU:0, one launch (start us, length us, event | category | flops | bytes accessed | tf_op | source)
XLA Modules:
  0.0 159.6 jit_solution(12996164338905576264)
XLA Ops:
  7.2 0.0 copy-start
  7.2 0.0 all-gather.2.cloned.1.call-start
  7.2 0.9 slice.19
  8.1 0.2 fusion.52
  8.3 0.7 slice.18
  9.0 0.1 select_reduce_fusion
  9.1 1.7 %convolution_convert_fusion.1 = bf16[256,2048]{1,0:T(8,128)(2,1)S(1)} fusion(bf16[256,2048]{1,0:T(8,128)(2,1)} %param.7, s32[256]{0:T(256)S(1)} %compare_select_fusion.1), kind=kOutput, calls=%fused_computation.29 | convolution fusion | flops 269025280 | bytes 2098176 | tf_op jit(solution)/shard_map/dot_general | solution.py:27
  10.8 1.7 %fusion.30 = bf16[256,2048]{1,0:T(8,128)(2,1)S(1)} fusion(bf16[256,2048]{1,0:T(8,128)(2,1)} %param.13, f32[256]{0:T(256)S(1)} %select_reduce_fusion, s32[256]{0:T(256)S(1)} %compare_select_fusion.1), kind=kOutput, calls=%fused_computation.27 | convolution fusion | flops 269549568 | bytes 2099200 | tf_op jit(solution)/shard_map/dot_general | solution.py:27
  12.5 0.2 pad_maximum_fusion
  12.7 55.4 %all_to_all.15 = bf16[8,32,4096]{2,1,0:T(8,128)(2,1)} all-to-all(bf16[8,32,4096]{2,1,0:T(8,128)(2,1)S(1)} %bitcast.56), channel_id=1, replica_groups=mesh['rep'=4,'ep'=8] {'ep'}, dimensions={0} | all-to-all | bytes 4194304 | tf_op jit(solution)/shard_map/all_to_all | solution.py:58
  68.1 0.0 all-gather.2.cloned.1.call-update
  68.1 0.0 copy-done
  68.1 0.0 copy-start.1
  68.1 0.0 copy-start.4
  68.1 2.4 %fusion.14 = f32[256,768]{1,0:T(8,128)S(1)} fusion(bf16[1,768,2048]{2,1,0:T(8,128)(2,1)S(1)} %copy-done, bf16[256,4096]{1,0:T(8,128)(2,1)} %bitcast.53), kind=kOutput, calls=%fused_computation.14 | convolution fusion | flops 805306368 | bytes 4980736 | tf_op jit(solution)/shard_map/dot_general | solution.py:15
  70.5 0.0 copy-done.1
  70.5 0.4 copy-done.4
  70.9 0.0 copy-start.6
  71.0 0.0 copy-start.3
  71.0 1.0 fusion.10
  72.0 1.2 copy-done.3
  73.2 0.0 copy-start.8
  73.2 2.0 %fusion.31 = bf16[256,2048]{1,0:T(8,128)(2,1)} fusion(bf16[1,768,2048]{2,1,0:T(8,128)(2,1)S(1)} %copy-done.3, f32[256,768]{1,0:T(8,128)S(1)} %fusion.10, f32[256,768]{1,0:T(8,128)S(1)} %fusion.14), kind=kOutput, calls=%fused_computation.30 | convolution fusion | flops 807010304 | bytes 5767168 | tf_op jit(solution)/shard_map/dot_general | solution.py:27
  75.2 0.0 copy-done.6
  75.2 0.0 copy-done.8
  75.2 4.3 %all-to-all-start.1 = ((bf16[8,32,2048]{2,1,0:T(8,128)(2,1)}), bf16[8,32,2048]{2,1,0:T(8,128)(2,1)}, u32[]{:S(2)}, u32[]{:S(2)}) async-start(bf16[8,32,2048]{2,1,0:T(8,128)(2,1)} %bitcast.58), calls=%async_computation.1 | async-start | bytes 2097152 | tf_op jit(solution)/shard_map/all_to_all | solution.py:78
  79.4 0.0 copy-start.5
  79.4 0.0 copy-start.7
  79.5 3.5 %fusion.4 = f32[256,768]{1,0:T(8,128)S(1)} fusion(bf16[1,768,2048]{2,1,0:T(8,128)(2,1)} %param.12, bf16[256,4096]{1,0:T(8,128)(2,1)} %bitcast.54), kind=kOutput, calls=%fused_computation.4 | convolution fusion | flops 805306368 | bytes 4980736 | tf_op jit(solution)/shard_map/dot_general | solution.py:15
  82.9 0.0 copy-done.5
  83.0 0.0 copy-done.7
  83.0 0.0 copy-start.9
  83.0 1.0 fusion.8
  84.0 0.1 copy-done.9
  84.1 2.2 %fusion.27 = bf16[256,2048]{1,0:T(8,128)(2,1)} fusion(f32[256,2048]{1,0:T(8,128)S(1)} %fusion.8, bf16[1,768,2048]{2,1,0:T(8,128)(2,1)S(1)} %copy-done, f32[256,768]{1,0:T(8,128)S(1)} %copy-done.7, f32[256,768]{1,0:T(8,128)S(1)} %fusion.4, f32[256,768]{1,0:T(8,128)S(1)} %copy-done.9), kind=kOutput, calls=%fused_computation.26 | convolution fusion | flops 808321024 | bytes 8650752 | tf_op jit(solution)/shard_map/dot_general | solution.py:27
  86.3 18.2 %all-to-all-done.1 = bf16[8,32,2048]{2,1,0:T(8,128)(2,1)} async-done(((bf16[8,32,2048]{2,1,0:T(8,128)(2,1)}), bf16[8,32,2048]{2,1,0:T(8,128)(2,1)}, u32[]{:S(2)}, u32[]{:S(2)}) %all-to-all-start.1) | async-done | bytes 1048608 | tf_op jit(solution)/shard_map/all_to_all | solution.py:78
  104.5 4.4 %all-to-all-start.2 = ((bf16[8,32,2048]{2,1,0:T(8,128)(2,1)}), bf16[8,32,2048]{2,1,0:T(8,128)(2,1)}, u32[]{:S(2)}, u32[]{:S(2)}) async-start(bf16[8,32,2048]{2,1,0:T(8,128)(2,1)} %bitcast.57), calls=%async_computation.2 | async-start | bytes 2097152 | tf_op jit(solution)/shard_map/all_to_all | solution.py:92
  109.0 0.1 pad.2.clone
  109.1 0.1 pad.3.clone
  109.2 0.1 pad.1.clone
  109.2 0.7 compare_select_fusion
  109.9 3.1 %multiply_reduce_fusion = (f32[256]{0:T(256)S(1)}, bf16[256,2048]{1,0:T(8,128)(2,1)}) fusion(bf16[256,2048]{1,0:T(8,128)(2,1)} %param.13, f32[256]{0:T(256)S(1)} %bitcast.62, bf16[256,2048]{1,0:T(8,128)(2,1)} %bitcast.10, s32[256]{0:T(256)S(1)} %bitcast.59), kind=kOutput, calls=%fused_computation.38 | convolution fusion | flops 271122176 | bytes 3148800 | tf_op jit(solution)/shard_map/dot_general | solution.py:27
  113.1 0.7 maximum_maximum_fusion
  113.8 20.4 %all-to-all-done.2 = bf16[8,32,2048]{2,1,0:T(8,128)(2,1)} async-done(((bf16[8,32,2048]{2,1,0:T(8,128)(2,1)}), bf16[8,32,2048]{2,1,0:T(8,128)(2,1)}, u32[]{:S(2)}, u32[]{:S(2)}) %all-to-all-start.2) | async-done | bytes 1048608 | tf_op jit(solution)/shard_map/all_to_all | solution.py:92
  134.2 2.7 %convolution_convert_fusion = bf16[256,2048]{1,0:T(8,128)(2,1)} fusion(bf16[256,2048]{1,0:T(8,128)(2,1)} %bitcast.12, s32[256]{0:T(256)S(1)} %bitcast.60), kind=kOutput, calls=%fused_computation.28 | convolution fusion | flops 269025280 | bytes 2098176 | tf_op jit(solution)/shard_map/dot_general | solution.py:27
  136.9 0.0 all-gather.2.cloned.1.call-done
  136.9 0.0 copy-start.2
  136.9 3.9 %fusion.23 = f32[1024,192]{0,1:T(8,128)S(1)} fusion(bf16[1024,4096]{1,0:T(8,128)(2,1)} %all-gather.2.cloned.1.call-done, bf16[1,768,2048]{2,1,0:T(8,128)(2,1)S(1)} %copy-done, s32[]{:T(128)S(6)} %select_n.28), kind=kOutput, calls=%fused_computation.22 | convolution fusion | flops 805306368 | bytes 5767172 | tf_op jit(solution)/shard_map/dot_general | solution.py:15
  140.8 0.8 copy-done.2
  141.5 2.7 %fusion.2 = f32[1024,192]{0,1:T(8,128)S(1)} fusion(bf16[1024,4096]{1,0:T(8,128)(2,1)S(1)} %copy-done.2, bf16[1,768,2048]{2,1,0:T(8,128)(2,1)} %param.12, s32[]{:T(128)S(6)} %select_n.28), kind=kOutput, calls=%fused_computation.2 | convolution fusion | flops 805306368 | bytes 5767172 | tf_op jit(solution)/shard_map/dot_general | solution.py:15
  144.2 2.7 %fusion.25 = f32[1024,192]{0,1:T(8,128)S(1)} fusion(bf16[1024,4096]{1,0:T(8,128)(2,1)S(1)} %copy-done.2, bf16[1,768,2048]{2,1,0:T(8,128)(2,1)} %param.11, s32[]{:T(128)S(6)} %select_n.28), kind=kOutput, calls=%fused_computation.24 | convolution fusion | flops 805306368 | bytes 5767172 | tf_op jit(solution)/shard_map/dot_general | solution.py:15
  146.9 1.9 %fusion.43 = bf16[1,192,2048]{2,1,0:T(8,128)(2,1)} fusion(bf16[1024,4096]{1,0:T(8,128)(2,1)S(1)} %copy-done.2, f32[1024,192]{0,1:T(8,128)S(1)} %fusion.25, f32[1024,192]{0,1:T(8,128)S(1)} %fusion.23), kind=kOutput, calls=%fused_computation.34 | convolution fusion | flops 806879232 | bytes 6553600 | tf_op jit(solution)/shard_map/dot_general | solution.py:21
  148.8 2.0 %fusion.49 = bf16[1,192,2048]{2,1,0:T(8,128)(2,1)} fusion(bf16[1024,4096]{1,0:T(8,128)(2,1)S(1)} %copy-done.2, f32[1024,192]{0,1:T(8,128)S(1)} %fusion.23, f32[1024,192]{0,1:T(8,128)S(1)} %fusion.2, f32[1024,192]{0,1:T(8,128)S(1)} %fusion.25), kind=kOutput, calls=%fused_computation.36 | convolution fusion | flops 807665664 | bytes 7340032 | tf_op jit(solution)/shard_map/dot_general | solution.py:21
  150.8 1.9 %fusion.46 = bf16[1,192,2048]{2,1,0:T(8,128)(2,1)} fusion(bf16[1024,4096]{1,0:T(8,128)(2,1)S(1)} %copy-done.2, f32[1024,192]{0,1:T(8,128)S(1)} %fusion.2, f32[1024,192]{0,1:T(8,128)S(1)} %fusion.23), kind=kOutput, calls=%fused_computation.35 | convolution fusion | flops 806879232 | bytes 6553600 | tf_op jit(solution)/shard_map/dot_general | solution.py:21
  (4 shorter events, 0.0 us)
Async XLA Ops:
  7.2 60.9 %copy-start = (bf16[1,768,2048]{2,1,0:T(8,128)(2,1)S(1)}, bf16[1,768,2048]{2,1,0:T(8,128)(2,1)}, u32[]{:S(2)}) copy-start(bf16[1,768,2048]{2,1,0:T(8,128)(2,1)} %param.10) | copy-start | bytes 9437188
  7.2 129.7 %all-gather.2.cloned.1.call-start = ((), (), s32[]{:S(2)}) async-start(), calls=%async_computation.3 | async-start | bytes 10485760 | tf_op jit(solution)/shard_map/all_gather | solution.py:66
  68.1 2.4 %copy-start.1 = (bf16[8,32,4096]{2,1,0:T(8,128)(2,1)S(1)}, bf16[8,32,4096]{2,1,0:T(8,128)(2,1)}, u32[]{:S(2)}) copy-start(bf16[8,32,4096]{2,1,0:T(8,128)(2,1)} %all_to_all.15) | copy-start | bytes 6291460
  68.1 2.8 %copy-start.4 = (bf16[1,768,2048]{2,1,0:T(8,128)(2,1)S(1)}, bf16[1,768,2048]{2,1,0:T(8,128)(2,1)}, u32[]{:S(2)}) copy-start(bf16[1,768,2048]{2,1,0:T(8,128)(2,1)} %param.11) | copy-start | bytes 9437188
  70.9 4.2 %copy-start.6 = (f32[256,768]{1,0:T(8,128)}, f32[256,768]{1,0:T(8,128)S(1)}, u32[]{:S(2)}) copy-start(f32[256,768]{1,0:T(8,128)S(1)} %fusion.14) | copy-start | bytes 2359300
  71.0 2.2 %copy-start.3 = (bf16[1,768,2048]{2,1,0:T(8,128)(2,1)S(1)}, bf16[1,768,2048]{2,1,0:T(8,128)(2,1)}, u32[]{:S(2)}) copy-start(bf16[1,768,2048]{2,1,0:T(8,128)(2,1)} %param.12) | copy-start | bytes 9437188
  73.2 2.0 %copy-start.8 = (f32[256,768]{1,0:T(8,128)}, f32[256,768]{1,0:T(8,128)S(1)}, u32[]{:S(2)}) copy-start(f32[256,768]{1,0:T(8,128)S(1)} %fusion.10) | copy-start | bytes 2359300
  75.2 29.4 %all-to-all-start.1 = ((bf16[8,32,2048]{2,1,0:T(8,128)(2,1)}), bf16[8,32,2048]{2,1,0:T(8,128)(2,1)}, u32[]{:S(2)}, u32[]{:S(2)}) async-start(bf16[8,32,2048]{2,1,0:T(8,128)(2,1)} %bitcast.58), calls=%async_computation.1 | async-start | bytes 2097152 | tf_op jit(solution)/shard_map/all_to_all | solution.py:78
  79.4 3.5 %copy-start.5 = (bf16[1,768,2048]{2,1,0:T(8,128)(2,1)S(1)}, bf16[1,768,2048]{2,1,0:T(8,128)(2,1)}, u32[]{:S(2)}) copy-start(bf16[1,768,2048]{2,1,0:T(8,128)(2,1)} %param.11) | copy-start | bytes 9437188
  79.4 3.5 %copy-start.7 = (f32[256,768]{1,0:T(8,128)S(1)}, f32[256,768]{1,0:T(8,128)}, u32[]{:S(2)}) copy-start(f32[256,768]{1,0:T(8,128)} %copy-done.6) | copy-start | bytes 2359300
  83.0 1.1 copy-start.9
  104.5 29.7 %all-to-all-start.2 = ((bf16[8,32,2048]{2,1,0:T(8,128)(2,1)}), bf16[8,32,2048]{2,1,0:T(8,128)(2,1)}, u32[]{:S(2)}, u32[]{:S(2)}) async-start(bf16[8,32,2048]{2,1,0:T(8,128)(2,1)} %bitcast.57), calls=%async_computation.2 | async-start | bytes 2097152 | tf_op jit(solution)/shard_map/all_to_all | solution.py:92
  136.9 4.6 %copy-start.2 = (bf16[1024,4096]{1,0:T(8,128)(2,1)S(1)}, bf16[1024,4096]{1,0:T(8,128)(2,1)}, u32[]{:S(2)}) copy-start(bf16[1024,4096]{1,0:T(8,128)(2,1)} %all-gather.2.cloned.1.call-done) | copy-start | bytes 25165828
Sparse Core Ops, SparseCore 0:
  68.2 57.3 all-gather.1

commit v2 on v1

--- a/solution.py
+++ b/solution.py
@@ -54,19 +54,20 @@
     grad_rows = matmul(pick, out_grad)
     scaled_grad = (slot_gate[:, None] * grad_rows).astype(jnp.bfloat16)
 
-    outgoing = jnp.concatenate([send_rows, scaled_grad], axis=1)
-    received = lax.all_to_all(
-        outgoing.reshape(experts, per_pair, 2 * feature_width),
-        "ep",
-        split_axis=0,
-        concat_axis=0,
-        tiled=True,
-    ).reshape(total_slots, 2 * feature_width)
+    def exchange(rows):
+        return lax.all_to_all(
+            rows.reshape(experts, per_pair, feature_width),
+            "ep",
+            split_axis=0,
+            concat_axis=0,
+            tiled=True,
+        ).reshape(total_slots, feature_width)
 
-    gathered = lax.all_gather(received, "rep", axis=0, tiled=True)
+    rows_in = exchange(send_rows)
+    rows_all = lax.all_gather(rows_in, "rep", axis=0, tiled=True)
+    grad_in = exchange(scaled_grad)
+    grad_all = lax.all_gather(grad_in, "rep", axis=0, tiled=True)
 
-    rows_in = received[:, :feature_width]
-    grad_in = received[:, feature_width:]
     gate_mat = w_gate[0]
     up_mat = w_up[0]
     down_mat = w_down[0]
@@ -75,13 +76,8 @@
     activated = jax.nn.silu(pre_gate)
     hidden = (activated * pre_up).astype(jnp.bfloat16)
     expert_out = matmul(hidden, down_mat).astype(jnp.bfloat16)
-    returned = lax.all_to_all(
-        expert_out.reshape(experts, per_pair, feature_width),
-        "ep",
-        split_axis=0,
-        concat_axis=0,
-        tiled=True,
-    ).reshape(total_slots, feature_width)
+    expert_out, rows_all = lax.optimization_barrier((expert_out, rows_all))
+    returned = exchange(expert_out)
 
     hidden_grad = rows_times(grad_in, down_mat)
     gate_pre_grad = (hidden_grad * pre_up * silu_grad(pre_gate)).astype(jnp.bfloat16)
@@ -89,13 +85,8 @@
     token_part = (
         matmul(gate_pre_grad, gate_mat) + matmul(up_pre_grad, up_mat)
     ).astype(jnp.bfloat16)
-    part_back = lax.all_to_all(
-        token_part.reshape(experts, per_pair, feature_width),
-        "ep",
-        split_axis=0,
-        concat_axis=0,
-        tiled=True,
-    ).reshape(total_slots, feature_width)
+    token_part, grad_all = lax.optimization_barrier((token_part, grad_all))
+    part_back = exchange(token_part)
 
     slot_grid = slot_index.reshape(tok_count, live_cols)
     gate_grid = flat_gates.reshape(tok_count, live_cols)
@@ -120,8 +111,6 @@
     gate_share = lax.dynamic_slice_in_dim(gate_mat, start, share, axis=0)
     up_share = lax.dynamic_slice_in_dim(up_mat, start, share, axis=0)
     down_share = lax.dynamic_slice_in_dim(down_mat, start, share, axis=0)
-    rows_all = gathered[:, :feature_width]
-    grad_all = gathered[:, feature_width:]
     pre_gate_s = rows_times(rows_all, gate_share)
     pre_up_s = rows_times(rows_all, up_share)
     activated_s = jax.nn.silu(pre_gate_s)

time: 160 us -> 165 us (1.031)
  blocking collectives: 55.4 us -> 61.9 us
  waiting for transfers between devices: 38.7 us -> 33.1 us
  matrix products: 36.6 us -> 40.6 us
    all_to_all x2, waiting for transfers between devices: 38.7 us -> 13.1 us  [exchange(): lax.all_to_all(rows.reshape(experts, per_pair, feature_width), 'ep', spli...]
    all_gather x1 -> x2, waiting for transfers between devices: 0.01 us -> 20 us  [the longest x1 20 us: body(): rows_all = lax.all_gather(rows_in, 'rep', axis=0, tiled=True)]
    all_to_all x1 -> x2, blocking collectives: 55.4 us -> 61.9 us  [exchange(): lax.all_to_all(rows.reshape(experts, per_pair, feature_width), 'ep', spli...]
    dot_general x8, matrix products: 14.6 us -> 16.9 us  [matmul(): return jnp.dot(left, right, preferred_element_type=jnp.float32)]
    dot_general x6, matrix products: 16.1 us -> 17.8 us  [rows_times(): lax.dot_general(left, right, (((1,), (1,)), ((), ())), preferred_element_...]
  transfers between devices with their start and end apart: 3 -> 4, of which waited for: 2 -> 2; matrix products, arithmetic and copies ran while one was open for 12% -> 22% of each run, Pallas kernels for 0% -> 0%
where the time goes in v2:
time: 165 us; the launch traced here: 164 us
  blocking collectives  61.9 us (38%)
  matrix products  40.6 us (25%)
  waiting for transfers between devices  33.1 us (20%)
  between operations  14.3 us (9%)
  starting transfers between devices  9.79 us (6%)
  local copies, waits for them, and re-layouts  3.22 us (2%)
    all_to_all x2, blocking collectives, exchange(): lax.all_to_all(rows.reshape(experts, per_pair, feature_width), 'ep', spli...  61.9 us
    all_gather x1, waiting for transfers between devices, body(): rows_all = lax.all_gather(rows_in, 'rep', axis=0, tiled=True)  20 us
    dot_general x6, matrix products, rows_times(): lax.dot_general(left, right, (((1,), (1,)), ((), ())), preferred_element_...  17.8 us
    dot_general x8, matrix products, matmul(): return jnp.dot(left, right, preferred_element_type=jnp.float32)  16.9 us
    all_to_all x2, waiting for transfers between devices, exchange(): lax.all_to_all(rows.reshape(experts, per_pair, feature_width), 'ep', spli...  13.1 us
    all_to_all x2, starting transfers between devices, exchange(): lax.all_to_all(rows.reshape(experts, per_pair, feature_width), 'ep', spli...  9.71 us
    dot_general x3, matrix products, inner_rows(): lax.dot_general(left, right, (((0,), (0,)), ((), ())), preferred_element_...  5.87 us
  transfers between devices with their start and end apart: 4, of which 2 were waited for; matrix products, arithmetic and copies ran while one was open for 22% of the time, Pallas kernels for 0%

profile of v2, /device:TPU:0, one launch (start us, length us, event | category | flops | bytes accessed | tf_op | source)
XLA Modules:
  0.0 164.3 jit_solution(10896555405209462706)
XLA Ops:
  7.2 0.0 copy-start
  7.2 0.0 all-gather.5.cloned.1.call-start
  7.2 0.9 slice.7
  8.1 0.2 fusion.25
  8.3 0.7 slice.6
  9.0 0.1 select_reduce_fusion
  9.1 1.7 %fusion.18 = bf16[256,2048]{1,0:T(8,128)(2,1)S(1)} fusion(bf16[256,2048]{1,0:T(8,128)(2,1)} %param.13, f32[256]{0:T(256)S(1)} %select_reduce_fusion, s32[256]{0:T(256)S(1)} %compare_select_fusion.1), kind=kOutput, calls=%fused_computation.15 | convolution fusion | flops 269549568 | bytes 2099200 | tf_op jit(solution)/shard_map/dot_general | solution.py:27
  10.8 32.9 %all_to_all.20 = bf16[8,32,2048]{2,1,0:T(8,128)(2,1)} all-to-all(bf16[8,32,2048]{2,1,0:T(8,128)(2,1)S(1)} %bitcast.63), channel_id=1, replica_groups=mesh['rep'=4,'ep'=8] {'ep'}, dimensions={0} | all-to-all | bytes 2097152 | tf_op jit(solution)/shard_map/all_to_all | solution.py:58
  43.7 0.0 all-gather.5.cloned.1.call-update
  43.7 0.0 all-gather.3.cloned.1.call-start
  43.8 1.7 %convolution_convert_fusion.1 = bf16[256,2048]{1,0:T(8,128)(2,1)S(1)} fusion(bf16[256,2048]{1,0:T(8,128)(2,1)} %param.7, s32[256]{0:T(256)S(1)} %compare_select_fusion.1), kind=kOutput, calls=%fused_computation.17 | convolution fusion | flops 269025280 | bytes 2098176 | tf_op jit(solution)/shard_map/dot_general | solution.py:27
  45.5 29.0 %all_to_all.21 = bf16[8,32,2048]{2,1,0:T(8,128)(2,1)} all-to-all(bf16[8,32,2048]{2,1,0:T(8,128)(2,1)S(1)} %bitcast.69), channel_id=1, replica_groups=mesh['rep'=4,'ep'=8] {'ep'}, dimensions={0} | all-to-all | bytes 2097152 | tf_op jit(solution)/shard_map/all_to_all | solution.py:58
  74.4 0.0 all-gather.3.cloned.1.call-update
  74.5 0.0 copy-start.1
  74.5 3.3 %fusion = f32[256,768]{1,0:T(8,128)S(1)} fusion(bf16[256,2048]{1,0:T(8,128)(2,1)} %bitcast.68, bf16[1,768,2048]{2,1,0:T(8,128)(2,1)} %param.12), kind=kOutput, calls=%fused_computation | convolution fusion | flops 805306368 | bytes 4980736 | tf_op jit(solution)/shard_map/dot_general | solution.py:15
  77.8 0.0 copy-done
  77.8 0.0 copy-done.1
  77.8 0.0 copy-start.5
  77.8 1.0 fusion.10
  78.8 0.9 copy-done.5
  79.7 0.0 copy-start.8
  79.7 1.0 fusion.6
  80.7 0.0 copy-start.9
  80.7 1.0 fusion.4
  81.8 0.0 copy-done.8
  81.8 0.0 copy-done.9
  81.8 2.2 %fusion.15 = bf16[256,2048]{1,0:T(8,128)(2,1)} fusion(f32[256,2048]{1,0:T(8,128)S(1)} %fusion.4, bf16[1,768,2048]{2,1,0:T(8,128)(2,1)S(1)} %copy-done, f32[256,768]{1,0:T(8,128)S(1)} %fusion.10, f32[256,768]{1,0:T(8,128)S(1)} %fusion, f32[256,768]{1,0:T(8,128)S(1)} %fusion.6), kind=kOutput, calls=%fused_computation.14 | convolution fusion | flops 808321024 | bytes 8650752 | tf_op jit(solution)/shard_map/dot_general | solution.py:27
  84.0 0.0 all-gather.5.cloned.1.call-done
  84.0 4.3 %all-to-all-start.3 = ((bf16[8,32,2048]{2,1,0:T(8,128)(2,1)}), bf16[8,32,2048]{2,1,0:T(8,128)(2,1)}, u32[]{:S(2)}, u32[]{:S(2)}) async-start(bf16[8,32,2048]{2,1,0:T(8,128)(2,1)} %bitcast.70), calls=%async_computation.3 | async-start | bytes 2097152 | tf_op jit(solution)/shard_map/all_to_all | solution.py:58
  88.3 0.1 pad.2.clone
  88.4 0.1 pad.3.clone
  88.4 0.1 pad.1.clone
  88.5 0.7 compare_select_fusion
  89.2 4.4 %fusion.19 = bf16[256,2048]{1,0:T(8,128)(2,1)} fusion(bf16[1,768,2048]{2,1,0:T(8,128)(2,1)} %param.12, f32[256,768]{1,0:T(8,128)} %copy-done.9, f32[256,768]{1,0:T(8,128)} %copy-done.8), kind=kOutput, calls=%fused_computation.18 | convolution fusion | flops 807010304 | bytes 5767168 | tf_op jit(solution)/shard_map/dot_general | solution.py:27
  93.6 20.0 %all-gather.3.cloned.1.call-done = bf16[1024,2048]{1,0:T(8,128)(2,1)} async-done(((bf16[256,2048]{1,0:T(8,128)(2,1)}), bf16[1024,2048]{1,0:T(8,128)(2,1)}) %all-gather.3.cloned.1.call-update) | async-done | bytes 4194320 | tf_op jit(solution)/shard_map/all_gather | solution.py:67
  113.6 0.0 copy-start.3
  113.6 4.7 %fusion.26 = f32[1024,192]{0,1:T(8,128)} fusion(bf16[1024,2048]{1,0:T(8,128)(2,1)} %all-gather.3.cloned.1.call-done, bf16[1,768,2048]{2,1,0:T(8,128)(2,1)S(1)} %copy-done, s32[]{:T(128)S(6)} %select_n.28), kind=kOutput, calls=%fused_computation.29 | convolution fusion | flops 805306368 | bytes 5767172 | tf_op jit(solution)/shard_map/dot_general | solution.py:15
  118.3 0.0 copy-done.3
  118.3 3.6 %fusion.28 = f32[1024,192]{0,1:T(8,128)} fusion(bf16[1024,2048]{1,0:T(8,128)(2,1)S(1)} %copy-done.3, bf16[1,768,2048]{2,1,0:T(8,128)(2,1)} %param.11, s32[]{:T(128)S(6)} %select_n.28), kind=kOutput, calls=%fused_computation.31 | convolution fusion | flops 805306368 | bytes 5767172 | tf_op jit(solution)/shard_map/dot_general | solution.py:15
  121.9 0.0 all-to-all-done.3
  121.9 5.4 %all-to-all-start.1 = ((bf16[8,32,2048]{2,1,0:T(8,128)(2,1)}), bf16[8,32,2048]{2,1,0:T(8,128)(2,1)}, u32[]{:S(2)}, u32[]{:S(2)}) async-start(bf16[8,32,2048]{2,1,0:T(8,128)(2,1)} %bitcast.71), calls=%async_computation.1 | async-start | bytes 2097152 | tf_op jit(solution)/shard_map/all_to_all | solution.py:58
  127.4 0.0 copy-start.2
  127.4 0.0 copy-start.6
  127.4 0.0 copy-start.7
  127.4 4.1 %fusion.30 = f32[1024,192]{0,1:T(8,128)S(1)} fusion(bf16[1024,2048]{1,0:T(8,128)(2,1)} %all-gather.5.cloned.1.call-done, bf16[1,768,2048]{2,1,0:T(8,128)(2,1)} %param.12, s32[]{:T(128)S(6)} %select_n.28), kind=kOutput, calls=%fused_computation.33 | convolution fusion | flops 805306368 | bytes 5767172 | tf_op jit(solution)/shard_map/dot_general | solution.py:15
  131.5 0.0 copy-done.2
  131.5 0.0 copy-done.6
  131.5 0.0 copy-done.7
  131.5 0.0 copy-start.4
  131.5 1.9 %fusion.24 = bf16[1,192,2048]{2,1,0:T(8,128)(2,1)} fusion(bf16[1024,2048]{1,0:T(8,128)(2,1)S(1)} %copy-done.2, f32[1024,192]{0,1:T(8,128)S(1)} %copy-done.7, f32[1024,192]{0,1:T(8,128)S(1)} %copy-done.6), kind=kOutput, calls=%fused_computation.24 | convolution fusion | flops 806879232 | bytes 6553600 | tf_op jit(solution)/shard_map/dot_general | solution.py:21
  133.5 0.5 copy-done.4
  134.0 1.9 %fusion.23 = bf16[1,192,2048]{2,1,0:T(8,128)(2,1)} fusion(bf16[1024,2048]{1,0:T(8,128)(2,1)S(1)} %copy-done.4, f32[1024,192]{0,1:T(8,128)S(1)} %fusion.30, f32[1024,192]{0,1:T(8,128)S(1)} %copy-done.6), kind=kOutput, calls=%fused_computation.23 | convolution fusion | flops 806879232 | bytes 6553600 | tf_op jit(solution)/shard_map/dot_general | solution.py:21
  135.9 2.0 %fusion.22 = bf16[1,192,2048]{2,1,0:T(8,128)(2,1)} fusion(bf16[1024,2048]{1,0:T(8,128)(2,1)S(1)} %copy-done.4, f32[1024,192]{0,1:T(8,128)S(1)} %copy-done.6, f32[1024,192]{0,1:T(8,128)S(1)} %fusion.30, f32[1024,192]{0,1:T(8,128)S(1)} %copy-done.7), kind=kOutput, calls=%fused_computation.22 | convolution fusion | flops 807665664 | bytes 7340032 | tf_op jit(solution)/shard_map/dot_general | solution.py:21
  137.9 2.7 %convolution_convert_fusion = bf16[256,2048]{1,0:T(8,128)(2,1)} fusion(bf16[256,2048]{1,0:T(8,128)(2,1)} %bitcast.14, s32[256]{0:T(256)S(1)} %bitcast.72), kind=kOutput, calls=%fused_computation.16 | convolution fusion | flops 269025280 | bytes 2098176 | tf_op jit(solution)/shard_map/dot_general | solution.py:27
  140.6 13.1 %all-to-all-done.1 = bf16[8,32,2048]{2,1,0:T(8,128)(2,1)} async-done(((bf16[8,32,2048]{2,1,0:T(8,128)(2,1)}), bf16[8,32,2048]{2,1,0:T(8,128)(2,1)}, u32[]{:S(2)}, u32[]{:S(2)}) %all-to-all-start.1) | async-done | bytes 1048608 | tf_op jit(solution)/shard_map/all_to_all | solution.py:58
  153.7 3.1 %multiply_reduce_fusion = (f32[256]{0:T(256)S(1)}, bf16[256,2048]{1,0:T(8,128)(2,1)}) fusion(bf16[256,2048]{1,0:T(8,128)(2,1)} %param.13, f32[256]{0:T(256)S(1)} %bitcast.75, bf16[256,2048]{1,0:T(8,128)(2,1)} %bitcast.10, s32[256]{0:T(256)S(1)} %bitcast.73), kind=kOutput, calls=%fused_computation.25 | convolution fusion | flops 271122176 | bytes 3148800 | tf_op jit(solution)/shard_map/dot_general | solution.py:27
  156.8 0.7 maximum_maximum_fusion
  (4 shorter events, 0.0 us)
Async XLA Ops:
  7.2 70.6 %copy-start = (bf16[1,768,2048]{2,1,0:T(8,128)(2,1)S(1)}, bf16[1,768,2048]{2,1,0:T(8,128)(2,1)}, u32[]{:S(2)}) copy-start(bf16[1,768,2048]{2,1,0:T(8,128)(2,1)} %param.10) | copy-start | bytes 9437188
  7.2 76.8 %all-gather.5.cloned.1.call-start = ((), (), s32[]{:S(2)}) async-start(), calls=%async_computation.5 | async-start | bytes 5242880 | tf_op jit(solution)/shard_map/all_gather | solution.py:69
  43.7 69.8 %all-gather.3.cloned.1.call-start = ((), (), s32[]{:S(2)}) async-start(), calls=%async_computation.4 | async-start | bytes 5242880 | tf_op jit(solution)/shard_map/all_gather | solution.py:67
  74.5 3.3 %copy-start.1 = (bf16[8,32,2048]{2,1,0:T(8,128)(2,1)S(1)}, bf16[8,32,2048]{2,1,0:T(8,128)(2,1)}, u32[]{:S(2)}) copy-start(bf16[8,32,2048]{2,1,0:T(8,128)(2,1)} %all_to_all.21) | copy-start | bytes 3145732
  77.8 1.9 %copy-start.5 = (bf16[1,768,2048]{2,1,0:T(8,128)(2,1)S(1)}, bf16[1,768,2048]{2,1,0:T(8,128)(2,1)}, u32[]{:S(2)}) copy-start(bf16[1,768,2048]{2,1,0:T(8,128)(2,1)} %param.11) | copy-start | bytes 9437188
  79.7 2.1 %copy-start.8 = (f32[256,768]{1,0:T(8,128)}, f32[256,768]{1,0:T(8,128)S(1)}, u32[]{:S(2)}) copy-start(f32[256,768]{1,0:T(8,128)S(1)} %fusion.10) | copy-start | bytes 2359300
  80.7 1.1 copy-start.9
  84.0 38.0 %all-to-all-start.3 = ((bf16[8,32,2048]{2,1,0:T(8,128)(2,1)}), bf16[8,32,2048]{2,1,0:T(8,128)(2,1)}, u32[]{:S(2)}, u32[]{:S(2)}) async-start(bf16[8,32,2048]{2,1,0:T(8,128)(2,1)} %bitcast.70), calls=%async_computation.3 | async-start | bytes 2097152 | tf_op jit(solution)/shard_map/all_to_all | solution.py:58
  113.6 4.8 %copy-start.3 = (bf16[1024,2048]{1,0:T(8,128)(2,1)S(1)}, bf16[1024,2048]{1,0:T(8,128)(2,1)}, u32[]{:S(2)}) copy-start(bf16[1024,2048]{1,0:T(8,128)(2,1)} %all-gather.3.cloned.1.call-done) | copy-start | bytes 12582916
  121.9 31.7 %all-to-all-start.1 = ((bf16[8,32,2048]{2,1,0:T(8,128)(2,1)}), bf16[8,32,2048]{2,1,0:T(8,128)(2,1)}, u32[]{:S(2)}, u32[]{:S(2)}) async-start(bf16[8,32,2048]{2,1,0:T(8,128)(2,1)} %bitcast.71), calls=%async_computation.1 | async-start | bytes 2097152 | tf_op jit(solution)/shard_map/all_to_all | solution.py:58
  127.4 4.1 %copy-start.2 = (bf16[1024,2048]{1,0:T(8,128)(2,1)S(1)}, bf16[1024,2048]{1,0:T(8,128)(2,1)}, u32[]{:S(2)}) copy-start(bf16[1024,2048]{1,0:T(8,128)(2,1)} %all-gather.5.cloned.1.call-done) | copy-start | bytes 12582916
  127.4 4.1 %copy-start.6 = (f32[1024,192]{0,1:T(8,128)S(1)}, f32[1024,192]{0,1:T(8,128)}, u32[]{:S(2)}) copy-start(f32[1024,192]{0,1:T(8,128)} %fusion.26) | copy-start | bytes 2359300
  127.4 4.1 %copy-start.7 = (f32[1024,192]{0,1:T(8,128)S(1)}, f32[1024,192]{0,1:T(8,128)}, u32[]{:S(2)}) copy-start(f32[1024,192]{0,1:T(8,128)} %fusion.28) | copy-start | bytes 2359300
  131.5 2.5 %copy-start.4 = (bf16[1024,2048]{1,0:T(8,128)(2,1)S(1)}, bf16[1024,2048]{1,0:T(8,128)(2,1)}, u32[]{:S(2)}) copy-start(bf16[1024,2048]{1,0:T(8,128)(2,1)} %all-gather.3.cloned.1.call-done) | copy-start | bytes 12582916
Sparse Core Ops, SparseCore 0:
  43.9 33.5 all-gather.4
  79.0 34.5 all-gather.2

commit v3 on v1

--- a/solution.py
+++ b/solution.py
@@ -63,7 +63,11 @@
         tiled=True,
     ).reshape(total_slots, 2 * feature_width)
 
-    gathered = lax.all_gather(received, "rep", axis=0, tiled=True)
+    copies = lax.axis_size("rep")
+    if copies == 4:
+        far = lax.ppermute(received, "rep", [(r, r ^ 2) for r in range(copies)])
+    else:
+        gathered = lax.all_gather(received, "rep", axis=0, tiled=True)
 
     rows_in = received[:, :feature_width]
     grad_in = received[:, feature_width:]
@@ -89,6 +93,11 @@
     token_part = (
         matmul(gate_pre_grad, gate_mat) + matmul(up_pre_grad, up_mat)
     ).astype(jnp.bfloat16)
+    if copies == 4:
+        token_part, far = lax.optimization_barrier((token_part, far))
+        pair = jnp.concatenate([received, far], axis=0)
+        near = lax.ppermute(pair, "rep", [(r, r ^ 1) for r in range(copies)])
+        gathered = jnp.concatenate([pair, near], axis=0)
     part_back = lax.all_to_all(
         token_part.reshape(experts, per_pair, feature_width),
         "ep",
@@ -113,7 +122,6 @@
         [jnp.zeros((tok_count,), jnp.float32)] * (top_count - live_cols)
     )
     gates_grad = jnp.stack(gate_cols, axis=1)
-    tokens_grad = matmul(back_pick, part_back).astype(jnp.bfloat16)
 
     share = gate_mat.shape[0] // lax.axis_size("rep")
     start = lax.axis_index("rep") * share
@@ -132,6 +140,10 @@
     gate_w_grad = inner_rows(gate_pre_grad_s, rows_all).astype(jnp.bfloat16)[None]
     up_w_grad = inner_rows(up_pre_grad_s, rows_all).astype(jnp.bfloat16)[None]
     down_w_grad = inner_rows(hidden_s, grad_all).astype(jnp.bfloat16)[None]
+    part_back, gate_w_grad, up_w_grad, down_w_grad = lax.optimization_barrier(
+        (part_back, gate_w_grad, up_w_grad, down_w_grad)
+    )
+    tokens_grad = matmul(back_pick, part_back).astype(jnp.bfloat16)
     return (layer_out, tokens_grad, gates_grad, gate_w_grad, up_w_grad, down_w_grad)
 
 

time: 160 us -> 181 us (1.13)
  waiting for transfers between devices: 38.7 us -> 71.6 us
  between operations: 14.2 us -> 0.81 us
  other arithmetic: 1.71 us -> 8.63 us
  matrix products: 36.6 us -> 30.4 us
    ppermute x0 -> x2, waiting for transfers between devices: none -> 37.5 us  [the longest x1 37.5 us: body(): far = lax.ppermute(received, 'rep', [(r, r ^ 2) for r in range(copies)])]
    all_to_all x1, waiting for transfers between devices: 20.4 us -> 8.45 us  [body(): lax.all_to_all(token_part.reshape(experts, per_pair, feature_width), 'ep'...]
    all_to_all x1, waiting for transfers between devices: 18.2 us -> 25.6 us  [body(): lax.all_to_all(expert_out.reshape(experts, per_pair, feature_width), 'ep'...]
    concatenate x0 -> x2, other arithmetic: none -> 6.92 us  [the longest x1 4.28 us: body(): gathered = jnp.concatenate([pair, near], axis=0)]
    dot_general x6, matrix products: 16.1 us -> 9.91 us  [rows_times(): lax.dot_general(left, right, (((1,), (1,)), ((), ())), preferred_element_...]
  transfers between devices with their start and end apart: 3 -> 4, of which waited for: 2 -> 3; matrix products, arithmetic and copies ran while one was open for 12% -> 17% of each run, Pallas kernels for 0% -> 0%
where the time goes in v3:
time: 181 us; the launch traced here: 180 us
  waiting for transfers between devices  71.6 us (40%)
  blocking collectives  55.6 us (31%)
  matrix products  30.4 us (17%)
  starting transfers between devices  10.3 us (6%)
  other arithmetic  8.63 us (5%)
  local copies, waits for them, and re-layouts  2.76 us (2%)
    all_to_all x1, blocking collectives, body(): lax.all_to_all(outgoing.reshape(experts, per_pair, 2 * feature_width), 'e...  55.6 us
    ppermute x1, waiting for transfers between devices, body(): far = lax.ppermute(received, 'rep', [(r, r ^ 2) for r in range(copies)])  37.5 us
    all_to_all x1, waiting for transfers between devices, body(): lax.all_to_all(expert_out.reshape(experts, per_pair, feature_width), 'ep'...  25.6 us
    dot_general x8, matrix products, matmul(): return jnp.dot(left, right, preferred_element_type=jnp.float32)  14.6 us
    dot_general x6, matrix products, rows_times(): lax.dot_general(left, right, (((1,), (1,)), ((), ())), preferred_element_...  9.91 us
    all_to_all x1, waiting for transfers between devices, body(): lax.all_to_all(token_part.reshape(experts, per_pair, feature_width), 'ep'...  8.45 us
    dot_general x3, matrix products, inner_rows(): lax.dot_general(left, right, (((0,), (0,)), ((), ())), preferred_element_...  5.87 us
    all_to_all x1, starting transfers between devices, body(): lax.all_to_all(token_part.reshape(experts, per_pair, feature_width), 'ep'...  4.42 us
  transfers between devices with their start and end apart: 4, of which 3 were waited for; matrix products, arithmetic and copies ran while one was open for 17% of the time, Pallas kernels for 0%

profile of v3, /device:TPU:0, one launch (start us, length us, event | category | flops | bytes accessed | tf_op | source)
XLA Modules:
  0.0 180.0 jit_solution(8391373007093774642)
XLA Ops:
  0.6 0.0 copy-start
  0.6 0.8 slice.18
  1.5 0.8 slice.19
  2.3 0.2 fusion.52
  2.5 0.1 select_reduce_fusion
  2.6 1.7 convolution_convert_fusion.1
  4.3 1.7 fusion.30
  6.0 0.2 pad_maximum_fusion.2
  6.2 0.0 copy-start.4
  6.2 55.6 %all_to_all.15 = bf16[8,32,4096]{2,1,0:T(8,128)(2,1)S(1)} all-to-all(bf16[8,32,4096]{2,1,0:T(8,128)(2,1)S(1)} %bitcast.58), channel_id=1, replica_groups=mesh['rep'=4,'ep'=8] {'ep'}, dimensions={0} | all-to-all | bytes 4194304 | tf_op jit(solution)/shard_map/all_to_all | solution.py:58
  61.8 0.0 copy-start.1
  61.8 1.5 collective-permute-start
  63.3 0.0 copy-done.4
  63.3 1.0 fusion.10
  64.3 0.0 copy-done
  64.3 0.0 copy-start.3
  64.3 1.0 fusion.14
  65.4 0.9 copy-done.3
  66.2 1.0 fusion.4
  67.3 1.0 fusion.8
  68.3 2.2 %fusion.27 = bf16[256,2048]{1,0:T(8,128)(2,1)} fusion(f32[256,2048]{1,0:T(8,128)S(1)} %fusion.8, bf16[1,768,2048]{2,1,0:T(8,128)(2,1)S(1)} %copy-done, f32[256,768]{1,0:T(8,128)S(1)} %fusion.14, f32[256,768]{1,0:T(8,128)S(1)} %fusion.4, f32[256,768]{1,0:T(8,128)S(1)} %fusion.10), kind=kOutput, calls=%fused_computation.28 | convolution fusion | flops 808321024 | bytes 8650752 | tf_op jit(solution)/shard_map/dot_general | solution.py:27
  70.5 37.5 %collective-permute-done = bf16[256,4096]{1,0:T(8,128)(2,1)S(1)} collective-permute-done((bf16[256,4096]{1,0:T(8,128)(2,1)S(1)}, bf16[256,4096]{1,0:T(8,128)(2,1)S(1)}, u32[]{:S(2)}, u32[]{:S(2)}) %collective-permute-start) | collective-permute-done | bytes 2097184 | tf_op jit(solution)/shard_map/ppermute | solution.py:68
  108.0 0.0 copy-done.1
  108.0 0.0 copy-start.2
  108.0 2.6 %pad_maximum_fusion.1 = bf16[512,4096]{1,0:T(8,128)(2,1)} fusion(bf16[256,4096]{1,0:T(8,128)(2,1)S(1)} %collective-permute-done, bf16[256,4096]{1,0:T(8,128)(2,1)S(1)} %bitcast.56), kind=kLoop, calls=%fused_computation.1 | loop fusion | flops 8388608 | bytes 8388608 | tf_op jit(solution)/shard_map/concatenate | solution.py:98
  110.7 0.0 copy-done.2
  110.7 0.0 collective-permute-start.1
  110.7 2.0 %fusion.31 = bf16[256,2048]{1,0:T(8,128)(2,1)} fusion(bf16[1,768,2048]{2,1,0:T(8,128)(2,1)S(1)} %copy-done.3, f32[256,768]{1,0:T(8,128)S(1)} %fusion.10, f32[256,768]{1,0:T(8,128)S(1)} %fusion.14), kind=kOutput, calls=%fused_computation.32 | convolution fusion | flops 807010304 | bytes 5767168 | tf_op jit(solution)/shard_map/dot_general | solution.py:27
  112.7 4.4 %all-to-all-start.1 = ((bf16[8,32,2048]{2,1,0:T(8,128)(2,1)}), bf16[8,32,2048]{2,1,0:T(8,128)(2,1)}, u32[]{:S(2)}, u32[]{:S(2)}) async-start(bf16[8,32,2048]{2,1,0:T(8,128)(2,1)} %bitcast.60), calls=%async_computation.1 | async-start | bytes 2097152 | tf_op jit(solution)/shard_map/all_to_all | solution.py:82
  117.0 0.1 pad.3.clone
  117.1 0.1 pad.2.clone
  117.2 0.1 pad.1.clone
  117.3 0.7 compare_select_fusion
  118.0 25.6 %all-to-all-done.1 = bf16[8,32,2048]{2,1,0:T(8,128)(2,1)} async-done(((bf16[8,32,2048]{2,1,0:T(8,128)(2,1)}), bf16[8,32,2048]{2,1,0:T(8,128)(2,1)}, u32[]{:S(2)}, u32[]{:S(2)}) %all-to-all-start.1) | async-done | bytes 1048608 | tf_op jit(solution)/shard_map/all_to_all | solution.py:82
  143.6 3.1 %multiply_reduce_fusion = (f32[256]{0:T(256)S(1)}, bf16[256,2048]{1,0:T(8,128)(2,1)}) fusion(bf16[256,2048]{1,0:T(8,128)(2,1)} %param.13, f32[256]{0:T(256)S(1)} %bitcast.64, bf16[256,2048]{1,0:T(8,128)(2,1)} %bitcast.10, s32[256]{0:T(256)S(1)} %bitcast.61), kind=kOutput, calls=%fused_computation.40 | convolution fusion | flops 271122176 | bytes 3148800 | tf_op jit(solution)/shard_map/dot_general | solution.py:27
  146.8 0.7 maximum_maximum_fusion
  147.4 4.4 %all-to-all-start.2 = ((bf16[8,32,2048]{2,1,0:T(8,128)(2,1)}), bf16[8,32,2048]{2,1,0:T(8,128)(2,1)}, u32[]{:S(2)}, u32[]{:S(2)}) async-start(bf16[8,32,2048]{2,1,0:T(8,128)(2,1)} %bitcast.59), calls=%async_computation.2 | async-start | bytes 2097152 | tf_op jit(solution)/shard_map/all_to_all | solution.py:101
  151.9 0.0 collective-permute-done.1
  151.9 4.3 %pad_maximum_fusion = bf16[1024,4096]{1,0:T(8,128)(2,1)S(1)} fusion(bf16[512,4096]{1,0:T(8,128)(2,1)} %collective-permute-done.1, bf16[256,4096]{1,0:T(8,128)(2,1)} %copy-done.2, bf16[256,4096]{1,0:T(8,128)(2,1)} %bitcast.57), kind=kLoop, calls=%fused_computation | loop fusion | flops 25165824 | bytes 16777216 | tf_op jit(solution)/shard_map/concatenate | solution.py:100
  156.2 1.5 fusion.23
  157.7 2.7 %fusion.2 = f32[1024,192]{0,1:T(8,128)S(1)} fusion(bf16[1024,4096]{1,0:T(8,128)(2,1)S(1)} %pad_maximum_fusion, bf16[1,768,2048]{2,1,0:T(8,128)(2,1)} %param.12, s32[]{:T(128)S(6)} %select_n.28), kind=kOutput, calls=%fused_computation.4 | convolution fusion | flops 805306368 | bytes 5767172 | tf_op jit(solution)/shard_map/dot_general | solution.py:15
  160.4 2.7 %fusion.25 = f32[1024,192]{0,1:T(8,128)S(1)} fusion(bf16[1024,4096]{1,0:T(8,128)(2,1)S(1)} %pad_maximum_fusion, bf16[1,768,2048]{2,1,0:T(8,128)(2,1)} %param.11, s32[]{:T(128)S(6)} %select_n.28), kind=kOutput, calls=%fused_computation.26 | convolution fusion | flops 805306368 | bytes 5767172 | tf_op jit(solution)/shard_map/dot_general | solution.py:15
  163.0 1.9 %fusion.46 = bf16[1,192,2048]{2,1,0:T(8,128)(2,1)} fusion(bf16[1024,4096]{1,0:T(8,128)(2,1)S(1)} %pad_maximum_fusion, f32[1024,192]{0,1:T(8,128)S(1)} %fusion.2, f32[1024,192]{0,1:T(8,128)S(1)} %fusion.23), kind=kOutput, calls=%fused_computation.37 | convolution fusion | flops 806879232 | bytes 6553600 | tf_op jit(solution)/shard_map/dot_general | solution.py:21
  165.0 1.9 %fusion.43 = bf16[1,192,2048]{2,1,0:T(8,128)(2,1)} fusion(bf16[1024,4096]{1,0:T(8,128)(2,1)S(1)} %pad_maximum_fusion, f32[1024,192]{0,1:T(8,128)S(1)} %fusion.25, f32[1024,192]{0,1:T(8,128)S(1)} %fusion.23), kind=kOutput, calls=%fused_computation.36 | convolution fusion | flops 806879232 | bytes 6553600 | tf_op jit(solution)/shard_map/dot_general | solution.py:21
  166.9 2.0 %fusion.49 = bf16[1,192,2048]{2,1,0:T(8,128)(2,1)} fusion(bf16[1024,4096]{1,0:T(8,128)(2,1)S(1)} %pad_maximum_fusion, f32[1024,192]{0,1:T(8,128)S(1)} %fusion.23, f32[1024,192]{0,1:T(8,128)S(1)} %fusion.2, f32[1024,192]{0,1:T(8,128)S(1)} %fusion.25), kind=kOutput, calls=%fused_computation.38 | convolution fusion | flops 807665664 | bytes 7340032 | tf_op jit(solution)/shard_map/dot_general | solution.py:21
  168.9 8.4 %all-to-all-done.2 = bf16[8,32,2048]{2,1,0:T(8,128)(2,1)} async-done(((bf16[8,32,2048]{2,1,0:T(8,128)(2,1)}), bf16[8,32,2048]{2,1,0:T(8,128)(2,1)}, u32[]{:S(2)}, u32[]{:S(2)}) %all-to-all-start.2) | async-done | bytes 1048608 | tf_op jit(solution)/shard_map/all_to_all | solution.py:101
  177.4 2.7 %convolution_convert_fusion = bf16[256,2048]{1,0:T(8,128)(2,1)} fusion(bf16[256,2048]{1,0:T(8,128)(2,1)} %bitcast.12, s32[256]{0:T(256)S(1)} %bitcast.62), kind=kOutput, calls=%fused_computation.30 | convolution fusion | flops 269025280 | bytes 2098176 | tf_op jit(solution)/shard_map/dot_general | solution.py:27
  (4 shorter events, 0.0 us)
Async XLA Ops:
  0.6 63.7 %copy-start = (bf16[1,768,2048]{2,1,0:T(8,128)(2,1)S(1)}, bf16[1,768,2048]{2,1,0:T(8,128)(2,1)}, u32[]{:S(2)}) copy-start(bf16[1,768,2048]{2,1,0:T(8,128)(2,1)} %param.10) | copy-start | bytes 9437188
  6.2 57.1 %copy-start.4 = (bf16[1,768,2048]{2,1,0:T(8,128)(2,1)S(1)}, bf16[1,768,2048]{2,1,0:T(8,128)(2,1)}, u32[]{:S(2)}) copy-start(bf16[1,768,2048]{2,1,0:T(8,128)(2,1)} %param.11) | copy-start | bytes 9437188
  61.8 46.2 %copy-start.1 = (bf16[8,32,4096]{2,1,0:T(8,128)(2,1)}, bf16[8,32,4096]{2,1,0:T(8,128)(2,1)S(1)}, u32[]{:S(2)}) copy-start(bf16[8,32,4096]{2,1,0:T(8,128)(2,1)S(1)} %all_to_all.15) | copy-start | bytes 6291460
  61.8 46.2 %collective-permute-start = (bf16[256,4096]{1,0:T(8,128)(2,1)S(1)}, bf16[256,4096]{1,0:T(8,128)(2,1)S(1)}, u32[]{:S(2)}, u32[]{:S(2)}) collective-permute-start(bf16[256,4096]{1,0:T(8,128)(2,1)S(1)} %bitcast.52), channel_id=1, source_target_pairs={{0,16},{8,24},{16,0},{24,8},{1,17},{9,25},{17,1},{25,9},{2,18},{10... | collective-permute-start | bytes 6291464 | tf_op jit(solution)/shard_map/ppermute | solution.py:68
  64.3 1.9 %copy-start.3 = (bf16[1,768,2048]{2,1,0:T(8,128)(2,1)S(1)}, bf16[1,768,2048]{2,1,0:T(8,128)(2,1)}, u32[]{:S(2)}) copy-start(bf16[1,768,2048]{2,1,0:T(8,128)(2,1)} %param.12) | copy-start | bytes 9437188
  108.0 2.6 %copy-start.2 = (bf16[256,4096]{1,0:T(8,128)(2,1)}, bf16[256,4096]{1,0:T(8,128)(2,1)S(1)}, u32[]{:S(2)}) copy-start(bf16[256,4096]{1,0:T(8,128)(2,1)S(1)} %collective-permute-done) | copy-start | bytes 6291460
  110.7 41.2 %collective-permute-start.1 = (bf16[512,4096]{1,0:T(8,128)(2,1)}, bf16[512,4096]{1,0:T(8,128)(2,1)}, u32[]{:S(2)}, u32[]{:S(2)}) collective-permute-start(bf16[512,4096]{1,0:T(8,128)(2,1)} %pad_maximum_fusion.1), channel_id=1, source_target_pairs={{0,8},{8,0},{16,24},{24,16},{1,9},{9,1},{17,25},{25,17},{2,10},{10... | collective-permute-start | bytes 12582920 | tf_op jit(solution)/shard_map/ppermute | solution.py:99
  112.7 31.0 %all-to-all-start.1 = ((bf16[8,32,2048]{2,1,0:T(8,128)(2,1)}), bf16[8,32,2048]{2,1,0:T(8,128)(2,1)}, u32[]{:S(2)}, u32[]{:S(2)}) async-start(bf16[8,32,2048]{2,1,0:T(8,128)(2,1)} %bitcast.60), calls=%async_computation.1 | async-start | bytes 2097152 | tf_op jit(solution)/shard_map/all_to_all | solution.py:82
  147.4 29.9 %all-to-all-start.2 = ((bf16[8,32,2048]{2,1,0:T(8,128)(2,1)}), bf16[8,32,2048]{2,1,0:T(8,128)(2,1)}, u32[]{:S(2)}, u32[]{:S(2)}) async-start(bf16[8,32,2048]{2,1,0:T(8,128)(2,1)} %bitcast.59), calls=%async_computation.2 | async-start | bytes 2097152 | tf_op jit(solution)/shard_map/all_to_all | solution.py:101

commit v4 on v1

--- a/solution.py
+++ b/solution.py
@@ -113,7 +113,6 @@
         [jnp.zeros((tok_count,), jnp.float32)] * (top_count - live_cols)
     )
     gates_grad = jnp.stack(gate_cols, axis=1)
-    tokens_grad = matmul(back_pick, part_back).astype(jnp.bfloat16)
 
     share = gate_mat.shape[0] // lax.axis_size("rep")
     start = lax.axis_index("rep") * share
@@ -132,6 +131,10 @@
     gate_w_grad = inner_rows(gate_pre_grad_s, rows_all).astype(jnp.bfloat16)[None]
     up_w_grad = inner_rows(up_pre_grad_s, rows_all).astype(jnp.bfloat16)[None]
     down_w_grad = inner_rows(hidden_s, grad_all).astype(jnp.bfloat16)[None]
+    part_back, gate_w_grad, up_w_grad, down_w_grad = lax.optimization_barrier(
+        (part_back, gate_w_grad, up_w_grad, down_w_grad)
+    )
+    tokens_grad = matmul(back_pick, part_back).astype(jnp.bfloat16)
     return (layer_out, tokens_grad, gates_grad, gate_w_grad, up_w_grad, down_w_grad)
 
 

time: 160 us -> 152 us (0.950)
  waiting for transfers between devices: 38.7 us -> 29 us
    all_to_all x1, waiting for transfers between devices: 20.4 us -> 0.01 us  [body(): lax.all_to_all(token_part.reshape(experts, per_pair, feature_width), 'ep'...]
    all_gather x1, waiting for transfers between devices: 0.01 us -> 12.2 us  [body(): gathered = lax.all_gather(received, 'rep', axis=0, tiled=True)]
  transfers between devices with their start and end apart: 3 -> 3, of which waited for: 2 -> 2; matrix products, arithmetic and copies ran while one was open for 12% -> 22% of each run, Pallas kernels for 0% -> 0%
where the time goes in v4:
time: 152 us; the launch traced here: 151 us
  blocking collectives  55.4 us (36%)
  matrix products  37.6 us (25%)
  waiting for transfers between devices  29 us (19%)
  between operations  14.2 us (9%)
  starting transfers between devices  8.78 us (6%)
  local copies, waits for them, and re-layouts  4.2 us (3%)
  other arithmetic  1.86 us (1%)
    all_to_all x1, blocking collectives, body(): lax.all_to_all(outgoing.reshape(experts, per_pair, 2 * feature_width), 'e...  55.4 us
    dot_general x6, matrix products, rows_times(): lax.dot_general(left, right, (((1,), (1,)), ((), ())), preferred_element_...  17.1 us
    all_to_all x1, waiting for transfers between devices, body(): lax.all_to_all(expert_out.reshape(experts, per_pair, feature_width), 'ep'...  16.7 us
    dot_general x8, matrix products, matmul(): return jnp.dot(left, right, preferred_element_type=jnp.float32)  14.6 us
    all_gather x1, waiting for transfers between devices, body(): gathered = lax.all_gather(received, 'rep', axis=0, tiled=True)  12.2 us
    dot_general x3, matrix products, inner_rows(): lax.dot_general(left, right, (((0,), (0,)), ((), ())), preferred_element_...  5.87 us
    all_to_all x1, starting transfers between devices, body(): lax.all_to_all(token_part.reshape(experts, per_pair, feature_width), 'ep'...  4.43 us
    all_to_all x1, starting transfers between devices, body(): lax.all_to_all(expert_out.reshape(experts, per_pair, feature_width), 'ep'...  4.31 us
  transfers between devices with their start and end apart: 3, of which 2 were waited for; matrix products, arithmetic and copies ran while one was open for 22% of the time, Pallas kernels for 0%

profile of v4, /device:TPU:0, one launch (start us, length us, event | category | flops | bytes accessed | tf_op | source)
XLA Modules:
  0.0 151.0 jit_solution(11133994885519121761)
XLA Ops:
  7.2 0.0 copy-start
  7.2 0.0 all-gather.2.cloned.1.call-start
  7.2 0.8 slice.18
  8.1 0.8 slice.19
  8.8 0.2 fusion.52
  9.0 0.1 select_reduce_fusion
  9.2 1.7 %convolution_convert_fusion.1 = bf16[256,2048]{1,0:T(8,128)(2,1)S(1)} fusion(bf16[256,2048]{1,0:T(8,128)(2,1)} %param.7, s32[256]{0:T(256)S(1)} %compare_select_fusion.1), kind=kOutput, calls=%fused_computation.29 | convolution fusion | flops 269025280 | bytes 2098176 | tf_op jit(solution)/shard_map/dot_general | solution.py:27
  10.8 1.7 %fusion.30 = bf16[256,2048]{1,0:T(8,128)(2,1)S(1)} fusion(bf16[256,2048]{1,0:T(8,128)(2,1)} %param.13, f32[256]{0:T(256)S(1)} %select_reduce_fusion, s32[256]{0:T(256)S(1)} %compare_select_fusion.1), kind=kOutput, calls=%fused_computation.27 | convolution fusion | flops 269549568 | bytes 2099200 | tf_op jit(solution)/shard_map/dot_general | solution.py:27
  12.5 0.2 pad_maximum_fusion
  12.7 55.4 %all_to_all.15 = bf16[8,32,4096]{2,1,0:T(8,128)(2,1)} all-to-all(bf16[8,32,4096]{2,1,0:T(8,128)(2,1)S(1)} %bitcast.56), channel_id=1, replica_groups=mesh['rep'=4,'ep'=8] {'ep'}, dimensions={0} | all-to-all | bytes 4194304 | tf_op jit(solution)/shard_map/all_to_all | solution.py:58
  68.1 0.0 all-gather.2.cloned.1.call-update
  68.2 0.0 copy-start.1
  68.2 3.4 %fusion.10 = f32[256,768]{1,0:T(8,128)S(1)} fusion(bf16[1,768,2048]{2,1,0:T(8,128)(2,1)} %param.11, bf16[256,4096]{1,0:T(8,128)(2,1)} %bitcast.53), kind=kOutput, calls=%fused_computation.10 | convolution fusion | flops 805306368 | bytes 4980736 | tf_op jit(solution)/shard_map/dot_general | solution.py:15
  71.5 0.0 copy-done
  71.6 0.0 copy-done.1
  71.6 0.0 copy-start.5
  71.6 0.0 copy-start.3
  71.6 1.0 fusion.14
  72.6 1.4 copy-done.3
  74.0 0.0 copy-start.7
  74.0 2.0 %fusion.31 = bf16[256,2048]{1,0:T(8,128)(2,1)} fusion(bf16[1,768,2048]{2,1,0:T(8,128)(2,1)S(1)} %copy-done.3, f32[256,768]{1,0:T(8,128)S(1)} %fusion.10, f32[256,768]{1,0:T(8,128)S(1)} %fusion.14), kind=kOutput, calls=%fused_computation.30 | convolution fusion | flops 807010304 | bytes 5767168 | tf_op jit(solution)/shard_map/dot_general | solution.py:27
  76.0 0.0 copy-done.5
  76.1 0.0 copy-done.7
  76.1 4.3 %all-to-all-start.1 = ((bf16[8,32,2048]{2,1,0:T(8,128)(2,1)}), bf16[8,32,2048]{2,1,0:T(8,128)(2,1)}, u32[]{:S(2)}, u32[]{:S(2)}) async-start(bf16[8,32,2048]{2,1,0:T(8,128)(2,1)} %bitcast.57), calls=%async_computation.1 | async-start | bytes 2097152 | tf_op jit(solution)/shard_map/all_to_all | solution.py:78
  80.4 0.1 pad.3.clone
  80.5 0.1 pad.2.clone
  80.5 0.1 pad.1.clone
  80.6 0.0 copy-start.4
  80.6 0.0 copy-start.8
  80.6 0.9 compare_select_fusion
  81.5 3.6 %fusion.4 = f32[256,768]{1,0:T(8,128)S(1)} fusion(bf16[1,768,2048]{2,1,0:T(8,128)(2,1)} %param.12, bf16[256,4096]{1,0:T(8,128)(2,1)} %bitcast.54), kind=kOutput, calls=%fused_computation.4 | convolution fusion | flops 805306368 | bytes 4980736 | tf_op jit(solution)/shard_map/dot_general | solution.py:15
  85.0 0.0 copy-done.4
  85.1 0.0 copy-done.8
  85.1 0.0 copy-start.6
  85.1 1.0 fusion.8
  86.1 0.1 copy-done.6
  86.2 2.2 %fusion.27 = bf16[256,2048]{1,0:T(8,128)(2,1)} fusion(f32[256,2048]{1,0:T(8,128)S(1)} %fusion.8, bf16[1,768,2048]{2,1,0:T(8,128)(2,1)S(1)} %copy-done, f32[256,768]{1,0:T(8,128)S(1)} %copy-done.8, f32[256,768]{1,0:T(8,128)S(1)} %fusion.4, f32[256,768]{1,0:T(8,128)S(1)} %copy-done.6), kind=kOutput, calls=%fused_computation.26 | convolution fusion | flops 808321024 | bytes 8650752 | tf_op jit(solution)/shard_map/dot_general | solution.py:27
  88.4 16.7 %all-to-all-done.1 = bf16[8,32,2048]{2,1,0:T(8,128)(2,1)} async-done(((bf16[8,32,2048]{2,1,0:T(8,128)(2,1)}), bf16[8,32,2048]{2,1,0:T(8,128)(2,1)}, u32[]{:S(2)}, u32[]{:S(2)}) %all-to-all-start.1) | async-done | bytes 1048608 | tf_op jit(solution)/shard_map/all_to_all | solution.py:78
  105.1 4.4 %all-to-all-start.2 = ((bf16[8,32,2048]{2,1,0:T(8,128)(2,1)}), bf16[8,32,2048]{2,1,0:T(8,128)(2,1)}, u32[]{:S(2)}, u32[]{:S(2)}) async-start(bf16[8,32,2048]{2,1,0:T(8,128)(2,1)} %bitcast.58), calls=%async_computation.2 | async-start | bytes 2097152 | tf_op jit(solution)/shard_map/all_to_all | solution.py:92
  109.6 3.2 %multiply_reduce_fusion = (f32[256]{0:T(256)S(1)}, bf16[256,2048]{1,0:T(8,128)(2,1)}) fusion(bf16[256,2048]{1,0:T(8,128)(2,1)} %param.13, f32[256]{0:T(256)S(1)} %bitcast.62, bf16[256,2048]{1,0:T(8,128)(2,1)} %bitcast.10, s32[256]{0:T(256)S(1)} %bitcast.59), kind=kOutput, calls=%fused_computation.38 | convolution fusion | flops 271122176 | bytes 3148800 | tf_op jit(solution)/shard_map/dot_general | solution.py:27
  112.7 0.7 maximum_maximum_fusion
  113.4 12.2 %all-gather.2.cloned.1.call-done = bf16[1024,4096]{1,0:T(8,128)(2,1)} async-done(((bf16[256,4096]{1,0:T(8,128)(2,1)}), bf16[1024,4096]{1,0:T(8,128)(2,1)}) %all-gather.2.cloned.1.call-update) | async-done | bytes 8388624 | tf_op jit(solution)/shard_map/all_gather | solution.py:66
  125.6 0.0 copy-start.2
  125.6 3.9 %fusion.23 = f32[1024,192]{0,1:T(8,128)S(1)} fusion(bf16[1024,4096]{1,0:T(8,128)(2,1)} %all-gather.2.cloned.1.call-done, bf16[1,768,2048]{2,1,0:T(8,128)(2,1)S(1)} %copy-done, s32[]{:T(128)S(6)} %select_n.28), kind=kOutput, calls=%fused_computation.22 | convolution fusion | flops 805306368 | bytes 5767172 | tf_op jit(solution)/shard_map/dot_general | solution.py:15
  129.5 0.8 copy-done.2
  130.3 2.7 %fusion.2 = f32[1024,192]{0,1:T(8,128)S(1)} fusion(bf16[1024,4096]{1,0:T(8,128)(2,1)S(1)} %copy-done.2, bf16[1,768,2048]{2,1,0:T(8,128)(2,1)} %param.12, s32[]{:T(128)S(6)} %select_n.28), kind=kOutput, calls=%fused_computation.2 | convolution fusion | flops 805306368 | bytes 5767172 | tf_op jit(solution)/shard_map/dot_general | solution.py:15
  132.9 2.7 %fusion.25 = f32[1024,192]{0,1:T(8,128)S(1)} fusion(bf16[1024,4096]{1,0:T(8,128)(2,1)S(1)} %copy-done.2, bf16[1,768,2048]{2,1,0:T(8,128)(2,1)} %param.11, s32[]{:T(128)S(6)} %select_n.28), kind=kOutput, calls=%fused_computation.24 | convolution fusion | flops 805306368 | bytes 5767172 | tf_op jit(solution)/shard_map/dot_general | solution.py:15
  135.6 1.9 %fusion.46 = bf16[1,192,2048]{2,1,0:T(8,128)(2,1)} fusion(bf16[1024,4096]{1,0:T(8,128)(2,1)S(1)} %copy-done.2, f32[1024,192]{0,1:T(8,128)S(1)} %fusion.2, f32[1024,192]{0,1:T(8,128)S(1)} %fusion.23), kind=kOutput, calls=%fused_computation.35 | convolution fusion | flops 806879232 | bytes 6553600 | tf_op jit(solution)/shard_map/dot_general | solution.py:21
  137.5 1.9 %fusion.43 = bf16[1,192,2048]{2,1,0:T(8,128)(2,1)} fusion(bf16[1024,4096]{1,0:T(8,128)(2,1)S(1)} %copy-done.2, f32[1024,192]{0,1:T(8,128)S(1)} %fusion.25, f32[1024,192]{0,1:T(8,128)S(1)} %fusion.23), kind=kOutput, calls=%fused_computation.34 | convolution fusion | flops 806879232 | bytes 6553600 | tf_op jit(solution)/shard_map/dot_general | solution.py:21
  139.5 2.0 %fusion.49 = bf16[1,192,2048]{2,1,0:T(8,128)(2,1)} fusion(bf16[1024,4096]{1,0:T(8,128)(2,1)S(1)} %copy-done.2, f32[1024,192]{0,1:T(8,128)S(1)} %fusion.23, f32[1024,192]{0,1:T(8,128)S(1)} %fusion.2, f32[1024,192]{0,1:T(8,128)S(1)} %fusion.25), kind=kOutput, calls=%fused_computation.36 | convolution fusion | flops 807665664 | bytes 7340032 | tf_op jit(solution)/shard_map/dot_general | solution.py:21
  141.5 0.0 all-to-all-done.2
  141.5 2.7 %convolution_convert_fusion = bf16[256,2048]{1,0:T(8,128)(2,1)} fusion(bf16[256,2048]{1,0:T(8,128)(2,1)} %bitcast.12, s32[256]{0:T(256)S(1)} %bitcast.60), kind=kOutput, calls=%fused_computation.28 | convolution fusion | flops 269025280 | bytes 2098176 | tf_op jit(solution)/shard_map/dot_general | solution.py:27
  (4 shorter events, 0.0 us)
Async XLA Ops:
  7.2 64.4 %copy-start = (bf16[1,768,2048]{2,1,0:T(8,128)(2,1)S(1)}, bf16[1,768,2048]{2,1,0:T(8,128)(2,1)}, u32[]{:S(2)}) copy-start(bf16[1,768,2048]{2,1,0:T(8,128)(2,1)} %param.10) | copy-start | bytes 9437188
  7.2 118.5 %all-gather.2.cloned.1.call-start = ((), (), s32[]{:S(2)}) async-start(), calls=%async_computation.3 | async-start | bytes 10485760 | tf_op jit(solution)/shard_map/all_gather | solution.py:66
  68.2 3.4 %copy-start.1 = (bf16[8,32,4096]{2,1,0:T(8,128)(2,1)S(1)}, bf16[8,32,4096]{2,1,0:T(8,128)(2,1)}, u32[]{:S(2)}) copy-start(bf16[8,32,4096]{2,1,0:T(8,128)(2,1)} %all_to_all.15) | copy-start | bytes 6291460
  71.6 4.5 %copy-start.5 = (f32[256,768]{1,0:T(8,128)}, f32[256,768]{1,0:T(8,128)S(1)}, u32[]{:S(2)}) copy-start(f32[256,768]{1,0:T(8,128)S(1)} %fusion.10) | copy-start | bytes 2359300
  71.6 2.5 %copy-start.3 = (bf16[1,768,2048]{2,1,0:T(8,128)(2,1)S(1)}, bf16[1,768,2048]{2,1,0:T(8,128)(2,1)}, u32[]{:S(2)}) copy-start(bf16[1,768,2048]{2,1,0:T(8,128)(2,1)} %param.12) | copy-start | bytes 9437188
  74.0 2.0 %copy-start.7 = (f32[256,768]{1,0:T(8,128)}, f32[256,768]{1,0:T(8,128)S(1)}, u32[]{:S(2)}) copy-start(f32[256,768]{1,0:T(8,128)S(1)} %fusion.14) | copy-start | bytes 2359300
  76.1 29.1 %all-to-all-start.1 = ((bf16[8,32,2048]{2,1,0:T(8,128)(2,1)}), bf16[8,32,2048]{2,1,0:T(8,128)(2,1)}, u32[]{:S(2)}, u32[]{:S(2)}) async-start(bf16[8,32,2048]{2,1,0:T(8,128)(2,1)} %bitcast.57), calls=%async_computation.1 | async-start | bytes 2097152 | tf_op jit(solution)/shard_map/all_to_all | solution.py:78
  80.6 4.4 %copy-start.4 = (bf16[1,768,2048]{2,1,0:T(8,128)(2,1)S(1)}, bf16[1,768,2048]{2,1,0:T(8,128)(2,1)}, u32[]{:S(2)}) copy-start(bf16[1,768,2048]{2,1,0:T(8,128)(2,1)} %param.11) | copy-start | bytes 9437188
  80.6 4.4 %copy-start.8 = (f32[256,768]{1,0:T(8,128)S(1)}, f32[256,768]{1,0:T(8,128)}, u32[]{:S(2)}) copy-start(f32[256,768]{1,0:T(8,128)} %copy-done.7) | copy-start | bytes 2359300
  85.1 1.2 copy-start.6
  105.1 36.4 %all-to-all-start.2 = ((bf16[8,32,2048]{2,1,0:T(8,128)(2,1)}), bf16[8,32,2048]{2,1,0:T(8,128)(2,1)}, u32[]{:S(2)}, u32[]{:S(2)}) async-start(bf16[8,32,2048]{2,1,0:T(8,128)(2,1)} %bitcast.58), calls=%async_computation.2 | async-start | bytes 2097152 | tf_op jit(solution)/shard_map/all_to_all | solution.py:92
  125.6 4.6 %copy-start.2 = (bf16[1024,4096]{1,0:T(8,128)(2,1)S(1)}, bf16[1024,4096]{1,0:T(8,128)(2,1)}, u32[]{:S(2)}) copy-start(bf16[1024,4096]{1,0:T(8,128)(2,1)} %all-gather.2.cloned.1.call-done) | copy-start | bytes 25165828
Sparse Core Ops, SparseCore 0:
  68.3 57.3 all-gather.1

commit v5 on v4

--- a/solution.py
+++ b/solution.py
@@ -121,15 +121,19 @@
     down_share = lax.dynamic_slice_in_dim(down_mat, start, share, axis=0)
     rows_all = gathered[:, :feature_width]
     grad_all = gathered[:, feature_width:]
-    pre_gate_s = rows_times(rows_all, gate_share)
-    pre_up_s = rows_times(rows_all, up_share)
+    pre_both = rows_times(rows_all, jnp.concatenate([gate_share, up_share], axis=0))
+    pre_gate_s = pre_both[:, :share]
+    pre_up_s = pre_both[:, share:]
     activated_s = jax.nn.silu(pre_gate_s)
     hidden_s = (activated_s * pre_up_s).astype(jnp.bfloat16)
     hidden_grad_s = rows_times(grad_all, down_share)
     gate_pre_grad_s = (hidden_grad_s * pre_up_s * silu_grad(pre_gate_s)).astype(jnp.bfloat16)
     up_pre_grad_s = (hidden_grad_s * activated_s).astype(jnp.bfloat16)
-    gate_w_grad = inner_rows(gate_pre_grad_s, rows_all).astype(jnp.bfloat16)[None]
-    up_w_grad = inner_rows(up_pre_grad_s, rows_all).astype(jnp.bfloat16)[None]
+    both_w_grad = inner_rows(
+        jnp.concatenate([gate_pre_grad_s, up_pre_grad_s], axis=1), rows_all
+    ).astype(jnp.bfloat16)
+    gate_w_grad = both_w_grad[:share][None]
+    up_w_grad = both_w_grad[share:][None]
     down_w_grad = inner_rows(hidden_s, grad_all).astype(jnp.bfloat16)[None]
     part_back, gate_w_grad, up_w_grad, down_w_grad = lax.optimization_barrier(
         (part_back, gate_w_grad, up_w_grad, down_w_grad)

time: 152 us -> 148 us (0.974)
  matrix products: 37.6 us -> 30 us
  local copies, waits for them, and re-layouts: 4.2 us -> 8.92 us
    dot_general x6 -> x5, matrix products: 17.1 us -> 11.7 us  [rows_times(): lax.dot_general(left, right, (((1,), (1,)), ((), ())), preferred_element_...]
    dynamic_slice x0 -> x1, local copies, waits for them, and re-layouts: none -> 2.7 us  [body(): up_share = lax.dynamic_slice_in_dim(up_mat, start, share, axis=0)]
    dot_general x3 -> x2, matrix products: 5.87 us -> 3.76 us  [inner_rows(): lax.dot_general(left, right, (((0,), (0,)), ((), ())), preferred_element_...]
    all_to_all x1, waiting for transfers between devices: 16.7 us -> 14.9 us  [body(): lax.all_to_all(expert_out.reshape(experts, per_pair, feature_width), 'ep'...]
    unnamed x18 -> x22, local copies, waits for them, and re-layouts: 2.37 us -> 3.08 us
  transfers between devices with their start and end apart: 3 -> 3, of which waited for: 2 -> 2; matrix products, arithmetic and copies ran while one was open for 22% -> 20% of each run, Pallas kernels for 0% -> 0%
where the time goes in v5:
time: 148 us; the launch traced here: 147 us
  blocking collectives  55.4 us (37%)
  matrix products  30 us (20%)
  waiting for transfers between devices  27.9 us (19%)
  between operations  14.2 us (10%)
  local copies, waits for them, and re-layouts  8.92 us (6%)
  starting transfers between devices  8.71 us (6%)
  other arithmetic  1.87 us (1%)
    all_to_all x1, blocking collectives, body(): lax.all_to_all(outgoing.reshape(experts, per_pair, 2 * feature_width), 'e...  55.4 us
    all_to_all x1, waiting for transfers between devices, body(): lax.all_to_all(expert_out.reshape(experts, per_pair, feature_width), 'ep'...  14.9 us
    dot_general x8, matrix products, matmul(): return jnp.dot(left, right, preferred_element_type=jnp.float32)  14.5 us
    all_gather x1, waiting for transfers between devices, body(): gathered = lax.all_gather(received, 'rep', axis=0, tiled=True)  13 us
    dot_general x5, matrix products, rows_times(): lax.dot_general(left, right, (((1,), (1,)), ((), ())), preferred_element_...  11.7 us
    all_to_all x1, starting transfers between devices, body(): lax.all_to_all(token_part.reshape(experts, per_pair, feature_width), 'ep'...  4.42 us
    all_to_all x1, starting transfers between devices, body(): lax.all_to_all(expert_out.reshape(experts, per_pair, feature_width), 'ep'...  4.26 us
    dot_general x2, matrix products, inner_rows(): lax.dot_general(left, right, (((0,), (0,)), ((), ())), preferred_element_...  3.76 us
  transfers between devices with their start and end apart: 3, of which 2 were waited for; matrix products, arithmetic and copies ran while one was open for 20% of the time, Pallas kernels for 0%

profile of v5, /device:TPU:0, one launch (start us, length us, event | category | flops | bytes accessed | tf_op | source)
XLA Modules:
  0.0 147.1 jit_solution(9401291888817018612)
XLA Ops:
  7.2 0.0 copy-start
  7.2 0.0 all-gather.2.cloned.1.call-start
  7.2 0.8 slice.30
  8.1 0.8 slice.31
  8.8 0.2 fusion.42
  9.0 0.1 select_reduce_fusion
  9.2 1.7 %convolution_convert_fusion.1 = bf16[256,2048]{1,0:T(8,128)(2,1)S(1)} fusion(bf16[256,2048]{1,0:T(8,128)(2,1)} %param.7, s32[256]{0:T(256)S(1)} %compare_select_fusion.1), kind=kOutput, calls=%fused_computation.26 | convolution fusion | flops 269025280 | bytes 2098176 | tf_op jit(solution)/shard_map/dot_general | solution.py:27
  10.8 1.7 %fusion.29 = bf16[256,2048]{1,0:T(8,128)(2,1)S(1)} fusion(bf16[256,2048]{1,0:T(8,128)(2,1)} %param.13, f32[256]{0:T(256)S(1)} %select_reduce_fusion, s32[256]{0:T(256)S(1)} %compare_select_fusion.1), kind=kOutput, calls=%fused_computation.24 | convolution fusion | flops 269549568 | bytes 2099200 | tf_op jit(solution)/shard_map/dot_general | solution.py:27
  12.5 0.2 pad_maximum_fusion
  12.7 55.4 %all_to_all.15 = bf16[8,32,4096]{2,1,0:T(8,128)(2,1)} all-to-all(bf16[8,32,4096]{2,1,0:T(8,128)(2,1)S(1)} %bitcast.56), channel_id=1, replica_groups=mesh['rep'=4,'ep'=8] {'ep'}, dimensions={0} | all-to-all | bytes 4194304 | tf_op jit(solution)/shard_map/all_to_all | solution.py:58
  68.1 0.0 all-gather.2.cloned.1.call-update
  68.2 0.0 copy-start.1
  68.2 0.0 copy-start.3
  68.2 3.4 %fusion.18 = f32[256,768]{1,0:T(8,128)S(1)} fusion(bf16[1,768,2048]{2,1,0:T(8,128)(2,1)} %param.10, bf16[256,4096]{1,0:T(8,128)(2,1)} %bitcast.53), kind=kOutput, calls=%fused_computation.18 | convolution fusion | flops 805306368 | bytes 4980736 | tf_op jit(solution)/shard_map/dot_general | solution.py:15
  71.6 0.0 copy-done.1
  71.6 0.4 copy-done.3
  71.9 0.0 copy-start.7
  71.9 1.0 fusion.14
  73.0 0.0 copy-done
  73.0 0.0 copy-start.9
  73.0 2.0 %fusion.30 = bf16[256,2048]{1,0:T(8,128)(2,1)} fusion(bf16[1,768,2048]{2,1,0:T(8,128)(2,1)S(1)} %copy-done, f32[256,768]{1,0:T(8,128)S(1)} %fusion.14, f32[256,768]{1,0:T(8,128)S(1)} %fusion.18), kind=kOutput, calls=%fused_computation.27 | convolution fusion | flops 807010304 | bytes 5767168 | tf_op jit(solution)/shard_map/dot_general | solution.py:27
  75.0 0.0 copy-done.7
  75.0 0.0 copy-done.9
  75.0 4.3 %all-to-all-start.1 = ((bf16[8,32,2048]{2,1,0:T(8,128)(2,1)}), bf16[8,32,2048]{2,1,0:T(8,128)(2,1)}, u32[]{:S(2)}, u32[]{:S(2)}) async-start(bf16[8,32,2048]{2,1,0:T(8,128)(2,1)} %bitcast.57), calls=%async_computation.1 | async-start | bytes 2097152 | tf_op jit(solution)/shard_map/all_to_all | solution.py:78
  79.3 0.1 pad.1.clone
  79.4 0.1 pad.3.clone
  79.5 0.1 pad.2.clone
  79.6 0.0 copy-start.2
  79.6 0.9 compare_select_fusion
  80.4 2.7 %dynamic-slice_bitcast_fusion = (bf16[192,2048]{1,0:T(8,128)(2,1)}, bf16[192,2048]{1,0:T(8,128)(2,1)}) fusion(bf16[1,768,2048]{2,1,0:T(8,128)(2,1)} %param.11, s32[]{:T(128)S(6)} %select_n.28, bf16[1,768,2048]{2,1,0:T(8,128)(2,1)} %param.10), kind=kLoop, calls=%fused_computation.52 | loop fusion | bytes 3145732 | tf_op jit(solution)/shard_map/dynamic_slice | solution.py:120
  83.1 0.0 copy-done.2
  83.1 0.0 copy-start.4
  83.1 0.0 copy-start.8
  83.1 1.0 fusion.8
  84.1 0.9 copy-done.4
  85.0 0.2 copy-done.8
  85.2 0.0 copy-start.5
  85.2 0.0 copy-start.10
  85.2 1.0 fusion.12
  86.2 0.9 copy-done.5
  87.2 0.2 copy-done.10
  87.3 2.1 %fusion.26 = bf16[256,2048]{1,0:T(8,128)(2,1)} fusion(f32[256,2048]{1,0:T(8,128)S(1)} %fusion.12, bf16[1,768,2048]{2,1,0:T(8,128)(2,1)S(1)} %copy-done.5, f32[256,768]{1,0:T(8,128)S(1)} %copy-done.8, f32[256,768]{1,0:T(8,128)S(1)} %fusion.8, f32[256,768]{1,0:T(8,128)S(1)} %copy-done.10), kind=kOutput, calls=%fused_computation.23 | convolution fusion | flops 808321024 | bytes 8650752 | tf_op jit(solution)/shard_map/dot_general | solution.py:27
  89.5 14.9 %all-to-all-done.1 = bf16[8,32,2048]{2,1,0:T(8,128)(2,1)} async-done(((bf16[8,32,2048]{2,1,0:T(8,128)(2,1)}), bf16[8,32,2048]{2,1,0:T(8,128)(2,1)}, u32[]{:S(2)}, u32[]{:S(2)}) %all-to-all-start.1) | async-done | bytes 1048608 | tf_op jit(solution)/shard_map/all_to_all | solution.py:78
  104.4 4.4 %all-to-all-start.2 = ((bf16[8,32,2048]{2,1,0:T(8,128)(2,1)}), bf16[8,32,2048]{2,1,0:T(8,128)(2,1)}, u32[]{:S(2)}, u32[]{:S(2)}) async-start(bf16[8,32,2048]{2,1,0:T(8,128)(2,1)} %bitcast.58), calls=%async_computation.2 | async-start | bytes 2097152 | tf_op jit(solution)/shard_map/all_to_all | solution.py:92
  108.8 3.2 %multiply_reduce_fusion = (f32[256]{0:T(256)S(1)}, bf16[256,2048]{1,0:T(8,128)(2,1)}) fusion(bf16[256,2048]{1,0:T(8,128)(2,1)} %param.13, f32[256]{0:T(256)S(1)} %bitcast.62, bf16[256,2048]{1,0:T(8,128)(2,1)} %bitcast.10, s32[256]{0:T(256)S(1)} %bitcast.59), kind=kOutput, calls=%fused_computation.31 | convolution fusion | flops 271122176 | bytes 3148800 | tf_op jit(solution)/shard_map/dot_general | solution.py:27
  112.0 0.7 maximum_maximum_fusion
  112.7 13.0 %all-gather.2.cloned.1.call-done = bf16[1024,4096]{1,0:T(8,128)(2,1)} async-done(((bf16[256,4096]{1,0:T(8,128)(2,1)}), bf16[1024,4096]{1,0:T(8,128)(2,1)}) %all-gather.2.cloned.1.call-update) | async-done | bytes 8388624 | tf_op jit(solution)/shard_map/all_gather | solution.py:66
  125.7 0.0 copy-start.6
  125.7 4.6 %fusion.2 = f32[1024,384]{0,1:T(8,128)S(1)} fusion(bf16[1024,4096]{1,0:T(8,128)(2,1)} %all-gather.2.cloned.1.call-done, bf16[192,2048]{1,0:T(8,128)(2,1)} %get-tuple-element.20, bf16[192,2048]{1,0:T(8,128)(2,1)} %get-tuple-element.21), kind=kOutput, calls=%fused_computation.2 | convolution fusion | flops 1613758464 | bytes 7340032 | tf_op jit(solution)/shard_map/dot_general | solution.py:15
  130.3 0.5 copy-done.6
  130.8 1.7 %multiply_convert_fusion.3 = (bf16[1024,192]{0,1:T(8,128)(2,1)S(1)}, bf16[1024,192]{0,1:T(8,128)(2,1)S(1)}) fusion(f32[1024,384]{0,1:T(8,128)S(1)} %fusion.2, bf16[1,768,2048]{2,1,0:T(8,128)(2,1)S(1)} %copy-done, s32[]{:T(128)S(6)} %select_n.28, bf16[1024,4096]{1,0:T(8,128)(2,1)S(1)} %copy-done.6), kind=kOutput, calls=%fused_computation.49 | convolution fusion | flops 807862272 | bytes 7340036 | tf_op jit(solution)/shard_map/dot_general | solution.py:15
  132.5 1.8 %fusion.20 = bf16[384,2048]{1,0:T(8,128)(2,1)S(1)} fusion(bf16[1024,4096]{1,0:T(8,128)(2,1)S(1)} %copy-done.6, bf16[1024,192]{0,1:T(8,128)(2,1)S(1)} %get-tuple-element.15, bf16[1024,192]{0,1:T(8,128)(2,1)S(1)} %get-tuple-element.14), kind=kOutput, calls=%fused_computation.20 | convolution fusion | flops 1612972032 | bytes 6553600 | tf_op jit(solution)/shard_map/dot_general | solution.py:21
  134.3 1.9 %fusion.36 = bf16[1,192,2048]{2,1,0:T(8,128)(2,1)} fusion(bf16[1024,4096]{1,0:T(8,128)(2,1)S(1)} %copy-done.6, f32[1024,384]{0,1:T(8,128)S(1)} %fusion.2), kind=kOutput, calls=%fused_computation.29 | convolution fusion | flops 806879232 | bytes 6553600 | tf_op jit(solution)/shard_map/dot_general | solution.py:21
  136.3 1.3 slice_bitcast_fusion
  137.6 0.0 all-to-all-done.2
  137.6 2.7 %convolution_convert_fusion = bf16[256,2048]{1,0:T(8,128)(2,1)} fusion(bf16[256,2048]{1,0:T(8,128)(2,1)} %bitcast.12, s32[256]{0:T(256)S(1)} %bitcast.60), kind=kOutput, calls=%fused_computation.25 | convolution fusion | flops 269025280 | bytes 2098176 | tf_op jit(solution)/shard_map/dot_general | solution.py:27
  (4 shorter events, 0.0 us)
Async XLA Ops:
  7.2 65.8 %copy-start = (bf16[1,768,2048]{2,1,0:T(8,128)(2,1)S(1)}, bf16[1,768,2048]{2,1,0:T(8,128)(2,1)}, u32[]{:S(2)}) copy-start(bf16[1,768,2048]{2,1,0:T(8,128)(2,1)} %param.12) | copy-start | bytes 9437188
  7.2 118.5 %all-gather.2.cloned.1.call-start = ((), (), s32[]{:S(2)}) async-start(), calls=%async_computation.3 | async-start | bytes 10485760 | tf_op jit(solution)/shard_map/all_gather | solution.py:66
  68.2 3.4 %copy-start.1 = (bf16[8,32,4096]{2,1,0:T(8,128)(2,1)S(1)}, bf16[8,32,4096]{2,1,0:T(8,128)(2,1)}, u32[]{:S(2)}) copy-start(bf16[8,32,4096]{2,1,0:T(8,128)(2,1)} %all_to_all.15) | copy-start | bytes 6291460
  68.2 3.8 %copy-start.3 = (bf16[1,768,2048]{2,1,0:T(8,128)(2,1)S(1)}, bf16[1,768,2048]{2,1,0:T(8,128)(2,1)}, u32[]{:S(2)}) copy-start(bf16[1,768,2048]{2,1,0:T(8,128)(2,1)} %param.11) | copy-start | bytes 9437188
  71.9 3.1 %copy-start.7 = (f32[256,768]{1,0:T(8,128)}, f32[256,768]{1,0:T(8,128)S(1)}, u32[]{:S(2)}) copy-start(f32[256,768]{1,0:T(8,128)S(1)} %fusion.18) | copy-start | bytes 2359300
  73.0 2.0 %copy-start.9 = (f32[256,768]{1,0:T(8,128)}, f32[256,768]{1,0:T(8,128)S(1)}, u32[]{:S(2)}) copy-start(f32[256,768]{1,0:T(8,128)S(1)} %fusion.14) | copy-start | bytes 2359300
  75.0 29.4 %all-to-all-start.1 = ((bf16[8,32,2048]{2,1,0:T(8,128)(2,1)}), bf16[8,32,2048]{2,1,0:T(8,128)(2,1)}, u32[]{:S(2)}, u32[]{:S(2)}) async-start(bf16[8,32,2048]{2,1,0:T(8,128)(2,1)} %bitcast.57), calls=%async_computation.1 | async-start | bytes 2097152 | tf_op jit(solution)/shard_map/all_to_all | solution.py:78
  79.6 3.6 %copy-start.2 = (bf16[8,32,4096]{2,1,0:T(8,128)(2,1)S(1)}, bf16[8,32,4096]{2,1,0:T(8,128)(2,1)}, u32[]{:S(2)}) copy-start(bf16[8,32,4096]{2,1,0:T(8,128)(2,1)} %all_to_all.15) | copy-start | bytes 6291460
  83.1 1.9 %copy-start.4 = (bf16[1,768,2048]{2,1,0:T(8,128)(2,1)S(1)}, bf16[1,768,2048]{2,1,0:T(8,128)(2,1)}, u32[]{:S(2)}) copy-start(bf16[1,768,2048]{2,1,0:T(8,128)(2,1)} %param.11) | copy-start | bytes 9437188
  83.1 2.1 %copy-start.8 = (f32[256,768]{1,0:T(8,128)S(1)}, f32[256,768]{1,0:T(8,128)}, u32[]{:S(2)}) copy-start(f32[256,768]{1,0:T(8,128)} %copy-done.7) | copy-start | bytes 2359300
  85.2 2.0 %copy-start.5 = (bf16[1,768,2048]{2,1,0:T(8,128)(2,1)S(1)}, bf16[1,768,2048]{2,1,0:T(8,128)(2,1)}, u32[]{:S(2)}) copy-start(bf16[1,768,2048]{2,1,0:T(8,128)(2,1)} %param.10) | copy-start | bytes 9437188
  85.2 2.2 %copy-start.10 = (f32[256,768]{1,0:T(8,128)S(1)}, f32[256,768]{1,0:T(8,128)}, u32[]{:S(2)}) copy-start(f32[256,768]{1,0:T(8,128)} %copy-done.9) | copy-start | bytes 2359300
  104.4 33.2 %all-to-all-start.2 = ((bf16[8,32,2048]{2,1,0:T(8,128)(2,1)}), bf16[8,32,2048]{2,1,0:T(8,128)(2,1)}, u32[]{:S(2)}, u32[]{:S(2)}) async-start(bf16[8,32,2048]{2,1,0:T(8,128)(2,1)} %bitcast.58), calls=%async_computation.2 | async-start | bytes 2097152 | tf_op jit(solution)/shard_map/all_to_all | solution.py:92
  125.7 5.1 %copy-start.6 = (bf16[1024,4096]{1,0:T(8,128)(2,1)S(1)}, bf16[1024,4096]{1,0:T(8,128)(2,1)}, u32[]{:S(2)}) copy-start(bf16[1024,4096]{1,0:T(8,128)(2,1)} %all-gather.2.cloned.1.call-done) | copy-start | bytes 25165828
Sparse Core Ops, SparseCore 0:
  68.3 57.3 all-gather.1

commit v6 on v5

--- a/solution.py
+++ b/solution.py
@@ -50,6 +50,7 @@
     hit = slot_ids[:, None] == slot_index[None, :]
     slot_gate = jnp.sum(jnp.where(hit, flat_gates[None, :], 0.0), axis=1)
     pick = jnp.any(hit.reshape(total_slots, tok_count, live_cols), axis=2).astype(jnp.bfloat16)
+    pick = lax.optimization_barrier(pick)
     send_rows = matmul(pick, tokens).astype(jnp.bfloat16)
     grad_rows = matmul(pick, out_grad)
     scaled_grad = (slot_gate[:, None] * grad_rows).astype(jnp.bfloat16)
@@ -109,6 +110,7 @@
         layer_sum = layer_sum + gate_grid[:, col : col + 1] * out_rows
         gate_cols.append(jnp.sum(out_grad.astype(jnp.float32) * out_rows, axis=1))
     layer_out = layer_sum.astype(jnp.bfloat16)
+    back_pick = lax.optimization_barrier(back_pick)
     gate_cols.extend(
         [jnp.zeros((tok_count,), jnp.float32)] * (top_count - live_cols)
     )

time: 148 us -> 148 us (level)
  no operation moved by 1% of the time
where the time goes in v6:
time: 148 us; the launch traced here: 147 us
  blocking collectives  55.4 us (37%)
  matrix products  30 us (20%)
  waiting for transfers between devices  27.9 us (19%)
  between operations  14.2 us (10%)
  local copies, waits for them, and re-layouts  9.05 us (6%)
  starting transfers between devices  8.71 us (6%)
  other arithmetic  1.85 us (1%)
    all_to_all x1, blocking collectives, body(): lax.all_to_all(outgoing.reshape(experts, per_pair, 2 * feature_width), 'e...  55.4 us
    all_to_all x1, waiting for transfers between devices, body(): lax.all_to_all(expert_out.reshape(experts, per_pair, feature_width), 'ep'...  14.9 us
    dot_general x8, matrix products, matmul(): return jnp.dot(left, right, preferred_element_type=jnp.float32)  14.5 us
    all_gather x1, waiting for transfers between devices, body(): gathered = lax.all_gather(received, 'rep', axis=0, tiled=True)  13 us
    dot_general x5, matrix products, rows_times(): lax.dot_general(left, right, (((1,), (1,)), ((), ())), preferred_element_...  11.7 us
    all_to_all x1, starting transfers between devices, body(): lax.all_to_all(token_part.reshape(experts, per_pair, feature_width), 'ep'...  4.42 us
    all_to_all x1, starting transfers between devices, body(): lax.all_to_all(expert_out.reshape(experts, per_pair, feature_width), 'ep'...  4.26 us
    dot_general x2, matrix products, inner_rows(): lax.dot_general(left, right, (((0,), (0,)), ((), ())), preferred_element_...  3.76 us
  transfers between devices with their start and end apart: 3, of which 2 were waited for; matrix products, arithmetic and copies ran while one was open for 20% of the time, Pallas kernels for 0%

profile of v6, /device:TPU:0, one launch (start us, length us, event | category | flops | bytes accessed | tf_op | source)
XLA Modules:
  0.0 147.1 jit_solution(17382451441314853799)
XLA Ops:
  7.2 0.0 copy-start
  7.2 0.0 all-gather.2.cloned.1.call-start
  7.2 0.8 slice.30
  8.1 0.8 slice.31
  8.8 0.2 fusion.42
  9.1 0.1 select_reduce_fusion
  9.2 1.7 %convolution_convert_fusion.1 = bf16[256,2048]{1,0:T(8,128)(2,1)S(1)} fusion(bf16[256,256]{1,0:T(8,128)(2,1)S(1)} %fusion.54, bf16[256,2048]{1,0:T(8,128)(2,1)} %param.7), kind=kOutput, calls=%fused_computation.26 | convolution fusion | flops 268959744 | bytes 2228224 | tf_op jit(solution)/shard_map/dot_general | solution.py:27
  10.9 1.7 %fusion.29 = bf16[256,2048]{1,0:T(8,128)(2,1)S(1)} fusion(bf16[256,256]{1,0:T(8,128)(2,1)S(1)} %fusion.54, bf16[256,2048]{1,0:T(8,128)(2,1)} %param.13, f32[256]{0:T(256)S(1)} %select_reduce_fusion), kind=kOutput, calls=%fused_computation.24 | convolution fusion | flops 269484032 | bytes 2229248 | tf_op jit(solution)/shard_map/dot_general | solution.py:27
  12.5 0.2 pad_maximum_fusion
  12.8 55.4 %all_to_all.15 = bf16[8,32,4096]{2,1,0:T(8,128)(2,1)} all-to-all(bf16[8,32,4096]{2,1,0:T(8,128)(2,1)S(1)} %bitcast.59), channel_id=1, replica_groups=mesh['rep'=4,'ep'=8] {'ep'}, dimensions={0} | all-to-all | bytes 4194304 | tf_op jit(solution)/shard_map/all_to_all | solution.py:59
  68.2 0.0 all-gather.2.cloned.1.call-update
  68.2 0.0 copy-start.1
  68.2 0.0 copy-start.3
  68.2 3.4 %fusion.18 = f32[256,768]{1,0:T(8,128)S(1)} fusion(bf16[1,768,2048]{2,1,0:T(8,128)(2,1)} %param.10, bf16[256,4096]{1,0:T(8,128)(2,1)} %bitcast.56), kind=kOutput, calls=%fused_computation.18 | convolution fusion | flops 805306368 | bytes 4980736 | tf_op jit(solution)/shard_map/dot_general | solution.py:15
  71.6 0.0 copy-done.1
  71.6 0.4 copy-done.3
  72.0 0.0 copy-start.7
  72.0 1.0 fusion.14
  73.0 0.0 copy-done
  73.0 0.0 copy-start.9
  73.0 2.0 %fusion.30 = bf16[256,2048]{1,0:T(8,128)(2,1)} fusion(bf16[1,768,2048]{2,1,0:T(8,128)(2,1)S(1)} %copy-done, f32[256,768]{1,0:T(8,128)S(1)} %fusion.14, f32[256,768]{1,0:T(8,128)S(1)} %fusion.18), kind=kOutput, calls=%fused_computation.27 | convolution fusion | flops 807010304 | bytes 5767168 | tf_op jit(solution)/shard_map/dot_general | solution.py:27
  75.0 0.0 copy-done.7
  75.1 0.0 copy-done.9
  75.1 4.3 %all-to-all-start.1 = ((bf16[8,32,2048]{2,1,0:T(8,128)(2,1)}), bf16[8,32,2048]{2,1,0:T(8,128)(2,1)}, u32[]{:S(2)}, u32[]{:S(2)}) async-start(bf16[8,32,2048]{2,1,0:T(8,128)(2,1)} %bitcast.61), calls=%async_computation.1 | async-start | bytes 2097152 | tf_op jit(solution)/shard_map/all_to_all | solution.py:79
  79.3 0.7 compare_select_fusion
  80.0 0.1 pad.1.clone
  80.1 0.1 pad.3.clone
  80.2 0.1 pad.2.clone
  80.3 0.1 fusion.55
  80.4 0.0 copy-start.2
  80.4 2.9 %dynamic-slice_bitcast_fusion = (bf16[192,2048]{1,0:T(8,128)(2,1)}, bf16[192,2048]{1,0:T(8,128)(2,1)}) fusion(bf16[1,768,2048]{2,1,0:T(8,128)(2,1)} %param.11, s32[]{:T(128)S(6)} %select_n.28, bf16[1,768,2048]{2,1,0:T(8,128)(2,1)} %param.10), kind=kLoop, calls=%fused_computation.52 | loop fusion | bytes 3145732 | tf_op jit(solution)/shard_map/dynamic_slice | solution.py:122
  83.2 0.0 copy-done.2
  83.2 0.0 copy-start.4
  83.2 0.0 copy-start.8
  83.2 1.0 fusion.8
  84.3 0.9 copy-done.4
  85.1 0.2 copy-done.8
  85.3 0.0 copy-start.5
  85.3 0.0 copy-start.10
  85.3 1.0 fusion.12
  86.3 0.9 copy-done.5
  87.3 0.2 copy-done.10
  87.4 2.1 %fusion.26 = bf16[256,2048]{1,0:T(8,128)(2,1)} fusion(f32[256,2048]{1,0:T(8,128)S(1)} %fusion.12, bf16[1,768,2048]{2,1,0:T(8,128)(2,1)S(1)} %copy-done.5, f32[256,768]{1,0:T(8,128)S(1)} %copy-done.8, f32[256,768]{1,0:T(8,128)S(1)} %fusion.8, f32[256,768]{1,0:T(8,128)S(1)} %copy-done.10), kind=kOutput, calls=%fused_computation.23 | convolution fusion | flops 808321024 | bytes 8650752 | tf_op jit(solution)/shard_map/dot_general | solution.py:27
  89.6 14.9 %all-to-all-done.1 = bf16[8,32,2048]{2,1,0:T(8,128)(2,1)} async-done(((bf16[8,32,2048]{2,1,0:T(8,128)(2,1)}), bf16[8,32,2048]{2,1,0:T(8,128)(2,1)}, u32[]{:S(2)}, u32[]{:S(2)}) %all-to-all-start.1) | async-done | bytes 1048608 | tf_op jit(solution)/shard_map/all_to_all | solution.py:79
  104.5 4.4 %all-to-all-start.2 = ((bf16[8,32,2048]{2,1,0:T(8,128)(2,1)}), bf16[8,32,2048]{2,1,0:T(8,128)(2,1)}, u32[]{:S(2)}, u32[]{:S(2)}) async-start(bf16[8,32,2048]{2,1,0:T(8,128)(2,1)} %bitcast.60), calls=%async_computation.2 | async-start | bytes 2097152 | tf_op jit(solution)/shard_map/all_to_all | solution.py:93
  108.9 3.2 %multiply_reduce_fusion = (f32[256]{0:T(256)S(1)}, bf16[256,2048]{1,0:T(8,128)(2,1)}) fusion(bf16[256,2048]{1,0:T(8,128)(2,1)} %param.13, f32[256]{0:T(256)S(1)} %bitcast.65, bf16[256,2048]{1,0:T(8,128)(2,1)} %bitcast.10, s32[256]{0:T(256)S(1)} %bitcast.63), kind=kOutput, calls=%fused_computation.31 | convolution fusion | flops 271122176 | bytes 3148800 | tf_op jit(solution)/shard_map/dot_general | solution.py:27
  112.0 0.7 maximum_maximum_fusion
  112.7 13.0 %all-gather.2.cloned.1.call-done = bf16[1024,4096]{1,0:T(8,128)(2,1)} async-done(((bf16[256,4096]{1,0:T(8,128)(2,1)}), bf16[1024,4096]{1,0:T(8,128)(2,1)}) %all-gather.2.cloned.1.call-update) | async-done | bytes 8388624 | tf_op jit(solution)/shard_map/all_gather | solution.py:67
  125.7 0.0 copy-start.6
  125.7 4.6 %fusion.2 = f32[1024,384]{0,1:T(8,128)S(1)} fusion(bf16[1024,4096]{1,0:T(8,128)(2,1)} %all-gather.2.cloned.1.call-done, bf16[192,2048]{1,0:T(8,128)(2,1)} %get-tuple-element.20, bf16[192,2048]{1,0:T(8,128)(2,1)} %get-tuple-element.21), kind=kOutput, calls=%fused_computation.2 | convolution fusion | flops 1613758464 | bytes 7340032 | tf_op jit(solution)/shard_map/dot_general | solution.py:15
  130.3 0.5 copy-done.6
  130.8 1.7 %multiply_convert_fusion.3 = (bf16[1024,192]{0,1:T(8,128)(2,1)S(1)}, bf16[1024,192]{0,1:T(8,128)(2,1)S(1)}) fusion(f32[1024,384]{0,1:T(8,128)S(1)} %fusion.2, bf16[1,768,2048]{2,1,0:T(8,128)(2,1)S(1)} %copy-done, s32[]{:T(128)S(6)} %select_n.28, bf16[1024,4096]{1,0:T(8,128)(2,1)S(1)} %copy-done.6), kind=kOutput, calls=%fused_computation.49 | convolution fusion | flops 807862272 | bytes 7340036 | tf_op jit(solution)/shard_map/dot_general | solution.py:15
  132.5 1.8 %fusion.20 = bf16[384,2048]{1,0:T(8,128)(2,1)S(1)} fusion(bf16[1024,4096]{1,0:T(8,128)(2,1)S(1)} %copy-done.6, bf16[1024,192]{0,1:T(8,128)(2,1)S(1)} %get-tuple-element.15, bf16[1024,192]{0,1:T(8,128)(2,1)S(1)} %get-tuple-element.14), kind=kOutput, calls=%fused_computation.20 | convolution fusion | flops 1612972032 | bytes 6553600 | tf_op jit(solution)/shard_map/dot_general | solution.py:21
  134.4 1.9 %fusion.36 = bf16[1,192,2048]{2,1,0:T(8,128)(2,1)} fusion(bf16[1024,4096]{1,0:T(8,128)(2,1)S(1)} %copy-done.6, f32[1024,384]{0,1:T(8,128)S(1)} %fusion.2), kind=kOutput, calls=%fused_computation.29 | convolution fusion | flops 806879232 | bytes 6553600 | tf_op jit(solution)/shard_map/dot_general | solution.py:21
  136.3 1.3 slice_bitcast_fusion
  137.6 0.0 all-to-all-done.2
  137.6 2.6 %convolution_convert_fusion = bf16[256,2048]{1,0:T(8,128)(2,1)} fusion(bf16[256,256]{1,0:T(8,128)(2,1)S(1)} %fusion.55, bf16[256,2048]{1,0:T(8,128)(2,1)} %bitcast.12), kind=kOutput, calls=%fused_computation.25 | convolution fusion | flops 268959744 | bytes 2228224 | tf_op jit(solution)/shard_map/dot_general | solution.py:27
  (5 shorter events, 0.0 us)
Async XLA Ops:
  7.2 65.8 %copy-start = (bf16[1,768,2048]{2,1,0:T(8,128)(2,1)S(1)}, bf16[1,768,2048]{2,1,0:T(8,128)(2,1)}, u32[]{:S(2)}) copy-start(bf16[1,768,2048]{2,1,0:T(8,128)(2,1)} %param.12) | copy-start | bytes 9437188
  7.2 118.5 %all-gather.2.cloned.1.call-start = ((), (), s32[]{:S(2)}) async-start(), calls=%async_computation.3 | async-start | bytes 10485760 | tf_op jit(solution)/shard_map/all_gather | solution.py:67
  68.2 3.4 %copy-start.1 = (bf16[8,32,4096]{2,1,0:T(8,128)(2,1)S(1)}, bf16[8,32,4096]{2,1,0:T(8,128)(2,1)}, u32[]{:S(2)}) copy-start(bf16[8,32,4096]{2,1,0:T(8,128)(2,1)} %all_to_all.15) | copy-start | bytes 6291460
  68.2 3.8 %copy-start.3 = (bf16[1,768,2048]{2,1,0:T(8,128)(2,1)S(1)}, bf16[1,768,2048]{2,1,0:T(8,128)(2,1)}, u32[]{:S(2)}) copy-start(bf16[1,768,2048]{2,1,0:T(8,128)(2,1)} %param.11) | copy-start | bytes 9437188
  72.0 3.1 %copy-start.7 = (f32[256,768]{1,0:T(8,128)}, f32[256,768]{1,0:T(8,128)S(1)}, u32[]{:S(2)}) copy-start(f32[256,768]{1,0:T(8,128)S(1)} %fusion.18) | copy-start | bytes 2359300
  73.0 2.0 %copy-start.9 = (f32[256,768]{1,0:T(8,128)}, f32[256,768]{1,0:T(8,128)S(1)}, u32[]{:S(2)}) copy-start(f32[256,768]{1,0:T(8,128)S(1)} %fusion.14) | copy-start | bytes 2359300
  75.1 29.4 %all-to-all-start.1 = ((bf16[8,32,2048]{2,1,0:T(8,128)(2,1)}), bf16[8,32,2048]{2,1,0:T(8,128)(2,1)}, u32[]{:S(2)}, u32[]{:S(2)}) async-start(bf16[8,32,2048]{2,1,0:T(8,128)(2,1)} %bitcast.61), calls=%async_computation.1 | async-start | bytes 2097152 | tf_op jit(solution)/shard_map/all_to_all | solution.py:79
  80.4 2.9 %copy-start.2 = (bf16[8,32,4096]{2,1,0:T(8,128)(2,1)S(1)}, bf16[8,32,4096]{2,1,0:T(8,128)(2,1)}, u32[]{:S(2)}) copy-start(bf16[8,32,4096]{2,1,0:T(8,128)(2,1)} %all_to_all.15) | copy-start | bytes 6291460
  83.2 1.9 %copy-start.4 = (bf16[1,768,2048]{2,1,0:T(8,128)(2,1)S(1)}, bf16[1,768,2048]{2,1,0:T(8,128)(2,1)}, u32[]{:S(2)}) copy-start(bf16[1,768,2048]{2,1,0:T(8,128)(2,1)} %param.11) | copy-start | bytes 9437188
  83.2 2.1 %copy-start.8 = (f32[256,768]{1,0:T(8,128)S(1)}, f32[256,768]{1,0:T(8,128)}, u32[]{:S(2)}) copy-start(f32[256,768]{1,0:T(8,128)} %copy-done.7) | copy-start | bytes 2359300
  85.3 1.9 %copy-start.5 = (bf16[1,768,2048]{2,1,0:T(8,128)(2,1)S(1)}, bf16[1,768,2048]{2,1,0:T(8,128)(2,1)}, u32[]{:S(2)}) copy-start(bf16[1,768,2048]{2,1,0:T(8,128)(2,1)} %param.10) | copy-start | bytes 9437188
  85.3 2.1 %copy-start.10 = (f32[256,768]{1,0:T(8,128)S(1)}, f32[256,768]{1,0:T(8,128)}, u32[]{:S(2)}) copy-start(f32[256,768]{1,0:T(8,128)} %copy-done.9) | copy-start | bytes 2359300
  104.5 33.2 %all-to-all-start.2 = ((bf16[8,32,2048]{2,1,0:T(8,128)(2,1)}), bf16[8,32,2048]{2,1,0:T(8,128)(2,1)}, u32[]{:S(2)}, u32[]{:S(2)}) async-start(bf16[8,32,2048]{2,1,0:T(8,128)(2,1)} %bitcast.60), calls=%async_computation.2 | async-start | bytes 2097152 | tf_op jit(solution)/shard_map/all_to_all | solution.py:93
  125.7 5.1 %copy-start.6 = (bf16[1024,4096]{1,0:T(8,128)(2,1)S(1)}, bf16[1024,4096]{1,0:T(8,128)(2,1)}, u32[]{:S(2)}) copy-start(bf16[1024,4096]{1,0:T(8,128)(2,1)} %all-gather.2.cloned.1.call-done) | copy-start | bytes 25165828
Sparse Core Ops, SparseCore 0:
  68.3 57.3 all-gather.1

commit v7 on v5

--- a/solution.py
+++ b/solution.py
@@ -75,6 +75,7 @@
     activated = jax.nn.silu(pre_gate)
     hidden = (activated * pre_up).astype(jnp.bfloat16)
     expert_out = matmul(hidden, down_mat).astype(jnp.bfloat16)
+    expert_out, grad_in = lax.optimization_barrier((expert_out, grad_in))
     returned = lax.all_to_all(
         expert_out.reshape(experts, per_pair, feature_width),
         "ep",
@@ -114,27 +115,28 @@
     )
     gates_grad = jnp.stack(gate_cols, axis=1)
 
-    share = gate_mat.shape[0] // lax.axis_size("rep")
-    start = lax.axis_index("rep") * share
-    gate_share = lax.dynamic_slice_in_dim(gate_mat, start, share, axis=0)
-    up_share = lax.dynamic_slice_in_dim(up_mat, start, share, axis=0)
-    down_share = lax.dynamic_slice_in_dim(down_mat, start, share, axis=0)
+    copies = lax.axis_size("rep")
+    share = gate_mat.shape[0] // copies
+
+    def by_share(values):
+        return values.reshape(total_slots, copies, share).transpose(1, 0, 2)
+
+    own_terms = jnp.concatenate(
+        [by_share(gate_pre_grad), by_share(up_pre_grad), by_share(hidden)], axis=2
+    )
+    me = lax.axis_index("rep")
+    blocks = [own_terms[me]] + [
+        lax.ppermute(own_terms[me ^ k], "rep", [(r, r ^ k) for r in range(copies)])
+        for k in range(1, copies)
+    ]
+    order = jnp.arange(copies, dtype=jnp.int32) ^ me.astype(jnp.int32)
+    terms = jnp.take(jnp.stack(blocks), order, axis=0).reshape(copies * total_slots, 3 * share)
     rows_all = gathered[:, :feature_width]
     grad_all = gathered[:, feature_width:]
-    pre_both = rows_times(rows_all, jnp.concatenate([gate_share, up_share], axis=0))
-    pre_gate_s = pre_both[:, :share]
-    pre_up_s = pre_both[:, share:]
-    activated_s = jax.nn.silu(pre_gate_s)
-    hidden_s = (activated_s * pre_up_s).astype(jnp.bfloat16)
-    hidden_grad_s = rows_times(grad_all, down_share)
-    gate_pre_grad_s = (hidden_grad_s * pre_up_s * silu_grad(pre_gate_s)).astype(jnp.bfloat16)
-    up_pre_grad_s = (hidden_grad_s * activated_s).astype(jnp.bfloat16)
-    both_w_grad = inner_rows(
-        jnp.concatenate([gate_pre_grad_s, up_pre_grad_s], axis=1), rows_all
-    ).astype(jnp.bfloat16)
+    both_w_grad = inner_rows(terms[:, : 2 * share], rows_all).astype(jnp.bfloat16)
     gate_w_grad = both_w_grad[:share][None]
     up_w_grad = both_w_grad[share:][None]
-    down_w_grad = inner_rows(hidden_s, grad_all).astype(jnp.bfloat16)[None]
+    down_w_grad = inner_rows(terms[:, 2 * share :], grad_all).astype(jnp.bfloat16)[None]
     part_back, gate_w_grad, up_w_grad, down_w_grad = lax.optimization_barrier(
         (part_back, gate_w_grad, up_w_grad, down_w_grad)
     )

time: 148 us -> 171 us (1.16)
  waiting for transfers between devices: 27.9 us -> 35.9 us
  local copies, waits for them, and re-layouts: 8.92 us -> 16.3 us
  other arithmetic: 1.87 us -> 5.66 us
  starting transfers between devices: 8.71 us -> 12.2 us
    ppermute x0 -> x3, waiting for transfers between devices: none -> 22.5 us  [body(): lax.ppermute(own_terms[me ^ k], 'rep', [(r, r ^ k) for r in range(copies)])]
    all_to_all x1, waiting for transfers between devices: 14.9 us -> 0.01 us  [body(): lax.all_to_all(expert_out.reshape(experts, per_pair, feature_width), 'ep'...]
    all_to_all x1, waiting for transfers between devices: 0.01 us -> 13.3 us  [body(): lax.all_to_all(token_part.reshape(experts, per_pair, feature_width), 'ep'...]
    all_gather x1, waiting for transfers between devices: 13 us -> 0.01 us  [body(): gathered = lax.all_gather(received, 'rep', axis=0, tiled=True)]
    dot_general x2, matrix products: 3.76 us -> 8.26 us  [inner_rows(): lax.dot_general(left, right, (((0,), (0,)), ((), ())), preferred_element_...]
    gather x0 -> x2, local copies, waits for them, and re-layouts: none -> 4.36 us  [body(): jnp.take(jnp.stack(blocks), order, axis=0)]
    convert_element_type x0 -> x3, local copies, waits for them, and re-layouts: none -> 3.75 us  [the longest x1 1.91 us: body(): up_pre_grad = (hidden_grad * activated).astype(jnp.bfloat16)]
    dynamic_slice x1, local copies, waits for them, and re-layouts: 2.7 us -> 0.09 us  [body(): own_terms[me]]
  transfers between devices with their start and end apart: 3 -> 6, of which waited for: 2 -> 3; matrix products, arithmetic and copies ran while one was open for 20% -> 26% of each run, Pallas kernels for 0% -> 0%
where the time goes in v7:
time: 171 us; the launch traced here: 170 us
  blocking collectives  55.4 us (32%)
  waiting for transfers between devices  35.9 us (21%)
  matrix products  30.5 us (18%)
  local copies, waits for them, and re-layouts  16.3 us (10%)
  between operations  14.2 us (8%)
  starting transfers between devices  12.2 us (7%)
  other arithmetic  5.66 us (3%)
    all_to_all x1, blocking collectives, body(): lax.all_to_all(outgoing.reshape(experts, per_pair, 2 * feature_width), 'e...  55.4 us
    ppermute x3, waiting for transfers between devices, body(): lax.ppermute(own_terms[me ^ k], 'rep', [(r, r ^ k) for r in range(copies)])  22.5 us
    all_to_all x1, waiting for transfers between devices, body(): lax.all_to_all(token_part.reshape(experts, per_pair, feature_width), 'ep'...  13.3 us
    dot_general x8, matrix products, matmul(): return jnp.dot(left, right, preferred_element_type=jnp.float32)  13.1 us
    dot_general x3, matrix products, rows_times(): lax.dot_general(left, right, (((1,), (1,)), ((), ())), preferred_element_...  9.14 us
    dot_general x2, matrix products, inner_rows(): lax.dot_general(left, right, (((0,), (0,)), ((), ())), preferred_element_...  8.26 us
    all_to_all x1, starting transfers between devices, body(): lax.all_to_all(token_part.reshape(experts, per_pair, feature_width), 'ep'...  5.93 us
    gather x2, local copies, waits for them, and re-layouts, body(): jnp.take(jnp.stack(blocks), order, axis=0)  4.36 us
  transfers between devices with their start and end apart: 6, of which 3 were waited for; matrix products, arithmetic and copies ran while one was open for 26% of the time, Pallas kernels for 0%

profile of v7, /device:TPU:0, one launch (start us, length us, event | category | flops | bytes accessed | tf_op | source)
XLA Modules:
  0.0 170.2 jit_solution(13311265176872074278)
XLA Ops:
  7.2 0.0 copy-start
  7.2 0.0 all-gather.2.cloned.1.call-start
  7.2 0.0 copy-start.7
  7.2 0.9 slice.31
  8.1 0.2 fusion.35
  8.3 0.8 slice.30
  9.1 0.1 select_reduce_fusion
  9.3 1.7 convolution_convert_fusion.1
  10.9 0.0 copy-done.7
  10.9 0.5 fusion.25
  11.4 0.2 pad_maximum_fusion
  11.6 55.4 %all_to_all.15 = bf16[8,32,4096]{2,1,0:T(8,128)(2,1)} all-to-all(bf16[8,32,4096]{2,1,0:T(8,128)(2,1)S(1)} %bitcast.77), channel_id=1, replica_groups=mesh['rep'=4,'ep'=8] {'ep'}, dimensions={0} | all-to-all | bytes 4194304 | tf_op jit(solution)/shard_map/all_to_all | solution.py:58
  67.0 0.0 all-gather.2.cloned.1.call-update
  67.1 0.1 broadcast_in_dim.57
  67.2 0.6 pad.2.clone
  67.7 0.6 pad.3.clone
  68.3 0.6 pad.1.clone
  69.0 0.0 copy-start.1
  69.0 0.8 compare_select_fusion
  69.8 2.3 %slice.43 = bf16[256,2048]{1,0:T(8,128)(2,1)} slice(bf16[256,4096]{1,0:T(8,128)(2,1)} %bitcast.74), slice={[0:256], [2048:4096]} | slice | bytes 2097152 | tf_op jit(solution)/shard_map/slice | solution.py:69
  72.1 0.0 copy-done.1
  72.1 3.6 %fusion.14 = f32[256,768]{1,0:T(8,128)S(1)} fusion(bf16[1,768,2048]{2,1,0:T(8,128)(2,1)} %param.10, bf16[256,4096]{1,0:T(8,128)(2,1)S(1)} %bitcast.75), kind=kOutput, calls=%fused_computation.15 | convolution fusion | flops 805306368 | bytes 4980736 | tf_op jit(solution)/shard_map/dot_general | solution.py:15
  75.7 0.1 copy-done.3
  75.9 1.9 %multiply_convert_fusion.3 = (bf16[256,768]{1,0:T(8,128)(2,1)S(1)}, f32[256,768]{1,0:T(8,128)}) fusion(f32[256,768]{1,0:T(8,128)S(1)} %fusion.14, bf16[1,768,2048]{2,1,0:T(8,128)(2,1)S(1)} %copy-done.3, bf16[256,4096]{1,0:T(8,128)(2,1)S(1)} %bitcast.76), kind=kOutput, calls=%fused_computation.42 | convolution fusion | flops 806486016 | bytes 6160384 | tf_op jit(solution)/shard_map/dot_general | solution.py:15
  77.8 0.0 copy-done.11
  77.8 0.9 copy.19
  78.7 0.0 copy-done
  78.7 2.0 %fusion.26 = bf16[256,2048]{1,0:T(8,128)(2,1)} fusion(bf16[256,768]{1,0:T(8,128)(2,1)S(1)} %get-tuple-element.28, bf16[1,768,2048]{2,1,0:T(8,128)(2,1)S(1)} %copy-done), kind=kOutput, calls=%fused_computation.24 | convolution fusion | flops 805830656 | bytes 4587520 | tf_op jit(solution)/shard_map/dot_general | solution.py:27
  80.7 4.3 %all-to-all-start.1 = ((bf16[8,32,2048]{2,1,0:T(8,128)(2,1)}), bf16[8,32,2048]{2,1,0:T(8,128)(2,1)}, u32[]{:S(2)}, u32[]{:S(2)}) async-start(bf16[8,32,2048]{2,1,0:T(8,128)(2,1)} %bitcast.84), calls=%async_computation.1 | async-start | bytes 2097152 | tf_op jit(solution)/shard_map/all_to_all | solution.py:79
  84.9 3.6 %multiply_convert_fusion.2 = (bf16[256,768]{1,0:T(8,128)(2,1)S(1)}, bf16[256,768]{1,0:T(8,128)(2,1)}) fusion(f32[256,768]{1,0:T(8,128)} %copy-done.11, f32[256,768]{1,0:T(8,128)} %get-tuple-element.29, bf16[256,2048]{1,0:T(8,128)(2,1)} %slice.43, bf16[1,768,2048]{2,1,0:T(8,128)(2,1)S(1)} %copy-done), kind=kOutput, calls=%fused_computation.41 | convolution fusion | flops 807862272 | bytes 6553600 | tf_op jit(solution)/shard_map/dot_general | solution.py:15
  88.6 0.9 copy.17
  89.5 1.9 %copy.18 = bf16[256,768]{0,1:T(8,128)(2,1)} copy(bf16[256,768]{1,0:T(8,128)(2,1)} %get-tuple-element.23) | data formatting | bytes 786432 | tf_op jit(solution)/shard_map/convert_element_type | solution.py:89
  91.4 1.5 pad_maximum_fusion.1
  92.9 0.1 constant_dynamic-slice_fusion
  93.0 0.1 collective-permute-start
  93.0 1.6 collective-permute-start.1
  94.7 0.3 collective-permute-start.2
  94.9 0.0 copy-done.4
  94.9 0.0 copy-done.5
  94.9 1.0 fusion.8
  95.9 0.7 copy-done.2
  96.6 2.1 %fusion.22 = bf16[256,2048]{1,0:T(8,128)(2,1)} fusion(f32[256,2048]{1,0:T(8,128)S(1)} %fusion.8, bf16[256,768]{1,0:T(8,128)(2,1)S(1)} %get-tuple-element.22, bf16[1,768,2048]{2,1,0:T(8,128)(2,1)S(1)} %copy-done.2), kind=kOutput, calls=%fused_computation.20 | convolution fusion | flops 806354944 | bytes 6684672 | tf_op jit(solution)/shard_map/dot_general | solution.py:27
  98.7 0.0 collective-permute-done
  98.7 10.6 %collective-permute-done.1 = bf16[256,576]{0,1:T(8,128)(2,1)S(1)} collective-permute-done((bf16[256,576]{0,1:T(8,128)(2,1)S(1)}, bf16[256,576]{0,1:T(8,128)(2,1)S(1)}, u32[]{:S(2)}, u32[]{:S(2)}) %collective-permute-start.1) | collective-permute-done | bytes 294944 | tf_op jit(solution)/shard_map/ppermute | solution.py:129
  109.3 12.0 %collective-permute-done.2 = bf16[256,576]{0,1:T(8,128)(2,1)S(1)} collective-permute-done((bf16[256,576]{0,1:T(8,128)(2,1)S(1)}, bf16[256,576]{0,1:T(8,128)(2,1)S(1)}, u32[]{:S(2)}, u32[]{:S(2)}) %collective-permute-start.2) | collective-permute-done | bytes 294944 | tf_op jit(solution)/shard_map/ppermute | solution.py:129
  121.2 1.2 pad_maximum_fusion.2
  122.4 2.9 %gather_fusion = bf16[4,256,576]{1,2,0:T(8,128)(2,1)} fusion(bf16[4,256,576]{1,2,0:T(8,128)(2,1)} %pad_maximum_fusion.2, s32[1024]{0:T(1024)S(1)} %pad_clamp_fusion), kind=kCustom, calls=%fused_computation | custom fusion | bytes 2359312 | tf_op jit(solution)/shard_map/jit(_take)/gather | solution.py:133
  125.3 1.4 copy.21
  126.8 1.1 broadcast_select_fusion
  127.9 0.0 all-to-all-done.1
  127.9 5.9 %all-to-all-start.2 = ((bf16[8,32,2048]{2,1,0:T(8,128)(2,1)}), bf16[8,32,2048]{2,1,0:T(8,128)(2,1)}, u32[]{:S(2)}, u32[]{:S(2)}) async-start(bf16[8,32,2048]{2,1,0:T(8,128)(2,1)} %bitcast.80), calls=%async_computation.2 | async-start | bytes 2097152 | tf_op jit(solution)/shard_map/all_to_all | solution.py:93
  133.9 0.0 copy-start.9
  133.9 0.0 copy-start.10
  133.9 3.2 %multiply_reduce_fusion = (f32[256]{0:T(256)S(1)}, bf16[256,2048]{1,0:T(8,128)(2,1)}) fusion(bf16[256,2048]{1,0:T(8,128)(2,1)} %param.13, f32[256]{0:T(256)S(1)} %bitcast.91, bf16[256,2048]{1,0:T(8,128)(2,1)} %bitcast.10, s32[256]{0:T(256)S(1)} %bitcast.88), kind=kOutput, calls=%fused_computation.28 | convolution fusion | flops 271122176 | bytes 3148800 | tf_op jit(solution)/shard_map/dot_general | solution.py:27
  137.0 0.0 copy-done.8
  137.0 0.0 copy-done.9
  137.0 0.0 copy-done.10
  137.0 0.7 maximum_maximum_fusion
  137.7 4.3 %fusion.32 = bf16[1,192,2048]{2,1,0:T(8,128)(2,1)} fusion(bf16[1024,4096]{1,0:T(8,128)(2,1)} %all-gather.2.cloned.1.call-done, bf16[1024,576]{0,1:T(8,128)(2,1)} %broadcast_select_fusion), kind=kOutput, calls=%fused_computation.26 | convolution fusion | flops 805699584 | bytes 5373952 | tf_op jit(solution)/shard_map/dot_general | solution.py:21
  142.0 0.0 copy-done.6
  142.0 4.0 %fusion.16 = bf16[384,2048]{1,0:T(8,128)(2,1)S(1)} fusion(bf16[1024,4096]{1,0:T(8,128)(2,1)} %all-gather.2.cloned.1.call-done, bf16[1024,576]{0,1:T(8,128)(2,1)S(1)} %copy-done.6), kind=kOutput, calls=%fused_computation.17 | convolution fusion | flops 1611399168 | bytes 6553600 | tf_op jit(solution)/shard_map/dot_general | solution.py:21
  146.0 1.3 slice_bitcast_fusion
  147.3 13.3 %all-to-all-done.2 = bf16[8,32,2048]{2,1,0:T(8,128)(2,1)} async-done(((bf16[8,32,2048]{2,1,0:T(8,128)(2,1)}), bf16[8,32,2048]{2,1,0:T(8,128)(2,1)}, u32[]{:S(2)}, u32[]{:S(2)}) %all-to-all-start.2) | async-done | bytes 1048608 | tf_op jit(solution)/shard_map/all_to_all | solution.py:93
  160.6 2.7 %convolution_convert_fusion = bf16[256,2048]{1,0:T(8,128)(2,1)} fusion(bf16[256,2048]{1,0:T(8,128)(2,1)} %bitcast.12, s32[256]{0:T(256)S(1)} %bitcast.89), kind=kOutput, calls=%fused_computation.22 | convolution fusion | flops 269025280 | bytes 2098176 | tf_op jit(solution)/shard_map/dot_general | solution.py:27
  (16 shorter events, 0.1 us)
Async XLA Ops:
  7.2 71.6 %copy-start = (bf16[1,768,2048]{2,1,0:T(8,128)(2,1)S(1)}, bf16[1,768,2048]{2,1,0:T(8,128)(2,1)}, u32[]{:S(2)}) copy-start(bf16[1,768,2048]{2,1,0:T(8,128)(2,1)} %param.12) | copy-start | bytes 9437188
  7.2 130.5 %all-gather.2.cloned.1.call-start = ((), (), s32[]{:S(2)}) async-start(), calls=%async_computation.3 | async-start | bytes 10485760 | tf_op jit(solution)/shard_map/all_gather | solution.py:66
  7.2 3.7 %copy-start.7 = (bf16[256,2048]{1,0:T(8,128)(2,1)S(1)}, bf16[256,2048]{1,0:T(8,128)(2,1)}, u32[]{:S(2)}) copy-start(bf16[256,2048]{1,0:T(8,128)(2,1)} %param.13) | copy-start | bytes 3145732
  69.0 3.2 %copy-start.1 = (bf16[8,32,4096]{2,1,0:T(8,128)(2,1)S(1)}, bf16[8,32,4096]{2,1,0:T(8,128)(2,1)}, u32[]{:S(2)}) copy-start(bf16[8,32,4096]{2,1,0:T(8,128)(2,1)} %all_to_all.15) | copy-start | bytes 6291460
  72.1 3.7 %copy-start.3 = (bf16[1,768,2048]{2,1,0:T(8,128)(2,1)S(1)}, bf16[1,768,2048]{2,1,0:T(8,128)(2,1)}, u32[]{:S(2)}) copy-start(bf16[1,768,2048]{2,1,0:T(8,128)(2,1)} %param.11) | copy-start | bytes 9437188
  75.9 1.9 %copy-start.11 = (f32[256,768]{1,0:T(8,128)}, f32[256,768]{1,0:T(8,128)S(1)}, u32[]{:S(2)}) copy-start(f32[256,768]{1,0:T(8,128)S(1)} %fusion.14) | copy-start | bytes 2359300
  80.7 47.2 %all-to-all-start.1 = ((bf16[8,32,2048]{2,1,0:T(8,128)(2,1)}), bf16[8,32,2048]{2,1,0:T(8,128)(2,1)}, u32[]{:S(2)}, u32[]{:S(2)}) async-start(bf16[8,32,2048]{2,1,0:T(8,128)(2,1)} %bitcast.84), calls=%async_computation.1 | async-start | bytes 2097152 | tf_op jit(solution)/shard_map/all_to_all | solution.py:79
  91.4 3.5 %copy-start.4 = (bf16[1,768,2048]{2,1,0:T(8,128)(2,1)S(1)}, bf16[1,768,2048]{2,1,0:T(8,128)(2,1)}, u32[]{:S(2)}) copy-start(bf16[1,768,2048]{2,1,0:T(8,128)(2,1)} %param.11) | copy-start | bytes 9437188
  91.4 3.5 %copy-start.5 = (bf16[256,768]{1,0:T(8,128)(2,1)S(1)}, bf16[256,768]{1,0:T(8,128)(2,1)}, u32[]{:S(2)}) copy-start(bf16[256,768]{1,0:T(8,128)(2,1)} %get-tuple-element.23) | copy-start | bytes 1179652
  93.0 5.7 %collective-permute-start = (bf16[256,576]{0,1:T(8,128)(2,1)S(1)}, bf16[256,576]{0,1:T(8,128)(2,1)S(1)}, u32[]{:S(2)}, u32[]{:S(2)}) collective-permute-start(bf16[256,576]{0,1:T(8,128)(2,1)S(1)} %get-tuple-element.27), channel_id=1, source_target_pairs={{0,8},{8,0},{16,24},{24,16},{1,9},{9,1},{17,25},{25,17},{2,10},{10... | collective-permute-start | bytes 884744 | tf_op jit(solution)/shard_map/ppermute | solution.py:129
  93.0 16.2 %collective-permute-start.1 = (bf16[256,576]{0,1:T(8,128)(2,1)S(1)}, bf16[256,576]{0,1:T(8,128)(2,1)S(1)}, u32[]{:S(2)}, u32[]{:S(2)}) collective-permute-start(bf16[256,576]{0,1:T(8,128)(2,1)S(1)} %get-tuple-element.26), channel_id=1, source_target_pairs={{0,16},{8,24},{16,0},{24,8},{1,17},{9,25},{17,1},{25,9},{2,18},{10... | collective-permute-start | bytes 884744 | tf_op jit(solution)/shard_map/ppermute | solution.py:129
  94.7 2.0 %copy-start.2 = (bf16[1,768,2048]{2,1,0:T(8,128)(2,1)S(1)}, bf16[1,768,2048]{2,1,0:T(8,128)(2,1)}, u32[]{:S(2)}) copy-start(bf16[1,768,2048]{2,1,0:T(8,128)(2,1)} %param.10) | copy-start | bytes 9437188
  94.7 26.6 %collective-permute-start.2 = (bf16[256,576]{0,1:T(8,128)(2,1)S(1)}, bf16[256,576]{0,1:T(8,128)(2,1)S(1)}, u32[]{:S(2)}, u32[]{:S(2)}) collective-permute-start(bf16[256,576]{0,1:T(8,128)(2,1)S(1)} %get-tuple-element.25), channel_id=1, source_target_pairs={{0,24},{8,16},{16,8},{24,0},{1,25},{9,17},{17,9},{25,1},{2,26},{10... | collective-permute-start | bytes 884744 | tf_op jit(solution)/shard_map/ppermute | solution.py:129
  127.9 32.7 %all-to-all-start.2 = ((bf16[8,32,2048]{2,1,0:T(8,128)(2,1)}), bf16[8,32,2048]{2,1,0:T(8,128)(2,1)}, u32[]{:S(2)}, u32[]{:S(2)}) async-start(bf16[8,32,2048]{2,1,0:T(8,128)(2,1)} %bitcast.80), calls=%async_computation.2 | async-start | bytes 2097152 | tf_op jit(solution)/shard_map/all_to_all | solution.py:93
  133.8 3.2 %copy-start.8 = (f32[8]{0:T(128)S(1)}, f32[8]{0:T(128)}, u32[]{:S(2)}) copy-start(f32[8]{0:T(128)} %pad.2.clone) | copy-start | bytes 100
  133.9 3.2 %copy-start.9 = (f32[8]{0:T(128)S(1)}, f32[8]{0:T(128)}, u32[]{:S(2)}) copy-start(f32[8]{0:T(128)} %pad.3.clone) | copy-start | bytes 100
  133.9 3.2 %copy-start.10 = (f32[8]{0:T(128)S(1)}, f32[8]{0:T(128)}, u32[]{:S(2)}) copy-start(f32[8]{0:T(128)} %pad.1.clone) | copy-start | bytes 100
  137.7 4.3 %copy-start.6 = (bf16[1024,576]{0,1:T(8,128)(2,1)S(1)}, bf16[1024,576]{0,1:T(8,128)(2,1)}, u32[]{:S(2)}) copy-start(bf16[1024,576]{0,1:T(8,128)(2,1)} %broadcast_select_fusion) | copy-start | bytes 3538948
Sparse Core Ops, SparseCore 0:
  67.2 70.0 all-gather.1

commit v8 on v5

--- a/solution.py
+++ b/solution.py
@@ -36,8 +36,16 @@
     live_cols = min(top_count, -(-experts // STRIPE))
     assigned = tok_count * live_cols
 
-    flat_ids = expert_ids[:, :live_cols].reshape(-1)
-    flat_gates = gate_weights[:, :live_cols].reshape(-1)
+    column_pick = (
+        jnp.arange(top_count, dtype=jnp.int32)[None, :, None]
+        == jnp.arange(live_cols, dtype=jnp.int32)[None, None, :]
+    )
+    flat_ids = jnp.sum(
+        jnp.where(column_pick, expert_ids[:, :, None], 0), axis=1
+    ).reshape(-1)
+    flat_gates = jnp.sum(
+        jnp.where(column_pick, gate_weights[:, :, None], 0.0), axis=1
+    ).reshape(-1)
     live_mask = flat_ids < experts
     onehot = flat_ids[:, None] == jnp.arange(experts, dtype=jnp.int32)[None, :]
     position = jnp.arange(assigned, dtype=jnp.int32)

time: 148 us -> 148 us (level)
    reduce_sum x0 -> x2, other arithmetic: none -> 1.71 us  [the longest x1 0.93 us: body(): jnp.sum(jnp.where(column_pick, expert_ids[:, :, None], 0), axis=1)]
    slice x2 -> x0, local copies, waits for them, and re-layouts: 1.6 us -> none  [the longest x1 0.85 us: body(): flat_gates = gate_weights[:, :live_cols].reshape(-1)]
where the time goes in v8:
time: 148 us; the launch traced here: 147 us
  blocking collectives  55.4 us (37%)
  matrix products  30 us (20%)
  waiting for transfers between devices  28.6 us (19%)
  between operations  14.2 us (10%)
  starting transfers between devices  8.71 us (6%)
  local copies, waits for them, and re-layouts  7.61 us (5%)
  other arithmetic  2.72 us (2%)
    all_to_all x1, blocking collectives, body(): lax.all_to_all(outgoing.reshape(experts, per_pair, 2 * feature_width), 'e...  55.4 us
    all_to_all x1, waiting for transfers between devices, body(): lax.all_to_all(expert_out.reshape(experts, per_pair, feature_width), 'ep'...  15.6 us
    dot_general x8, matrix products, matmul(): return jnp.dot(left, right, preferred_element_type=jnp.float32)  14.5 us
    all_gather x1, waiting for transfers between devices, body(): gathered = lax.all_gather(received, 'rep', axis=0, tiled=True)  13 us
    dot_general x5, matrix products, rows_times(): lax.dot_general(left, right, (((1,), (1,)), ((), ())), preferred_element_...  11.7 us
    all_to_all x1, starting transfers between devices, body(): lax.all_to_all(token_part.reshape(experts, per_pair, feature_width), 'ep'...  4.42 us
    all_to_all x1, starting transfers between devices, body(): lax.all_to_all(expert_out.reshape(experts, per_pair, feature_width), 'ep'...  4.25 us
    dot_general x2, matrix products, inner_rows(): lax.dot_general(left, right, (((0,), (0,)), ((), ())), preferred_element_...  3.76 us
  transfers between devices with their start and end apart: 3, of which 2 were waited for; matrix products, arithmetic and copies ran while one was open for 20% of the time, Pallas kernels for 0%

profile of v8, /device:TPU:0, one launch (start us, length us, event | category | flops | bytes accessed | tf_op | source)
XLA Modules:
  0.0 147.2 jit_solution(16481736086634309677)
XLA Ops:
  7.2 0.0 copy-start
  7.2 0.0 all-gather.2.cloned.1.call-start
  7.2 0.9 select_reduce_fusion.1
  8.2 0.8 select_reduce_fusion.2
  9.0 0.2 fusion.42
  9.2 0.1 select_reduce_fusion
  9.3 1.7 %convolution_convert_fusion.1 = bf16[256,2048]{1,0:T(8,128)(2,1)S(1)} fusion(bf16[256,2048]{1,0:T(8,128)(2,1)} %param.7, s32[256]{0:T(256)S(1)} %compare_select_fusion), kind=kOutput, calls=%fused_computation.26 | convolution fusion | flops 269025280 | bytes 2098176 | tf_op jit(solution)/shard_map/dot_general | solution.py:27
  11.0 1.7 %fusion.29 = bf16[256,2048]{1,0:T(8,128)(2,1)S(1)} fusion(bf16[256,2048]{1,0:T(8,128)(2,1)} %param.13, f32[256]{0:T(256)S(1)} %select_reduce_fusion, s32[256]{0:T(256)S(1)} %compare_select_fusion), kind=kOutput, calls=%fused_computation.24 | convolution fusion | flops 269549568 | bytes 2099200 | tf_op jit(solution)/shard_map/dot_general | solution.py:27
  12.6 0.2 pad_maximum_fusion
  12.9 55.4 %all_to_all.15 = bf16[8,32,4096]{2,1,0:T(8,128)(2,1)} all-to-all(bf16[8,32,4096]{2,1,0:T(8,128)(2,1)S(1)} %bitcast.52), channel_id=1, replica_groups=mesh['rep'=4,'ep'=8] {'ep'}, dimensions={0} | all-to-all | bytes 4194304 | tf_op jit(solution)/shard_map/all_to_all | solution.py:66
  68.2 0.0 all-gather.2.cloned.1.call-update
  68.3 0.0 copy-start.1
  68.3 0.0 copy-start.3
  68.3 3.4 %fusion.18 = f32[256,768]{1,0:T(8,128)S(1)} fusion(bf16[1,768,2048]{2,1,0:T(8,128)(2,1)} %param.10, bf16[256,4096]{1,0:T(8,128)(2,1)} %bitcast.49), kind=kOutput, calls=%fused_computation.18 | convolution fusion | flops 805306368 | bytes 4980736 | tf_op jit(solution)/shard_map/dot_general | solution.py:15
  71.7 0.0 copy-done.1
  71.7 0.4 copy-done.3
  72.1 0.0 copy-start.7
  72.1 1.0 fusion.14
  73.1 0.0 copy-done
  73.1 0.0 copy-start.9
  73.1 2.0 %fusion.30 = bf16[256,2048]{1,0:T(8,128)(2,1)} fusion(bf16[1,768,2048]{2,1,0:T(8,128)(2,1)S(1)} %copy-done, f32[256,768]{1,0:T(8,128)S(1)} %fusion.14, f32[256,768]{1,0:T(8,128)S(1)} %fusion.18), kind=kOutput, calls=%fused_computation.27 | convolution fusion | flops 807010304 | bytes 5767168 | tf_op jit(solution)/shard_map/dot_general | solution.py:27
  75.1 0.0 copy-done.7
  75.1 0.0 copy-done.9
  75.1 4.2 %all-to-all-start.1 = ((bf16[8,32,2048]{2,1,0:T(8,128)(2,1)}), bf16[8,32,2048]{2,1,0:T(8,128)(2,1)}, u32[]{:S(2)}, u32[]{:S(2)}) async-start(bf16[8,32,2048]{2,1,0:T(8,128)(2,1)} %bitcast.54), calls=%async_computation.1 | async-start | bytes 2097152 | tf_op jit(solution)/shard_map/all_to_all | solution.py:86
  79.4 0.1 pad.1.clone
  79.5 0.1 pad.3.clone
  79.6 0.1 pad.2.clone
  79.6 0.0 copy-start.2
  79.6 3.0 %dynamic-slice_bitcast_fusion = (bf16[192,2048]{1,0:T(8,128)(2,1)}, bf16[192,2048]{1,0:T(8,128)(2,1)}) fusion(bf16[1,768,2048]{2,1,0:T(8,128)(2,1)} %param.11, s32[]{:T(128)S(6)} %select_n.40, bf16[1,768,2048]{2,1,0:T(8,128)(2,1)} %param.10), kind=kLoop, calls=%fused_computation.52 | loop fusion | bytes 3145732 | tf_op jit(solution)/shard_map/dynamic_slice | solution.py:128
  82.6 0.0 copy-done.2
  82.6 0.0 copy-start.4
  82.6 0.0 copy-start.8
  82.6 1.0 fusion.8
  83.6 0.9 copy-done.4
  84.5 0.2 copy-done.8
  84.7 0.0 copy-start.5
  84.7 0.0 copy-start.10
  84.7 1.0 fusion.12
  85.7 0.9 copy-done.5
  86.7 0.2 copy-done.10
  86.9 2.1 %fusion.26 = bf16[256,2048]{1,0:T(8,128)(2,1)} fusion(f32[256,2048]{1,0:T(8,128)S(1)} %fusion.12, bf16[1,768,2048]{2,1,0:T(8,128)(2,1)S(1)} %copy-done.5, f32[256,768]{1,0:T(8,128)S(1)} %copy-done.8, f32[256,768]{1,0:T(8,128)S(1)} %fusion.8, f32[256,768]{1,0:T(8,128)S(1)} %copy-done.10), kind=kOutput, calls=%fused_computation.23 | convolution fusion | flops 808321024 | bytes 8650752 | tf_op jit(solution)/shard_map/dot_general | solution.py:27
  89.0 15.6 %all-to-all-done.1 = bf16[8,32,2048]{2,1,0:T(8,128)(2,1)} async-done(((bf16[8,32,2048]{2,1,0:T(8,128)(2,1)}), bf16[8,32,2048]{2,1,0:T(8,128)(2,1)}, u32[]{:S(2)}, u32[]{:S(2)}) %all-to-all-start.1) | async-done | bytes 1048608 | tf_op jit(solution)/shard_map/all_to_all | solution.py:86
  104.5 4.4 %all-to-all-start.2 = ((bf16[8,32,2048]{2,1,0:T(8,128)(2,1)}), bf16[8,32,2048]{2,1,0:T(8,128)(2,1)}, u32[]{:S(2)}, u32[]{:S(2)}) async-start(bf16[8,32,2048]{2,1,0:T(8,128)(2,1)} %bitcast.53), calls=%async_computation.2 | async-start | bytes 2097152 | tf_op jit(solution)/shard_map/all_to_all | solution.py:100
  109.0 3.2 %multiply_reduce_fusion = (f32[256]{0:T(256)S(1)}, bf16[256,2048]{1,0:T(8,128)(2,1)}) fusion(bf16[256,2048]{1,0:T(8,128)(2,1)} %param.13, f32[256]{0:T(256)S(1)} %select_reduce_fusion.2, bf16[256,2048]{1,0:T(8,128)(2,1)} %bitcast.6, s32[256]{0:T(256)S(1)} %compare_select_fusion), kind=kOutput, calls=%fused_computation.31 | convolution fusion | flops 271122176 | bytes 3148800 | tf_op jit(solution)/shard_map/dot_general | solution.py:27
  112.1 0.7 maximum_maximum_fusion
  112.8 13.0 %all-gather.2.cloned.1.call-done = bf16[1024,4096]{1,0:T(8,128)(2,1)} async-done(((bf16[256,4096]{1,0:T(8,128)(2,1)}), bf16[1024,4096]{1,0:T(8,128)(2,1)}) %all-gather.2.cloned.1.call-update) | async-done | bytes 8388624 | tf_op jit(solution)/shard_map/all_gather | solution.py:74
  125.8 0.0 copy-start.6
  125.8 4.6 %fusion.2 = f32[1024,384]{0,1:T(8,128)S(1)} fusion(bf16[1024,4096]{1,0:T(8,128)(2,1)} %all-gather.2.cloned.1.call-done, bf16[192,2048]{1,0:T(8,128)(2,1)} %get-tuple-element.20, bf16[192,2048]{1,0:T(8,128)(2,1)} %get-tuple-element.21), kind=kOutput, calls=%fused_computation.2 | convolution fusion | flops 1613758464 | bytes 7340032 | tf_op jit(solution)/shard_map/dot_general | solution.py:15
  130.4 0.5 copy-done.6
  130.9 1.7 %multiply_convert_fusion.3 = (bf16[1024,192]{0,1:T(8,128)(2,1)S(1)}, bf16[1024,192]{0,1:T(8,128)(2,1)S(1)}) fusion(f32[1024,384]{0,1:T(8,128)S(1)} %fusion.2, bf16[1,768,2048]{2,1,0:T(8,128)(2,1)S(1)} %copy-done, s32[]{:T(128)S(6)} %select_n.40, bf16[1024,4096]{1,0:T(8,128)(2,1)S(1)} %copy-done.6), kind=kOutput, calls=%fused_computation.49 | convolution fusion | flops 807862272 | bytes 7340036 | tf_op jit(solution)/shard_map/dot_general | solution.py:15
  132.6 1.8 %fusion.20 = bf16[384,2048]{1,0:T(8,128)(2,1)S(1)} fusion(bf16[1024,4096]{1,0:T(8,128)(2,1)S(1)} %copy-done.6, bf16[1024,192]{0,1:T(8,128)(2,1)S(1)} %get-tuple-element.15, bf16[1024,192]{0,1:T(8,128)(2,1)S(1)} %get-tuple-element.14), kind=kOutput, calls=%fused_computation.20 | convolution fusion | flops 1612972032 | bytes 6553600 | tf_op jit(solution)/shard_map/dot_general | solution.py:21
  134.4 1.9 %fusion.36 = bf16[1,192,2048]{2,1,0:T(8,128)(2,1)} fusion(bf16[1024,4096]{1,0:T(8,128)(2,1)S(1)} %copy-done.6, f32[1024,384]{0,1:T(8,128)S(1)} %fusion.2), kind=kOutput, calls=%fused_computation.29 | convolution fusion | flops 806879232 | bytes 6553600 | tf_op jit(solution)/shard_map/dot_general | solution.py:21
  136.4 1.3 slice_bitcast_fusion
  137.7 0.0 all-to-all-done.2
  137.7 2.7 %convolution_convert_fusion = bf16[256,2048]{1,0:T(8,128)(2,1)} fusion(bf16[256,2048]{1,0:T(8,128)(2,1)} %bitcast.8, s32[256]{0:T(256)S(1)} %compare_select_fusion), kind=kOutput, calls=%fused_computation.25 | convolution fusion | flops 269025280 | bytes 2098176 | tf_op jit(solution)/shard_map/dot_general | solution.py:27
  (4 shorter events, 0.0 us)
Async XLA Ops:
  7.2 65.9 %copy-start = (bf16[1,768,2048]{2,1,0:T(8,128)(2,1)S(1)}, bf16[1,768,2048]{2,1,0:T(8,128)(2,1)}, u32[]{:S(2)}) copy-start(bf16[1,768,2048]{2,1,0:T(8,128)(2,1)} %param.12) | copy-start | bytes 9437188
  7.2 118.6 %all-gather.2.cloned.1.call-start = ((), (), s32[]{:S(2)}) async-start(), calls=%async_computation.3 | async-start | bytes 10485760 | tf_op jit(solution)/shard_map/all_gather | solution.py:74
  68.3 3.4 %copy-start.1 = (bf16[8,32,4096]{2,1,0:T(8,128)(2,1)S(1)}, bf16[8,32,4096]{2,1,0:T(8,128)(2,1)}, u32[]{:S(2)}) copy-start(bf16[8,32,4096]{2,1,0:T(8,128)(2,1)} %all_to_all.15) | copy-start | bytes 6291460
  68.3 3.8 %copy-start.3 = (bf16[1,768,2048]{2,1,0:T(8,128)(2,1)S(1)}, bf16[1,768,2048]{2,1,0:T(8,128)(2,1)}, u32[]{:S(2)}) copy-start(bf16[1,768,2048]{2,1,0:T(8,128)(2,1)} %param.11) | copy-start | bytes 9437188
  72.1 3.1 %copy-start.7 = (f32[256,768]{1,0:T(8,128)}, f32[256,768]{1,0:T(8,128)S(1)}, u32[]{:S(2)}) copy-start(f32[256,768]{1,0:T(8,128)S(1)} %fusion.18) | copy-start | bytes 2359300
  73.1 2.0 %copy-start.9 = (f32[256,768]{1,0:T(8,128)}, f32[256,768]{1,0:T(8,128)S(1)}, u32[]{:S(2)}) copy-start(f32[256,768]{1,0:T(8,128)S(1)} %fusion.14) | copy-start | bytes 2359300
  75.1 29.4 %all-to-all-start.1 = ((bf16[8,32,2048]{2,1,0:T(8,128)(2,1)}), bf16[8,32,2048]{2,1,0:T(8,128)(2,1)}, u32[]{:S(2)}, u32[]{:S(2)}) async-start(bf16[8,32,2048]{2,1,0:T(8,128)(2,1)} %bitcast.54), calls=%async_computation.1 | async-start | bytes 2097152 | tf_op jit(solution)/shard_map/all_to_all | solution.py:86
  79.6 3.0 %copy-start.2 = (bf16[8,32,4096]{2,1,0:T(8,128)(2,1)S(1)}, bf16[8,32,4096]{2,1,0:T(8,128)(2,1)}, u32[]{:S(2)}) copy-start(bf16[8,32,4096]{2,1,0:T(8,128)(2,1)} %all_to_all.15) | copy-start | bytes 6291460
  82.6 1.9 %copy-start.4 = (bf16[1,768,2048]{2,1,0:T(8,128)(2,1)S(1)}, bf16[1,768,2048]{2,1,0:T(8,128)(2,1)}, u32[]{:S(2)}) copy-start(bf16[1,768,2048]{2,1,0:T(8,128)(2,1)} %param.11) | copy-start | bytes 9437188
  82.6 2.1 %copy-start.8 = (f32[256,768]{1,0:T(8,128)S(1)}, f32[256,768]{1,0:T(8,128)}, u32[]{:S(2)}) copy-start(f32[256,768]{1,0:T(8,128)} %copy-done.7) | copy-start | bytes 2359300
  84.7 2.0 %copy-start.5 = (bf16[1,768,2048]{2,1,0:T(8,128)(2,1)S(1)}, bf16[1,768,2048]{2,1,0:T(8,128)(2,1)}, u32[]{:S(2)}) copy-start(bf16[1,768,2048]{2,1,0:T(8,128)(2,1)} %param.10) | copy-start | bytes 9437188
  84.7 2.2 %copy-start.10 = (f32[256,768]{1,0:T(8,128)S(1)}, f32[256,768]{1,0:T(8,128)}, u32[]{:S(2)}) copy-start(f32[256,768]{1,0:T(8,128)} %copy-done.9) | copy-start | bytes 2359300
  104.5 33.2 %all-to-all-start.2 = ((bf16[8,32,2048]{2,1,0:T(8,128)(2,1)}), bf16[8,32,2048]{2,1,0:T(8,128)(2,1)}, u32[]{:S(2)}, u32[]{:S(2)}) async-start(bf16[8,32,2048]{2,1,0:T(8,128)(2,1)} %bitcast.53), calls=%async_computation.2 | async-start | bytes 2097152 | tf_op jit(solution)/shard_map/all_to_all | solution.py:100
  125.8 5.1 %copy-start.6 = (bf16[1024,4096]{1,0:T(8,128)(2,1)S(1)}, bf16[1024,4096]{1,0:T(8,128)(2,1)}, u32[]{:S(2)}) copy-start(bf16[1024,4096]{1,0:T(8,128)(2,1)} %all-gather.2.cloned.1.call-done) | copy-start | bytes 25165828
Sparse Core Ops, SparseCore 0:
  68.4 57.3 all-gather.1

commit v9 on v5

--- a/solution.py
+++ b/solution.py
@@ -63,7 +63,11 @@
         tiled=True,
     ).reshape(total_slots, 2 * feature_width)
 
-    gathered = lax.all_gather(received, "rep", axis=0, tiled=True)
+    copies = lax.axis_size("rep")
+    if copies == 4:
+        far = lax.ppermute(received, "rep", [(r, r ^ 2) for r in range(copies)])
+    else:
+        gathered = lax.all_gather(received, "rep", axis=0, tiled=True)
 
     rows_in = received[:, :feature_width]
     grad_in = received[:, feature_width:]
@@ -75,6 +79,7 @@
     activated = jax.nn.silu(pre_gate)
     hidden = (activated * pre_up).astype(jnp.bfloat16)
     expert_out = matmul(hidden, down_mat).astype(jnp.bfloat16)
+    expert_out, grad_in = lax.optimization_barrier((expert_out, grad_in))
     returned = lax.all_to_all(
         expert_out.reshape(experts, per_pair, feature_width),
         "ep",
@@ -97,6 +102,11 @@
         tiled=True,
     ).reshape(total_slots, feature_width)
 
+    if copies == 4:
+        returned, far = lax.optimization_barrier((returned, far))
+        pair = jnp.concatenate([received, far], axis=0)
+        near = lax.ppermute(pair, "rep", [(r, r ^ 1) for r in range(copies)])
+        gathered = jnp.concatenate([pair, near], axis=0)
     slot_grid = slot_index.reshape(tok_count, live_cols)
     gate_grid = flat_gates.reshape(tok_count, live_cols)
     layer_sum = jnp.zeros((tok_count, feature_width), jnp.float32)
@@ -114,7 +124,7 @@
     )
     gates_grad = jnp.stack(gate_cols, axis=1)
 
-    share = gate_mat.shape[0] // lax.axis_size("rep")
+    share = gate_mat.shape[0] // copies
     start = lax.axis_index("rep") * share
     gate_share = lax.dynamic_slice_in_dim(gate_mat, start, share, axis=0)
     up_share = lax.dynamic_slice_in_dim(up_mat, start, share, axis=0)

time: 148 us -> 156 us (1.054)
  blocking collectives: 55.4 us -> 84.2 us
  between operations: 14.2 us -> 0.88 us
  other arithmetic: 1.87 us -> 8.37 us
  matrix products: 30 us -> 24 us
  waiting for transfers between devices: 27.9 us -> 22.8 us
  starting transfers between devices: 8.71 us -> 5.94 us
    all_to_all x0 -> x1, blocking collectives: none -> 28.7 us  [body(): lax.all_to_all(expert_out.reshape(experts, per_pair, feature_width), 'ep'...]
    all_to_all x1 -> x0, waiting for transfers between devices: 14.9 us -> none  [body(): lax.all_to_all(expert_out.reshape(experts, per_pair, feature_width), 'ep'...]
    all_gather x1 -> x0, waiting for transfers between devices: 13 us -> none  [body(): gathered = lax.all_gather(received, 'rep', axis=0, tiled=True)]
    ppermute x0 -> x2, waiting for transfers between devices: none -> 12.9 us  [the longest x1 12.9 us: body(): far = lax.ppermute(received, 'rep', [(r, r ^ 2) for r in range(copies)])]
    all_to_all x1, waiting for transfers between devices: 0.01 us -> 9.92 us  [body(): lax.all_to_all(token_part.reshape(experts, per_pair, feature_width), 'ep'...]
    concatenate x0 -> x2, other arithmetic: none -> 6.57 us  [the longest x1 3.93 us: body(): gathered = jnp.concatenate([pair, near], axis=0)]
    dot_general x5, matrix products: 11.7 us -> 6.62 us  [rows_times(): lax.dot_general(left, right, (((1,), (1,)), ((), ())), preferred_element_...]
    all_to_all x1 -> x0, starting transfers between devices: 4.26 us -> none  [body(): lax.all_to_all(expert_out.reshape(experts, per_pair, feature_width), 'ep'...]
  transfers between devices with their start and end apart: 3 -> 3, of which waited for: 2 -> 2; matrix products, arithmetic and copies ran while one was open for 20% -> 18% of each run, Pallas kernels for 0% -> 0%
where the time goes in v9:
time: 156 us
  blocking collectives  84.2 us (54%)
  matrix products  24 us (15%)
  waiting for transfers between devices  22.8 us (15%)
  local copies, waits for them, and re-layouts  9.26 us (6%)
  other arithmetic  8.37 us (5%)
  starting transfers between devices  5.94 us (4%)
    all_to_all x1, blocking collectives, body(): lax.all_to_all(outgoing.reshape(experts, per_pair, 2 * feature_width), 'e...  55.6 us
    all_to_all x1, blocking collectives, body(): lax.all_to_all(expert_out.reshape(experts, per_pair, feature_width), 'ep'...  28.7 us
    dot_general x8, matrix products, matmul(): return jnp.dot(left, right, preferred_element_type=jnp.float32)  13.7 us
    ppermute x1, waiting for transfers between devices, body(): far = lax.ppermute(received, 'rep', [(r, r ^ 2) for r in range(copies)])  12.9 us
    all_to_all x1, waiting for transfers between devices, body(): lax.all_to_all(token_part.reshape(experts, per_pair, feature_width), 'ep'...  9.92 us
    dot_general x5, matrix products, rows_times(): lax.dot_general(left, right, (((1,), (1,)), ((), ())), preferred_element_...  6.62 us
    all_to_all x1, starting transfers between devices, body(): lax.all_to_all(token_part.reshape(experts, per_pair, feature_width), 'ep'...  4.43 us
    concatenate x1, other arithmetic, body(): gathered = jnp.concatenate([pair, near], axis=0)  3.93 us
  transfers between devices with their start and end apart: 3, of which 2 were waited for; matrix products, arithmetic and copies ran while one was open for 18% of the time, Pallas kernels for 0%

profile of v9, /device:TPU:0, one launch (start us, length us, event | category | flops | bytes accessed | tf_op | source)
XLA Modules:
  0.0 155.5 jit_solution(3347026174392227483)
XLA Ops:
  0.6 0.0 copy-start
  0.6 0.8 slice.30
  1.5 0.8 slice.31
  2.3 0.2 fusion.42
  2.5 0.1 select_reduce_fusion
  2.6 1.7 %convolution_convert_fusion.1 = bf16[256,2048]{1,0:T(8,128)(2,1)S(1)} fusion(bf16[256,2048]{1,0:T(8,128)(2,1)} %param.7, s32[256]{0:T(256)S(1)} %compare_select_fusion.1), kind=kOutput, calls=%fused_computation.28 | convolution fusion | flops 269025280 | bytes 2098176 | tf_op jit(solution)/shard_map/dot_general | solution.py:27
  4.3 1.7 %fusion.29 = bf16[256,2048]{1,0:T(8,128)(2,1)S(1)} fusion(bf16[256,2048]{1,0:T(8,128)(2,1)} %param.13, f32[256]{0:T(256)S(1)} %select_reduce_fusion, s32[256]{0:T(256)S(1)} %compare_select_fusion.1), kind=kOutput, calls=%fused_computation.26 | convolution fusion | flops 269549568 | bytes 2099200 | tf_op jit(solution)/shard_map/dot_general | solution.py:27
  6.0 0.2 pad_maximum_fusion.2
  6.2 0.0 copy-start.7
  6.2 55.6 %all_to_all.15 = bf16[8,32,4096]{2,1,0:T(8,128)(2,1)S(1)} all-to-all(bf16[8,32,4096]{2,1,0:T(8,128)(2,1)S(1)} %bitcast.59), channel_id=1, replica_groups=mesh['rep'=4,'ep'=8] {'ep'}, dimensions={0} | all-to-all | bytes 4194304 | tf_op jit(solution)/shard_map/all_to_all | solution.py:58
  61.8 1.2 slice.41
  63.0 0.0 copy-start.9
  63.0 1.5 collective-permute-start
  64.5 0.0 copy-done.7
  64.5 1.0 fusion.14
  65.5 0.0 copy-done.9
  65.5 0.0 copy-start.11
  65.5 1.0 fusion.18
  66.6 0.0 copy-done
  66.6 0.0 copy-start.13
  66.6 1.0 fusion.30
  67.7 0.0 copy-done.11
  67.7 0.0 copy-done.13
  67.7 28.7 %all_to_all.16 = bf16[8,32,2048]{2,1,0:T(8,128)(2,1)} all-to-all(bf16[8,32,2048]{2,1,0:T(8,128)(2,1)S(1)} %bitcast.62), channel_id=1, replica_groups=mesh['rep'=4,'ep'=8] {'ep'}, dimensions={0} | all-to-all | bytes 2097152 | tf_op jit(solution)/shard_map/all_to_all | solution.py:83
  96.3 12.9 %collective-permute-done = bf16[256,4096]{1,0:T(8,128)(2,1)S(1)} collective-permute-done((bf16[256,4096]{1,0:T(8,128)(2,1)S(1)}, bf16[256,4096]{1,0:T(8,128)(2,1)S(1)}, u32[]{:S(2)}, u32[]{:S(2)}) %collective-permute-start) | collective-permute-done | bytes 2097184 | tf_op jit(solution)/shard_map/ppermute | solution.py:68
  109.2 0.0 copy-start.3
  109.2 0.0 copy-done.1
  109.2 2.6 %pad_maximum_fusion.1 = bf16[512,4096]{1,0:T(8,128)(2,1)} fusion(bf16[256,4096]{1,0:T(8,128)(2,1)S(1)} %collective-permute-done, bf16[256,4096]{1,0:T(8,128)(2,1)S(1)} %bitcast.57), kind=kLoop, calls=%fused_computation.1 | loop fusion | flops 8388608 | bytes 8388608 | tf_op jit(solution)/shard_map/concatenate | solution.py:107
  111.9 0.0 copy-done.3
  111.9 0.0 collective-permute-start.1
  111.9 0.1 pad.3.clone
  112.0 0.1 pad.2.clone
  112.1 0.1 pad.1.clone
  112.1 0.0 copy-start.4
  112.1 0.8 compare_select_fusion
  112.9 2.7 %dynamic-slice_bitcast_fusion = (bf16[192,2048]{1,0:T(8,128)(2,1)}, bf16[192,2048]{1,0:T(8,128)(2,1)}) fusion(bf16[1,768,2048]{2,1,0:T(8,128)(2,1)} %param.11, s32[]{:T(128)S(6)} %select_n.28, bf16[1,768,2048]{2,1,0:T(8,128)(2,1)} %param.10), kind=kLoop, calls=%fused_computation.53 | loop fusion | bytes 3145732 | tf_op jit(solution)/shard_map/dynamic_slice | solution.py:130
  115.6 0.0 copy-done.4
  115.6 0.0 copy-start.8
  115.6 0.0 copy-start.14
  115.6 1.0 fusion.8
  116.7 0.9 copy-done.8
  117.5 0.2 copy-done.14
  117.7 0.0 copy-start.10
  117.7 0.0 copy-start.12
  117.7 1.0 fusion.12
  118.8 0.9 copy-done.10
  119.6 0.2 copy-done.12
  119.8 2.1 %fusion.26 = bf16[256,2048]{1,0:T(8,128)(2,1)} fusion(f32[256,2048]{1,0:T(8,128)S(1)} %fusion.12, bf16[1,768,2048]{2,1,0:T(8,128)(2,1)S(1)} %copy-done.10, f32[256,768]{1,0:T(8,128)S(1)} %copy-done.14, f32[256,768]{1,0:T(8,128)S(1)} %fusion.8, f32[256,768]{1,0:T(8,128)S(1)} %copy-done.12), kind=kOutput, calls=%fused_computation.25 | convolution fusion | flops 808321024 | bytes 8650752 | tf_op jit(solution)/shard_map/dot_general | solution.py:27
  121.9 4.4 %all-to-all-start.2 = ((bf16[8,32,2048]{2,1,0:T(8,128)(2,1)}), bf16[8,32,2048]{2,1,0:T(8,128)(2,1)}, u32[]{:S(2)}, u32[]{:S(2)}) async-start(bf16[8,32,2048]{2,1,0:T(8,128)(2,1)} %bitcast.61), calls=%async_computation.2 | async-start | bytes 2097152 | tf_op jit(solution)/shard_map/all_to_all | solution.py:97
  126.3 0.0 copy-start.2
  126.3 3.3 %multiply_reduce_fusion = (f32[256]{0:T(256)S(1)}, bf16[256,2048]{1,0:T(8,128)(2,1)}) fusion(bf16[256,2048]{1,0:T(8,128)(2,1)} %param.13, f32[256]{0:T(256)S(1)} %bitcast.66, bf16[256,2048]{1,0:T(8,128)(2,1)} %bitcast.60, s32[256]{0:T(256)S(1)} %bitcast.63), kind=kOutput, calls=%fused_computation.33 | convolution fusion | flops 271122176 | bytes 3148800 | tf_op jit(solution)/shard_map/dot_general | solution.py:27
  129.6 0.7 maximum_maximum_fusion
  130.3 0.0 collective-permute-done.1
  130.3 0.0 copy-done.2
  130.3 3.9 %pad_maximum_fusion = bf16[1024,4096]{1,0:T(8,128)(2,1)S(1)} fusion(bf16[512,4096]{1,0:T(8,128)(2,1)} %collective-permute-done.1, bf16[256,4096]{1,0:T(8,128)(2,1)} %copy-done.3, bf16[256,4096]{1,0:T(8,128)(2,1)S(1)} %bitcast.58), kind=kLoop, calls=%fused_computation | loop fusion | flops 25165824 | bytes 16777216 | tf_op jit(solution)/shard_map/concatenate | solution.py:109
  134.3 0.0 copy-done.5
  134.3 0.0 copy-done.6
  134.3 1.8 %fusion.2 = f32[1024,384]{0,1:T(8,128)S(1)} fusion(bf16[1024,4096]{1,0:T(8,128)(2,1)S(1)} %pad_maximum_fusion, bf16[192,2048]{1,0:T(8,128)(2,1)S(1)} %copy-done.5, bf16[192,2048]{1,0:T(8,128)(2,1)S(1)} %copy-done.6), kind=kOutput, calls=%fused_computation.4 | convolution fusion | flops 1613758464 | bytes 7340032 | tf_op jit(solution)/shard_map/dot_general | solution.py:15
  136.1 1.7 %multiply_convert_fusion.3 = (bf16[1024,192]{0,1:T(8,128)(2,1)S(1)}, bf16[1024,192]{0,1:T(8,128)(2,1)S(1)}) fusion(f32[1024,384]{0,1:T(8,128)S(1)} %fusion.2, bf16[1,768,2048]{2,1,0:T(8,128)(2,1)S(1)} %copy-done, s32[]{:T(128)S(6)} %select_n.28, bf16[1024,4096]{1,0:T(8,128)(2,1)S(1)} %pad_maximum_fusion), kind=kOutput, calls=%fused_computation.50 | convolution fusion | flops 807862272 | bytes 7340036 | tf_op jit(solution)/shard_map/dot_general | solution.py:15
  137.8 1.8 %fusion.20 = bf16[384,2048]{1,0:T(8,128)(2,1)S(1)} fusion(bf16[1024,4096]{1,0:T(8,128)(2,1)S(1)} %pad_maximum_fusion, bf16[1024,192]{0,1:T(8,128)(2,1)S(1)} %get-tuple-element.23, bf16[1024,192]{0,1:T(8,128)(2,1)S(1)} %get-tuple-element.22), kind=kOutput, calls=%fused_computation.22 | convolution fusion | flops 1612972032 | bytes 6553600 | tf_op jit(solution)/shard_map/dot_general | solution.py:21
  139.7 1.9 %fusion.36 = bf16[1,192,2048]{2,1,0:T(8,128)(2,1)} fusion(bf16[1024,4096]{1,0:T(8,128)(2,1)S(1)} %pad_maximum_fusion, f32[1024,384]{0,1:T(8,128)S(1)} %fusion.2), kind=kOutput, calls=%fused_computation.31 | convolution fusion | flops 806879232 | bytes 6553600 | tf_op jit(solution)/shard_map/dot_general | solution.py:21
  141.6 1.3 slice_bitcast_fusion
  142.9 9.9 %all-to-all-done.2 = bf16[8,32,2048]{2,1,0:T(8,128)(2,1)} async-done(((bf16[8,32,2048]{2,1,0:T(8,128)(2,1)}), bf16[8,32,2048]{2,1,0:T(8,128)(2,1)}, u32[]{:S(2)}, u32[]{:S(2)}) %all-to-all-start.2) | async-done | bytes 1048608 | tf_op jit(solution)/shard_map/all_to_all | solution.py:97
  152.8 2.7 %convolution_convert_fusion = bf16[256,2048]{1,0:T(8,128)(2,1)} fusion(bf16[256,2048]{1,0:T(8,128)(2,1)} %bitcast.12, s32[256]{0:T(256)S(1)} %bitcast.64), kind=kOutput, calls=%fused_computation.27 | convolution fusion | flops 269025280 | bytes 2098176 | tf_op jit(solution)/shard_map/dot_general | solution.py:27
  (7 shorter events, 0.0 us)
Async XLA Ops:
  0.6 66.0 %copy-start = (bf16[1,768,2048]{2,1,0:T(8,128)(2,1)S(1)}, bf16[1,768,2048]{2,1,0:T(8,128)(2,1)}, u32[]{:S(2)}) copy-start(bf16[1,768,2048]{2,1,0:T(8,128)(2,1)} %param.12) | copy-start | bytes 9437188
  6.2 58.3 %copy-start.7 = (bf16[1,768,2048]{2,1,0:T(8,128)(2,1)S(1)}, bf16[1,768,2048]{2,1,0:T(8,128)(2,1)}, u32[]{:S(2)}) copy-start(bf16[1,768,2048]{2,1,0:T(8,128)(2,1)} %param.11) | copy-start | bytes 9437188
  61.8 47.4 %copy-start.1 = (bf16[8,32,4096]{2,1,0:T(8,128)(2,1)}, bf16[8,32,4096]{2,1,0:T(8,128)(2,1)S(1)}, u32[]{:S(2)}) copy-start(bf16[8,32,4096]{2,1,0:T(8,128)(2,1)S(1)} %all_to_all.15) | copy-start | bytes 6291460
  63.0 2.5 %copy-start.9 = (bf16[1,768,2048]{2,1,0:T(8,128)(2,1)S(1)}, bf16[1,768,2048]{2,1,0:T(8,128)(2,1)}, u32[]{:S(2)}) copy-start(bf16[1,768,2048]{2,1,0:T(8,128)(2,1)} %param.10) | copy-start | bytes 9437188
  63.0 46.2 %collective-permute-start = (bf16[256,4096]{1,0:T(8,128)(2,1)S(1)}, bf16[256,4096]{1,0:T(8,128)(2,1)S(1)}, u32[]{:S(2)}, u32[]{:S(2)}) collective-permute-start(bf16[256,4096]{1,0:T(8,128)(2,1)S(1)} %bitcast.54), channel_id=1, source_target_pairs={{0,16},{8,24},{16,0},{24,8},{1,17},{9,25},{17,1},{25,9},{2,18},{10... | collective-permute-start | bytes 6291464 | tf_op jit(solution)/shard_map/ppermute | solution.py:68
  65.5 2.1 %copy-start.11 = (f32[256,768]{1,0:T(8,128)}, f32[256,768]{1,0:T(8,128)S(1)}, u32[]{:S(2)}) copy-start(f32[256,768]{1,0:T(8,128)S(1)} %fusion.14) | copy-start | bytes 2359300
  66.6 1.1 copy-start.13
  109.2 2.7 %copy-start.3 = (bf16[256,4096]{1,0:T(8,128)(2,1)}, bf16[256,4096]{1,0:T(8,128)(2,1)S(1)}, u32[]{:S(2)}) copy-start(bf16[256,4096]{1,0:T(8,128)(2,1)S(1)} %collective-permute-done) | copy-start | bytes 6291460
  111.9 18.4 %collective-permute-start.1 = (bf16[512,4096]{1,0:T(8,128)(2,1)}, bf16[512,4096]{1,0:T(8,128)(2,1)}, u32[]{:S(2)}, u32[]{:S(2)}) collective-permute-start(bf16[512,4096]{1,0:T(8,128)(2,1)} %pad_maximum_fusion.1), channel_id=1, source_target_pairs={{0,8},{8,0},{16,24},{24,16},{1,9},{9,1},{17,25},{25,17},{2,10},{10... | collective-permute-start | bytes 12582920 | tf_op jit(solution)/shard_map/ppermute | solution.py:108
  112.1 3.5 %copy-start.4 = (bf16[256,2048]{1,0:T(8,128)(2,1)S(1)}, bf16[256,2048]{1,0:T(8,128)(2,1)}, u32[]{:S(2)}) copy-start(bf16[256,2048]{1,0:T(8,128)(2,1)} %slice.41) | copy-start | bytes 3145732
  115.6 1.9 %copy-start.8 = (bf16[1,768,2048]{2,1,0:T(8,128)(2,1)S(1)}, bf16[1,768,2048]{2,1,0:T(8,128)(2,1)}, u32[]{:S(2)}) copy-start(bf16[1,768,2048]{2,1,0:T(8,128)(2,1)} %param.11) | copy-start | bytes 9437188
  115.6 2.1 %copy-start.14 = (f32[256,768]{1,0:T(8,128)S(1)}, f32[256,768]{1,0:T(8,128)}, u32[]{:S(2)}) copy-start(f32[256,768]{1,0:T(8,128)} %copy-done.13) | copy-start | bytes 2359300
  117.7 1.9 %copy-start.10 = (bf16[1,768,2048]{2,1,0:T(8,128)(2,1)S(1)}, bf16[1,768,2048]{2,1,0:T(8,128)(2,1)}, u32[]{:S(2)}) copy-start(bf16[1,768,2048]{2,1,0:T(8,128)(2,1)} %param.10) | copy-start | bytes 9437188
  117.7 2.1 %copy-start.12 = (f32[256,768]{1,0:T(8,128)S(1)}, f32[256,768]{1,0:T(8,128)}, u32[]{:S(2)}) copy-start(f32[256,768]{1,0:T(8,128)} %copy-done.11) | copy-start | bytes 2359300
  121.9 31.0 %all-to-all-start.2 = ((bf16[8,32,2048]{2,1,0:T(8,128)(2,1)}), bf16[8,32,2048]{2,1,0:T(8,128)(2,1)}, u32[]{:S(2)}, u32[]{:S(2)}) async-start(bf16[8,32,2048]{2,1,0:T(8,128)(2,1)} %bitcast.61), calls=%async_computation.2 | async-start | bytes 2097152 | tf_op jit(solution)/shard_map/all_to_all | solution.py:97
  126.3 4.0 %copy-start.2 = (bf16[8,32,4096]{2,1,0:T(8,128)(2,1)S(1)}, bf16[8,32,4096]{2,1,0:T(8,128)(2,1)}, u32[]{:S(2)}) copy-start(bf16[8,32,4096]{2,1,0:T(8,128)(2,1)} %copy-done.1) | copy-start | bytes 6291460
  130.3 3.9 %copy-start.5 = (bf16[192,2048]{1,0:T(8,128)(2,1)S(1)}, bf16[192,2048]{1,0:T(8,128)(2,1)}, u32[]{:S(2)}) copy-start(bf16[192,2048]{1,0:T(8,128)(2,1)} %get-tuple-element.28) | copy-start | bytes 2359300
  130.3 4.0 %copy-start.6 = (bf16[192,2048]{1,0:T(8,128)(2,1)S(1)}, bf16[192,2048]{1,0:T(8,128)(2,1)}, u32[]{:S(2)}) copy-start(bf16[192,2048]{1,0:T(8,128)(2,1)} %get-tuple-element.29) | copy-start | bytes 2359300

commit v10 on v4

--- a/solution.py
+++ b/solution.py
@@ -63,7 +63,13 @@
         tiled=True,
     ).reshape(total_slots, 2 * feature_width)
 
-    gathered = lax.all_gather(received, "rep", axis=0, tiled=True)
+    copies = lax.axis_size("rep")
+    by_pieces = copies == 4
+    if by_pieces:
+        near = lax.ppermute(received, "rep", [(r, r ^ 1) for r in range(copies)])
+        far = lax.ppermute(received, "rep", [(r, r ^ 2) for r in range(copies)])
+    else:
+        gathered = lax.all_gather(received, "rep", axis=0, tiled=True)
 
     rows_in = received[:, :feature_width]
     grad_in = received[:, feature_width:]
@@ -97,6 +103,8 @@
         tiled=True,
     ).reshape(total_slots, feature_width)
 
+    if by_pieces:
+        returned, near = lax.optimization_barrier((returned, near))
     slot_grid = slot_index.reshape(tok_count, live_cols)
     gate_grid = flat_gates.reshape(tok_count, live_cols)
     layer_sum = jnp.zeros((tok_count, feature_width), jnp.float32)
@@ -108,29 +116,44 @@
         out_rows = matmul(col_pick, returned)
         layer_sum = layer_sum + gate_grid[:, col : col + 1] * out_rows
         gate_cols.append(jnp.sum(out_grad.astype(jnp.float32) * out_rows, axis=1))
+    if by_pieces:
+        layer_sum, far = lax.optimization_barrier((layer_sum, far))
+        near_far = lax.ppermute(far, "rep", [(r, r ^ 1) for r in range(copies)])
+        pieces = [received, near, far, near_far]
+    else:
+        pieces = [gathered]
     layer_out = layer_sum.astype(jnp.bfloat16)
     gate_cols.extend(
         [jnp.zeros((tok_count,), jnp.float32)] * (top_count - live_cols)
     )
     gates_grad = jnp.stack(gate_cols, axis=1)
 
-    share = gate_mat.shape[0] // lax.axis_size("rep")
+    share = gate_mat.shape[0] // copies
     start = lax.axis_index("rep") * share
     gate_share = lax.dynamic_slice_in_dim(gate_mat, start, share, axis=0)
     up_share = lax.dynamic_slice_in_dim(up_mat, start, share, axis=0)
     down_share = lax.dynamic_slice_in_dim(down_mat, start, share, axis=0)
-    rows_all = gathered[:, :feature_width]
-    grad_all = gathered[:, feature_width:]
-    pre_gate_s = rows_times(rows_all, gate_share)
-    pre_up_s = rows_times(rows_all, up_share)
-    activated_s = jax.nn.silu(pre_gate_s)
-    hidden_s = (activated_s * pre_up_s).astype(jnp.bfloat16)
-    hidden_grad_s = rows_times(grad_all, down_share)
-    gate_pre_grad_s = (hidden_grad_s * pre_up_s * silu_grad(pre_gate_s)).astype(jnp.bfloat16)
-    up_pre_grad_s = (hidden_grad_s * activated_s).astype(jnp.bfloat16)
-    gate_w_grad = inner_rows(gate_pre_grad_s, rows_all).astype(jnp.bfloat16)[None]
-    up_w_grad = inner_rows(up_pre_grad_s, rows_all).astype(jnp.bfloat16)[None]
-    down_w_grad = inner_rows(hidden_s, grad_all).astype(jnp.bfloat16)[None]
+    both_sum = None
+    down_sum = None
+    stacked_share = jnp.concatenate([gate_share, up_share], axis=0)
+    for piece in pieces:
+        rows_p = piece[:, :feature_width]
+        grad_p = piece[:, feature_width:]
+        pre_both = rows_times(rows_p, stacked_share)
+        pre_gate_s = pre_both[:, :share]
+        pre_up_s = pre_both[:, share:]
+        activated_s = jax.nn.silu(pre_gate_s)
+        hidden_s = (activated_s * pre_up_s).astype(jnp.bfloat16)
+        hidden_grad_s = rows_times(grad_p, down_share)
+        gate_pre_grad_s = (hidden_grad_s * pre_up_s * silu_grad(pre_gate_s)).astype(jnp.bfloat16)
+        up_pre_grad_s = (hidden_grad_s * activated_s).astype(jnp.bfloat16)
+        both_p = inner_rows(jnp.concatenate([gate_pre_grad_s, up_pre_grad_s], axis=1), rows_p)
+        down_p = inner_rows(hidden_s, grad_p)
+        both_sum = both_p if both_sum is None else both_sum + both_p
+        down_sum = down_p if down_sum is None else down_sum + down_p
+    gate_w_grad = both_sum[:share].astype(jnp.bfloat16)[None]
+    up_w_grad = both_sum[share:].astype(jnp.bfloat16)[None]
+    down_w_grad = down_sum.astype(jnp.bfloat16)[None]
     part_back, gate_w_grad, up_w_grad, down_w_grad = lax.optimization_barrier(
         (part_back, gate_w_grad, up_w_grad, down_w_grad)
     )

time: 152 us -> 136 us (0.89)
  blocking collectives: 55.4 us -> 0 us
  waiting for transfers between devices: 29 us -> 55.7 us
  between operations: 14.2 us -> 0.92 us
  matrix products: 37.6 us -> 49.2 us
  starting transfers between devices: 8.78 us -> 17.5 us
  local copies, waits for them, and re-layouts: 4.2 us -> 8.64 us
    all_to_all x1 -> x0, blocking collectives: 55.4 us -> none  [body(): lax.all_to_all(outgoing.reshape(experts, per_pair, 2 * feature_width), 'e...]
    all_to_all x0 -> x1, waiting for transfers between devices: none -> 44.7 us  [body(): lax.all_to_all(outgoing.reshape(experts, per_pair, 2 * feature_width), 'e...]
    all_gather x1 -> x0, waiting for transfers between devices: 12.2 us -> none  [body(): gathered = lax.all_gather(received, 'rep', axis=0, tiled=True)]
    dot_general x3 -> x8, matrix products: 5.87 us -> 15.2 us  [inner_rows(): lax.dot_general(left, right, (((0,), (0,)), ((), ())), preferred_element_...]
    all_to_all x0 -> x1, starting transfers between devices: none -> 7.26 us  [body(): lax.all_to_all(outgoing.reshape(experts, per_pair, 2 * feature_width), 'e...]
    all_to_all x1, waiting for transfers between devices: 16.7 us -> 9.7 us  [body(): lax.all_to_all(expert_out.reshape(experts, per_pair, feature_width), 'ep'...]
    dot_general x6 -> x11, matrix products: 17.1 us -> 21 us  [rows_times(): lax.dot_general(left, right, (((1,), (1,)), ((), ())), preferred_element_...]
    dynamic_slice x0 -> x1, local copies, waits for them, and re-layouts: none -> 2.71 us  [body(): up_share = lax.dynamic_slice_in_dim(up_mat, start, share, axis=0)]
  transfers between devices with their start and end apart: 3 -> 6, of which waited for: 2 -> 4; matrix products, arithmetic and copies ran while one was open for 22% -> 33% of each run, Pallas kernels for 0% -> 0%
where the time goes in v10:
time: 136 us; the launch traced here: 135 us
  waiting for transfers between devices  55.7 us (41%)
  matrix products  49.2 us (36%)
  starting transfers between devices  17.5 us (13%)
  local copies, waits for them, and re-layouts  8.64 us (6%)
  other arithmetic  3.34 us (2%)
    all_to_all x1, waiting for transfers between devices, body(): lax.all_to_all(outgoing.reshape(experts, per_pair, 2 * feature_width), 'e...  44.7 us
    dot_general x11, matrix products, rows_times(): lax.dot_general(left, right, (((1,), (1,)), ((), ())), preferred_element_...  21 us
    dot_general x8, matrix products, inner_rows(): lax.dot_general(left, right, (((0,), (0,)), ((), ())), preferred_element_...  15.2 us
    dot_general x8, matrix products, matmul(): return jnp.dot(left, right, preferred_element_type=jnp.float32)  13 us
    all_to_all x1, waiting for transfers between devices, body(): lax.all_to_all(expert_out.reshape(experts, per_pair, feature_width), 'ep'...  9.7 us
    all_to_all x1, starting transfers between devices, body(): lax.all_to_all(outgoing.reshape(experts, per_pair, 2 * feature_width), 'e...  7.26 us
    all_to_all x1, starting transfers between devices, body(): lax.all_to_all(token_part.reshape(experts, per_pair, feature_width), 'ep'...  4.42 us
    all_to_all x1, starting transfers between devices, body(): lax.all_to_all(expert_out.reshape(experts, per_pair, feature_width), 'ep'...  4.24 us
  transfers between devices with their start and end apart: 6, of which 4 were waited for; matrix products, arithmetic and copies ran while one was open for 33% of the time, Pallas kernels for 0%

profile of v10, /device:TPU:0, one launch (start us, length us, event | category | flops | bytes accessed | tf_op | source)
XLA Modules:
  0.0 135.3 jit_solution(4738631010706776916)
XLA Ops:
  0.6 0.0 copy-start
  0.6 0.0 copy-start.3
  0.7 0.9 slice.64
  1.5 0.8 slice.65
  2.3 0.2 fusion.24
  2.5 0.1 select_reduce_fusion
  2.6 1.7 %convolution_convert_fusion.1 = bf16[256,2048]{1,0:T(8,128)(2,1)S(1)} fusion(bf16[256,2048]{1,0:T(8,128)(2,1)} %param.7, s32[256]{0:T(256)S(1)} %compare_select_fusion.1), kind=kOutput, calls=%fused_computation.21 | convolution fusion | flops 269025280 | bytes 2098176 | tf_op jit(solution)/shard_map/dot_general | solution.py:27
  4.3 0.0 copy-done.3
  4.3 0.4 fusion.18
  4.8 1.6 %pad_maximum_fusion = bf16[256,4096]{1,0:T(8,128)(2,1)} fusion(bf16[256,2048]{1,0:T(8,128)(2,1)S(1)} %fusion.18, bf16[256,2048]{1,0:T(8,128)(2,1)S(1)} %convolution_convert_fusion.1), kind=kLoop, calls=%fused_computation.25 | loop fusion | flops 4194304 | bytes 4194304 | tf_op jit(solution)/shard_map/concatenate | solution.py:57
  6.3 7.3 %all-to-all-start = ((bf16[8,32,4096]{2,1,0:T(8,128)(2,1)}), bf16[8,32,4096]{2,1,0:T(8,128)(2,1)}, u32[]{:S(2)}, u32[]{:S(2)}) async-start(bf16[8,32,4096]{2,1,0:T(8,128)(2,1)} %bitcast.64), calls=%async_computation | async-start | bytes 4194304 | tf_op jit(solution)/shard_map/all_to_all | solution.py:58
  13.6 0.1 pad.1.clone
  13.7 0.1 pad.3.clone
  13.8 0.1 pad.2.clone
  13.8 0.7 compare_select_fusion
  14.5 2.7 %dynamic-slice_bitcast_fusion = (bf16[192,2048]{1,0:T(8,128)(2,1)}, bf16[192,2048]{1,0:T(8,128)(2,1)}) fusion(bf16[1,768,2048]{2,1,0:T(8,128)(2,1)} %param.11, s32[]{:T(128)S(6)} %select_n.28, bf16[1,768,2048]{2,1,0:T(8,128)(2,1)} %param.10), kind=kLoop, calls=%fused_computation.62 | loop fusion | bytes 3145732 | tf_op jit(solution)/shard_map/dynamic_slice | solution.py:134
  17.3 44.7 %all-to-all-done = bf16[8,32,4096]{2,1,0:T(8,128)(2,1)} async-done(((bf16[8,32,4096]{2,1,0:T(8,128)(2,1)}), bf16[8,32,4096]{2,1,0:T(8,128)(2,1)}, u32[]{:S(2)}, u32[]{:S(2)}) %all-to-all-start) | async-done | bytes 2097184 | tf_op jit(solution)/shard_map/all_to_all | solution.py:58
  61.9 3.4 %fusion.10 = f32[256,768]{1,0:T(8,128)S(1)} fusion(bf16[1,768,2048]{2,1,0:T(8,128)(2,1)} %param.10, bf16[256,4096]{1,0:T(8,128)(2,1)} %bitcast.5), kind=kOutput, calls=%fused_computation.10 | convolution fusion | flops 805306368 | bytes 4980736 | tf_op jit(solution)/shard_map/dot_general | solution.py:15
  65.3 0.0 copy-start.10
  65.3 2.5 %fusion.6 = f32[256,768]{1,0:T(8,128)S(1)} fusion(bf16[1,768,2048]{2,1,0:T(8,128)(2,1)S(1)} %copy-done.7, bf16[256,4096]{1,0:T(8,128)(2,1)} %bitcast.5), kind=kOutput, calls=%fused_computation.6 | convolution fusion | flops 805306368 | bytes 4980736 | tf_op jit(solution)/shard_map/dot_general | solution.py:15
  67.9 0.0 copy-start.12
  67.9 1.6 %collective-permute-start.1 = (bf16[256,4096]{1,0:T(8,128)(2,1)}, bf16[256,4096]{1,0:T(8,128)(2,1)}, u32[]{:S(2)}, u32[]{:S(2)}) collective-permute-start(bf16[256,4096]{1,0:T(8,128)(2,1)} %bitcast.5), channel_id=1, source_target_pairs={{0,16},{8,24},{16,0},{24,8},{1,17},{9,25},{17,1},{25,9},{2,18},{10... | collective-permute-start | bytes 6291464 | tf_op jit(solution)/shard_map/ppermute | solution.py:70
  69.5 0.0 collective-permute-start
  69.5 0.0 copy-done
  69.5 2.0 %fusion.19 = bf16[256,2048]{1,0:T(8,128)(2,1)} fusion(bf16[1,768,2048]{2,1,0:T(8,128)(2,1)S(1)} %copy-done, f32[256,768]{1,0:T(8,128)S(1)} %fusion.6, f32[256,768]{1,0:T(8,128)S(1)} %fusion.10), kind=kOutput, calls=%fused_computation.22 | convolution fusion | flops 807010304 | bytes 5767168 | tf_op jit(solution)/shard_map/dot_general | solution.py:27
  71.5 4.2 %all-to-all-start.1 = ((bf16[8,32,2048]{2,1,0:T(8,128)(2,1)}), bf16[8,32,2048]{2,1,0:T(8,128)(2,1)}, u32[]{:S(2)}, u32[]{:S(2)}) async-start(bf16[8,32,2048]{2,1,0:T(8,128)(2,1)} %bitcast.66), calls=%async_computation.1 | async-start | bytes 2097152 | tf_op jit(solution)/shard_map/all_to_all | solution.py:84
  75.8 2.3 %fusion.57 = f32[256,384]{0,1:T(8,128)S(1)} fusion(bf16[256,4096]{1,0:T(8,128)(2,1)} %bitcast.5, bf16[192,2048]{1,0:T(8,128)(2,1)} %get-tuple-element.34, bf16[192,2048]{1,0:T(8,128)(2,1)} %get-tuple-element.35), kind=kOutput, calls=%fused_computation.71 | convolution fusion | flops 405798912 | bytes 3014656 | tf_op jit(solution)/shard_map/dot_general | solution.py:15
  78.1 1.7 %multiply_convert_fusion.17 = (bf16[256,192]{0,1:T(8,128)(2,1)S(1)}, bf16[256,192]{0,1:T(8,128)(2,1)S(1)}) fusion(f32[256,384]{0,1:T(8,128)S(1)} %fusion.57, bf16[1,768,2048]{2,1,0:T(8,128)(2,1)S(1)} %copy-done, s32[]{:T(128)S(6)} %select_n.28, bf16[256,4096]{1,0:T(8,128)(2,1)} %bitcast.5), kind=kOutput, calls=%fused_computation.114 | convolution fusion | flops 201965568 | bytes 2424836 | tf_op jit(solution)/shard_map/dot_general | solution.py:15
  79.8 3.5 %fusion.55 = f32[384,2048]{1,0:T(8,128)} fusion(bf16[256,4096]{1,0:T(8,128)(2,1)} %bitcast.5, bf16[256,192]{0,1:T(8,128)(2,1)S(1)} %get-tuple-element.29, bf16[256,192]{0,1:T(8,128)(2,1)S(1)} %get-tuple-element.28), kind=kOutput, calls=%fused_computation.69 | convolution fusion | flops 403046400 | bytes 4390912 | tf_op jit(solution)/shard_map/dot_general | solution.py:21
  83.3 2.4 %fusion = f32[256,768]{1,0:T(8,128)S(1)} fusion(bf16[1,768,2048]{2,1,0:T(8,128)(2,1)S(1)} %copy-done, bf16[256,4096]{1,0:T(8,128)(2,1)} %bitcast.5), kind=kOutput, calls=%fused_computation | convolution fusion | flops 805306368 | bytes 4980736 | tf_op jit(solution)/shard_map/dot_general | solution.py:15
  85.7 0.0 copy-start.11
  85.7 2.8 %fusion.45 = f32[192,2048]{1,0:T(8,128)} fusion(bf16[256,4096]{1,0:T(8,128)(2,1)} %bitcast.5, f32[256,384]{0,1:T(8,128)S(1)} %fusion.57), kind=kOutput, calls=%fused_computation.51 | convolution fusion | flops 201621504 | bytes 3014656 | tf_op jit(solution)/shard_map/dot_general | solution.py:21
  88.5 1.0 fusion.4
  89.6 0.9 copy-done.9
  90.4 0.2 copy-done.13
  90.6 2.2 %fusion.15 = bf16[256,2048]{1,0:T(8,128)(2,1)} fusion(f32[256,2048]{1,0:T(8,128)S(1)} %fusion.4, bf16[1,768,2048]{2,1,0:T(8,128)(2,1)S(1)} %copy-done.9, f32[256,768]{1,0:T(8,128)S(1)} %copy-done.11, f32[256,768]{1,0:T(8,128)S(1)} %fusion, f32[256,768]{1,0:T(8,128)S(1)} %copy-done.13), kind=kOutput, calls=%fused_computation.15 | convolution fusion | flops 808321024 | bytes 8650752 | tf_op jit(solution)/shard_map/dot_general | solution.py:27
  92.8 9.7 %all-to-all-done.1 = bf16[8,32,2048]{2,1,0:T(8,128)(2,1)} async-done(((bf16[8,32,2048]{2,1,0:T(8,128)(2,1)}), bf16[8,32,2048]{2,1,0:T(8,128)(2,1)}, u32[]{:S(2)}, u32[]{:S(2)}) %all-to-all-start.1) | async-done | bytes 1048608 | tf_op jit(solution)/shard_map/all_to_all | solution.py:84
  102.5 4.4 %all-to-all-start.2 = ((bf16[8,32,2048]{2,1,0:T(8,128)(2,1)}), bf16[8,32,2048]{2,1,0:T(8,128)(2,1)}, u32[]{:S(2)}, u32[]{:S(2)}) async-start(bf16[8,32,2048]{2,1,0:T(8,128)(2,1)} %bitcast.65), calls=%async_computation.2 | async-start | bytes 2097152 | tf_op jit(solution)/shard_map/all_to_all | solution.py:98
  106.9 0.0 collective-permute-done
  106.9 2.3 %fusion.40 = f32[256,384]{0,1:T(8,128)S(1)} fusion(bf16[256,4096]{1,0:T(8,128)(2,1)} %collective-permute-done, bf16[192,2048]{1,0:T(8,128)(2,1)} %get-tuple-element.34, bf16[192,2048]{1,0:T(8,128)(2,1)} %get-tuple-element.35), kind=kOutput, calls=%fused_computation.46 | convolution fusion | flops 405798912 | bytes 3014656 | tf_op jit(solution)/shard_map/dot_general | solution.py:15
  109.2 1.7 %multiply_convert_fusion.15 = (bf16[256,192]{0,1:T(8,128)(2,1)S(1)}, bf16[256,192]{0,1:T(8,128)(2,1)S(1)}) fusion(f32[256,384]{0,1:T(8,128)S(1)} %fusion.40, bf16[1,768,2048]{2,1,0:T(8,128)(2,1)S(1)} %copy-done, s32[]{:T(128)S(6)} %select_n.28, bf16[256,4096]{1,0:T(8,128)(2,1)} %collective-permute-done), kind=kOutput, calls=%fused_computation.110 | convolution fusion | flops 201965568 | bytes 2424836 | tf_op jit(solution)/shard_map/dot_general | solution.py:15
  111.0 0.0 copy-start.4
  111.0 2.8 %broadcast_multiply_fusion = (bf16[256,2048]{1,0:T(8,128)(2,1)}, f32[256,2048]{1,0:T(8,128)S(1)}) fusion(f32[256]{0:T(256)S(1)} %bitcast.70, bf16[256,2048]{1,0:T(8,128)(2,1)} %bitcast.10, s32[256]{0:T(256)S(1)} %bitcast.67), kind=kOutput, calls=%fused_computation.30 | convolution fusion | flops 269549568 | bytes 4196352 | tf_op jit(solution)/shard_map/dot_general | solution.py:27
  113.7 0.7 collective-permute-done.1
  114.5 0.0 collective-permute-start.2
  114.5 0.3 multiply_reduce_fusion
  114.8 0.1 copy-done.5
  114.9 0.2 copy-done.6
  115.1 1.8 %fusion.33 = f32[256,384]{0,1:T(8,128)S(1)} fusion(bf16[256,4096]{1,0:T(8,128)(2,1)} %collective-permute-done.1, bf16[192,2048]{1,0:T(8,128)(2,1)S(1)} %copy-done.5, bf16[192,2048]{1,0:T(8,128)(2,1)S(1)} %copy-done.6), kind=kOutput, calls=%fused_computation.39 | convolution fusion | flops 405798912 | bytes 3014656 | tf_op jit(solution)/shard_map/dot_general | solution.py:15
  116.9 1.7 %multiply_convert_fusion.13 = (bf16[256,192]{0,1:T(8,128)(2,1)S(1)}, bf16[256,192]{0,1:T(8,128)(2,1)S(1)}) fusion(f32[256,384]{0,1:T(8,128)S(1)} %fusion.33, bf16[1,768,2048]{2,1,0:T(8,128)(2,1)S(1)} %copy-done, s32[]{:T(128)S(6)} %select_n.28, bf16[256,4096]{1,0:T(8,128)(2,1)} %collective-permute-done.1), kind=kOutput, calls=%fused_computation.106 | convolution fusion | flops 201965568 | bytes 2424836 | tf_op jit(solution)/shard_map/dot_general | solution.py:15
  118.7 1.8 %fusion.38 = f32[384,2048]{1,0:T(8,128)S(1)} fusion(bf16[256,4096]{1,0:T(8,128)(2,1)} %collective-permute-done, bf16[256,192]{0,1:T(8,128)(2,1)S(1)} %get-tuple-element.27, bf16[256,192]{0,1:T(8,128)(2,1)S(1)} %get-tuple-element.26), kind=kOutput, calls=%fused_computation.44 | convolution fusion | flops 403046400 | bytes 4390912 | tf_op jit(solution)/shard_map/dot_general | solution.py:21
  120.5 1.9 %fusion.31 = f32[384,2048]{1,0:T(8,128)S(1)} fusion(bf16[256,4096]{1,0:T(8,128)(2,1)} %collective-permute-done.1, bf16[256,192]{0,1:T(8,128)(2,1)S(1)} %get-tuple-element.31, bf16[256,192]{0,1:T(8,128)(2,1)S(1)} %get-tuple-element.30), kind=kOutput, calls=%fused_computation.37 | convolution fusion | flops 403046400 | bytes 4390912 | tf_op jit(solution)/shard_map/dot_general | solution.py:21
  122.4 1.6 %convolution_add_fusion.2 = f32[192,2048]{1,0:T(8,128)S(1)} fusion(f32[192,2048]{1,0:T(8,128)S(1)} %copy-done.2, bf16[256,4096]{1,0:T(8,128)(2,1)} %collective-permute-done, f32[256,384]{0,1:T(8,128)S(1)} %fusion.40), kind=kOutput, calls=%fused_computation.18 | convolution fusion | flops 202014720 | bytes 4587520 | tf_op jit(solution)/shard_map/dot_general | solution.py:21
  124.1 1.6 %convolution_add_fusion.1 = f32[192,2048]{1,0:T(8,128)S(1)} fusion(f32[192,2048]{1,0:T(8,128)S(1)} %convolution_add_fusion.2, bf16[256,4096]{1,0:T(8,128)(2,1)} %collective-permute-done.1, f32[256,384]{0,1:T(8,128)S(1)} %fusion.33), kind=kOutput, calls=%fused_computation.17 | convolution fusion | flops 202014720 | bytes 4587520 | tf_op jit(solution)/shard_map/dot_general | solution.py:21
  125.7 0.7 maximum_maximum_fusion
  126.4 0.0 collective-permute-done.2
  126.4 0.6 fusion.26
  127.0 1.3 fusion.23
  128.3 0.5 multiply_convert_fusion.11
  128.8 1.4 %copy-done.1 = f32[384,2048]{1,0:T(8,128)S(1)} copy-done((f32[384,2048]{1,0:T(8,128)S(1)}, f32[384,2048]{1,0:T(8,128)}, u32[]{:S(2)}) %copy-start.1) | copy-done | bytes 3145752
  130.2 0.6 add_convert_fusion
  130.8 1.2 slice_bitcast_fusion
  132.0 0.6 all-to-all-done.2
  132.6 2.7 %convolution_convert_fusion = bf16[256,2048]{1,0:T(8,128)(2,1)} fusion(bf16[256,2048]{1,0:T(8,128)(2,1)} %bitcast.12, s32[256]{0:T(256)S(1)} %bitcast.68), kind=kOutput, calls=%fused_computation.20 | convolution fusion | flops 269025280 | bytes 2098176 | tf_op jit(solution)/shard_map/dot_general | solution.py:27
  (19 shorter events, 0.0 us)
Async XLA Ops:
  0.6 68.9 %copy-start = (bf16[1,768,2048]{2,1,0:T(8,128)(2,1)S(1)}, bf16[1,768,2048]{2,1,0:T(8,128)(2,1)}, u32[]{:S(2)}) copy-start(bf16[1,768,2048]{2,1,0:T(8,128)(2,1)} %param.12) | copy-start | bytes 9437188
  0.6 3.7 %copy-start.3 = (bf16[256,2048]{1,0:T(8,128)(2,1)S(1)}, bf16[256,2048]{1,0:T(8,128)(2,1)}, u32[]{:S(2)}) copy-start(bf16[256,2048]{1,0:T(8,128)(2,1)} %param.13) | copy-start | bytes 3145732
  6.3 55.6 %all-to-all-start = ((bf16[8,32,4096]{2,1,0:T(8,128)(2,1)}), bf16[8,32,4096]{2,1,0:T(8,128)(2,1)}, u32[]{:S(2)}, u32[]{:S(2)}) async-start(bf16[8,32,4096]{2,1,0:T(8,128)(2,1)} %bitcast.64), calls=%async_computation | async-start | bytes 4194304 | tf_op jit(solution)/shard_map/all_to_all | solution.py:58
  61.9 3.4 %copy-start.7 = (bf16[1,768,2048]{2,1,0:T(8,128)(2,1)S(1)}, bf16[1,768,2048]{2,1,0:T(8,128)(2,1)}, u32[]{:S(2)}) copy-start(bf16[1,768,2048]{2,1,0:T(8,128)(2,1)} %param.11) | copy-start | bytes 9437188
  65.3 4.2 %copy-start.10 = (f32[256,768]{1,0:T(8,128)}, f32[256,768]{1,0:T(8,128)S(1)}, u32[]{:S(2)}) copy-start(f32[256,768]{1,0:T(8,128)S(1)} %fusion.10) | copy-start | bytes 2359300
  67.9 3.6 %copy-start.12 = (f32[256,768]{1,0:T(8,128)}, f32[256,768]{1,0:T(8,128)S(1)}, u32[]{:S(2)}) copy-start(f32[256,768]{1,0:T(8,128)S(1)} %fusion.6) | copy-start | bytes 2359300
  67.9 46.6 %collective-permute-start.1 = (bf16[256,4096]{1,0:T(8,128)(2,1)}, bf16[256,4096]{1,0:T(8,128)(2,1)}, u32[]{:S(2)}, u32[]{:S(2)}) collective-permute-start(bf16[256,4096]{1,0:T(8,128)(2,1)} %bitcast.5), channel_id=1, source_target_pairs={{0,16},{8,24},{16,0},{24,8},{1,17},{9,25},{17,1},{25,9},{2,18},{10... | collective-permute-start | bytes 6291464 | tf_op jit(solution)/shard_map/ppermute | solution.py:70
  69.5 37.4 %collective-permute-start = (bf16[256,4096]{1,0:T(8,128)(2,1)}, bf16[256,4096]{1,0:T(8,128)(2,1)}, u32[]{:S(2)}, u32[]{:S(2)}) collective-permute-start(bf16[256,4096]{1,0:T(8,128)(2,1)} %bitcast.5), channel_id=1, source_target_pairs={{0,8},{8,0},{16,24},{24,16},{1,9},{9,1},{17,25},{25,17},{2,10},{10... | collective-permute-start | bytes 6291464 | tf_op jit(solution)/shard_map/ppermute | solution.py:69
  71.5 31.0 %all-to-all-start.1 = ((bf16[8,32,2048]{2,1,0:T(8,128)(2,1)}), bf16[8,32,2048]{2,1,0:T(8,128)(2,1)}, u32[]{:S(2)}, u32[]{:S(2)}) async-start(bf16[8,32,2048]{2,1,0:T(8,128)(2,1)} %bitcast.66), calls=%async_computation.1 | async-start | bytes 2097152 | tf_op jit(solution)/shard_map/all_to_all | solution.py:84
  83.3 5.3 %copy-start.8 = (bf16[1,768,2048]{2,1,0:T(8,128)(2,1)S(1)}, bf16[1,768,2048]{2,1,0:T(8,128)(2,1)}, u32[]{:S(2)}) copy-start(bf16[1,768,2048]{2,1,0:T(8,128)(2,1)} %param.11) | copy-start | bytes 9437188
  85.7 2.8 %copy-start.11 = (f32[256,768]{1,0:T(8,128)S(1)}, f32[256,768]{1,0:T(8,128)}, u32[]{:S(2)}) copy-start(f32[256,768]{1,0:T(8,128)} %copy-done.10) | copy-start | bytes 2359300
  88.5 1.9 %copy-start.9 = (bf16[1,768,2048]{2,1,0:T(8,128)(2,1)S(1)}, bf16[1,768,2048]{2,1,0:T(8,128)(2,1)}, u32[]{:S(2)}) copy-start(bf16[1,768,2048]{2,1,0:T(8,128)(2,1)} %param.10) | copy-start | bytes 9437188
  88.5 2.1 %copy-start.13 = (f32[256,768]{1,0:T(8,128)S(1)}, f32[256,768]{1,0:T(8,128)}, u32[]{:S(2)}) copy-start(f32[256,768]{1,0:T(8,128)} %copy-done.12) | copy-start | bytes 2359300
  102.5 30.2 %all-to-all-start.2 = ((bf16[8,32,2048]{2,1,0:T(8,128)(2,1)}), bf16[8,32,2048]{2,1,0:T(8,128)(2,1)}, u32[]{:S(2)}, u32[]{:S(2)}) async-start(bf16[8,32,2048]{2,1,0:T(8,128)(2,1)} %bitcast.65), calls=%async_computation.2 | async-start | bytes 2097152 | tf_op jit(solution)/shard_map/all_to_all | solution.py:98
  111.0 3.5 %copy-start.4 = (bf16[256,2048]{1,0:T(8,128)(2,1)S(1)}, bf16[256,2048]{1,0:T(8,128)(2,1)}, u32[]{:S(2)}) copy-start(bf16[256,2048]{1,0:T(8,128)(2,1)} %param.13) | copy-start | bytes 3145732
  113.7 1.1 copy-start.5
  113.7 1.4 %copy-start.6 = (bf16[192,2048]{1,0:T(8,128)(2,1)S(1)}, bf16[192,2048]{1,0:T(8,128)(2,1)}, u32[]{:S(2)}) copy-start(bf16[192,2048]{1,0:T(8,128)(2,1)} %get-tuple-element.35) | copy-start | bytes 2359300
  114.5 11.9 %collective-permute-start.2 = (bf16[256,4096]{1,0:T(8,128)(2,1)}, bf16[256,4096]{1,0:T(8,128)(2,1)S(1)}, u32[]{:S(2)}, u32[]{:S(2)}) collective-permute-start(bf16[256,4096]{1,0:T(8,128)(2,1)} %collective-permute-done.1), channel_id=1, source_target_pairs={{0,8},{8,0},{16,24},{24,16},{1,9},{9,1},{17,25},{25,17},{2,10},{10... | collective-permute-start | bytes 6291464 | tf_op jit(solution)/shard_map/ppermute | solution.py:121
  120.5 1.9 %copy-start.2 = (f32[192,2048]{1,0:T(8,128)S(1)}, f32[192,2048]{1,0:T(8,128)}, u32[]{:S(2)}) copy-start(f32[192,2048]{1,0:T(8,128)} %fusion.45) | copy-start | bytes 4718596
  128.3 1.9 %copy-start.1 = (f32[384,2048]{1,0:T(8,128)S(1)}, f32[384,2048]{1,0:T(8,128)}, u32[]{:S(2)}) copy-start(f32[384,2048]{1,0:T(8,128)} %fusion.55) | copy-start | bytes 9437188

commit v11 on v10

--- a/solution.py
+++ b/solution.py
@@ -67,7 +67,9 @@
     by_pieces = copies == 4
     if by_pieces:
         near = lax.ppermute(received, "rep", [(r, r ^ 1) for r in range(copies)])
-        far = lax.ppermute(received, "rep", [(r, r ^ 2) for r in range(copies)])
+        half = total_slots // 2
+        far_first = lax.ppermute(received[:half], "rep", [(r, r ^ 2) for r in range(copies)])
+        far_second = lax.ppermute(received[half:], "rep", [(r, r ^ 2) for r in range(copies)])
     else:
         gathered = lax.all_gather(received, "rep", axis=0, tiled=True)
 
@@ -76,8 +78,11 @@
     gate_mat = w_gate[0]
     up_mat = w_up[0]
     down_mat = w_down[0]
-    pre_gate = rows_times(rows_in, gate_mat)
-    pre_up = rows_times(rows_in, up_mat)
+    gate_up_mat = jnp.concatenate([gate_mat, up_mat], axis=0)
+    hidden_units = gate_mat.shape[0]
+    pre_both_own = rows_times(rows_in, gate_up_mat)
+    pre_gate = pre_both_own[:, :hidden_units]
+    pre_up = pre_both_own[:, hidden_units:]
     activated = jax.nn.silu(pre_gate)
     hidden = (activated * pre_up).astype(jnp.bfloat16)
     expert_out = matmul(hidden, down_mat).astype(jnp.bfloat16)
@@ -92,8 +97,8 @@
     hidden_grad = rows_times(grad_in, down_mat)
     gate_pre_grad = (hidden_grad * pre_up * silu_grad(pre_gate)).astype(jnp.bfloat16)
     up_pre_grad = (hidden_grad * activated).astype(jnp.bfloat16)
-    token_part = (
-        matmul(gate_pre_grad, gate_mat) + matmul(up_pre_grad, up_mat)
+    token_part = matmul(
+        jnp.concatenate([gate_pre_grad, up_pre_grad], axis=1), gate_up_mat
     ).astype(jnp.bfloat16)
     part_back = lax.all_to_all(
         token_part.reshape(experts, per_pair, feature_width),
@@ -104,7 +109,8 @@
     ).reshape(total_slots, feature_width)
 
     if by_pieces:
-        returned, near = lax.optimization_barrier((returned, near))
+        returned, near, far_first = lax.optimization_barrier((returned, near, far_first))
+        near_far_first = lax.ppermute(far_first, "rep", [(r, r ^ 1) for r in range(copies)])
     slot_grid = slot_index.reshape(tok_count, live_cols)
     gate_grid = flat_gates.reshape(tok_count, live_cols)
     layer_sum = jnp.zeros((tok_count, feature_width), jnp.float32)
@@ -117,9 +123,9 @@
         layer_sum = layer_sum + gate_grid[:, col : col + 1] * out_rows
         gate_cols.append(jnp.sum(out_grad.astype(jnp.float32) * out_rows, axis=1))
     if by_pieces:
-        layer_sum, far = lax.optimization_barrier((layer_sum, far))
-        near_far = lax.ppermute(far, "rep", [(r, r ^ 1) for r in range(copies)])
-        pieces = [received, near, far, near_far]
+        layer_sum, far_second = lax.optimization_barrier((layer_sum, far_second))
+        near_far_second = lax.ppermute(far_second, "rep", [(r, r ^ 1) for r in range(copies)])
+        pieces = [received, near, far_first, near_far_first, far_second, near_far_second]
     else:
         pieces = [gathered]
     layer_out = layer_sum.astype(jnp.bfloat16)

time: 136 us -> 155 us (1.14)
  waiting for transfers between devices: 55.7 us -> 66.1 us
  matrix products: 49.2 us -> 55.1 us
  local copies, waits for them, and re-layouts: 8.64 us -> 10.5 us
    ppermute x2 -> x4, waiting for transfers between devices: 0.75 us -> 15.4 us  [the longest x1 15.4 us: body(): lax.ppermute(received[half:], 'rep', [(r, r ^ 2) for r in range(copies)])]
    dot_general x8 -> x12, matrix products: 15.2 us -> 19 us  [inner_rows(): lax.dot_general(left, right, (((0,), (0,)), ((), ())), preferred_element_...]
    all_to_all x1, waiting for transfers between devices: 9.7 us -> 5.99 us  [body(): lax.all_to_all(expert_out.reshape(experts, per_pair, feature_width), 'ep'...]
    slice x0 -> x1, local copies, waits for them, and re-layouts: none -> 3.19 us  [body(): received[half:]]
    dot_general x11 -> x14, matrix products: 21 us -> 23.4 us  [rows_times(): lax.dot_general(left, right, (((1,), (1,)), ((), ())), preferred_element_...]
    dot_general x8 -> x7, matrix products: 13 us -> 12.6 us  [matmul(): return jnp.dot(left, right, preferred_element_type=jnp.float32)]
  transfers between devices with their start and end apart: 6 -> 8, of which waited for: 4 -> 3; matrix products, arithmetic and copies ran while one was open for 33% -> 38% of each run, Pallas kernels for 0% -> 0%
where the time goes in v11:
time: 155 us; the launch traced here: 154 us
  waiting for transfers between devices  66.1 us (43%)
  matrix products  55.1 us (36%)
  starting transfers between devices  18.2 us (12%)
  local copies, waits for them, and re-layouts  10.5 us (7%)
  other arithmetic  3.34 us (2%)
    all_to_all x1, waiting for transfers between devices, body(): lax.all_to_all(outgoing.reshape(experts, per_pair, 2 * feature_width), 'e...  44.7 us
    dot_general x14, matrix products, rows_times(): lax.dot_general(left, right, (((1,), (1,)), ((), ())), preferred_element_...  23.4 us
    dot_general x12, matrix products, inner_rows(): lax.dot_general(left, right, (((0,), (0,)), ((), ())), preferred_element_...  19 us
    ppermute x1, waiting for transfers between devices, body(): lax.ppermute(received[half:], 'rep', [(r, r ^ 2) for r in range(copies)])  15.4 us
    dot_general x7, matrix products, matmul(): return jnp.dot(left, right, preferred_element_type=jnp.float32)  12.6 us
    all_to_all x1, starting transfers between devices, body(): lax.all_to_all(outgoing.reshape(experts, per_pair, 2 * feature_width), 'e...  7.26 us
    all_to_all x1, waiting for transfers between devices, body(): lax.all_to_all(expert_out.reshape(experts, per_pair, feature_width), 'ep'...  5.99 us
    all_to_all x1, starting transfers between devices, body(): lax.all_to_all(token_part.reshape(experts, per_pair, feature_width), 'ep'...  4.43 us
  transfers between devices with their start and end apart: 8, of which 3 were waited for; matrix products, arithmetic and copies ran while one was open for 38% of the time, Pallas kernels for 0%

profile of v11, /device:TPU:0, one launch (start us, length us, event | category | flops | bytes accessed | tf_op | source)
XLA Modules:
  0.0 154.2 jit_solution(16271011517448153862)
XLA Ops:
  0.6 0.0 copy-start
  0.6 0.0 copy-start.3
  0.7 0.9 slice.106
  1.5 0.8 slice.107
  2.3 0.2 fusion.14
  2.5 0.1 select_reduce_fusion
  2.6 1.7 %convolution_convert_fusion.1 = bf16[256,2048]{1,0:T(8,128)(2,1)S(1)} fusion(bf16[256,2048]{1,0:T(8,128)(2,1)} %param.7, s32[256]{0:T(256)S(1)} %compare_select_fusion.1), kind=kOutput, calls=%fused_computation.16 | convolution fusion | flops 269025280 | bytes 2098176 | tf_op jit(solution)/shard_map/dot_general | solution.py:27
  4.3 0.4 fusion.6
  4.8 1.5 %pad_maximum_fusion.5 = bf16[256,4096]{1,0:T(8,128)(2,1)} fusion(bf16[256,2048]{1,0:T(8,128)(2,1)S(1)} %fusion.6, bf16[256,2048]{1,0:T(8,128)(2,1)S(1)} %convolution_convert_fusion.1), kind=kLoop, calls=%fused_computation.21 | loop fusion | flops 4194304 | bytes 4194304 | tf_op jit(solution)/shard_map/concatenate | solution.py:57
  6.3 7.3 %all-to-all-start = ((bf16[8,32,4096]{2,1,0:T(8,128)(2,1)}), bf16[8,32,4096]{2,1,0:T(8,128)(2,1)}, u32[]{:S(2)}, u32[]{:S(2)}) async-start(bf16[8,32,4096]{2,1,0:T(8,128)(2,1)} %bitcast.64), calls=%async_computation | async-start | bytes 4194304 | tf_op jit(solution)/shard_map/all_to_all | solution.py:58
  13.6 0.1 pad.1.clone
  13.7 0.1 pad.3.clone
  13.8 0.1 pad.2.clone
  13.8 0.7 compare_select_fusion
  14.5 2.7 %dynamic-slice_bitcast_fusion = (bf16[192,2048]{1,0:T(8,128)(2,1)}, bf16[192,2048]{1,0:T(8,128)(2,1)}) fusion(bf16[1,768,2048]{2,1,0:T(8,128)(2,1)} %param.11, s32[]{:T(128)S(6)} %select_n.28, bf16[1,768,2048]{2,1,0:T(8,128)(2,1)} %param.10), kind=kLoop, calls=%fused_computation.59 | loop fusion | bytes 3145732 | tf_op jit(solution)/shard_map/dynamic_slice | solution.py:140
  17.2 44.7 %all-to-all-done = bf16[8,32,4096]{2,1,0:T(8,128)(2,1)} async-done(((bf16[8,32,4096]{2,1,0:T(8,128)(2,1)}), bf16[8,32,4096]{2,1,0:T(8,128)(2,1)}, u32[]{:S(2)}, u32[]{:S(2)}) %all-to-all-start) | async-done | bytes 2097184 | tf_op jit(solution)/shard_map/all_to_all | solution.py:58
  61.9 5.0 %fusion.1 = f32[256,1536]{1,0:T(8,128)S(1)} fusion(bf16[768,2048]{1,0:T(8,128)(2,1)} %bitcast.67, bf16[768,2048]{1,0:T(8,128)(2,1)} %bitcast.69, bf16[256,4096]{1,0:T(8,128)(2,1)} %bitcast.5), kind=kOutput, calls=%fused_computation.2 | convolution fusion | flops 1623195648 | bytes 8912896 | tf_op jit(solution)/shard_map/dot_general | solution.py:15
  67.0 2.0 %fusion.9 = bf16[256,2048]{1,0:T(8,128)(2,1)} fusion(bf16[1,768,2048]{2,1,0:T(8,128)(2,1)S(1)} %copy-done, f32[256,1536]{1,0:T(8,128)S(1)} %fusion.1), kind=kOutput, calls=%fused_computation.18 | convolution fusion | flops 807010304 | bytes 5767168 | tf_op jit(solution)/shard_map/dot_general | solution.py:27
  69.0 4.2 %all-to-all-start.1 = ((bf16[8,32,2048]{2,1,0:T(8,128)(2,1)}), bf16[8,32,2048]{2,1,0:T(8,128)(2,1)}, u32[]{:S(2)}, u32[]{:S(2)}) async-start(bf16[8,32,2048]{2,1,0:T(8,128)(2,1)} %bitcast.66), calls=%async_computation.1 | async-start | bytes 2097152 | tf_op jit(solution)/shard_map/all_to_all | solution.py:89
  73.2 0.0 copy-start.5
  73.2 0.0 copy-start.7
  73.3 3.2 %fusion.134 = (bf16[4,32,4096]{2,1,0:T(8,128)(2,1)}, bf16[4,32,4096]{2,1,0:T(8,128)(2,1)}) fusion(bf16[8,32,4096]{2,1,0:T(8,128)(2,1)} %all-to-all-done), kind=kLoop, calls=%fused_computation.179 | loop fusion | bytes 4194304 | tf_op jit(solution)/shard_map/slice | solution.py:72
  76.4 1.5 collective-permute-start.1
  78.0 2.0 %fusion.29 = f32[256,384]{0,1:T(8,128)S(1)} fusion(bf16[256,4096]{1,0:T(8,128)(2,1)} %bitcast.5, bf16[192,2048]{1,0:T(8,128)(2,1)S(1)} %copy-done.5, bf16[192,2048]{1,0:T(8,128)(2,1)S(1)} %copy-done.7), kind=kOutput, calls=%fused_computation.41 | convolution fusion | flops 405798912 | bytes 3014656 | tf_op jit(solution)/shard_map/dot_general | solution.py:15
  80.0 2.4 %multiply_convert_fusion.1 = (bf16[256,768]{1,0:T(8,128)(2,1)S(1)}, bf16[256,768]{1,0:T(8,128)(2,1)S(1)}) fusion(f32[256,1536]{1,0:T(8,128)S(1)} %copy-done.12, bf16[1,768,2048]{2,1,0:T(8,128)(2,1)S(1)} %copy-done, bf16[256,4096]{1,0:T(8,128)(2,1)} %bitcast.5), kind=kOutput, calls=%fused_computation.62 | convolution fusion | flops 807862272 | bytes 6553600 | tf_op jit(solution)/shard_map/dot_general | solution.py:15
  82.4 1.7 %multiply_convert_fusion.9 = (bf16[256,192]{0,1:T(8,128)(2,1)S(1)}, bf16[256,192]{0,1:T(8,128)(2,1)S(1)}) fusion(f32[256,384]{0,1:T(8,128)S(1)} %fusion.29, bf16[1,768,2048]{2,1,0:T(8,128)(2,1)S(1)} %copy-done, s32[]{:T(128)S(6)} %select_n.28, bf16[256,4096]{1,0:T(8,128)(2,1)} %bitcast.5), kind=kOutput, calls=%fused_computation.114 | convolution fusion | flops 201965568 | bytes 2424836 | tf_op jit(solution)/shard_map/dot_general | solution.py:15
  84.2 0.6 collective-permute-start.2
  84.7 3.6 %fusion.27 = f32[384,2048]{1,0:T(8,128)} fusion(bf16[256,4096]{1,0:T(8,128)(2,1)} %bitcast.5, bf16[256,192]{0,1:T(8,128)(2,1)S(1)} %get-tuple-element.33, bf16[256,192]{0,1:T(8,128)(2,1)S(1)} %get-tuple-element.32), kind=kOutput, calls=%fused_computation.39 | convolution fusion | flops 403046400 | bytes 4390912 | tf_op jit(solution)/shard_map/dot_general | solution.py:21
  88.3 2.8 %fusion.22 = f32[192,2048]{1,0:T(8,128)} fusion(bf16[256,4096]{1,0:T(8,128)(2,1)} %bitcast.5, f32[256,384]{0,1:T(8,128)S(1)} %fusion.29), kind=kOutput, calls=%fused_computation.34 | convolution fusion | flops 201621504 | bytes 3014656 | tf_op jit(solution)/shard_map/dot_general | solution.py:21
  91.1 2.8 %fusion.7 = bf16[256,2048]{1,0:T(8,128)(2,1)} fusion(bf16[768,2048]{1,0:T(8,128)(2,1)S(1)} %bitcast.68, bf16[768,2048]{1,0:T(8,128)(2,1)S(1)} %bitcast.70, bf16[256,768]{1,0:T(8,128)(2,1)S(1)} %get-tuple-element.25, bf16[256,768]{1,0:T(8,128)(2,1)S(1)} %get-tuple-element.24), kind=kOutput, calls=%fused_computation.14 | convolution fusion | flops 1625292800 | bytes 8126464 | tf_op jit(solution)/shard_map/dot_general | solution.py:27
  94.0 6.0 %all-to-all-done.1 = bf16[8,32,2048]{2,1,0:T(8,128)(2,1)} async-done(((bf16[8,32,2048]{2,1,0:T(8,128)(2,1)}), bf16[8,32,2048]{2,1,0:T(8,128)(2,1)}, u32[]{:S(2)}, u32[]{:S(2)}) %all-to-all-start.1) | async-done | bytes 1048608 | tf_op jit(solution)/shard_map/all_to_all | solution.py:89
  99.9 4.4 %all-to-all-start.2 = ((bf16[8,32,2048]{2,1,0:T(8,128)(2,1)}), bf16[8,32,2048]{2,1,0:T(8,128)(2,1)}, u32[]{:S(2)}, u32[]{:S(2)}) async-start(bf16[8,32,2048]{2,1,0:T(8,128)(2,1)} %bitcast.65), calls=%async_computation.2 | async-start | bytes 2097152 | tf_op jit(solution)/shard_map/all_to_all | solution.py:103
  104.4 0.1 collective-permute-start.3
  104.5 2.1 %fusion.66 = f32[128,384]{0,1:T(8,128)S(1)} fusion(bf16[128,4096]{1,0:T(8,128)(2,1)} %collective-permute-done.1, bf16[192,2048]{1,0:T(8,128)(2,1)} %get-tuple-element.44, bf16[192,2048]{1,0:T(8,128)(2,1)} %get-tuple-element.45), kind=kOutput, calls=%fused_computation.86 | convolution fusion | flops 204472320 | bytes 2293760 | tf_op jit(solution)/shard_map/dot_general | solution.py:15
  106.6 0.0 copy-start.6
  106.6 0.0 copy-start.8
  106.6 2.8 %broadcast_multiply_fusion = (bf16[256,2048]{1,0:T(8,128)(2,1)}, f32[256,2048]{1,0:T(8,128)S(1)}) fusion(f32[256]{0:T(256)S(1)} %bitcast.74, bf16[256,2048]{1,0:T(8,128)(2,1)} %bitcast.10, s32[256]{0:T(256)S(1)} %bitcast.71), kind=kOutput, calls=%fused_computation.26 | convolution fusion | flops 269549568 | bytes 4196352 | tf_op jit(solution)/shard_map/dot_general | solution.py:27
  109.4 15.4 %collective-permute-done.2 = bf16[128,4096]{1,0:T(8,128)(2,1)} collective-permute-done((bf16[128,4096]{1,0:T(8,128)(2,1)}, bf16[128,4096]{1,0:T(8,128)(2,1)}, u32[]{:S(2)}, u32[]{:S(2)}) %collective-permute-start.2) | collective-permute-done | bytes 1048608 | tf_op jit(solution)/shard_map/ppermute | solution.py:72
  124.8 1.6 %fusion.59 = f32[128,384]{0,1:T(8,128)S(1)} fusion(bf16[128,4096]{1,0:T(8,128)(2,1)} %collective-permute-done.2, bf16[192,2048]{1,0:T(8,128)(2,1)S(1)} %copy-done.6, bf16[192,2048]{1,0:T(8,128)(2,1)S(1)} %copy-done.8), kind=kOutput, calls=%fused_computation.79 | convolution fusion | flops 204472320 | bytes 2293760 | tf_op jit(solution)/shard_map/dot_general | solution.py:15
  126.4 0.1 collective-permute-start.4
  126.5 1.4 multiply_convert_fusion.19
  127.9 1.4 fusion.61
  129.4 1.4 multiply_convert_fusion.23
  130.8 1.9 %fusion.17 = f32[256,384]{0,1:T(8,128)S(1)} fusion(bf16[256,4096]{1,0:T(8,128)(2,1)} %collective-permute-done, bf16[192,2048]{1,0:T(8,128)(2,1)S(1)} %copy-done.6, bf16[192,2048]{1,0:T(8,128)(2,1)S(1)} %copy-done.8), kind=kOutput, calls=%fused_computation.29 | convolution fusion | flops 405798912 | bytes 3014656 | tf_op jit(solution)/shard_map/dot_general | solution.py:15
  132.7 1.6 %convolution_add_fusion.3 = f32[192,2048]{1,0:T(8,128)S(1)} fusion(f32[192,2048]{1,0:T(8,128)S(1)} %copy-done.2, bf16[256,4096]{1,0:T(8,128)(2,1)} %collective-permute-done, f32[256,384]{0,1:T(8,128)S(1)} %fusion.17), kind=kOutput, calls=%fused_computation.12 | convolution fusion | flops 202014720 | bytes 4587520 | tf_op jit(solution)/shard_map/dot_general | solution.py:21
  134.4 1.4 convolution_add_fusion.2
  135.8 1.6 %fusion.57 = f32[384,2048]{1,0:T(8,128)S(1)} fusion(bf16[128,4096]{1,0:T(8,128)(2,1)} %collective-permute-done.2, bf16[128,192]{0,1:T(8,128)(2,1)S(1)} %get-tuple-element.41, bf16[128,192]{0,1:T(8,128)(2,1)S(1)} %get-tuple-element.40), kind=kOutput, calls=%fused_computation.77 | convolution fusion | flops 201523200 | bytes 3768320 | tf_op jit(solution)/shard_map/dot_general | solution.py:21
  137.4 1.6 %fusion.64 = f32[384,2048]{1,0:T(8,128)S(1)} fusion(bf16[128,4096]{1,0:T(8,128)(2,1)} %collective-permute-done.1, bf16[128,192]{0,1:T(8,128)(2,1)S(1)} %get-tuple-element.37, bf16[128,192]{0,1:T(8,128)(2,1)S(1)} %get-tuple-element.36), kind=kOutput, calls=%fused_computation.84 | convolution fusion | flops 201523200 | bytes 3768320 | tf_op jit(solution)/shard_map/dot_general | solution.py:21
  139.0 0.0 copy-start.4
  139.0 1.8 %multiply_convert_fusion.7 = (bf16[256,192]{0,1:T(8,128)(2,1)S(1)}, bf16[256,192]{0,1:T(8,128)(2,1)S(1)}) fusion(f32[256,384]{0,1:T(8,128)S(1)} %fusion.17, bf16[1,768,2048]{2,1,0:T(8,128)(2,1)S(1)} %copy-done, s32[]{:T(128)S(6)} %select_n.28, bf16[256,4096]{1,0:T(8,128)(2,1)} %collective-permute-done), kind=kOutput, calls=%fused_computation.110 | convolution fusion | flops 201965568 | bytes 2424836 | tf_op jit(solution)/shard_map/dot_general | solution.py:15
  140.9 0.3 multiply_reduce_fusion
  141.1 0.7 maximum_maximum_fusion
  141.8 1.8 %fusion.15 = f32[384,2048]{1,0:T(8,128)S(1)} fusion(bf16[256,4096]{1,0:T(8,128)(2,1)} %collective-permute-done, bf16[256,192]{0,1:T(8,128)(2,1)S(1)} %get-tuple-element.31, bf16[256,192]{0,1:T(8,128)(2,1)S(1)} %get-tuple-element.30), kind=kOutput, calls=%fused_computation.27 | convolution fusion | flops 403046400 | bytes 4390912 | tf_op jit(solution)/shard_map/dot_general | solution.py:21
  143.6 0.6 fusion.53
  144.2 0.4 multiply_convert_fusion.21
  144.6 0.6 fusion.47
  145.2 0.4 fusion.8
  145.6 1.3 fusion.13
  146.9 0.4 multiply_convert_fusion.17
  147.3 0.6 fusion.51
  147.8 1.3 copy-done.1
  149.2 1.0 add_convert_fusion
  150.2 1.3 slice_bitcast_fusion
  151.5 2.7 %convolution_convert_fusion = bf16[256,2048]{1,0:T(8,128)(2,1)} fusion(bf16[256,2048]{1,0:T(8,128)(2,1)} %bitcast.14, s32[256]{0:T(256)S(1)} %bitcast.72), kind=kOutput, calls=%fused_computation.15 | convolution fusion | flops 269025280 | bytes 2098176 | tf_op jit(solution)/shard_map/dot_general | solution.py:27
  (28 shorter events, 0.1 us)
Async XLA Ops:
  0.6 66.3 %copy-start = (bf16[1,768,2048]{2,1,0:T(8,128)(2,1)S(1)}, bf16[1,768,2048]{2,1,0:T(8,128)(2,1)}, u32[]{:S(2)}) copy-start(bf16[1,768,2048]{2,1,0:T(8,128)(2,1)} %param.12) | copy-start | bytes 9437188
  0.6 3.7 %copy-start.3 = (bf16[256,2048]{1,0:T(8,128)(2,1)S(1)}, bf16[256,2048]{1,0:T(8,128)(2,1)}, u32[]{:S(2)}) copy-start(bf16[256,2048]{1,0:T(8,128)(2,1)} %param.13) | copy-start | bytes 3145732
  6.3 55.6 %all-to-all-start = ((bf16[8,32,4096]{2,1,0:T(8,128)(2,1)}), bf16[8,32,4096]{2,1,0:T(8,128)(2,1)}, u32[]{:S(2)}, u32[]{:S(2)}) async-start(bf16[8,32,4096]{2,1,0:T(8,128)(2,1)} %bitcast.64), calls=%async_computation | async-start | bytes 4194304 | tf_op jit(solution)/shard_map/all_to_all | solution.py:58
  61.9 42.5 %collective-permute-start = (bf16[256,4096]{1,0:T(8,128)(2,1)}, bf16[256,4096]{1,0:T(8,128)(2,1)}, u32[]{:S(2)}, u32[]{:S(2)}) collective-permute-start(bf16[256,4096]{1,0:T(8,128)(2,1)} %bitcast.5), channel_id=1, source_target_pairs={{0,8},{8,0},{16,24},{24,16},{1,9},{9,1},{17,25},{25,17},{2,10},{10... | collective-permute-start | bytes 6291464 | tf_op jit(solution)/shard_map/ppermute | solution.py:69
  66.9 2.0 %copy-start.11 = (f32[256,1536]{1,0:T(8,128)}, f32[256,1536]{1,0:T(8,128)S(1)}, u32[]{:S(2)}) copy-start(f32[256,1536]{1,0:T(8,128)S(1)} %fusion.1) | copy-start | bytes 4718596
  69.0 31.0 %all-to-all-start.1 = ((bf16[8,32,2048]{2,1,0:T(8,128)(2,1)}), bf16[8,32,2048]{2,1,0:T(8,128)(2,1)}, u32[]{:S(2)}, u32[]{:S(2)}) async-start(bf16[8,32,2048]{2,1,0:T(8,128)(2,1)} %bitcast.66), calls=%async_computation.1 | async-start | bytes 2097152 | tf_op jit(solution)/shard_map/all_to_all | solution.py:89
  73.2 4.7 %copy-start.5 = (bf16[192,2048]{1,0:T(8,128)(2,1)S(1)}, bf16[192,2048]{1,0:T(8,128)(2,1)}, u32[]{:S(2)}) copy-start(bf16[192,2048]{1,0:T(8,128)(2,1)} %get-tuple-element.44) | copy-start | bytes 2359300
  73.2 4.7 %copy-start.7 = (bf16[192,2048]{1,0:T(8,128)(2,1)S(1)}, bf16[192,2048]{1,0:T(8,128)(2,1)}, u32[]{:S(2)}) copy-start(bf16[192,2048]{1,0:T(8,128)(2,1)} %get-tuple-element.45) | copy-start | bytes 2359300
  76.4 27.9 %collective-permute-start.1 = (bf16[128,4096]{1,0:T(8,128)(2,1)}, bf16[128,4096]{1,0:T(8,128)(2,1)}, u32[]{:S(2)}, u32[]{:S(2)}) collective-permute-start(bf16[128,4096]{1,0:T(8,128)(2,1)} %bitcast.11), channel_id=1, source_target_pairs={{0,16},{8,24},{16,0},{24,8},{1,17},{9,25},{17,1},{25,9},{2,18},{10... | collective-permute-start | bytes 3145736 | tf_op jit(solution)/shard_map/ppermute | solution.py:71
  78.0 2.0 %copy-start.12 = (f32[256,1536]{1,0:T(8,128)S(1)}, f32[256,1536]{1,0:T(8,128)}, u32[]{:S(2)}) copy-start(f32[256,1536]{1,0:T(8,128)} %copy-done.11) | copy-start | bytes 4718596
  84.2 40.7 %collective-permute-start.2 = (bf16[128,4096]{1,0:T(8,128)(2,1)}, bf16[128,4096]{1,0:T(8,128)(2,1)}, u32[]{:S(2)}, u32[]{:S(2)}) collective-permute-start(bf16[128,4096]{1,0:T(8,128)(2,1)} %bitcast.12), channel_id=1, source_target_pairs={{0,16},{8,24},{16,0},{24,8},{1,17},{9,25},{17,1},{25,9},{2,18},{10... | collective-permute-start | bytes 3145736 | tf_op jit(solution)/shard_map/ppermute | solution.py:72
  84.7 6.4 %copy-start.9 = (bf16[1,768,2048]{2,1,0:T(8,128)(2,1)S(1)}, bf16[1,768,2048]{2,1,0:T(8,128)(2,1)}, u32[]{:S(2)}) copy-start(bf16[1,768,2048]{2,1,0:T(8,128)(2,1)} %param.11) | copy-start | bytes 9437188
  84.7 6.4 %copy-start.10 = (bf16[1,768,2048]{2,1,0:T(8,128)(2,1)S(1)}, bf16[1,768,2048]{2,1,0:T(8,128)(2,1)}, u32[]{:S(2)}) copy-start(bf16[1,768,2048]{2,1,0:T(8,128)(2,1)} %param.10) | copy-start | bytes 9437188
  99.9 51.5 %all-to-all-start.2 = ((bf16[8,32,2048]{2,1,0:T(8,128)(2,1)}), bf16[8,32,2048]{2,1,0:T(8,128)(2,1)}, u32[]{:S(2)}, u32[]{:S(2)}) async-start(bf16[8,32,2048]{2,1,0:T(8,128)(2,1)} %bitcast.65), calls=%async_computation.2 | async-start | bytes 2097152 | tf_op jit(solution)/shard_map/all_to_all | solution.py:103
  104.4 39.2 %collective-permute-start.3 = (bf16[128,4096]{1,0:T(8,128)(2,1)}, bf16[128,4096]{1,0:T(8,128)(2,1)S(1)}, u32[]{:S(2)}, u32[]{:S(2)}) collective-permute-start(bf16[128,4096]{1,0:T(8,128)(2,1)} %collective-permute-done.1), channel_id=1, source_target_pairs={{0,8},{8,0},{16,24},{24,16},{1,9},{9,1},{17,25},{25,17},{2,10},{10... | collective-permute-start | bytes 3145736 | tf_op jit(solution)/shard_map/ppermute | solution.py:113
  106.6 18.2 %copy-start.6 = (bf16[192,2048]{1,0:T(8,128)(2,1)S(1)}, bf16[192,2048]{1,0:T(8,128)(2,1)}, u32[]{:S(2)}) copy-start(bf16[192,2048]{1,0:T(8,128)(2,1)} %get-tuple-element.44) | copy-start | bytes 2359300
  106.6 18.2 %copy-start.8 = (bf16[192,2048]{1,0:T(8,128)(2,1)S(1)}, bf16[192,2048]{1,0:T(8,128)(2,1)}, u32[]{:S(2)}) copy-start(bf16[192,2048]{1,0:T(8,128)(2,1)} %get-tuple-element.45) | copy-start | bytes 2359300
  126.4 18.2 %collective-permute-start.4 = (bf16[128,4096]{1,0:T(8,128)(2,1)}, bf16[128,4096]{1,0:T(8,128)(2,1)S(1)}, u32[]{:S(2)}, u32[]{:S(2)}) collective-permute-start(bf16[128,4096]{1,0:T(8,128)(2,1)} %collective-permute-done.2), channel_id=1, source_target_pairs={{0,8},{8,0},{16,24},{24,16},{1,9},{9,1},{17,25},{25,17},{2,10},{10... | collective-permute-start | bytes 3145736 | tf_op jit(solution)/shard_map/ppermute | solution.py:127
  130.8 2.0 %copy-start.2 = (f32[192,2048]{1,0:T(8,128)S(1)}, f32[192,2048]{1,0:T(8,128)}, u32[]{:S(2)}) copy-start(f32[192,2048]{1,0:T(8,128)} %fusion.22) | copy-start | bytes 4718596
  139.0 1.8 %copy-start.4 = (bf16[256,2048]{1,0:T(8,128)(2,1)S(1)}, bf16[256,2048]{1,0:T(8,128)(2,1)}, u32[]{:S(2)}) copy-start(bf16[256,2048]{1,0:T(8,128)(2,1)} %param.13) | copy-start | bytes 3145732
  147.3 1.9 %copy-start.1 = (f32[384,2048]{1,0:T(8,128)S(1)}, f32[384,2048]{1,0:T(8,128)}, u32[]{:S(2)}) copy-start(f32[384,2048]{1,0:T(8,128)} %fusion.27) | copy-start | bytes 9437188

commit v12 on v10

--- a/solution.py
+++ b/solution.py
@@ -76,8 +76,11 @@
     gate_mat = w_gate[0]
     up_mat = w_up[0]
     down_mat = w_down[0]
-    pre_gate = rows_times(rows_in, gate_mat)
-    pre_up = rows_times(rows_in, up_mat)
+    gate_up_mat = jnp.concatenate([gate_mat, up_mat], axis=0)
+    hidden_units = gate_mat.shape[0]
+    pre_both_own = rows_times(rows_in, gate_up_mat)
+    pre_gate = pre_both_own[:, :hidden_units]
+    pre_up = pre_both_own[:, hidden_units:]
     activated = jax.nn.silu(pre_gate)
     hidden = (activated * pre_up).astype(jnp.bfloat16)
     expert_out = matmul(hidden, down_mat).astype(jnp.bfloat16)
@@ -92,8 +95,8 @@
     hidden_grad = rows_times(grad_in, down_mat)
     gate_pre_grad = (hidden_grad * pre_up * silu_grad(pre_gate)).astype(jnp.bfloat16)
     up_pre_grad = (hidden_grad * activated).astype(jnp.bfloat16)
-    token_part = (
-        matmul(gate_pre_grad, gate_mat) + matmul(up_pre_grad, up_mat)
+    token_part = matmul(
+        jnp.concatenate([gate_pre_grad, up_pre_grad], axis=1), gate_up_mat
     ).astype(jnp.bfloat16)
     part_back = lax.all_to_all(
         token_part.reshape(experts, per_pair, feature_width),

time: 136 us -> 135 us (level)
    dot_general x11 -> x10, matrix products: 21 us -> 20.3 us  [rows_times(): lax.dot_general(left, right, (((1,), (1,)), ((), ())), preferred_element_...]
    dot_general x8 -> x7, matrix products: 13 us -> 12.6 us  [matmul(): return jnp.dot(left, right, preferred_element_type=jnp.float32)]
    unnamed x28 -> x22, local copies, waits for them, and re-layouts: 2.8 us -> 2.95 us
  transfers between devices with their start and end apart: 6 -> 6, of which waited for: 4 -> 3; matrix products, arithmetic and copies ran while one was open for 33% -> 36% of each run, Pallas kernels for 0% -> 0%
where the time goes in v12:
time: 135 us; the launch traced here: 134 us
  waiting for transfers between devices  55.7 us (41%)
  matrix products  48.1 us (36%)
  starting transfers between devices  17.5 us (13%)
  local copies, waits for them, and re-layouts  8.76 us (6%)
  other arithmetic  3.35 us (2%)
    all_to_all x1, waiting for transfers between devices, body(): lax.all_to_all(outgoing.reshape(experts, per_pair, 2 * feature_width), 'e...  44.7 us
    dot_general x10, matrix products, rows_times(): lax.dot_general(left, right, (((1,), (1,)), ((), ())), preferred_element_...  20.3 us
    dot_general x8, matrix products, inner_rows(): lax.dot_general(left, right, (((0,), (0,)), ((), ())), preferred_element_...  15.2 us
    dot_general x7, matrix products, matmul(): return jnp.dot(left, right, preferred_element_type=jnp.float32)  12.6 us
    all_to_all x1, waiting for transfers between devices, body(): lax.all_to_all(expert_out.reshape(experts, per_pair, feature_width), 'ep'...  10.4 us
    all_to_all x1, starting transfers between devices, body(): lax.all_to_all(outgoing.reshape(experts, per_pair, 2 * feature_width), 'e...  7.26 us
    all_to_all x1, starting transfers between devices, body(): lax.all_to_all(token_part.reshape(experts, per_pair, feature_width), 'ep'...  4.42 us
    all_to_all x1, starting transfers between devices, body(): lax.all_to_all(expert_out.reshape(experts, per_pair, feature_width), 'ep'...  4.24 us
  transfers between devices with their start and end apart: 6, of which 3 were waited for; matrix products, arithmetic and copies ran while one was open for 36% of the time, Pallas kernels for 0%

profile of v12, /device:TPU:0, one launch (start us, length us, event | category | flops | bytes accessed | tf_op | source)
XLA Modules:
  0.0 134.4 jit_solution(3506192710354658027)
XLA Ops:
  0.6 0.0 copy-start
  0.6 0.0 copy-start.3
  0.7 0.9 slice.70
  1.5 0.8 slice.71
  2.3 0.2 fusion.13
  2.5 0.1 select_reduce_fusion
  2.6 1.7 %convolution_convert_fusion.1 = bf16[256,2048]{1,0:T(8,128)(2,1)S(1)} fusion(bf16[256,2048]{1,0:T(8,128)(2,1)} %param.7, s32[256]{0:T(256)S(1)} %compare_select_fusion.1), kind=kOutput, calls=%fused_computation.15 | convolution fusion | flops 269025280 | bytes 2098176 | tf_op jit(solution)/shard_map/dot_general | solution.py:27
  4.3 0.0 copy-done.3
  4.3 0.4 fusion.6
  4.8 1.6 %pad_maximum_fusion.5 = bf16[256,4096]{1,0:T(8,128)(2,1)} fusion(bf16[256,2048]{1,0:T(8,128)(2,1)S(1)} %fusion.6, bf16[256,2048]{1,0:T(8,128)(2,1)S(1)} %convolution_convert_fusion.1), kind=kLoop, calls=%fused_computation.19 | loop fusion | flops 4194304 | bytes 4194304 | tf_op jit(solution)/shard_map/concatenate | solution.py:57
  6.4 7.3 %all-to-all-start = ((bf16[8,32,4096]{2,1,0:T(8,128)(2,1)}), bf16[8,32,4096]{2,1,0:T(8,128)(2,1)}, u32[]{:S(2)}, u32[]{:S(2)}) async-start(bf16[8,32,4096]{2,1,0:T(8,128)(2,1)} %bitcast.54), calls=%async_computation | async-start | bytes 4194304 | tf_op jit(solution)/shard_map/all_to_all | solution.py:58
  13.6 0.1 pad.1.clone
  13.7 0.1 pad.3.clone
  13.8 0.1 pad.2.clone
  13.9 0.7 compare_select_fusion
  14.6 2.7 %dynamic-slice_bitcast_fusion = (bf16[192,2048]{1,0:T(8,128)(2,1)}, bf16[192,2048]{1,0:T(8,128)(2,1)}) fusion(bf16[1,768,2048]{2,1,0:T(8,128)(2,1)} %param.11, s32[]{:T(128)S(6)} %select_n.28, bf16[1,768,2048]{2,1,0:T(8,128)(2,1)} %param.10), kind=kLoop, calls=%fused_computation.64 | loop fusion | bytes 3145732 | tf_op jit(solution)/shard_map/dynamic_slice | solution.py:137
  17.2 44.7 %all-to-all-done = bf16[8,32,4096]{2,1,0:T(8,128)(2,1)} async-done(((bf16[8,32,4096]{2,1,0:T(8,128)(2,1)}), bf16[8,32,4096]{2,1,0:T(8,128)(2,1)}, u32[]{:S(2)}, u32[]{:S(2)}) %all-to-all-start) | async-done | bytes 2097184 | tf_op jit(solution)/shard_map/all_to_all | solution.py:58
  61.9 1.5 %collective-permute-start.1 = (bf16[256,4096]{1,0:T(8,128)(2,1)}, bf16[256,4096]{1,0:T(8,128)(2,1)}, u32[]{:S(2)}, u32[]{:S(2)}) collective-permute-start(bf16[256,4096]{1,0:T(8,128)(2,1)} %bitcast.5), channel_id=1, source_target_pairs={{0,16},{8,24},{16,0},{24,8},{1,17},{9,25},{17,1},{25,9},{2,18},{10... | collective-permute-start | bytes 6291464 | tf_op jit(solution)/shard_map/ppermute | solution.py:70
  63.5 0.0 collective-permute-start
  63.5 5.0 %fusion.1 = f32[256,1536]{1,0:T(8,128)S(1)} fusion(bf16[768,2048]{1,0:T(8,128)(2,1)} %bitcast.57, bf16[768,2048]{1,0:T(8,128)(2,1)} %bitcast.59, bf16[256,4096]{1,0:T(8,128)(2,1)} %bitcast.5), kind=kOutput, calls=%fused_computation.2 | convolution fusion | flops 1623195648 | bytes 8912896 | tf_op jit(solution)/shard_map/dot_general | solution.py:15
  68.5 0.0 copy-done
  68.5 0.0 copy-start.9
  68.5 2.0 %fusion.8 = bf16[256,2048]{1,0:T(8,128)(2,1)} fusion(bf16[1,768,2048]{2,1,0:T(8,128)(2,1)S(1)} %copy-done, f32[256,1536]{1,0:T(8,128)S(1)} %fusion.1), kind=kOutput, calls=%fused_computation.16 | convolution fusion | flops 807010304 | bytes 5767168 | tf_op jit(solution)/shard_map/dot_general | solution.py:27
  70.5 0.0 copy-done.9
  70.5 4.2 %all-to-all-start.1 = ((bf16[8,32,2048]{2,1,0:T(8,128)(2,1)}), bf16[8,32,2048]{2,1,0:T(8,128)(2,1)}, u32[]{:S(2)}, u32[]{:S(2)}) async-start(bf16[8,32,2048]{2,1,0:T(8,128)(2,1)} %bitcast.56), calls=%async_computation.1 | async-start | bytes 2097152 | tf_op jit(solution)/shard_map/all_to_all | solution.py:87
  74.8 2.3 %fusion.41 = f32[256,384]{0,1:T(8,128)S(1)} fusion(bf16[256,4096]{1,0:T(8,128)(2,1)} %bitcast.5, bf16[192,2048]{1,0:T(8,128)(2,1)} %get-tuple-element.36, bf16[192,2048]{1,0:T(8,128)(2,1)} %get-tuple-element.37), kind=kOutput, calls=%fused_computation.52 | convolution fusion | flops 405798912 | bytes 3014656 | tf_op jit(solution)/shard_map/dot_general | solution.py:15
  77.1 1.7 %multiply_convert_fusion.15 = (bf16[256,192]{0,1:T(8,128)(2,1)S(1)}, bf16[256,192]{0,1:T(8,128)(2,1)S(1)}) fusion(f32[256,384]{0,1:T(8,128)S(1)} %fusion.41, bf16[1,768,2048]{2,1,0:T(8,128)(2,1)S(1)} %copy-done, s32[]{:T(128)S(6)} %select_n.28, bf16[256,4096]{1,0:T(8,128)(2,1)} %bitcast.5), kind=kOutput, calls=%fused_computation.109 | convolution fusion | flops 201965568 | bytes 2424836 | tf_op jit(solution)/shard_map/dot_general | solution.py:15
  78.8 2.8 %fusion.34 = f32[192,2048]{1,0:T(8,128)} fusion(bf16[256,4096]{1,0:T(8,128)(2,1)} %bitcast.5, f32[256,384]{0,1:T(8,128)S(1)} %fusion.41), kind=kOutput, calls=%fused_computation.45 | convolution fusion | flops 201621504 | bytes 3014656 | tf_op jit(solution)/shard_map/dot_general | solution.py:21
  81.6 3.6 %fusion.39 = f32[384,2048]{1,0:T(8,128)} fusion(bf16[256,4096]{1,0:T(8,128)(2,1)} %bitcast.5, bf16[256,192]{0,1:T(8,128)(2,1)S(1)} %get-tuple-element.31, bf16[256,192]{0,1:T(8,128)(2,1)S(1)} %get-tuple-element.30), kind=kOutput, calls=%fused_computation.50 | convolution fusion | flops 403046400 | bytes 4390912 | tf_op jit(solution)/shard_map/dot_general | solution.py:21
  85.1 0.0 copy-done.10
  85.2 2.6 %multiply_convert_fusion.1 = (bf16[256,768]{1,0:T(8,128)(2,1)S(1)}, bf16[256,768]{1,0:T(8,128)(2,1)S(1)}) fusion(f32[256,1536]{1,0:T(8,128)S(1)} %copy-done.10, bf16[1,768,2048]{2,1,0:T(8,128)(2,1)S(1)} %copy-done, bf16[256,4096]{1,0:T(8,128)(2,1)} %bitcast.5), kind=kOutput, calls=%fused_computation.67 | convolution fusion | flops 807862272 | bytes 6553600 | tf_op jit(solution)/shard_map/dot_general | solution.py:15
  87.8 0.0 copy-done.7
  87.8 0.5 copy-done.8
  88.3 2.8 %fusion.7 = bf16[256,2048]{1,0:T(8,128)(2,1)} fusion(bf16[768,2048]{1,0:T(8,128)(2,1)S(1)} %bitcast.58, bf16[768,2048]{1,0:T(8,128)(2,1)S(1)} %bitcast.60, bf16[256,768]{1,0:T(8,128)(2,1)S(1)} %get-tuple-element.23, bf16[256,768]{1,0:T(8,128)(2,1)S(1)} %get-tuple-element.22), kind=kOutput, calls=%fused_computation.13 | convolution fusion | flops 1625292800 | bytes 8126464 | tf_op jit(solution)/shard_map/dot_general | solution.py:27
  91.1 10.4 %all-to-all-done.1 = bf16[8,32,2048]{2,1,0:T(8,128)(2,1)} async-done(((bf16[8,32,2048]{2,1,0:T(8,128)(2,1)}), bf16[8,32,2048]{2,1,0:T(8,128)(2,1)}, u32[]{:S(2)}, u32[]{:S(2)}) %all-to-all-start.1) | async-done | bytes 1048608 | tf_op jit(solution)/shard_map/all_to_all | solution.py:87
  101.5 4.4 %all-to-all-start.2 = ((bf16[8,32,2048]{2,1,0:T(8,128)(2,1)}), bf16[8,32,2048]{2,1,0:T(8,128)(2,1)}, u32[]{:S(2)}, u32[]{:S(2)}) async-start(bf16[8,32,2048]{2,1,0:T(8,128)(2,1)} %bitcast.55), calls=%async_computation.2 | async-start | bytes 2097152 | tf_op jit(solution)/shard_map/all_to_all | solution.py:101
  105.9 0.0 collective-permute-done
  105.9 2.3 %fusion.29 = f32[256,384]{0,1:T(8,128)S(1)} fusion(bf16[256,4096]{1,0:T(8,128)(2,1)} %collective-permute-done, bf16[192,2048]{1,0:T(8,128)(2,1)} %get-tuple-element.36, bf16[192,2048]{1,0:T(8,128)(2,1)} %get-tuple-element.37), kind=kOutput, calls=%fused_computation.40 | convolution fusion | flops 405798912 | bytes 3014656 | tf_op jit(solution)/shard_map/dot_general | solution.py:15
  108.2 1.7 %multiply_convert_fusion.13 = (bf16[256,192]{0,1:T(8,128)(2,1)S(1)}, bf16[256,192]{0,1:T(8,128)(2,1)S(1)}) fusion(f32[256,384]{0,1:T(8,128)S(1)} %fusion.29, bf16[1,768,2048]{2,1,0:T(8,128)(2,1)S(1)} %copy-done, s32[]{:T(128)S(6)} %select_n.28, bf16[256,4096]{1,0:T(8,128)(2,1)} %collective-permute-done), kind=kOutput, calls=%fused_computation.105 | convolution fusion | flops 201965568 | bytes 2424836 | tf_op jit(solution)/shard_map/dot_general | solution.py:15
  110.0 0.0 copy-start.4
  110.0 2.8 %broadcast_multiply_fusion = (bf16[256,2048]{1,0:T(8,128)(2,1)}, f32[256,2048]{1,0:T(8,128)S(1)}) fusion(f32[256]{0:T(256)S(1)} %bitcast.64, bf16[256,2048]{1,0:T(8,128)(2,1)} %bitcast.10, s32[256]{0:T(256)S(1)} %bitcast.61), kind=kOutput, calls=%fused_computation.24 | convolution fusion | flops 269549568 | bytes 4196352 | tf_op jit(solution)/shard_map/dot_general | solution.py:27
  112.8 0.0 collective-permute-done.1
  112.8 0.1 collective-permute-start.2
  112.8 0.0 copy-done.4
  112.9 0.3 multiply_reduce_fusion
  113.1 0.8 copy-done.5
  113.9 0.2 copy-done.6
  114.1 1.8 %fusion.22 = f32[256,384]{0,1:T(8,128)S(1)} fusion(bf16[256,4096]{1,0:T(8,128)(2,1)} %collective-permute-done.1, bf16[192,2048]{1,0:T(8,128)(2,1)S(1)} %copy-done.5, bf16[192,2048]{1,0:T(8,128)(2,1)S(1)} %copy-done.6), kind=kOutput, calls=%fused_computation.33 | convolution fusion | flops 405798912 | bytes 3014656 | tf_op jit(solution)/shard_map/dot_general | solution.py:15
  116.0 1.7 %multiply_convert_fusion.11 = (bf16[256,192]{0,1:T(8,128)(2,1)S(1)}, bf16[256,192]{0,1:T(8,128)(2,1)S(1)}) fusion(f32[256,384]{0,1:T(8,128)S(1)} %fusion.22, bf16[1,768,2048]{2,1,0:T(8,128)(2,1)S(1)} %copy-done, s32[]{:T(128)S(6)} %select_n.28, bf16[256,4096]{1,0:T(8,128)(2,1)} %collective-permute-done.1), kind=kOutput, calls=%fused_computation.101 | convolution fusion | flops 201965568 | bytes 2424836 | tf_op jit(solution)/shard_map/dot_general | solution.py:15
  117.7 1.8 %fusion.27 = f32[384,2048]{1,0:T(8,128)S(1)} fusion(bf16[256,4096]{1,0:T(8,128)(2,1)} %collective-permute-done, bf16[256,192]{0,1:T(8,128)(2,1)S(1)} %get-tuple-element.29, bf16[256,192]{0,1:T(8,128)(2,1)S(1)} %get-tuple-element.28), kind=kOutput, calls=%fused_computation.38 | convolution fusion | flops 403046400 | bytes 4390912 | tf_op jit(solution)/shard_map/dot_general | solution.py:21
  119.5 0.0 copy-start.2
  119.5 1.9 %fusion.20 = f32[384,2048]{1,0:T(8,128)S(1)} fusion(bf16[256,4096]{1,0:T(8,128)(2,1)} %collective-permute-done.1, bf16[256,192]{0,1:T(8,128)(2,1)S(1)} %get-tuple-element.33, bf16[256,192]{0,1:T(8,128)(2,1)S(1)} %get-tuple-element.32), kind=kOutput, calls=%fused_computation.31 | convolution fusion | flops 403046400 | bytes 4390912 | tf_op jit(solution)/shard_map/dot_general | solution.py:21
  121.5 1.6 %convolution_add_fusion.2 = f32[192,2048]{1,0:T(8,128)S(1)} fusion(f32[192,2048]{1,0:T(8,128)S(1)} %copy-done.2, bf16[256,4096]{1,0:T(8,128)(2,1)} %collective-permute-done, f32[256,384]{0,1:T(8,128)S(1)} %fusion.29), kind=kOutput, calls=%fused_computation.11 | convolution fusion | flops 202014720 | bytes 4587520 | tf_op jit(solution)/shard_map/dot_general | solution.py:21
  123.1 1.6 %convolution_add_fusion.1 = f32[192,2048]{1,0:T(8,128)S(1)} fusion(f32[192,2048]{1,0:T(8,128)S(1)} %convolution_add_fusion.2, bf16[256,4096]{1,0:T(8,128)(2,1)} %collective-permute-done.1, f32[256,384]{0,1:T(8,128)S(1)} %fusion.22), kind=kOutput, calls=%fused_computation.10 | convolution fusion | flops 202014720 | bytes 4587520 | tf_op jit(solution)/shard_map/dot_general | solution.py:21
  124.7 0.7 maximum_maximum_fusion
  125.4 0.0 collective-permute-done.2
  125.4 0.6 fusion.15
  126.0 1.3 fusion.12
  127.3 0.5 multiply_convert_fusion.9
  127.8 1.4 %copy-done.1 = f32[384,2048]{1,0:T(8,128)S(1)} copy-done((f32[384,2048]{1,0:T(8,128)S(1)}, f32[384,2048]{1,0:T(8,128)}, u32[]{:S(2)}) %copy-start.1) | copy-done | bytes 3145752
  129.2 0.6 add_convert_fusion
  129.8 1.2 slice_bitcast_fusion
  131.1 0.6 all-to-all-done.2
  131.7 2.7 %convolution_convert_fusion = bf16[256,2048]{1,0:T(8,128)(2,1)} fusion(bf16[256,2048]{1,0:T(8,128)(2,1)} %bitcast.12, s32[256]{0:T(256)S(1)} %bitcast.62), kind=kOutput, calls=%fused_computation.14 | convolution fusion | flops 269025280 | bytes 2098176 | tf_op jit(solution)/shard_map/dot_general | solution.py:27
  (11 shorter events, 0.0 us)
Async XLA Ops:
  0.6 67.8 %copy-start = (bf16[1,768,2048]{2,1,0:T(8,128)(2,1)S(1)}, bf16[1,768,2048]{2,1,0:T(8,128)(2,1)}, u32[]{:S(2)}) copy-start(bf16[1,768,2048]{2,1,0:T(8,128)(2,1)} %param.12) | copy-start | bytes 9437188
  0.6 3.7 %copy-start.3 = (bf16[256,2048]{1,0:T(8,128)(2,1)S(1)}, bf16[256,2048]{1,0:T(8,128)(2,1)}, u32[]{:S(2)}) copy-start(bf16[256,2048]{1,0:T(8,128)(2,1)} %param.13) | copy-start | bytes 3145732
  6.4 55.6 %all-to-all-start = ((bf16[8,32,4096]{2,1,0:T(8,128)(2,1)}), bf16[8,32,4096]{2,1,0:T(8,128)(2,1)}, u32[]{:S(2)}, u32[]{:S(2)}) async-start(bf16[8,32,4096]{2,1,0:T(8,128)(2,1)} %bitcast.54), calls=%async_computation | async-start | bytes 4194304 | tf_op jit(solution)/shard_map/all_to_all | solution.py:58
  61.9 50.8 %collective-permute-start.1 = (bf16[256,4096]{1,0:T(8,128)(2,1)}, bf16[256,4096]{1,0:T(8,128)(2,1)}, u32[]{:S(2)}, u32[]{:S(2)}) collective-permute-start(bf16[256,4096]{1,0:T(8,128)(2,1)} %bitcast.5), channel_id=1, source_target_pairs={{0,16},{8,24},{16,0},{24,8},{1,17},{9,25},{17,1},{25,9},{2,18},{10... | collective-permute-start | bytes 6291464 | tf_op jit(solution)/shard_map/ppermute | solution.py:70
  63.5 42.5 %collective-permute-start = (bf16[256,4096]{1,0:T(8,128)(2,1)}, bf16[256,4096]{1,0:T(8,128)(2,1)}, u32[]{:S(2)}, u32[]{:S(2)}) collective-permute-start(bf16[256,4096]{1,0:T(8,128)(2,1)} %bitcast.5), channel_id=1, source_target_pairs={{0,8},{8,0},{16,24},{24,16},{1,9},{9,1},{17,25},{25,17},{2,10},{10... | collective-permute-start | bytes 6291464 | tf_op jit(solution)/shard_map/ppermute | solution.py:69
  68.5 2.0 %copy-start.9 = (f32[256,1536]{1,0:T(8,128)}, f32[256,1536]{1,0:T(8,128)S(1)}, u32[]{:S(2)}) copy-start(f32[256,1536]{1,0:T(8,128)S(1)} %fusion.1) | copy-start | bytes 4718596
  70.5 31.0 %all-to-all-start.1 = ((bf16[8,32,2048]{2,1,0:T(8,128)(2,1)}), bf16[8,32,2048]{2,1,0:T(8,128)(2,1)}, u32[]{:S(2)}, u32[]{:S(2)}) async-start(bf16[8,32,2048]{2,1,0:T(8,128)(2,1)} %bitcast.56), calls=%async_computation.1 | async-start | bytes 2097152 | tf_op jit(solution)/shard_map/all_to_all | solution.py:87
  81.6 3.6 %copy-start.10 = (f32[256,1536]{1,0:T(8,128)S(1)}, f32[256,1536]{1,0:T(8,128)}, u32[]{:S(2)}) copy-start(f32[256,1536]{1,0:T(8,128)} %copy-done.9) | copy-start | bytes 4718596
  85.1 2.6 %copy-start.7 = (bf16[1,768,2048]{2,1,0:T(8,128)(2,1)S(1)}, bf16[1,768,2048]{2,1,0:T(8,128)(2,1)}, u32[]{:S(2)}) copy-start(bf16[1,768,2048]{2,1,0:T(8,128)(2,1)} %param.11) | copy-start | bytes 9437188
  85.1 3.2 %copy-start.8 = (bf16[1,768,2048]{2,1,0:T(8,128)(2,1)S(1)}, bf16[1,768,2048]{2,1,0:T(8,128)(2,1)}, u32[]{:S(2)}) copy-start(bf16[1,768,2048]{2,1,0:T(8,128)(2,1)} %param.10) | copy-start | bytes 9437188
  101.5 30.2 %all-to-all-start.2 = ((bf16[8,32,2048]{2,1,0:T(8,128)(2,1)}), bf16[8,32,2048]{2,1,0:T(8,128)(2,1)}, u32[]{:S(2)}, u32[]{:S(2)}) async-start(bf16[8,32,2048]{2,1,0:T(8,128)(2,1)} %bitcast.55), calls=%async_computation.2 | async-start | bytes 2097152 | tf_op jit(solution)/shard_map/all_to_all | solution.py:101
  110.0 2.9 %copy-start.4 = (bf16[256,2048]{1,0:T(8,128)(2,1)S(1)}, bf16[256,2048]{1,0:T(8,128)(2,1)}, u32[]{:S(2)}) copy-start(bf16[256,2048]{1,0:T(8,128)(2,1)} %param.13) | copy-start | bytes 3145732
  112.8 1.1 copy-start.5
  112.8 1.4 %copy-start.6 = (bf16[192,2048]{1,0:T(8,128)(2,1)S(1)}, bf16[192,2048]{1,0:T(8,128)(2,1)}, u32[]{:S(2)}) copy-start(bf16[192,2048]{1,0:T(8,128)(2,1)} %get-tuple-element.37) | copy-start | bytes 2359300
  112.8 12.6 %collective-permute-start.2 = (bf16[256,4096]{1,0:T(8,128)(2,1)}, bf16[256,4096]{1,0:T(8,128)(2,1)S(1)}, u32[]{:S(2)}, u32[]{:S(2)}) collective-permute-start(bf16[256,4096]{1,0:T(8,128)(2,1)} %collective-permute-done.1), channel_id=1, source_target_pairs={{0,8},{8,0},{16,24},{24,16},{1,9},{9,1},{17,25},{25,17},{2,10},{10... | collective-permute-start | bytes 6291464 | tf_op jit(solution)/shard_map/ppermute | solution.py:124
  119.5 1.9 %copy-start.2 = (f32[192,2048]{1,0:T(8,128)S(1)}, f32[192,2048]{1,0:T(8,128)}, u32[]{:S(2)}) copy-start(f32[192,2048]{1,0:T(8,128)} %fusion.34) | copy-start | bytes 4718596
  127.3 1.9 %copy-start.1 = (f32[384,2048]{1,0:T(8,128)S(1)}, f32[384,2048]{1,0:T(8,128)}, u32[]{:S(2)}) copy-start(f32[384,2048]{1,0:T(8,128)} %fusion.39) | copy-start | bytes 9437188

commit v13 on v12

--- a/solution.py
+++ b/solution.py
@@ -50,11 +50,10 @@
     hit = slot_ids[:, None] == slot_index[None, :]
     slot_gate = jnp.sum(jnp.where(hit, flat_gates[None, :], 0.0), axis=1)
     pick = jnp.any(hit.reshape(total_slots, tok_count, live_cols), axis=2).astype(jnp.bfloat16)
-    send_rows = matmul(pick, tokens).astype(jnp.bfloat16)
-    grad_rows = matmul(pick, out_grad)
-    scaled_grad = (slot_gate[:, None] * grad_rows).astype(jnp.bfloat16)
-
-    outgoing = jnp.concatenate([send_rows, scaled_grad], axis=1)
+    picked = matmul(pick, jnp.concatenate([tokens, out_grad], axis=1))
+    column = jnp.arange(2 * feature_width, dtype=jnp.int32)[None, :]
+    row_scale = jnp.where(column < feature_width, 1.0, slot_gate[:, None])
+    outgoing = (row_scale * picked).astype(jnp.bfloat16)
     received = lax.all_to_all(
         outgoing.reshape(experts, per_pair, 2 * feature_width),
         "ep",

time: 135 us -> 135 us (level)
  other arithmetic: 3.35 us -> 1.79 us
  matrix products: 48.1 us -> 49.6 us
    concatenate x1 -> x0, other arithmetic: 1.56 us -> none  [body(): outgoing = jnp.concatenate([send_rows, scaled_grad], axis=1)]
    dot_general x7 -> x6, matrix products: 12.6 us -> 14.1 us  [matmul(): return jnp.dot(left, right, preferred_element_type=jnp.float32)]
    unnamed x22 -> x20, local copies, waits for them, and re-layouts: 2.95 us -> 2.94 us
where the time goes in v13:
time: 135 us; the launch traced here: 134 us
  waiting for transfers between devices  55.7 us (41%)
  matrix products  49.6 us (37%)
  starting transfers between devices  17.5 us (13%)
  local copies, waits for them, and re-layouts  8.74 us (6%)
  other arithmetic  1.79 us (1%)
    all_to_all x1, waiting for transfers between devices, body(): lax.all_to_all(outgoing.reshape(experts, per_pair, 2 * feature_width), 'e...  44.7 us
    dot_general x10, matrix products, rows_times(): lax.dot_general(left, right, (((1,), (1,)), ((), ())), preferred_element_...  20.3 us
    dot_general x8, matrix products, inner_rows(): lax.dot_general(left, right, (((0,), (0,)), ((), ())), preferred_element_...  15.2 us
    dot_general x6, matrix products, matmul(): return jnp.dot(left, right, preferred_element_type=jnp.float32)  14.1 us
    all_to_all x1, waiting for transfers between devices, body(): lax.all_to_all(expert_out.reshape(experts, per_pair, feature_width), 'ep'...  10.3 us
    all_to_all x1, starting transfers between devices, body(): lax.all_to_all(outgoing.reshape(experts, per_pair, 2 * feature_width), 'e...  7.25 us
    all_to_all x1, starting transfers between devices, body(): lax.all_to_all(token_part.reshape(experts, per_pair, feature_width), 'ep'...  4.43 us
    all_to_all x1, starting transfers between devices, body(): lax.all_to_all(expert_out.reshape(experts, per_pair, feature_width), 'ep'...  4.27 us
  transfers between devices with their start and end apart: 6, of which 3 were waited for; matrix products, arithmetic and copies ran while one was open for 36% of the time, Pallas kernels for 0%

profile of v13, /device:TPU:0, one launch (start us, length us, event | category | flops | bytes accessed | tf_op | source)
XLA Modules:
  0.0 134.3 jit_solution(16048958107241450592)
XLA Ops:
  0.6 0.0 copy-start
  0.7 0.9 slice.70
  1.5 0.8 slice.71
  2.3 0.2 fusion.16
  2.5 0.1 select_reduce_fusion
  2.6 3.6 %fusion = bf16[256,4096]{1,0:T(8,128)(2,1)} fusion(bf16[256,2048]{1,0:T(8,128)(2,1)} %param.13, bf16[256,2048]{1,0:T(8,128)(2,1)} %param.7, f32[256]{0:T(256)S(1)} %select_reduce_fusion, pred[4096]{0:T(1024)(128)(4,1)S(1)} %iota_compare_fusion.7, s32[256]{0:T(256)S(1)} %compare_select_fusion.1), kind=kOutput, calls=%fused_computation.2 | convolution fusion | flops 544276480 | bytes 4200448 | tf_op jit(solution)/shard_map/dot_general | solution.py:27
  6.2 7.3 %all-to-all-start = ((bf16[8,32,4096]{2,1,0:T(8,128)(2,1)}), bf16[8,32,4096]{2,1,0:T(8,128)(2,1)}, u32[]{:S(2)}, u32[]{:S(2)}) async-start(bf16[8,32,4096]{2,1,0:T(8,128)(2,1)} %bitcast.52), calls=%async_computation | async-start | bytes 4194304 | tf_op jit(solution)/shard_map/all_to_all | solution.py:57
  13.5 0.1 pad.1.clone
  13.6 0.1 pad.3.clone
  13.7 0.1 pad.2.clone
  13.7 0.7 compare_select_fusion
  14.4 2.7 %dynamic-slice_bitcast_fusion = (bf16[192,2048]{1,0:T(8,128)(2,1)}, bf16[192,2048]{1,0:T(8,128)(2,1)}) fusion(bf16[1,768,2048]{2,1,0:T(8,128)(2,1)} %param.11, s32[]{:T(128)S(6)} %select_n.33, bf16[1,768,2048]{2,1,0:T(8,128)(2,1)} %param.10), kind=kLoop, calls=%fused_computation.65 | loop fusion | bytes 3145732 | tf_op jit(solution)/shard_map/dynamic_slice | solution.py:136
  17.1 44.7 %all-to-all-done = bf16[8,32,4096]{2,1,0:T(8,128)(2,1)} async-done(((bf16[8,32,4096]{2,1,0:T(8,128)(2,1)}), bf16[8,32,4096]{2,1,0:T(8,128)(2,1)}, u32[]{:S(2)}, u32[]{:S(2)}) %all-to-all-start) | async-done | bytes 2097184 | tf_op jit(solution)/shard_map/all_to_all | solution.py:57
  61.8 1.5 %collective-permute-start.1 = (bf16[256,4096]{1,0:T(8,128)(2,1)}, bf16[256,4096]{1,0:T(8,128)(2,1)}, u32[]{:S(2)}, u32[]{:S(2)}) collective-permute-start(bf16[256,4096]{1,0:T(8,128)(2,1)} %bitcast.5), channel_id=1, source_target_pairs={{0,16},{8,24},{16,0},{24,8},{1,17},{9,25},{17,1},{25,9},{2,18},{10... | collective-permute-start | bytes 6291464 | tf_op jit(solution)/shard_map/ppermute | solution.py:69
  63.3 0.0 collective-permute-start
  63.4 5.0 %fusion.2 = f32[256,1536]{1,0:T(8,128)S(1)} fusion(bf16[768,2048]{1,0:T(8,128)(2,1)} %bitcast.55, bf16[768,2048]{1,0:T(8,128)(2,1)} %bitcast.57, bf16[256,4096]{1,0:T(8,128)(2,1)} %bitcast.5), kind=kOutput, calls=%fused_computation.4 | convolution fusion | flops 1623195648 | bytes 8912896 | tf_op jit(solution)/shard_map/dot_general | solution.py:15
  68.3 0.0 copy-done
  68.4 0.0 copy-start.8
  68.4 2.0 %fusion.8 = bf16[256,2048]{1,0:T(8,128)(2,1)} fusion(bf16[1,768,2048]{2,1,0:T(8,128)(2,1)S(1)} %copy-done, f32[256,1536]{1,0:T(8,128)S(1)} %fusion.2), kind=kOutput, calls=%fused_computation.15 | convolution fusion | flops 807010304 | bytes 5767168 | tf_op jit(solution)/shard_map/dot_general | solution.py:27
  70.4 0.0 copy-done.8
  70.4 4.3 %all-to-all-start.1 = ((bf16[8,32,2048]{2,1,0:T(8,128)(2,1)}), bf16[8,32,2048]{2,1,0:T(8,128)(2,1)}, u32[]{:S(2)}, u32[]{:S(2)}) async-start(bf16[8,32,2048]{2,1,0:T(8,128)(2,1)} %bitcast.54), calls=%async_computation.1 | async-start | bytes 2097152 | tf_op jit(solution)/shard_map/all_to_all | solution.py:86
  74.7 2.3 %fusion.44 = f32[256,384]{0,1:T(8,128)S(1)} fusion(bf16[256,4096]{1,0:T(8,128)(2,1)} %bitcast.5, bf16[192,2048]{1,0:T(8,128)(2,1)} %get-tuple-element.36, bf16[192,2048]{1,0:T(8,128)(2,1)} %get-tuple-element.37), kind=kOutput, calls=%fused_computation.53 | convolution fusion | flops 405798912 | bytes 3014656 | tf_op jit(solution)/shard_map/dot_general | solution.py:15
  77.0 1.7 %multiply_convert_fusion.15 = (bf16[256,192]{0,1:T(8,128)(2,1)S(1)}, bf16[256,192]{0,1:T(8,128)(2,1)S(1)}) fusion(f32[256,384]{0,1:T(8,128)S(1)} %fusion.44, bf16[1,768,2048]{2,1,0:T(8,128)(2,1)S(1)} %copy-done, s32[]{:T(128)S(6)} %select_n.33, bf16[256,4096]{1,0:T(8,128)(2,1)} %bitcast.5), kind=kOutput, calls=%fused_computation.110 | convolution fusion | flops 201965568 | bytes 2424836 | tf_op jit(solution)/shard_map/dot_general | solution.py:15
  78.7 2.8 %fusion.37 = f32[192,2048]{1,0:T(8,128)} fusion(bf16[256,4096]{1,0:T(8,128)(2,1)} %bitcast.5, f32[256,384]{0,1:T(8,128)S(1)} %fusion.44), kind=kOutput, calls=%fused_computation.46 | convolution fusion | flops 201621504 | bytes 3014656 | tf_op jit(solution)/shard_map/dot_general | solution.py:21
  81.5 0.0 copy-start.9
  81.5 3.6 %fusion.42 = f32[384,2048]{1,0:T(8,128)} fusion(bf16[256,4096]{1,0:T(8,128)(2,1)} %bitcast.5, bf16[256,192]{0,1:T(8,128)(2,1)S(1)} %get-tuple-element.31, bf16[256,192]{0,1:T(8,128)(2,1)S(1)} %get-tuple-element.30), kind=kOutput, calls=%fused_computation.51 | convolution fusion | flops 403046400 | bytes 4390912 | tf_op jit(solution)/shard_map/dot_general | solution.py:21
  85.1 0.0 copy-done.9
  85.1 0.0 copy-start.6
  85.1 0.0 copy-start.7
  85.1 2.6 %multiply_convert_fusion.1 = (bf16[256,768]{1,0:T(8,128)(2,1)S(1)}, bf16[256,768]{1,0:T(8,128)(2,1)S(1)}) fusion(f32[256,1536]{1,0:T(8,128)S(1)} %copy-done.9, bf16[1,768,2048]{2,1,0:T(8,128)(2,1)S(1)} %copy-done, bf16[256,4096]{1,0:T(8,128)(2,1)} %bitcast.5), kind=kOutput, calls=%fused_computation.68 | convolution fusion | flops 807862272 | bytes 6553600 | tf_op jit(solution)/shard_map/dot_general | solution.py:15
  87.7 0.0 copy-done.6
  87.7 0.5 copy-done.7
  88.2 2.8 %fusion.7 = bf16[256,2048]{1,0:T(8,128)(2,1)} fusion(bf16[768,2048]{1,0:T(8,128)(2,1)S(1)} %bitcast.56, bf16[768,2048]{1,0:T(8,128)(2,1)S(1)} %bitcast.58, bf16[256,768]{1,0:T(8,128)(2,1)S(1)} %get-tuple-element.23, bf16[256,768]{1,0:T(8,128)(2,1)S(1)} %get-tuple-element.22), kind=kOutput, calls=%fused_computation.13 | convolution fusion | flops 1625292800 | bytes 8126464 | tf_op jit(solution)/shard_map/dot_general | solution.py:27
  91.0 10.3 %all-to-all-done.1 = bf16[8,32,2048]{2,1,0:T(8,128)(2,1)} async-done(((bf16[8,32,2048]{2,1,0:T(8,128)(2,1)}), bf16[8,32,2048]{2,1,0:T(8,128)(2,1)}, u32[]{:S(2)}, u32[]{:S(2)}) %all-to-all-start.1) | async-done | bytes 1048608 | tf_op jit(solution)/shard_map/all_to_all | solution.py:86
  101.4 4.4 %all-to-all-start.2 = ((bf16[8,32,2048]{2,1,0:T(8,128)(2,1)}), bf16[8,32,2048]{2,1,0:T(8,128)(2,1)}, u32[]{:S(2)}, u32[]{:S(2)}) async-start(bf16[8,32,2048]{2,1,0:T(8,128)(2,1)} %bitcast.53), calls=%async_computation.2 | async-start | bytes 2097152 | tf_op jit(solution)/shard_map/all_to_all | solution.py:100
  105.8 0.0 collective-permute-done
  105.8 2.3 %fusion.32 = f32[256,384]{0,1:T(8,128)S(1)} fusion(bf16[256,4096]{1,0:T(8,128)(2,1)} %collective-permute-done, bf16[192,2048]{1,0:T(8,128)(2,1)} %get-tuple-element.36, bf16[192,2048]{1,0:T(8,128)(2,1)} %get-tuple-element.37), kind=kOutput, calls=%fused_computation.41 | convolution fusion | flops 405798912 | bytes 3014656 | tf_op jit(solution)/shard_map/dot_general | solution.py:15
  108.1 1.7 %multiply_convert_fusion.13 = (bf16[256,192]{0,1:T(8,128)(2,1)S(1)}, bf16[256,192]{0,1:T(8,128)(2,1)S(1)}) fusion(f32[256,384]{0,1:T(8,128)S(1)} %fusion.32, bf16[1,768,2048]{2,1,0:T(8,128)(2,1)S(1)} %copy-done, s32[]{:T(128)S(6)} %select_n.33, bf16[256,4096]{1,0:T(8,128)(2,1)} %collective-permute-done), kind=kOutput, calls=%fused_computation.106 | convolution fusion | flops 201965568 | bytes 2424836 | tf_op jit(solution)/shard_map/dot_general | solution.py:15
  109.9 0.0 copy-start.3
  109.9 2.8 %broadcast_multiply_fusion = (bf16[256,2048]{1,0:T(8,128)(2,1)}, f32[256,2048]{1,0:T(8,128)S(1)}) fusion(f32[256]{0:T(256)S(1)} %bitcast.62, bf16[256,2048]{1,0:T(8,128)(2,1)} %bitcast.10, s32[256]{0:T(256)S(1)} %bitcast.59), kind=kOutput, calls=%fused_computation.25 | convolution fusion | flops 269549568 | bytes 4196352 | tf_op jit(solution)/shard_map/dot_general | solution.py:27
  112.7 0.0 collective-permute-done.1
  112.7 0.1 collective-permute-start.2
  112.7 0.0 copy-done.3
  112.8 0.3 multiply_reduce_fusion
  113.0 0.8 copy-done.4
  113.8 0.2 copy-done.5
  114.0 1.8 %fusion.25 = f32[256,384]{0,1:T(8,128)S(1)} fusion(bf16[256,4096]{1,0:T(8,128)(2,1)} %collective-permute-done.1, bf16[192,2048]{1,0:T(8,128)(2,1)S(1)} %copy-done.4, bf16[192,2048]{1,0:T(8,128)(2,1)S(1)} %copy-done.5), kind=kOutput, calls=%fused_computation.34 | convolution fusion | flops 405798912 | bytes 3014656 | tf_op jit(solution)/shard_map/dot_general | solution.py:15
  115.9 1.7 %multiply_convert_fusion.11 = (bf16[256,192]{0,1:T(8,128)(2,1)S(1)}, bf16[256,192]{0,1:T(8,128)(2,1)S(1)}) fusion(f32[256,384]{0,1:T(8,128)S(1)} %fusion.25, bf16[1,768,2048]{2,1,0:T(8,128)(2,1)S(1)} %copy-done, s32[]{:T(128)S(6)} %select_n.33, bf16[256,4096]{1,0:T(8,128)(2,1)} %collective-permute-done.1), kind=kOutput, calls=%fused_computation.102 | convolution fusion | flops 201965568 | bytes 2424836 | tf_op jit(solution)/shard_map/dot_general | solution.py:15
  117.6 1.8 %fusion.30 = f32[384,2048]{1,0:T(8,128)S(1)} fusion(bf16[256,4096]{1,0:T(8,128)(2,1)} %collective-permute-done, bf16[256,192]{0,1:T(8,128)(2,1)S(1)} %get-tuple-element.29, bf16[256,192]{0,1:T(8,128)(2,1)S(1)} %get-tuple-element.28), kind=kOutput, calls=%fused_computation.39 | convolution fusion | flops 403046400 | bytes 4390912 | tf_op jit(solution)/shard_map/dot_general | solution.py:21
  119.4 0.0 copy-start.2
  119.4 1.9 %fusion.23 = f32[384,2048]{1,0:T(8,128)S(1)} fusion(bf16[256,4096]{1,0:T(8,128)(2,1)} %collective-permute-done.1, bf16[256,192]{0,1:T(8,128)(2,1)S(1)} %get-tuple-element.33, bf16[256,192]{0,1:T(8,128)(2,1)S(1)} %get-tuple-element.32), kind=kOutput, calls=%fused_computation.32 | convolution fusion | flops 403046400 | bytes 4390912 | tf_op jit(solution)/shard_map/dot_general | solution.py:21
  121.4 0.0 copy-done.2
  121.4 1.6 %convolution_add_fusion.2 = f32[192,2048]{1,0:T(8,128)S(1)} fusion(f32[192,2048]{1,0:T(8,128)S(1)} %copy-done.2, bf16[256,4096]{1,0:T(8,128)(2,1)} %collective-permute-done, f32[256,384]{0,1:T(8,128)S(1)} %fusion.32), kind=kOutput, calls=%fused_computation.12 | convolution fusion | flops 202014720 | bytes 4587520 | tf_op jit(solution)/shard_map/dot_general | solution.py:21
  123.0 1.6 %convolution_add_fusion.1 = f32[192,2048]{1,0:T(8,128)S(1)} fusion(f32[192,2048]{1,0:T(8,128)S(1)} %convolution_add_fusion.2, bf16[256,4096]{1,0:T(8,128)(2,1)} %collective-permute-done.1, f32[256,384]{0,1:T(8,128)S(1)} %fusion.25), kind=kOutput, calls=%fused_computation.11 | convolution fusion | flops 202014720 | bytes 4587520 | tf_op jit(solution)/shard_map/dot_general | solution.py:21
  124.6 0.7 maximum_maximum_fusion
  125.3 0.0 collective-permute-done.2
  125.3 0.6 fusion.18
  125.9 1.3 fusion.12
  127.2 0.5 multiply_convert_fusion.9
  127.7 1.4 %copy-done.1 = f32[384,2048]{1,0:T(8,128)S(1)} copy-done((f32[384,2048]{1,0:T(8,128)S(1)}, f32[384,2048]{1,0:T(8,128)}, u32[]{:S(2)}) %copy-start.1) | copy-done | bytes 3145752
  129.1 0.6 add_convert_fusion
  129.7 1.2 slice_bitcast_fusion
  131.0 0.6 all-to-all-done.2
  131.6 2.7 %convolution_convert_fusion = bf16[256,2048]{1,0:T(8,128)(2,1)} fusion(bf16[256,2048]{1,0:T(8,128)(2,1)} %bitcast.12, s32[256]{0:T(256)S(1)} %bitcast.60), kind=kOutput, calls=%fused_computation.14 | convolution fusion | flops 269025280 | bytes 2098176 | tf_op jit(solution)/shard_map/dot_general | solution.py:27
  (8 shorter events, 0.0 us)
Async XLA Ops:
  0.6 67.7 %copy-start = (bf16[1,768,2048]{2,1,0:T(8,128)(2,1)S(1)}, bf16[1,768,2048]{2,1,0:T(8,128)(2,1)}, u32[]{:S(2)}) copy-start(bf16[1,768,2048]{2,1,0:T(8,128)(2,1)} %param.12) | copy-start | bytes 9437188
  6.2 55.6 %all-to-all-start = ((bf16[8,32,4096]{2,1,0:T(8,128)(2,1)}), bf16[8,32,4096]{2,1,0:T(8,128)(2,1)}, u32[]{:S(2)}, u32[]{:S(2)}) async-start(bf16[8,32,4096]{2,1,0:T(8,128)(2,1)} %bitcast.52), calls=%async_computation | async-start | bytes 4194304 | tf_op jit(solution)/shard_map/all_to_all | solution.py:57
  61.8 50.8 %collective-permute-start.1 = (bf16[256,4096]{1,0:T(8,128)(2,1)}, bf16[256,4096]{1,0:T(8,128)(2,1)}, u32[]{:S(2)}, u32[]{:S(2)}) collective-permute-start(bf16[256,4096]{1,0:T(8,128)(2,1)} %bitcast.5), channel_id=1, source_target_pairs={{0,16},{8,24},{16,0},{24,8},{1,17},{9,25},{17,1},{25,9},{2,18},{10... | collective-permute-start | bytes 6291464 | tf_op jit(solution)/shard_map/ppermute | solution.py:69
  63.3 42.5 %collective-permute-start = (bf16[256,4096]{1,0:T(8,128)(2,1)}, bf16[256,4096]{1,0:T(8,128)(2,1)}, u32[]{:S(2)}, u32[]{:S(2)}) collective-permute-start(bf16[256,4096]{1,0:T(8,128)(2,1)} %bitcast.5), channel_id=1, source_target_pairs={{0,8},{8,0},{16,24},{24,16},{1,9},{9,1},{17,25},{25,17},{2,10},{10... | collective-permute-start | bytes 6291464 | tf_op jit(solution)/shard_map/ppermute | solution.py:68
  68.4 2.0 %copy-start.8 = (f32[256,1536]{1,0:T(8,128)}, f32[256,1536]{1,0:T(8,128)S(1)}, u32[]{:S(2)}) copy-start(f32[256,1536]{1,0:T(8,128)S(1)} %fusion.2) | copy-start | bytes 4718596
  70.4 31.0 %all-to-all-start.1 = ((bf16[8,32,2048]{2,1,0:T(8,128)(2,1)}), bf16[8,32,2048]{2,1,0:T(8,128)(2,1)}, u32[]{:S(2)}, u32[]{:S(2)}) async-start(bf16[8,32,2048]{2,1,0:T(8,128)(2,1)} %bitcast.54), calls=%async_computation.1 | async-start | bytes 2097152 | tf_op jit(solution)/shard_map/all_to_all | solution.py:86
  81.5 3.6 %copy-start.9 = (f32[256,1536]{1,0:T(8,128)S(1)}, f32[256,1536]{1,0:T(8,128)}, u32[]{:S(2)}) copy-start(f32[256,1536]{1,0:T(8,128)} %copy-done.8) | copy-start | bytes 4718596
  85.1 2.6 %copy-start.6 = (bf16[1,768,2048]{2,1,0:T(8,128)(2,1)S(1)}, bf16[1,768,2048]{2,1,0:T(8,128)(2,1)}, u32[]{:S(2)}) copy-start(bf16[1,768,2048]{2,1,0:T(8,128)(2,1)} %param.11) | copy-start | bytes 9437188
  85.1 3.2 %copy-start.7 = (bf16[1,768,2048]{2,1,0:T(8,128)(2,1)S(1)}, bf16[1,768,2048]{2,1,0:T(8,128)(2,1)}, u32[]{:S(2)}) copy-start(bf16[1,768,2048]{2,1,0:T(8,128)(2,1)} %param.10) | copy-start | bytes 9437188
  101.4 30.2 %all-to-all-start.2 = ((bf16[8,32,2048]{2,1,0:T(8,128)(2,1)}), bf16[8,32,2048]{2,1,0:T(8,128)(2,1)}, u32[]{:S(2)}, u32[]{:S(2)}) async-start(bf16[8,32,2048]{2,1,0:T(8,128)(2,1)} %bitcast.53), calls=%async_computation.2 | async-start | bytes 2097152 | tf_op jit(solution)/shard_map/all_to_all | solution.py:100
  109.9 2.9 %copy-start.3 = (bf16[256,2048]{1,0:T(8,128)(2,1)S(1)}, bf16[256,2048]{1,0:T(8,128)(2,1)}, u32[]{:S(2)}) copy-start(bf16[256,2048]{1,0:T(8,128)(2,1)} %param.13) | copy-start | bytes 3145732
  112.7 1.1 copy-start.4
  112.7 1.4 %copy-start.5 = (bf16[192,2048]{1,0:T(8,128)(2,1)S(1)}, bf16[192,2048]{1,0:T(8,128)(2,1)}, u32[]{:S(2)}) copy-start(bf16[192,2048]{1,0:T(8,128)(2,1)} %get-tuple-element.37) | copy-start | bytes 2359300
  112.7 12.6 %collective-permute-start.2 = (bf16[256,4096]{1,0:T(8,128)(2,1)}, bf16[256,4096]{1,0:T(8,128)(2,1)S(1)}, u32[]{:S(2)}, u32[]{:S(2)}) collective-permute-start(bf16[256,4096]{1,0:T(8,128)(2,1)} %collective-permute-done.1), channel_id=1, source_target_pairs={{0,8},{8,0},{16,24},{24,16},{1,9},{9,1},{17,25},{25,17},{2,10},{10... | collective-permute-start | bytes 6291464 | tf_op jit(solution)/shard_map/ppermute | solution.py:123
  119.4 1.9 %copy-start.2 = (f32[192,2048]{1,0:T(8,128)S(1)}, f32[192,2048]{1,0:T(8,128)}, u32[]{:S(2)}) copy-start(f32[192,2048]{1,0:T(8,128)} %fusion.37) | copy-start | bytes 4718596
  127.2 1.9 %copy-start.1 = (f32[384,2048]{1,0:T(8,128)S(1)}, f32[384,2048]{1,0:T(8,128)}, u32[]{:S(2)}) copy-start(f32[384,2048]{1,0:T(8,128)} %fusion.42) | copy-start | bytes 9437188

commit v14 on v12

--- a/solution.py
+++ b/solution.py
@@ -54,25 +54,31 @@
     grad_rows = matmul(pick, out_grad)
     scaled_grad = (slot_gate[:, None] * grad_rows).astype(jnp.bfloat16)
 
-    outgoing = jnp.concatenate([send_rows, scaled_grad], axis=1)
-    received = lax.all_to_all(
-        outgoing.reshape(experts, per_pair, 2 * feature_width),
-        "ep",
-        split_axis=0,
-        concat_axis=0,
-        tiled=True,
-    ).reshape(total_slots, 2 * feature_width)
+    def exchange(rows):
+        return lax.all_to_all(
+            rows.reshape(experts, per_pair, feature_width),
+            "ep",
+            split_axis=0,
+            concat_axis=0,
+            tiled=True,
+        ).reshape(total_slots, feature_width)
+
+    rows_in = exchange(send_rows)
+    grad_in = exchange(scaled_grad)
 
     copies = lax.axis_size("rep")
     by_pieces = copies == 4
-    if by_pieces:
-        near = lax.ppermute(received, "rep", [(r, r ^ 1) for r in range(copies)])
-        far = lax.ppermute(received, "rep", [(r, r ^ 2) for r in range(copies)])
+
+    def to_copy(values, step):
+        return lax.ppermute(values, "rep", [(r, r ^ step) for r in range(copies)])
+
+    if by_pieces:
+        far_rows = to_copy(rows_in, 2)
+        near_rows = to_copy(rows_in, 1)
     else:
-        gathered = lax.all_gather(received, "rep", axis=0, tiled=True)
-
-    rows_in = received[:, :feature_width]
-    grad_in = received[:, feature_width:]
+        gathered_rows = lax.all_gather(rows_in, "rep", axis=0, tiled=True)
+        gathered_grad = lax.all_gather(grad_in, "rep", axis=0, tiled=True)
+
     gate_mat = w_gate[0]
     up_mat = w_up[0]
     down_mat = w_down[0]
@@ -84,6 +90,10 @@
     activated = jax.nn.silu(pre_gate)
     hidden = (activated * pre_up).astype(jnp.bfloat16)
     expert_out = matmul(hidden, down_mat).astype(jnp.bfloat16)
+    expert_out, grad_in = lax.optimization_barrier((expert_out, grad_in))
+    if by_pieces:
+        far_grad = to_copy(grad_in, 2)
+        near_grad = to_copy(grad_in, 1)
     returned = lax.all_to_all(
         expert_out.reshape(experts, per_pair, feature_width),
         "ep",
@@ -107,7 +117,7 @@
     ).reshape(total_slots, feature_width)
 
     if by_pieces:
-        returned, near = lax.optimization_barrier((returned, near))
+        returned, near_rows, near_grad = lax.optimization_barrier((returned, near_rows, near_grad))
     slot_grid = slot_index.reshape(tok_count, live_cols)
     gate_grid = flat_gates.reshape(tok_count, live_cols)
     layer_sum = jnp.zeros((tok_count, feature_width), jnp.float32)
@@ -120,11 +130,15 @@
         layer_sum = layer_sum + gate_grid[:, col : col + 1] * out_rows
         gate_cols.append(jnp.sum(out_grad.astype(jnp.float32) * out_rows, axis=1))
     if by_pieces:
-        layer_sum, far = lax.optimization_barrier((layer_sum, far))
-        near_far = lax.ppermute(far, "rep", [(r, r ^ 1) for r in range(copies)])
-        pieces = [received, near, far, near_far]
+        layer_sum, far_rows, far_grad = lax.optimization_barrier((layer_sum, far_rows, far_grad))
+        pieces = [
+            (rows_in, grad_in),
+            (near_rows, near_grad),
+            (far_rows, far_grad),
+            (to_copy(far_rows, 1), to_copy(far_grad, 1)),
+        ]
     else:
-        pieces = [gathered]
+        pieces = [(gathered_rows, gathered_grad)]
     layer_out = layer_sum.astype(jnp.bfloat16)
     gate_cols.extend(
         [jnp.zeros((tok_count,), jnp.float32)] * (top_count - live_cols)
@@ -139,9 +153,7 @@
     both_sum = None
     down_sum = None
     stacked_share = jnp.concatenate([gate_share, up_share], axis=0)
-    for piece in pieces:
-        rows_p = piece[:, :feature_width]
-        grad_p = piece[:, feature_width:]
+    for rows_p, grad_p in pieces:
         pre_both = rows_times(rows_p, stacked_share)
         pre_gate_s = pre_both[:, :share]
         pre_up_s = pre_both[:, share:]

time: 135 us -> 134 us (level)
  waiting for transfers between devices: 55.7 us -> 48.9 us
  starting transfers between devices: 17.5 us -> 23.9 us
  matrix products: 48.1 us -> 50 us
  local copies, waits for them, and re-layouts: 8.76 us -> 7.02 us
  other arithmetic: 3.35 us -> 1.94 us
    all_to_all x1 -> x2, waiting for transfers between devices: 44.7 us -> 35.3 us  [exchange(): lax.all_to_all(rows.reshape(experts, per_pair, feature_width), 'ep', spli...]
    all_to_all x1 -> x2, starting transfers between devices: 7.26 us -> 11.5 us  [exchange(): lax.all_to_all(rows.reshape(experts, per_pair, feature_width), 'ep', spli...]
    dot_general x7, matrix products: 12.6 us -> 15.8 us  [matmul(): return jnp.dot(left, right, preferred_element_type=jnp.float32)]
    ppermute x3 -> x6, starting transfers between devices: 1.59 us -> 3.67 us  [to_copy(): return lax.ppermute(values, 'rep', [(r, r ^ step) for r in range(copies)])]
    all_to_all x1, waiting for transfers between devices: 0.62 us -> 2.63 us  [body(): lax.all_to_all(token_part.reshape(experts, per_pair, feature_width), 'ep'...]
    unnamed x22, local copies, waits for them, and re-layouts: 2.95 us -> 1.21 us
    concatenate x1 -> x0, other arithmetic: 1.56 us -> none  [body(): outgoing = jnp.concatenate([send_rows, scaled_grad], axis=1)]
  transfers between devices with their start and end apart: 6 -> 10, of which waited for: 3 -> 4; matrix products, arithmetic and copies ran while one was open for 36% -> 39% of each run, Pallas kernels for 0% -> 0%
where the time goes in v14:
time: 134 us; the launch traced here: 133 us
  matrix products  50 us (37%)
  waiting for transfers between devices  48.9 us (36%)
  starting transfers between devices  23.9 us (18%)
  local copies, waits for them, and re-layouts  7.02 us (5%)
  other arithmetic  1.94 us (1%)
    all_to_all x2, waiting for transfers between devices, exchange(): lax.all_to_all(rows.reshape(experts, per_pair, feature_width), 'ep', spli...  35.3 us
    dot_general x10, matrix products, rows_times(): lax.dot_general(left, right, (((1,), (1,)), ((), ())), preferred_element_...  19 us
    dot_general x7, matrix products, matmul(): return jnp.dot(left, right, preferred_element_type=jnp.float32)  15.8 us
    dot_general x8, matrix products, inner_rows(): lax.dot_general(left, right, (((0,), (0,)), ((), ())), preferred_element_...  15.3 us
    all_to_all x2, starting transfers between devices, exchange(): lax.all_to_all(rows.reshape(experts, per_pair, feature_width), 'ep', spli...  11.5 us
    all_to_all x1, waiting for transfers between devices, body(): lax.all_to_all(expert_out.reshape(experts, per_pair, feature_width), 'ep'...  10.9 us
    all_to_all x1, starting transfers between devices, body(): lax.all_to_all(token_part.reshape(experts, per_pair, feature_width), 'ep'...  4.41 us
    all_to_all x1, starting transfers between devices, body(): lax.all_to_all(expert_out.reshape(experts, per_pair, feature_width), 'ep'...  4.25 us
  transfers between devices with their start and end apart: 10, of which 4 were waited for; matrix products, arithmetic and copies ran while one was open for 39% of the time, Pallas kernels for 0%

profile of v14, /device:TPU:0, one launch (start us, length us, event | category | flops | bytes accessed | tf_op | source)
XLA Modules:
  0.0 132.7 jit_solution(9067826378230731438)
XLA Ops:
  0.6 0.0 copy-start
  0.6 0.9 slice.45
  1.5 0.2 fusion.14
  1.7 2.6 %convolution_convert_fusion.1 = bf16[256,2048]{1,0:T(8,128)(2,1)} fusion(bf16[256,2048]{1,0:T(8,128)(2,1)} %param.7, s32[256]{0:T(256)S(1)} %compare_select_fusion.1), kind=kOutput, calls=%fused_computation.14 | convolution fusion | flops 269025280 | bytes 2098176 | tf_op jit(solution)/shard_map/dot_general | solution.py:27
  4.4 7.3 %all-to-all-start = ((bf16[8,32,2048]{2,1,0:T(8,128)(2,1)}), bf16[8,32,2048]{2,1,0:T(8,128)(2,1)}, u32[]{:S(2)}, u32[]{:S(2)}) async-start(bf16[8,32,2048]{2,1,0:T(8,128)(2,1)} %bitcast.75), calls=%async_computation | async-start | bytes 2097152 | tf_op jit(solution)/shard_map/all_to_all | solution.py:58
  11.6 0.7 slice.44
  12.3 0.1 select_reduce_fusion
  12.4 2.6 %fusion.6 = bf16[256,2048]{1,0:T(8,128)(2,1)} fusion(bf16[256,2048]{1,0:T(8,128)(2,1)} %param.13, f32[256]{0:T(256)S(1)} %select_reduce_fusion, s32[256]{0:T(256)S(1)} %compare_select_fusion.1), kind=kOutput, calls=%fused_computation.11 | convolution fusion | flops 269549568 | bytes 2099200 | tf_op jit(solution)/shard_map/dot_general | solution.py:27
  15.1 22.4 %all-to-all-done = bf16[8,32,2048]{2,1,0:T(8,128)(2,1)} async-done(((bf16[8,32,2048]{2,1,0:T(8,128)(2,1)}), bf16[8,32,2048]{2,1,0:T(8,128)(2,1)}, u32[]{:S(2)}, u32[]{:S(2)}) %all-to-all-start) | async-done | bytes 1048608 | tf_op jit(solution)/shard_map/all_to_all | solution.py:58
  37.5 4.3 %all-to-all-start.1 = ((bf16[8,32,2048]{2,1,0:T(8,128)(2,1)}), bf16[8,32,2048]{2,1,0:T(8,128)(2,1)}, u32[]{:S(2)}, u32[]{:S(2)}) async-start(bf16[8,32,2048]{2,1,0:T(8,128)(2,1)} %bitcast.74), calls=%async_computation.1 | async-start | bytes 2097152 | tf_op jit(solution)/shard_map/all_to_all | solution.py:58
  41.8 0.1 pad.1.clone
  41.9 0.1 pad.3.clone
  42.0 0.1 pad.2.clone
  42.0 0.9 compare_select_fusion
  42.9 2.8 %dynamic-slice_bitcast_fusion = (bf16[192,2048]{1,0:T(8,128)(2,1)}, bf16[192,2048]{1,0:T(8,128)(2,1)}) fusion(bf16[1,768,2048]{2,1,0:T(8,128)(2,1)} %param.11, s32[]{:T(128)S(6)} %select_n.28, bf16[1,768,2048]{2,1,0:T(8,128)(2,1)} %param.10), kind=kLoop, calls=%fused_computation.37 | loop fusion | bytes 3145732 | tf_op jit(solution)/shard_map/dynamic_slice | solution.py:151
  45.7 1.5 %collective-permute-start.2 = (bf16[256,2048]{1,0:T(8,128)(2,1)}, bf16[256,2048]{1,0:T(8,128)(2,1)}, u32[]{:S(2)}, u32[]{:S(2)}) collective-permute-start(bf16[256,2048]{1,0:T(8,128)(2,1)} %bitcast.5), channel_id=1, source_target_pairs={{0,16},{8,24},{16,0},{24,8},{1,17},{9,25},{17,1},{25,9},{2,18},{10... | collective-permute-start | bytes 3145736 | tf_op jit(solution)/shard_map/ppermute | solution.py:73
  47.2 0.0 collective-permute-start
  47.2 4.0 %fusion.1 = f32[256,1536]{1,0:T(8,128)S(1)} fusion(bf16[256,2048]{1,0:T(8,128)(2,1)} %bitcast.5, bf16[768,2048]{1,0:T(8,128)(2,1)S(1)} %bitcast.78, bf16[768,2048]{1,0:T(8,128)(2,1)} %bitcast.80), kind=kOutput, calls=%fused_computation.2 | convolution fusion | flops 1623195648 | bytes 8912896 | tf_op jit(solution)/shard_map/dot_general | solution.py:15
  51.2 1.1 copy-done.9
  52.4 0.0 copy-done
  52.4 2.0 %fusion.9 = bf16[256,2048]{1,0:T(8,128)(2,1)} fusion(bf16[1,768,2048]{2,1,0:T(8,128)(2,1)S(1)} %copy-done, f32[256,1536]{1,0:T(8,128)S(1)} %fusion.1), kind=kOutput, calls=%fused_computation.16 | convolution fusion | flops 807010304 | bytes 5767168 | tf_op jit(solution)/shard_map/dot_general | solution.py:27
  54.4 12.9 %all-to-all-done.1 = bf16[8,32,2048]{2,1,0:T(8,128)(2,1)} async-done(((bf16[8,32,2048]{2,1,0:T(8,128)(2,1)}), bf16[8,32,2048]{2,1,0:T(8,128)(2,1)}, u32[]{:S(2)}, u32[]{:S(2)}) %all-to-all-start.1) | async-done | bytes 1048608 | tf_op jit(solution)/shard_map/all_to_all | solution.py:58
  67.3 1.5 %collective-permute-start.3 = (bf16[256,2048]{1,0:T(8,128)(2,1)}, bf16[256,2048]{1,0:T(8,128)(2,1)}, u32[]{:S(2)}, u32[]{:S(2)}) collective-permute-start(bf16[256,2048]{1,0:T(8,128)(2,1)} %bitcast.10), channel_id=1, source_target_pairs={{0,16},{8,24},{16,0},{24,8},{1,17},{9,25},{17,1},{25,9},{2,18},{10... | collective-permute-start | bytes 3145736 | tf_op jit(solution)/shard_map/ppermute | solution.py:73
  68.9 0.0 collective-permute-start.1
  68.9 4.3 %all-to-all-start.2 = ((bf16[8,32,2048]{2,1,0:T(8,128)(2,1)}), bf16[8,32,2048]{2,1,0:T(8,128)(2,1)}, u32[]{:S(2)}, u32[]{:S(2)}) async-start(bf16[8,32,2048]{2,1,0:T(8,128)(2,1)} %bitcast.77), calls=%async_computation.2 | async-start | bytes 2097152 | tf_op jit(solution)/shard_map/all_to_all | solution.py:97
  73.1 2.4 %fusion.84 = f32[256,384]{0,1:T(8,128)S(1)} fusion(bf16[256,2048]{1,0:T(8,128)(2,1)} %bitcast.5, bf16[192,2048]{1,0:T(8,128)(2,1)} %get-tuple-element.44, bf16[192,2048]{1,0:T(8,128)(2,1)} %get-tuple-element.45), kind=kOutput, calls=%fused_computation.118 | convolution fusion | flops 405798912 | bytes 3014656 | tf_op jit(solution)/shard_map/dot_general | solution.py:15
  75.6 2.5 %multiply_convert_fusion.1 = (bf16[256,768]{1,0:T(8,128)(2,1)S(1)}, bf16[256,768]{1,0:T(8,128)(2,1)S(1)}) fusion(f32[256,1536]{1,0:T(8,128)S(1)} %copy-done.10, bf16[256,2048]{1,0:T(8,128)(2,1)} %bitcast.10, bf16[1,768,2048]{2,1,0:T(8,128)(2,1)S(1)} %copy-done), kind=kOutput, calls=%fused_computation.40 | convolution fusion | flops 807862272 | bytes 6553600 | tf_op jit(solution)/shard_map/dot_general | solution.py:15
  78.0 1.7 %multiply_convert_fusion.15 = (bf16[256,192]{0,1:T(8,128)(2,1)S(1)}, bf16[256,192]{0,1:T(8,128)(2,1)S(1)}) fusion(f32[256,384]{0,1:T(8,128)S(1)} %fusion.84, bf16[256,2048]{1,0:T(8,128)(2,1)} %bitcast.10, bf16[1,768,2048]{2,1,0:T(8,128)(2,1)S(1)} %copy-done, s32[]{:T(128)S(6)} %select_n.28), kind=kOutput, calls=%fused_computation.86 | convolution fusion | flops 201965568 | bytes 2424836 | tf_op jit(solution)/shard_map/dot_general | solution.py:15
  79.8 0.0 copy-start.7
  79.8 0.0 copy-start.8
  79.8 2.9 %fusion.58 = f32[192,2048]{1,0:T(8,128)} fusion(bf16[256,2048]{1,0:T(8,128)(2,1)} %bitcast.10, f32[256,384]{0,1:T(8,128)S(1)} %fusion.84), kind=kOutput, calls=%fused_computation.93 | convolution fusion | flops 201621504 | bytes 3014656 | tf_op jit(solution)/shard_map/dot_general | solution.py:21
  82.7 3.4 %fusion.32 = f32[384,2048]{1,0:T(8,128)} fusion(bf16[256,2048]{1,0:T(8,128)(2,1)} %bitcast.5, bf16[256,192]{0,1:T(8,128)(2,1)S(1)} %get-tuple-element.39, bf16[256,192]{0,1:T(8,128)(2,1)S(1)} %get-tuple-element.38), kind=kOutput, calls=%fused_computation.53 | convolution fusion | flops 403046400 | bytes 4390912 | tf_op jit(solution)/shard_map/dot_general | solution.py:21
  86.2 2.8 %fusion.7 = bf16[256,2048]{1,0:T(8,128)(2,1)} fusion(bf16[768,2048]{1,0:T(8,128)(2,1)S(1)} %bitcast.79, bf16[768,2048]{1,0:T(8,128)(2,1)S(1)} %bitcast.81, bf16[256,768]{1,0:T(8,128)(2,1)S(1)} %get-tuple-element.31, bf16[256,768]{1,0:T(8,128)(2,1)S(1)} %get-tuple-element.30), kind=kOutput, calls=%fused_computation.12 | convolution fusion | flops 1625292800 | bytes 8126464 | tf_op jit(solution)/shard_map/dot_general | solution.py:27
  89.0 10.9 %all-to-all-done.2 = bf16[8,32,2048]{2,1,0:T(8,128)(2,1)} async-done(((bf16[8,32,2048]{2,1,0:T(8,128)(2,1)}), bf16[8,32,2048]{2,1,0:T(8,128)(2,1)}, u32[]{:S(2)}, u32[]{:S(2)}) %all-to-all-start.2) | async-done | bytes 1048608 | tf_op jit(solution)/shard_map/all_to_all | solution.py:97
  99.8 4.4 %all-to-all-start.3 = ((bf16[8,32,2048]{2,1,0:T(8,128)(2,1)}), bf16[8,32,2048]{2,1,0:T(8,128)(2,1)}, u32[]{:S(2)}, u32[]{:S(2)}) async-start(bf16[8,32,2048]{2,1,0:T(8,128)(2,1)} %bitcast.76), calls=%async_computation.3 | async-start | bytes 2097152 | tf_op jit(solution)/shard_map/all_to_all | solution.py:111
  104.3 0.0 copy-start.4
  104.3 0.0 copy-start.5
  104.3 0.0 collective-permute-done
  104.3 0.0 collective-permute-done.1
  104.3 2.8 %broadcast_multiply_fusion = (bf16[256,2048]{1,0:T(8,128)(2,1)}, f32[256,2048]{1,0:T(8,128)S(1)}) fusion(f32[256]{0:T(256)S(1)} %bitcast.85, bf16[256,2048]{1,0:T(8,128)(2,1)} %bitcast.12, s32[256]{0:T(256)S(1)} %bitcast.82), kind=kOutput, calls=%fused_computation.23 | convolution fusion | flops 269549568 | bytes 4196352 | tf_op jit(solution)/shard_map/dot_general | solution.py:27
  107.1 0.0 collective-permute-done.2
  107.1 0.0 collective-permute-done.3
  107.1 1.8 %fusion.82 = f32[256,384]{0,1:T(8,128)S(1)} fusion(bf16[256,2048]{1,0:T(8,128)(2,1)} %collective-permute-done.2, bf16[192,2048]{1,0:T(8,128)(2,1)S(1)} %copy-done.4, bf16[192,2048]{1,0:T(8,128)(2,1)S(1)} %copy-done.5), kind=kOutput, calls=%fused_computation.116 | convolution fusion | flops 405798912 | bytes 3014656 | tf_op jit(solution)/shard_map/dot_general | solution.py:15
  109.0 0.1 collective-permute-start.5
  109.0 1.8 %fusion.83 = f32[256,384]{0,1:T(8,128)S(1)} fusion(bf16[256,2048]{1,0:T(8,128)(2,1)} %collective-permute-done, bf16[192,2048]{1,0:T(8,128)(2,1)S(1)} %copy-done.4, bf16[192,2048]{1,0:T(8,128)(2,1)S(1)} %copy-done.5), kind=kOutput, calls=%fused_computation.117 | convolution fusion | flops 405798912 | bytes 3014656 | tf_op jit(solution)/shard_map/dot_general | solution.py:15
  110.9 0.6 collective-permute-start.4
  111.4 1.7 %multiply_convert_fusion.11 = (bf16[256,192]{0,1:T(8,128)(2,1)S(1)}, bf16[256,192]{0,1:T(8,128)(2,1)S(1)}) fusion(f32[256,384]{0,1:T(8,128)S(1)} %fusion.82, bf16[256,2048]{1,0:T(8,128)(2,1)} %collective-permute-done.3, bf16[1,768,2048]{2,1,0:T(8,128)(2,1)S(1)} %copy-done, s32[]{:T(128)S(6)} %select_n.28), kind=kOutput, calls=%fused_computation.78 | convolution fusion | flops 201965568 | bytes 2424836 | tf_op jit(solution)/shard_map/dot_general | solution.py:15
  113.2 0.0 copy-start.3
  113.2 1.8 %multiply_convert_fusion.13 = (bf16[256,192]{0,1:T(8,128)(2,1)S(1)}, bf16[256,192]{0,1:T(8,128)(2,1)S(1)}) fusion(f32[256,384]{0,1:T(8,128)S(1)} %fusion.83, bf16[256,2048]{1,0:T(8,128)(2,1)} %collective-permute-done.1, bf16[1,768,2048]{2,1,0:T(8,128)(2,1)S(1)} %copy-done, s32[]{:T(128)S(6)} %select_n.28), kind=kOutput, calls=%fused_computation.82 | convolution fusion | flops 201965568 | bytes 2424836 | tf_op jit(solution)/shard_map/dot_general | solution.py:15
  115.0 1.8 %fusion.36 = f32[384,2048]{1,0:T(8,128)S(1)} fusion(bf16[256,2048]{1,0:T(8,128)(2,1)} %collective-permute-done, bf16[256,192]{0,1:T(8,128)(2,1)S(1)} %get-tuple-element.37, bf16[256,192]{0,1:T(8,128)(2,1)S(1)} %get-tuple-element.36), kind=kOutput, calls=%fused_computation.57 | convolution fusion | flops 403046400 | bytes 4390912 | tf_op jit(solution)/shard_map/dot_general | solution.py:21
  116.8 0.3 multiply_reduce_fusion
  117.1 0.7 maximum_maximum_fusion
  117.8 1.8 %fusion.40 = f32[384,2048]{1,0:T(8,128)S(1)} fusion(bf16[256,2048]{1,0:T(8,128)(2,1)} %collective-permute-done.2, bf16[256,192]{0,1:T(8,128)(2,1)S(1)} %get-tuple-element.41, bf16[256,192]{0,1:T(8,128)(2,1)S(1)} %get-tuple-element.40), kind=kOutput, calls=%fused_computation.61 | convolution fusion | flops 403046400 | bytes 4390912 | tf_op jit(solution)/shard_map/dot_general | solution.py:21
  119.6 1.6 %convolution_add_fusion.1 = f32[192,2048]{1,0:T(8,128)S(1)} fusion(f32[192,2048]{1,0:T(8,128)S(1)} %copy-done.2, bf16[256,2048]{1,0:T(8,128)(2,1)} %collective-permute-done.1, f32[256,384]{0,1:T(8,128)S(1)} %fusion.83), kind=kOutput, calls=%fused_computation.10 | convolution fusion | flops 202014720 | bytes 4587520 | tf_op jit(solution)/shard_map/dot_general | solution.py:21
  121.3 0.0 collective-permute-done.5
  121.3 0.6 fusion.81
  121.9 0.0 collective-permute-done.4
  121.9 0.5 multiply_convert_fusion.9
  122.4 0.4 fusion.59
  122.8 2.7 %fusion.13 = bf16[1,192,2048]{2,1,0:T(8,128)(2,1)} fusion(f32[192,2048]{1,0:T(8,128)S(1)} %fusion.59, f32[192,2048]{1,0:T(8,128)S(1)} %convolution_add_fusion.1, bf16[256,2048]{1,0:T(8,128)(2,1)} %collective-permute-done.3, f32[256,384]{0,1:T(8,128)S(1)} %fusion.82), kind=kOutput, calls=%fused_computation.18 | convolution fusion | flops 202801152 | bytes 5373952 | tf_op jit(solution)/shard_map/dot_general | solution.py:21
  125.5 0.6 add_convert_fusion
  126.1 1.2 slice_bitcast_fusion
  127.4 2.6 %all-to-all-done.3 = bf16[8,32,2048]{2,1,0:T(8,128)(2,1)} async-done(((bf16[8,32,2048]{2,1,0:T(8,128)(2,1)}), bf16[8,32,2048]{2,1,0:T(8,128)(2,1)}, u32[]{:S(2)}, u32[]{:S(2)}) %all-to-all-start.3) | async-done | bytes 1048608 | tf_op jit(solution)/shard_map/all_to_all | solution.py:111
  130.0 2.7 %convolution_convert_fusion = bf16[256,2048]{1,0:T(8,128)(2,1)} fusion(bf16[256,2048]{1,0:T(8,128)(2,1)} %bitcast.14, s32[256]{0:T(256)S(1)} %bitcast.83), kind=kOutput, calls=%fused_computation.13 | convolution fusion | flops 269025280 | bytes 2098176 | tf_op jit(solution)/shard_map/dot_general | solution.py:27
  (18 shorter events, 0.0 us)
Async XLA Ops:
  0.6 51.8 %copy-start = (bf16[1,768,2048]{2,1,0:T(8,128)(2,1)S(1)}, bf16[1,768,2048]{2,1,0:T(8,128)(2,1)}, u32[]{:S(2)}) copy-start(bf16[1,768,2048]{2,1,0:T(8,128)(2,1)} %param.12) | copy-start | bytes 9437188
  4.4 33.1 %all-to-all-start = ((bf16[8,32,2048]{2,1,0:T(8,128)(2,1)}), bf16[8,32,2048]{2,1,0:T(8,128)(2,1)}, u32[]{:S(2)}, u32[]{:S(2)}) async-start(bf16[8,32,2048]{2,1,0:T(8,128)(2,1)} %bitcast.75), calls=%async_computation | async-start | bytes 2097152 | tf_op jit(solution)/shard_map/all_to_all | solution.py:58
  37.5 29.9 %all-to-all-start.1 = ((bf16[8,32,2048]{2,1,0:T(8,128)(2,1)}), bf16[8,32,2048]{2,1,0:T(8,128)(2,1)}, u32[]{:S(2)}, u32[]{:S(2)}) async-start(bf16[8,32,2048]{2,1,0:T(8,128)(2,1)} %bitcast.74), calls=%async_computation.1 | async-start | bytes 2097152 | tf_op jit(solution)/shard_map/all_to_all | solution.py:58
  42.0 5.2 %copy-start.6 = (bf16[1,768,2048]{2,1,0:T(8,128)(2,1)S(1)}, bf16[1,768,2048]{2,1,0:T(8,128)(2,1)}, u32[]{:S(2)}) copy-start(bf16[1,768,2048]{2,1,0:T(8,128)(2,1)} %param.11) | copy-start | bytes 9437188
  45.7 61.4 %collective-permute-start.2 = (bf16[256,2048]{1,0:T(8,128)(2,1)}, bf16[256,2048]{1,0:T(8,128)(2,1)}, u32[]{:S(2)}, u32[]{:S(2)}) collective-permute-start(bf16[256,2048]{1,0:T(8,128)(2,1)} %bitcast.5), channel_id=1, source_target_pairs={{0,16},{8,24},{16,0},{24,8},{1,17},{9,25},{17,1},{25,9},{2,18},{10... | collective-permute-start | bytes 3145736 | tf_op jit(solution)/shard_map/ppermute | solution.py:73
  47.2 57.1 %collective-permute-start = (bf16[256,2048]{1,0:T(8,128)(2,1)}, bf16[256,2048]{1,0:T(8,128)(2,1)}, u32[]{:S(2)}, u32[]{:S(2)}) collective-permute-start(bf16[256,2048]{1,0:T(8,128)(2,1)} %bitcast.5), channel_id=1, source_target_pairs={{0,8},{8,0},{16,24},{24,16},{1,9},{9,1},{17,25},{25,17},{2,10},{10... | collective-permute-start | bytes 3145736 | tf_op jit(solution)/shard_map/ppermute | solution.py:73
  51.2 1.2 copy-start.9
  67.3 39.8 %collective-permute-start.3 = (bf16[256,2048]{1,0:T(8,128)(2,1)}, bf16[256,2048]{1,0:T(8,128)(2,1)}, u32[]{:S(2)}, u32[]{:S(2)}) collective-permute-start(bf16[256,2048]{1,0:T(8,128)(2,1)} %bitcast.10), channel_id=1, source_target_pairs={{0,16},{8,24},{16,0},{24,8},{1,17},{9,25},{17,1},{25,9},{2,18},{10... | collective-permute-start | bytes 3145736 | tf_op jit(solution)/shard_map/ppermute | solution.py:73
  68.9 35.4 %collective-permute-start.1 = (bf16[256,2048]{1,0:T(8,128)(2,1)}, bf16[256,2048]{1,0:T(8,128)(2,1)}, u32[]{:S(2)}, u32[]{:S(2)}) collective-permute-start(bf16[256,2048]{1,0:T(8,128)(2,1)} %bitcast.10), channel_id=1, source_target_pairs={{0,8},{8,0},{16,24},{24,16},{1,9},{9,1},{17,25},{25,17},{2,10},{10... | collective-permute-start | bytes 3145736 | tf_op jit(solution)/shard_map/ppermute | solution.py:73
  68.9 31.0 %all-to-all-start.2 = ((bf16[8,32,2048]{2,1,0:T(8,128)(2,1)}), bf16[8,32,2048]{2,1,0:T(8,128)(2,1)}, u32[]{:S(2)}, u32[]{:S(2)}) async-start(bf16[8,32,2048]{2,1,0:T(8,128)(2,1)} %bitcast.77), calls=%async_computation.2 | async-start | bytes 2097152 | tf_op jit(solution)/shard_map/all_to_all | solution.py:97
  73.1 2.4 %copy-start.10 = (f32[256,1536]{1,0:T(8,128)S(1)}, f32[256,1536]{1,0:T(8,128)}, u32[]{:S(2)}) copy-start(f32[256,1536]{1,0:T(8,128)} %copy-done.9) | copy-start | bytes 4718596
  79.8 6.4 %copy-start.7 = (bf16[1,768,2048]{2,1,0:T(8,128)(2,1)S(1)}, bf16[1,768,2048]{2,1,0:T(8,128)(2,1)}, u32[]{:S(2)}) copy-start(bf16[1,768,2048]{2,1,0:T(8,128)(2,1)} %param.11) | copy-start | bytes 9437188
  79.8 6.4 %copy-start.8 = (bf16[1,768,2048]{2,1,0:T(8,128)(2,1)S(1)}, bf16[1,768,2048]{2,1,0:T(8,128)(2,1)}, u32[]{:S(2)}) copy-start(bf16[1,768,2048]{2,1,0:T(8,128)(2,1)} %param.10) | copy-start | bytes 9437188
  99.8 30.2 %all-to-all-start.3 = ((bf16[8,32,2048]{2,1,0:T(8,128)(2,1)}), bf16[8,32,2048]{2,1,0:T(8,128)(2,1)}, u32[]{:S(2)}, u32[]{:S(2)}) async-start(bf16[8,32,2048]{2,1,0:T(8,128)(2,1)} %bitcast.76), calls=%async_computation.3 | async-start | bytes 2097152 | tf_op jit(solution)/shard_map/all_to_all | solution.py:111
  104.3 2.9 %copy-start.4 = (bf16[192,2048]{1,0:T(8,128)(2,1)S(1)}, bf16[192,2048]{1,0:T(8,128)(2,1)}, u32[]{:S(2)}) copy-start(bf16[192,2048]{1,0:T(8,128)(2,1)} %get-tuple-element.44) | copy-start | bytes 2359300
  104.3 2.8 %copy-start.5 = (bf16[192,2048]{1,0:T(8,128)(2,1)S(1)}, bf16[192,2048]{1,0:T(8,128)(2,1)}, u32[]{:S(2)}) copy-start(bf16[192,2048]{1,0:T(8,128)(2,1)} %get-tuple-element.45) | copy-start | bytes 2359300
  109.0 12.3 %collective-permute-start.5 = (bf16[256,2048]{1,0:T(8,128)(2,1)}, bf16[256,2048]{1,0:T(8,128)(2,1)S(1)}, u32[]{:S(2)}, u32[]{:S(2)}) collective-permute-start(bf16[256,2048]{1,0:T(8,128)(2,1)} %collective-permute-done.2), channel_id=1, source_target_pairs={{0,8},{8,0},{16,24},{24,16},{1,9},{9,1},{17,25},{25,17},{2,10},{10... | collective-permute-start | bytes 3145736 | tf_op jit(solution)/shard_map/ppermute | solution.py:73
  110.9 11.0 %collective-permute-start.4 = (bf16[256,2048]{1,0:T(8,128)(2,1)}, bf16[256,2048]{1,0:T(8,128)(2,1)S(1)}, u32[]{:S(2)}, u32[]{:S(2)}) collective-permute-start(bf16[256,2048]{1,0:T(8,128)(2,1)} %collective-permute-done.3), channel_id=1, source_target_pairs={{0,8},{8,0},{16,24},{24,16},{1,9},{9,1},{17,25},{25,17},{2,10},{10... | collective-permute-start | bytes 3145736 | tf_op jit(solution)/shard_map/ppermute | solution.py:73
  113.2 3.7 %copy-start.3 = (bf16[256,2048]{1,0:T(8,128)(2,1)S(1)}, bf16[256,2048]{1,0:T(8,128)(2,1)}, u32[]{:S(2)}) copy-start(bf16[256,2048]{1,0:T(8,128)(2,1)} %param.13) | copy-start | bytes 3145732
  116.8 2.8 %copy-start.2 = (f32[192,2048]{1,0:T(8,128)S(1)}, f32[192,2048]{1,0:T(8,128)}, u32[]{:S(2)}) copy-start(f32[192,2048]{1,0:T(8,128)} %fusion.58) | copy-start | bytes 4718596
  122.8 2.7 %copy-start.1 = (f32[384,2048]{1,0:T(8,128)S(1)}, f32[384,2048]{1,0:T(8,128)}, u32[]{:S(2)}) copy-start(f32[384,2048]{1,0:T(8,128)} %fusion.32) | copy-start | bytes 9437188

commit v15 on v14

--- a/solution.py
+++ b/solution.py
@@ -91,9 +91,6 @@
     hidden = (activated * pre_up).astype(jnp.bfloat16)
     expert_out = matmul(hidden, down_mat).astype(jnp.bfloat16)
     expert_out, grad_in = lax.optimization_barrier((expert_out, grad_in))
-    if by_pieces:
-        far_grad = to_copy(grad_in, 2)
-        near_grad = to_copy(grad_in, 1)
     returned = lax.all_to_all(
         expert_out.reshape(experts, per_pair, feature_width),
         "ep",
@@ -108,6 +105,10 @@
     token_part = matmul(
         jnp.concatenate([gate_pre_grad, up_pre_grad], axis=1), gate_up_mat
     ).astype(jnp.bfloat16)
+    if by_pieces:
+        token_part, grad_out = lax.optimization_barrier((token_part, grad_in))
+        far_grad = to_copy(grad_out, 2)
+        near_grad = to_copy(grad_out, 1)
     part_back = lax.all_to_all(
         token_part.reshape(experts, per_pair, feature_width),
         "ep",

time: 134 us -> 130 us (0.970)
  waiting for transfers between devices: 48.9 us -> 45.1 us
    all_to_all x1, waiting for transfers between devices: 10.9 us -> 7.62 us  [body(): lax.all_to_all(expert_out.reshape(experts, per_pair, feature_width), 'ep'...]
  transfers between devices with their start and end apart: 10 -> 10, of which waited for: 4 -> 4; matrix products, arithmetic and copies ran while one was open for 39% -> 40% of each run, Pallas kernels for 0% -> 0%
where the time goes in v15:
time: 130 us; the launch traced here: 129 us
  matrix products  49.9 us (38%)
  waiting for transfers between devices  45.1 us (35%)
  starting transfers between devices  23.8 us (18%)
  local copies, waits for them, and re-layouts  7.6 us (6%)
  other arithmetic  1.94 us (1%)
    all_to_all x2, waiting for transfers between devices, exchange(): lax.all_to_all(rows.reshape(experts, per_pair, feature_width), 'ep', spli...  35.4 us
    dot_general x10, matrix products, rows_times(): lax.dot_general(left, right, (((1,), (1,)), ((), ())), preferred_element_...  19 us
    dot_general x7, matrix products, matmul(): return jnp.dot(left, right, preferred_element_type=jnp.float32)  15.8 us
    dot_general x8, matrix products, inner_rows(): lax.dot_general(left, right, (((0,), (0,)), ((), ())), preferred_element_...  15.1 us
    all_to_all x2, starting transfers between devices, exchange(): lax.all_to_all(rows.reshape(experts, per_pair, feature_width), 'ep', spli...  11.5 us
    all_to_all x1, waiting for transfers between devices, body(): lax.all_to_all(expert_out.reshape(experts, per_pair, feature_width), 'ep'...  7.62 us
    all_to_all x1, starting transfers between devices, body(): lax.all_to_all(token_part.reshape(experts, per_pair, feature_width), 'ep'...  4.41 us
    all_to_all x1, starting transfers between devices, body(): lax.all_to_all(expert_out.reshape(experts, per_pair, feature_width), 'ep'...  4.24 us
  transfers between devices with their start and end apart: 10, of which 4 were waited for; matrix products, arithmetic and copies ran while one was open for 40% of the time, Pallas kernels for 0%

profile of v15, /device:TPU:0, one launch (start us, length us, event | category | flops | bytes accessed | tf_op | source)
XLA Modules:
  0.0 129.3 jit_solution(9352168649783690748)
XLA Ops:
  0.6 0.0 copy-start
  0.6 0.9 slice.45
  1.5 0.2 fusion.14
  1.7 2.6 %convolution_convert_fusion.1 = bf16[256,2048]{1,0:T(8,128)(2,1)} fusion(bf16[256,2048]{1,0:T(8,128)(2,1)} %param.7, s32[256]{0:T(256)S(1)} %compare_select_fusion.1), kind=kOutput, calls=%fused_computation.14 | convolution fusion | flops 269025280 | bytes 2098176 | tf_op jit(solution)/shard_map/dot_general | solution.py:27
  4.4 7.3 %all-to-all-start = ((bf16[8,32,2048]{2,1,0:T(8,128)(2,1)}), bf16[8,32,2048]{2,1,0:T(8,128)(2,1)}, u32[]{:S(2)}, u32[]{:S(2)}) async-start(bf16[8,32,2048]{2,1,0:T(8,128)(2,1)} %bitcast.75), calls=%async_computation | async-start | bytes 2097152 | tf_op jit(solution)/shard_map/all_to_all | solution.py:58
  11.6 0.7 slice.44
  12.3 0.1 select_reduce_fusion
  12.4 2.6 %fusion.6 = bf16[256,2048]{1,0:T(8,128)(2,1)} fusion(bf16[256,2048]{1,0:T(8,128)(2,1)} %param.13, f32[256]{0:T(256)S(1)} %select_reduce_fusion, s32[256]{0:T(256)S(1)} %compare_select_fusion.1), kind=kOutput, calls=%fused_computation.11 | convolution fusion | flops 269549568 | bytes 2099200 | tf_op jit(solution)/shard_map/dot_general | solution.py:27
  15.1 22.4 %all-to-all-done = bf16[8,32,2048]{2,1,0:T(8,128)(2,1)} async-done(((bf16[8,32,2048]{2,1,0:T(8,128)(2,1)}), bf16[8,32,2048]{2,1,0:T(8,128)(2,1)}, u32[]{:S(2)}, u32[]{:S(2)}) %all-to-all-start) | async-done | bytes 1048608 | tf_op jit(solution)/shard_map/all_to_all | solution.py:58
  37.5 4.3 %all-to-all-start.1 = ((bf16[8,32,2048]{2,1,0:T(8,128)(2,1)}), bf16[8,32,2048]{2,1,0:T(8,128)(2,1)}, u32[]{:S(2)}, u32[]{:S(2)}) async-start(bf16[8,32,2048]{2,1,0:T(8,128)(2,1)} %bitcast.74), calls=%async_computation.1 | async-start | bytes 2097152 | tf_op jit(solution)/shard_map/all_to_all | solution.py:58
  41.8 0.1 pad.1.clone
  41.9 0.1 pad.3.clone
  41.9 0.1 pad.2.clone
  42.0 0.9 compare_select_fusion
  42.9 2.8 %dynamic-slice_bitcast_fusion = (bf16[192,2048]{1,0:T(8,128)(2,1)}, bf16[192,2048]{1,0:T(8,128)(2,1)}) fusion(bf16[1,768,2048]{2,1,0:T(8,128)(2,1)} %param.11, s32[]{:T(128)S(6)} %select_n.28, bf16[1,768,2048]{2,1,0:T(8,128)(2,1)} %param.10), kind=kLoop, calls=%fused_computation.37 | loop fusion | bytes 3145732 | tf_op jit(solution)/shard_map/dynamic_slice | solution.py:152
  45.7 1.5 %collective-permute-start.2 = (bf16[256,2048]{1,0:T(8,128)(2,1)}, bf16[256,2048]{1,0:T(8,128)(2,1)}, u32[]{:S(2)}, u32[]{:S(2)}) collective-permute-start(bf16[256,2048]{1,0:T(8,128)(2,1)} %bitcast.5), channel_id=1, source_target_pairs={{0,16},{8,24},{16,0},{24,8},{1,17},{9,25},{17,1},{25,9},{2,18},{10... | collective-permute-start | bytes 3145736 | tf_op jit(solution)/shard_map/ppermute | solution.py:73
  47.2 0.0 collective-permute-start
  47.2 4.0 %fusion.1 = f32[256,1536]{1,0:T(8,128)S(1)} fusion(bf16[256,2048]{1,0:T(8,128)(2,1)} %bitcast.5, bf16[768,2048]{1,0:T(8,128)(2,1)S(1)} %bitcast.78, bf16[768,2048]{1,0:T(8,128)(2,1)} %bitcast.80), kind=kOutput, calls=%fused_computation.2 | convolution fusion | flops 1623195648 | bytes 8912896 | tf_op jit(solution)/shard_map/dot_general | solution.py:15
  51.2 1.2 copy-done.11
  52.4 2.0 %fusion.9 = bf16[256,2048]{1,0:T(8,128)(2,1)} fusion(bf16[1,768,2048]{2,1,0:T(8,128)(2,1)S(1)} %copy-done, f32[256,1536]{1,0:T(8,128)S(1)} %fusion.1), kind=kOutput, calls=%fused_computation.16 | convolution fusion | flops 807010304 | bytes 5767168 | tf_op jit(solution)/shard_map/dot_general | solution.py:27
  54.4 12.9 %all-to-all-done.1 = bf16[8,32,2048]{2,1,0:T(8,128)(2,1)} async-done(((bf16[8,32,2048]{2,1,0:T(8,128)(2,1)}), bf16[8,32,2048]{2,1,0:T(8,128)(2,1)}, u32[]{:S(2)}, u32[]{:S(2)}) %all-to-all-start.1) | async-done | bytes 1048608 | tf_op jit(solution)/shard_map/all_to_all | solution.py:58
  67.3 4.2 %all-to-all-start.2 = ((bf16[8,32,2048]{2,1,0:T(8,128)(2,1)}), bf16[8,32,2048]{2,1,0:T(8,128)(2,1)}, u32[]{:S(2)}, u32[]{:S(2)}) async-start(bf16[8,32,2048]{2,1,0:T(8,128)(2,1)} %bitcast.77), calls=%async_computation.2 | async-start | bytes 2097152 | tf_op jit(solution)/shard_map/all_to_all | solution.py:94
  71.6 0.0 copy-start.9
  71.6 0.0 copy-start.10
  71.6 3.0 %multiply_convert_fusion.1 = (bf16[256,768]{1,0:T(8,128)(2,1)S(1)}, bf16[256,768]{1,0:T(8,128)(2,1)S(1)}) fusion(f32[256,1536]{1,0:T(8,128)} %copy-done.11, bf16[256,2048]{1,0:T(8,128)(2,1)} %bitcast.10, bf16[1,768,2048]{2,1,0:T(8,128)(2,1)S(1)} %copy-done), kind=kOutput, calls=%fused_computation.40 | convolution fusion | flops 807862272 | bytes 6553600 | tf_op jit(solution)/shard_map/dot_general | solution.py:15
  74.7 0.6 copy-done.10
  75.2 2.8 %fusion.7 = bf16[256,2048]{1,0:T(8,128)(2,1)} fusion(bf16[768,2048]{1,0:T(8,128)(2,1)S(1)} %bitcast.79, bf16[768,2048]{1,0:T(8,128)(2,1)S(1)} %bitcast.81, bf16[256,768]{1,0:T(8,128)(2,1)S(1)} %get-tuple-element.35, bf16[256,768]{1,0:T(8,128)(2,1)S(1)} %get-tuple-element.34), kind=kOutput, calls=%fused_computation.12 | convolution fusion | flops 1625292800 | bytes 8126464 | tf_op jit(solution)/shard_map/dot_general | solution.py:27
  78.1 1.5 %collective-permute-start.3 = (bf16[256,2048]{1,0:T(8,128)(2,1)}, bf16[256,2048]{1,0:T(8,128)(2,1)}, u32[]{:S(2)}, u32[]{:S(2)}) collective-permute-start(bf16[256,2048]{1,0:T(8,128)(2,1)} %bitcast.10), channel_id=1, source_target_pairs={{0,16},{8,24},{16,0},{24,8},{1,17},{9,25},{17,1},{25,9},{2,18},{10... | collective-permute-start | bytes 3145736 | tf_op jit(solution)/shard_map/ppermute | solution.py:73
  79.6 0.0 collective-permute-start.1
  79.6 1.8 %fusion.84 = f32[256,384]{0,1:T(8,128)S(1)} fusion(bf16[256,2048]{1,0:T(8,128)(2,1)} %bitcast.5, bf16[192,2048]{1,0:T(8,128)(2,1)S(1)} %copy-done.4, bf16[192,2048]{1,0:T(8,128)(2,1)S(1)} %copy-done.6), kind=kOutput, calls=%fused_computation.118 | convolution fusion | flops 405798912 | bytes 3014656 | tf_op jit(solution)/shard_map/dot_general | solution.py:15
  81.4 1.7 %multiply_convert_fusion.15 = (bf16[256,192]{0,1:T(8,128)(2,1)S(1)}, bf16[256,192]{0,1:T(8,128)(2,1)S(1)}) fusion(f32[256,384]{0,1:T(8,128)S(1)} %fusion.84, bf16[256,2048]{1,0:T(8,128)(2,1)} %bitcast.10, bf16[1,768,2048]{2,1,0:T(8,128)(2,1)S(1)} %copy-done, s32[]{:T(128)S(6)} %select_n.28), kind=kOutput, calls=%fused_computation.86 | convolution fusion | flops 201965568 | bytes 2424836 | tf_op jit(solution)/shard_map/dot_general | solution.py:15
  83.2 2.8 %fusion.58 = f32[192,2048]{1,0:T(8,128)} fusion(bf16[256,2048]{1,0:T(8,128)(2,1)} %bitcast.10, f32[256,384]{0,1:T(8,128)S(1)} %fusion.84), kind=kOutput, calls=%fused_computation.93 | convolution fusion | flops 201621504 | bytes 3014656 | tf_op jit(solution)/shard_map/dot_general | solution.py:21
  85.9 3.4 %fusion.32 = f32[384,2048]{1,0:T(8,128)} fusion(bf16[256,2048]{1,0:T(8,128)(2,1)} %bitcast.5, bf16[256,192]{0,1:T(8,128)(2,1)S(1)} %get-tuple-element.43, bf16[256,192]{0,1:T(8,128)(2,1)S(1)} %get-tuple-element.42), kind=kOutput, calls=%fused_computation.53 | convolution fusion | flops 403046400 | bytes 4390912 | tf_op jit(solution)/shard_map/dot_general | solution.py:21
  89.4 7.6 %all-to-all-done.2 = bf16[8,32,2048]{2,1,0:T(8,128)(2,1)} async-done(((bf16[8,32,2048]{2,1,0:T(8,128)(2,1)}), bf16[8,32,2048]{2,1,0:T(8,128)(2,1)}, u32[]{:S(2)}, u32[]{:S(2)}) %all-to-all-start.2) | async-done | bytes 1048608 | tf_op jit(solution)/shard_map/all_to_all | solution.py:94
  97.0 4.4 %all-to-all-start.3 = ((bf16[8,32,2048]{2,1,0:T(8,128)(2,1)}), bf16[8,32,2048]{2,1,0:T(8,128)(2,1)}, u32[]{:S(2)}, u32[]{:S(2)}) async-start(bf16[8,32,2048]{2,1,0:T(8,128)(2,1)} %bitcast.76), calls=%async_computation.3 | async-start | bytes 2097152 | tf_op jit(solution)/shard_map/all_to_all | solution.py:112
  101.4 0.0 copy-start.5
  101.4 0.0 copy-start.7
  101.4 0.0 collective-permute-done
  101.5 0.0 collective-permute-done.1
  101.5 2.8 %broadcast_multiply_fusion = (bf16[256,2048]{1,0:T(8,128)(2,1)}, f32[256,2048]{1,0:T(8,128)S(1)}) fusion(f32[256]{0:T(256)S(1)} %bitcast.85, bf16[256,2048]{1,0:T(8,128)(2,1)} %bitcast.12, s32[256]{0:T(256)S(1)} %bitcast.82), kind=kOutput, calls=%fused_computation.23 | convolution fusion | flops 269549568 | bytes 4196352 | tf_op jit(solution)/shard_map/dot_general | solution.py:27
  104.3 0.0 collective-permute-done.2
  104.3 0.0 collective-permute-done.3
  104.3 1.8 %fusion.82 = f32[256,384]{0,1:T(8,128)S(1)} fusion(bf16[256,2048]{1,0:T(8,128)(2,1)} %collective-permute-done.2, bf16[192,2048]{1,0:T(8,128)(2,1)S(1)} %copy-done.5, bf16[192,2048]{1,0:T(8,128)(2,1)S(1)} %copy-done.7), kind=kOutput, calls=%fused_computation.116 | convolution fusion | flops 405798912 | bytes 3014656 | tf_op jit(solution)/shard_map/dot_general | solution.py:15
  106.1 0.1 collective-permute-start.5
  106.2 1.8 %fusion.83 = f32[256,384]{0,1:T(8,128)S(1)} fusion(bf16[256,2048]{1,0:T(8,128)(2,1)} %collective-permute-done, bf16[192,2048]{1,0:T(8,128)(2,1)S(1)} %copy-done.5, bf16[192,2048]{1,0:T(8,128)(2,1)S(1)} %copy-done.7), kind=kOutput, calls=%fused_computation.117 | convolution fusion | flops 405798912 | bytes 3014656 | tf_op jit(solution)/shard_map/dot_general | solution.py:15
  108.0 0.6 collective-permute-start.4
  108.6 1.7 %multiply_convert_fusion.11 = (bf16[256,192]{0,1:T(8,128)(2,1)S(1)}, bf16[256,192]{0,1:T(8,128)(2,1)S(1)}) fusion(f32[256,384]{0,1:T(8,128)S(1)} %fusion.82, bf16[256,2048]{1,0:T(8,128)(2,1)} %collective-permute-done.3, bf16[1,768,2048]{2,1,0:T(8,128)(2,1)S(1)} %copy-done, s32[]{:T(128)S(6)} %select_n.28), kind=kOutput, calls=%fused_computation.78 | convolution fusion | flops 201965568 | bytes 2424836 | tf_op jit(solution)/shard_map/dot_general | solution.py:15
  110.3 0.0 copy-start.3
  110.3 1.8 %multiply_convert_fusion.13 = (bf16[256,192]{0,1:T(8,128)(2,1)S(1)}, bf16[256,192]{0,1:T(8,128)(2,1)S(1)}) fusion(f32[256,384]{0,1:T(8,128)S(1)} %fusion.83, bf16[256,2048]{1,0:T(8,128)(2,1)} %collective-permute-done.1, bf16[1,768,2048]{2,1,0:T(8,128)(2,1)S(1)} %copy-done, s32[]{:T(128)S(6)} %select_n.28), kind=kOutput, calls=%fused_computation.82 | convolution fusion | flops 201965568 | bytes 2424836 | tf_op jit(solution)/shard_map/dot_general | solution.py:15
  112.2 1.8 %fusion.36 = f32[384,2048]{1,0:T(8,128)S(1)} fusion(bf16[256,2048]{1,0:T(8,128)(2,1)} %collective-permute-done, bf16[256,192]{0,1:T(8,128)(2,1)S(1)} %get-tuple-element.41, bf16[256,192]{0,1:T(8,128)(2,1)S(1)} %get-tuple-element.40), kind=kOutput, calls=%fused_computation.57 | convolution fusion | flops 403046400 | bytes 4390912 | tf_op jit(solution)/shard_map/dot_general | solution.py:21
  114.0 0.3 multiply_reduce_fusion
  114.3 0.7 maximum_maximum_fusion
  115.0 1.8 %fusion.40 = f32[384,2048]{1,0:T(8,128)S(1)} fusion(bf16[256,2048]{1,0:T(8,128)(2,1)} %collective-permute-done.2, bf16[256,192]{0,1:T(8,128)(2,1)S(1)} %get-tuple-element.45, bf16[256,192]{0,1:T(8,128)(2,1)S(1)} %get-tuple-element.44), kind=kOutput, calls=%fused_computation.61 | convolution fusion | flops 403046400 | bytes 4390912 | tf_op jit(solution)/shard_map/dot_general | solution.py:21
  116.8 1.6 %convolution_add_fusion.1 = f32[192,2048]{1,0:T(8,128)S(1)} fusion(f32[192,2048]{1,0:T(8,128)S(1)} %copy-done.2, bf16[256,2048]{1,0:T(8,128)(2,1)} %collective-permute-done.1, f32[256,384]{0,1:T(8,128)S(1)} %fusion.83), kind=kOutput, calls=%fused_computation.10 | convolution fusion | flops 202014720 | bytes 4587520 | tf_op jit(solution)/shard_map/dot_general | solution.py:21
  118.4 0.0 collective-permute-done.5
  118.4 0.6 fusion.81
  119.0 0.0 collective-permute-done.4
  119.1 0.5 multiply_convert_fusion.9
  119.6 0.4 fusion.59
  120.0 2.7 %fusion.13 = bf16[1,192,2048]{2,1,0:T(8,128)(2,1)} fusion(f32[192,2048]{1,0:T(8,128)S(1)} %fusion.59, f32[192,2048]{1,0:T(8,128)S(1)} %convolution_add_fusion.1, bf16[256,2048]{1,0:T(8,128)(2,1)} %collective-permute-done.3, f32[256,384]{0,1:T(8,128)S(1)} %fusion.82), kind=kOutput, calls=%fused_computation.18 | convolution fusion | flops 202801152 | bytes 5373952 | tf_op jit(solution)/shard_map/dot_general | solution.py:21
  122.7 0.6 add_convert_fusion
  123.3 1.2 slice_bitcast_fusion
  124.5 2.1 %all-to-all-done.3 = bf16[8,32,2048]{2,1,0:T(8,128)(2,1)} async-done(((bf16[8,32,2048]{2,1,0:T(8,128)(2,1)}), bf16[8,32,2048]{2,1,0:T(8,128)(2,1)}, u32[]{:S(2)}, u32[]{:S(2)}) %all-to-all-start.3) | async-done | bytes 1048608 | tf_op jit(solution)/shard_map/all_to_all | solution.py:112
  126.6 2.7 %convolution_convert_fusion = bf16[256,2048]{1,0:T(8,128)(2,1)} fusion(bf16[256,2048]{1,0:T(8,128)(2,1)} %bitcast.14, s32[256]{0:T(256)S(1)} %bitcast.83), kind=kOutput, calls=%fused_computation.13 | convolution fusion | flops 269025280 | bytes 2098176 | tf_op jit(solution)/shard_map/dot_general | solution.py:27
  (20 shorter events, 0.0 us)
Async XLA Ops:
  0.6 51.8 %copy-start = (bf16[1,768,2048]{2,1,0:T(8,128)(2,1)S(1)}, bf16[1,768,2048]{2,1,0:T(8,128)(2,1)}, u32[]{:S(2)}) copy-start(bf16[1,768,2048]{2,1,0:T(8,128)(2,1)} %param.12) | copy-start | bytes 9437188
  4.4 33.1 %all-to-all-start = ((bf16[8,32,2048]{2,1,0:T(8,128)(2,1)}), bf16[8,32,2048]{2,1,0:T(8,128)(2,1)}, u32[]{:S(2)}, u32[]{:S(2)}) async-start(bf16[8,32,2048]{2,1,0:T(8,128)(2,1)} %bitcast.75), calls=%async_computation | async-start | bytes 2097152 | tf_op jit(solution)/shard_map/all_to_all | solution.py:58
  37.5 29.9 %all-to-all-start.1 = ((bf16[8,32,2048]{2,1,0:T(8,128)(2,1)}), bf16[8,32,2048]{2,1,0:T(8,128)(2,1)}, u32[]{:S(2)}, u32[]{:S(2)}) async-start(bf16[8,32,2048]{2,1,0:T(8,128)(2,1)} %bitcast.74), calls=%async_computation.1 | async-start | bytes 2097152 | tf_op jit(solution)/shard_map/all_to_all | solution.py:58
  42.0 5.2 %copy-start.8 = (bf16[1,768,2048]{2,1,0:T(8,128)(2,1)S(1)}, bf16[1,768,2048]{2,1,0:T(8,128)(2,1)}, u32[]{:S(2)}) copy-start(bf16[1,768,2048]{2,1,0:T(8,128)(2,1)} %param.11) | copy-start | bytes 9437188
  45.7 58.6 %collective-permute-start.2 = (bf16[256,2048]{1,0:T(8,128)(2,1)}, bf16[256,2048]{1,0:T(8,128)(2,1)}, u32[]{:S(2)}, u32[]{:S(2)}) collective-permute-start(bf16[256,2048]{1,0:T(8,128)(2,1)} %bitcast.5), channel_id=1, source_target_pairs={{0,16},{8,24},{16,0},{24,8},{1,17},{9,25},{17,1},{25,9},{2,18},{10... | collective-permute-start | bytes 3145736 | tf_op jit(solution)/shard_map/ppermute | solution.py:73
  47.2 54.3 %collective-permute-start = (bf16[256,2048]{1,0:T(8,128)(2,1)}, bf16[256,2048]{1,0:T(8,128)(2,1)}, u32[]{:S(2)}, u32[]{:S(2)}) collective-permute-start(bf16[256,2048]{1,0:T(8,128)(2,1)} %bitcast.5), channel_id=1, source_target_pairs={{0,8},{8,0},{16,24},{24,16},{1,9},{9,1},{17,25},{25,17},{2,10},{10... | collective-permute-start | bytes 3145736 | tf_op jit(solution)/shard_map/ppermute | solution.py:73
  51.2 1.2 copy-start.11
  67.3 29.6 %all-to-all-start.2 = ((bf16[8,32,2048]{2,1,0:T(8,128)(2,1)}), bf16[8,32,2048]{2,1,0:T(8,128)(2,1)}, u32[]{:S(2)}, u32[]{:S(2)}) async-start(bf16[8,32,2048]{2,1,0:T(8,128)(2,1)} %bitcast.77), calls=%async_computation.2 | async-start | bytes 2097152 | tf_op jit(solution)/shard_map/all_to_all | solution.py:94
  71.6 3.1 %copy-start.9 = (bf16[1,768,2048]{2,1,0:T(8,128)(2,1)S(1)}, bf16[1,768,2048]{2,1,0:T(8,128)(2,1)}, u32[]{:S(2)}) copy-start(bf16[1,768,2048]{2,1,0:T(8,128)(2,1)} %param.11) | copy-start | bytes 9437188
  71.6 3.6 %copy-start.10 = (bf16[1,768,2048]{2,1,0:T(8,128)(2,1)S(1)}, bf16[1,768,2048]{2,1,0:T(8,128)(2,1)}, u32[]{:S(2)}) copy-start(bf16[1,768,2048]{2,1,0:T(8,128)(2,1)} %param.10) | copy-start | bytes 9437188
  75.2 4.3 %copy-start.4 = (bf16[192,2048]{1,0:T(8,128)(2,1)S(1)}, bf16[192,2048]{1,0:T(8,128)(2,1)}, u32[]{:S(2)}) copy-start(bf16[192,2048]{1,0:T(8,128)(2,1)} %get-tuple-element.48) | copy-start | bytes 2359300
  75.2 4.3 %copy-start.6 = (bf16[192,2048]{1,0:T(8,128)(2,1)S(1)}, bf16[192,2048]{1,0:T(8,128)(2,1)}, u32[]{:S(2)}) copy-start(bf16[192,2048]{1,0:T(8,128)(2,1)} %get-tuple-element.49) | copy-start | bytes 2359300
  78.1 26.2 %collective-permute-start.3 = (bf16[256,2048]{1,0:T(8,128)(2,1)}, bf16[256,2048]{1,0:T(8,128)(2,1)}, u32[]{:S(2)}, u32[]{:S(2)}) collective-permute-start(bf16[256,2048]{1,0:T(8,128)(2,1)} %bitcast.10), channel_id=1, source_target_pairs={{0,16},{8,24},{16,0},{24,8},{1,17},{9,25},{17,1},{25,9},{2,18},{10... | collective-permute-start | bytes 3145736 | tf_op jit(solution)/shard_map/ppermute | solution.py:73
  79.6 21.9 %collective-permute-start.1 = (bf16[256,2048]{1,0:T(8,128)(2,1)}, bf16[256,2048]{1,0:T(8,128)(2,1)}, u32[]{:S(2)}, u32[]{:S(2)}) collective-permute-start(bf16[256,2048]{1,0:T(8,128)(2,1)} %bitcast.10), channel_id=1, source_target_pairs={{0,8},{8,0},{16,24},{24,16},{1,9},{9,1},{17,25},{25,17},{2,10},{10... | collective-permute-start | bytes 3145736 | tf_op jit(solution)/shard_map/ppermute | solution.py:73
  97.0 29.6 %all-to-all-start.3 = ((bf16[8,32,2048]{2,1,0:T(8,128)(2,1)}), bf16[8,32,2048]{2,1,0:T(8,128)(2,1)}, u32[]{:S(2)}, u32[]{:S(2)}) async-start(bf16[8,32,2048]{2,1,0:T(8,128)(2,1)} %bitcast.76), calls=%async_computation.3 | async-start | bytes 2097152 | tf_op jit(solution)/shard_map/all_to_all | solution.py:112
  101.4 2.9 %copy-start.5 = (bf16[192,2048]{1,0:T(8,128)(2,1)S(1)}, bf16[192,2048]{1,0:T(8,128)(2,1)}, u32[]{:S(2)}) copy-start(bf16[192,2048]{1,0:T(8,128)(2,1)} %get-tuple-element.48) | copy-start | bytes 2359300
  101.4 2.8 %copy-start.7 = (bf16[192,2048]{1,0:T(8,128)(2,1)S(1)}, bf16[192,2048]{1,0:T(8,128)(2,1)}, u32[]{:S(2)}) copy-start(bf16[192,2048]{1,0:T(8,128)(2,1)} %get-tuple-element.49) | copy-start | bytes 2359300
  106.1 12.3 %collective-permute-start.5 = (bf16[256,2048]{1,0:T(8,128)(2,1)}, bf16[256,2048]{1,0:T(8,128)(2,1)S(1)}, u32[]{:S(2)}, u32[]{:S(2)}) collective-permute-start(bf16[256,2048]{1,0:T(8,128)(2,1)} %collective-permute-done.2), channel_id=1, source_target_pairs={{0,8},{8,0},{16,24},{24,16},{1,9},{9,1},{17,25},{25,17},{2,10},{10... | collective-permute-start | bytes 3145736 | tf_op jit(solution)/shard_map/ppermute | solution.py:73
  108.0 11.0 %collective-permute-start.4 = (bf16[256,2048]{1,0:T(8,128)(2,1)}, bf16[256,2048]{1,0:T(8,128)(2,1)S(1)}, u32[]{:S(2)}, u32[]{:S(2)}) collective-permute-start(bf16[256,2048]{1,0:T(8,128)(2,1)} %collective-permute-done.3), channel_id=1, source_target_pairs={{0,8},{8,0},{16,24},{24,16},{1,9},{9,1},{17,25},{25,17},{2,10},{10... | collective-permute-start | bytes 3145736 | tf_op jit(solution)/shard_map/ppermute | solution.py:73
  110.3 3.7 %copy-start.3 = (bf16[256,2048]{1,0:T(8,128)(2,1)S(1)}, bf16[256,2048]{1,0:T(8,128)(2,1)}, u32[]{:S(2)}) copy-start(bf16[256,2048]{1,0:T(8,128)(2,1)} %param.13) | copy-start | bytes 3145732
  114.0 2.8 %copy-start.2 = (f32[192,2048]{1,0:T(8,128)S(1)}, f32[192,2048]{1,0:T(8,128)}, u32[]{:S(2)}) copy-start(f32[192,2048]{1,0:T(8,128)} %fusion.58) | copy-start | bytes 4718596
  120.0 2.7 %copy-start.1 = (f32[384,2048]{1,0:T(8,128)S(1)}, f32[384,2048]{1,0:T(8,128)}, u32[]{:S(2)}) copy-start(f32[384,2048]{1,0:T(8,128)} %fusion.32) | copy-start | bytes 9437188

commit v16 on v15

--- a/solution.py
+++ b/solution.py
@@ -173,7 +173,13 @@
     part_back, gate_w_grad, up_w_grad, down_w_grad = lax.optimization_barrier(
         (part_back, gate_w_grad, up_w_grad, down_w_grad)
     )
-    tokens_grad = matmul(back_pick, part_back).astype(jnp.bfloat16)
+    grad_total = jnp.zeros((tok_count, feature_width), jnp.float32)
+    for col in range(live_cols):
+        source_slot = jnp.where(slot_grid[:, col] < 0, total_slots, slot_grid[:, col])
+        grad_total = grad_total + jnp.take(
+            part_back, source_slot, axis=0, mode="fill", fill_value=0
+        ).astype(jnp.float32)
+    tokens_grad = grad_total.astype(jnp.bfloat16)
     return (layer_out, tokens_grad, gates_grad, gate_w_grad, up_w_grad, down_w_grad)
 
 

time: 130 us -> 135 us (1.038)
  local copies, waits for them, and re-layouts: 7.6 us -> 12.3 us
  matrix products: 49.9 us -> 47.2 us
  other arithmetic: 1.94 us -> 4.3 us
    gather x0 -> x1, local copies, waits for them, and re-layouts: none -> 4.69 us  [body(): jnp.take(part_back, source_slot, axis=0, mode='fill', fill_value=0)]
    dot_general x7 -> x6, matrix products: 15.8 us -> 13.1 us  [matmul(): return jnp.dot(left, right, preferred_element_type=jnp.float32)]
    select_n x0 -> x1, other arithmetic: none -> 2.33 us  [body(): jnp.take(part_back, source_slot, axis=0, mode='fill', fill_value=0)]
  transfers between devices with their start and end apart: 10 -> 10, of which waited for: 4 -> 4; matrix products, arithmetic and copies ran while one was open for 40% -> 38% of each run, Pallas kernels for 0% -> 0%
where the time goes in v16:
time: 135 us; the launch traced here: 134 us
  matrix products  47.2 us (35%)
  waiting for transfers between devices  45.1 us (33%)
  starting transfers between devices  23.8 us (18%)
  local copies, waits for them, and re-layouts  12.3 us (9%)
  other arithmetic  4.3 us (3%)
    all_to_all x2, waiting for transfers between devices, exchange(): lax.all_to_all(rows.reshape(experts, per_pair, feature_width), 'ep', spli...  35.4 us
    dot_general x10, matrix products, rows_times(): lax.dot_general(left, right, (((1,), (1,)), ((), ())), preferred_element_...  19 us
    dot_general x8, matrix products, inner_rows(): lax.dot_general(left, right, (((0,), (0,)), ((), ())), preferred_element_...  15.1 us
    dot_general x6, matrix products, matmul(): return jnp.dot(left, right, preferred_element_type=jnp.float32)  13.1 us
    all_to_all x2, starting transfers between devices, exchange(): lax.all_to_all(rows.reshape(experts, per_pair, feature_width), 'ep', spli...  11.5 us
    all_to_all x1, waiting for transfers between devices, body(): lax.all_to_all(expert_out.reshape(experts, per_pair, feature_width), 'ep'...  7.6 us
    gather x1, local copies, waits for them, and re-layouts, body(): jnp.take(part_back, source_slot, axis=0, mode='fill', fill_value=0)  4.69 us
    all_to_all x1, starting transfers between devices, body(): lax.all_to_all(token_part.reshape(experts, per_pair, feature_width), 'ep'...  4.41 us
  transfers between devices with their start and end apart: 10, of which 4 were waited for; matrix products, arithmetic and copies ran while one was open for 38% of the time, Pallas kernels for 0%

profile of v16, /device:TPU:0, one launch (start us, length us, event | category | flops | bytes accessed | tf_op | source)
XLA Modules:
  0.0 133.7 jit_solution(5199034054132368583)
XLA Ops:
  0.6 0.0 copy-start
  0.6 0.9 slice.45
  1.5 0.2 fusion.14
  1.7 2.6 %convolution_convert_fusion = bf16[256,2048]{1,0:T(8,128)(2,1)} fusion(bf16[256,2048]{1,0:T(8,128)(2,1)} %param.7, s32[256]{0:T(256)S(1)} %compare_select_fusion.3), kind=kOutput, calls=%fused_computation.14 | convolution fusion | flops 269025280 | bytes 2098176 | tf_op jit(solution)/shard_map/dot_general | solution.py:27
  4.4 7.3 %all-to-all-start = ((bf16[8,32,2048]{2,1,0:T(8,128)(2,1)}), bf16[8,32,2048]{2,1,0:T(8,128)(2,1)}, u32[]{:S(2)}, u32[]{:S(2)}) async-start(bf16[8,32,2048]{2,1,0:T(8,128)(2,1)} %bitcast.75), calls=%async_computation | async-start | bytes 2097152 | tf_op jit(solution)/shard_map/all_to_all | solution.py:58
  11.6 0.7 slice.44
  12.3 0.1 select_reduce_fusion
  12.4 2.6 %fusion.6 = bf16[256,2048]{1,0:T(8,128)(2,1)} fusion(bf16[256,2048]{1,0:T(8,128)(2,1)} %param.13, f32[256]{0:T(256)S(1)} %select_reduce_fusion, s32[256]{0:T(256)S(1)} %compare_select_fusion.3), kind=kOutput, calls=%fused_computation.12 | convolution fusion | flops 269549568 | bytes 2099200 | tf_op jit(solution)/shard_map/dot_general | solution.py:27
  15.1 22.4 %all-to-all-done = bf16[8,32,2048]{2,1,0:T(8,128)(2,1)} async-done(((bf16[8,32,2048]{2,1,0:T(8,128)(2,1)}), bf16[8,32,2048]{2,1,0:T(8,128)(2,1)}, u32[]{:S(2)}, u32[]{:S(2)}) %all-to-all-start) | async-done | bytes 1048608 | tf_op jit(solution)/shard_map/all_to_all | solution.py:58
  37.5 4.3 %all-to-all-start.1 = ((bf16[8,32,2048]{2,1,0:T(8,128)(2,1)}), bf16[8,32,2048]{2,1,0:T(8,128)(2,1)}, u32[]{:S(2)}, u32[]{:S(2)}) async-start(bf16[8,32,2048]{2,1,0:T(8,128)(2,1)} %bitcast.74), calls=%async_computation.1 | async-start | bytes 2097152 | tf_op jit(solution)/shard_map/all_to_all | solution.py:58
  41.8 0.1 pad.1.clone
  41.9 0.1 pad.3.clone
  41.9 0.1 pad.2.clone
  42.0 0.9 and_reduce_fusion
  42.9 2.8 %dynamic-slice_bitcast_fusion = (bf16[192,2048]{1,0:T(8,128)(2,1)}, bf16[192,2048]{1,0:T(8,128)(2,1)}) fusion(bf16[1,768,2048]{2,1,0:T(8,128)(2,1)} %param.11, s32[]{:T(128)S(6)} %select_n.49, bf16[1,768,2048]{2,1,0:T(8,128)(2,1)} %param.10), kind=kLoop, calls=%fused_computation.38 | loop fusion | bytes 3145732 | tf_op jit(solution)/shard_map/dynamic_slice | solution.py:152
  45.7 1.5 %collective-permute-start.2 = (bf16[256,2048]{1,0:T(8,128)(2,1)}, bf16[256,2048]{1,0:T(8,128)(2,1)}, u32[]{:S(2)}, u32[]{:S(2)}) collective-permute-start(bf16[256,2048]{1,0:T(8,128)(2,1)} %bitcast.5), channel_id=1, source_target_pairs={{0,16},{8,24},{16,0},{24,8},{1,17},{9,25},{17,1},{25,9},{2,18},{10... | collective-permute-start | bytes 3145736 | tf_op jit(solution)/shard_map/ppermute | solution.py:73
  47.2 0.0 collective-permute-start
  47.2 4.0 %fusion.1 = f32[256,1536]{1,0:T(8,128)S(1)} fusion(bf16[256,2048]{1,0:T(8,128)(2,1)} %bitcast.5, bf16[768,2048]{1,0:T(8,128)(2,1)S(1)} %bitcast.78, bf16[768,2048]{1,0:T(8,128)(2,1)} %bitcast.80), kind=kOutput, calls=%fused_computation.3 | convolution fusion | flops 1623195648 | bytes 8912896 | tf_op jit(solution)/shard_map/dot_general | solution.py:15
  51.2 1.2 copy-done.11
  52.4 2.0 %fusion.9 = bf16[256,2048]{1,0:T(8,128)(2,1)} fusion(bf16[1,768,2048]{2,1,0:T(8,128)(2,1)S(1)} %copy-done, f32[256,1536]{1,0:T(8,128)S(1)} %fusion.1), kind=kOutput, calls=%fused_computation.16 | convolution fusion | flops 807010304 | bytes 5767168 | tf_op jit(solution)/shard_map/dot_general | solution.py:27
  54.4 12.9 %all-to-all-done.1 = bf16[8,32,2048]{2,1,0:T(8,128)(2,1)} async-done(((bf16[8,32,2048]{2,1,0:T(8,128)(2,1)}), bf16[8,32,2048]{2,1,0:T(8,128)(2,1)}, u32[]{:S(2)}, u32[]{:S(2)}) %all-to-all-start.1) | async-done | bytes 1048608 | tf_op jit(solution)/shard_map/all_to_all | solution.py:58
  67.3 4.2 %all-to-all-start.2 = ((bf16[8,32,2048]{2,1,0:T(8,128)(2,1)}), bf16[8,32,2048]{2,1,0:T(8,128)(2,1)}, u32[]{:S(2)}, u32[]{:S(2)}) async-start(bf16[8,32,2048]{2,1,0:T(8,128)(2,1)} %bitcast.77), calls=%async_computation.2 | async-start | bytes 2097152 | tf_op jit(solution)/shard_map/all_to_all | solution.py:94
  71.6 0.0 copy-start.9
  71.6 0.0 copy-start.10
  71.6 3.0 %multiply_convert_fusion.1 = (bf16[256,768]{1,0:T(8,128)(2,1)S(1)}, bf16[256,768]{1,0:T(8,128)(2,1)S(1)}) fusion(f32[256,1536]{1,0:T(8,128)} %copy-done.11, bf16[256,2048]{1,0:T(8,128)(2,1)} %bitcast.10, bf16[1,768,2048]{2,1,0:T(8,128)(2,1)S(1)} %copy-done), kind=kOutput, calls=%fused_computation.41 | convolution fusion | flops 807862272 | bytes 6553600 | tf_op jit(solution)/shard_map/dot_general | solution.py:15
  74.7 0.6 copy-done.10
  75.2 2.8 %fusion.7 = bf16[256,2048]{1,0:T(8,128)(2,1)} fusion(bf16[768,2048]{1,0:T(8,128)(2,1)S(1)} %bitcast.79, bf16[768,2048]{1,0:T(8,128)(2,1)S(1)} %bitcast.81, bf16[256,768]{1,0:T(8,128)(2,1)S(1)} %get-tuple-element.38, bf16[256,768]{1,0:T(8,128)(2,1)S(1)} %get-tuple-element.37), kind=kOutput, calls=%fused_computation.13 | convolution fusion | flops 1625292800 | bytes 8126464 | tf_op jit(solution)/shard_map/dot_general | solution.py:27
  78.1 1.5 %collective-permute-start.3 = (bf16[256,2048]{1,0:T(8,128)(2,1)}, bf16[256,2048]{1,0:T(8,128)(2,1)}, u32[]{:S(2)}, u32[]{:S(2)}) collective-permute-start(bf16[256,2048]{1,0:T(8,128)(2,1)} %bitcast.10), channel_id=1, source_target_pairs={{0,16},{8,24},{16,0},{24,8},{1,17},{9,25},{17,1},{25,9},{2,18},{10... | collective-permute-start | bytes 3145736 | tf_op jit(solution)/shard_map/ppermute | solution.py:73
  79.6 0.0 collective-permute-start.1
  79.6 1.8 %fusion.83 = f32[256,384]{0,1:T(8,128)S(1)} fusion(bf16[256,2048]{1,0:T(8,128)(2,1)} %bitcast.5, bf16[192,2048]{1,0:T(8,128)(2,1)S(1)} %copy-done.4, bf16[192,2048]{1,0:T(8,128)(2,1)S(1)} %copy-done.6), kind=kOutput, calls=%fused_computation.122 | convolution fusion | flops 405798912 | bytes 3014656 | tf_op jit(solution)/shard_map/dot_general | solution.py:15
  81.4 1.7 %multiply_convert_fusion.15 = (bf16[256,192]{0,1:T(8,128)(2,1)S(1)}, bf16[256,192]{0,1:T(8,128)(2,1)S(1)}) fusion(f32[256,384]{0,1:T(8,128)S(1)} %fusion.83, bf16[256,2048]{1,0:T(8,128)(2,1)} %bitcast.10, bf16[1,768,2048]{2,1,0:T(8,128)(2,1)S(1)} %copy-done, s32[]{:T(128)S(6)} %select_n.49), kind=kOutput, calls=%fused_computation.87 | convolution fusion | flops 201965568 | bytes 2424836 | tf_op jit(solution)/shard_map/dot_general | solution.py:15
  83.2 2.8 %fusion.57 = f32[192,2048]{1,0:T(8,128)} fusion(bf16[256,2048]{1,0:T(8,128)(2,1)} %bitcast.10, f32[256,384]{0,1:T(8,128)S(1)} %fusion.83), kind=kOutput, calls=%fused_computation.93 | convolution fusion | flops 201621504 | bytes 3014656 | tf_op jit(solution)/shard_map/dot_general | solution.py:21
  86.0 3.4 %fusion.32 = f32[384,2048]{1,0:T(8,128)} fusion(bf16[256,2048]{1,0:T(8,128)(2,1)} %bitcast.5, bf16[256,192]{0,1:T(8,128)(2,1)S(1)} %get-tuple-element.46, bf16[256,192]{0,1:T(8,128)(2,1)S(1)} %get-tuple-element.45), kind=kOutput, calls=%fused_computation.54 | convolution fusion | flops 403046400 | bytes 4390912 | tf_op jit(solution)/shard_map/dot_general | solution.py:21
  89.4 7.6 %all-to-all-done.2 = bf16[8,32,2048]{2,1,0:T(8,128)(2,1)} async-done(((bf16[8,32,2048]{2,1,0:T(8,128)(2,1)}), bf16[8,32,2048]{2,1,0:T(8,128)(2,1)}, u32[]{:S(2)}, u32[]{:S(2)}) %all-to-all-start.2) | async-done | bytes 1048608 | tf_op jit(solution)/shard_map/all_to_all | solution.py:94
  97.0 4.4 %all-to-all-start.3 = ((bf16[8,32,2048]{2,1,0:T(8,128)(2,1)}), bf16[8,32,2048]{2,1,0:T(8,128)(2,1)}, u32[]{:S(2)}, u32[]{:S(2)}) async-start(bf16[8,32,2048]{2,1,0:T(8,128)(2,1)} %bitcast.76), calls=%async_computation.3 | async-start | bytes 2097152 | tf_op jit(solution)/shard_map/all_to_all | solution.py:112
  101.4 0.0 copy-start.5
  101.4 0.0 copy-start.7
  101.4 0.0 collective-permute-done
  101.5 0.0 collective-permute-done.1
  101.5 2.8 %broadcast_multiply_fusion = (bf16[256,2048]{1,0:T(8,128)(2,1)}, f32[256,2048]{1,0:T(8,128)S(1)}) fusion(f32[256]{0:T(256)S(1)} %bitcast.83, bf16[256,2048]{1,0:T(8,128)(2,1)} %bitcast.12, s32[256]{0:T(256)S(1)} %bitcast.89), kind=kOutput, calls=%fused_computation.23 | convolution fusion | flops 269549568 | bytes 4196352 | tf_op jit(solution)/shard_map/dot_general | solution.py:27
  104.3 0.0 collective-permute-done.2
  104.3 0.0 collective-permute-done.3
  104.3 1.8 %fusion.81 = f32[256,384]{0,1:T(8,128)S(1)} fusion(bf16[256,2048]{1,0:T(8,128)(2,1)} %collective-permute-done.2, bf16[192,2048]{1,0:T(8,128)(2,1)S(1)} %copy-done.5, bf16[192,2048]{1,0:T(8,128)(2,1)S(1)} %copy-done.7), kind=kOutput, calls=%fused_computation.120 | convolution fusion | flops 405798912 | bytes 3014656 | tf_op jit(solution)/shard_map/dot_general | solution.py:15
  106.1 0.1 collective-permute-start.5
  106.2 1.8 %fusion.82 = f32[256,384]{0,1:T(8,128)S(1)} fusion(bf16[256,2048]{1,0:T(8,128)(2,1)} %collective-permute-done, bf16[192,2048]{1,0:T(8,128)(2,1)S(1)} %copy-done.5, bf16[192,2048]{1,0:T(8,128)(2,1)S(1)} %copy-done.7), kind=kOutput, calls=%fused_computation.121 | convolution fusion | flops 405798912 | bytes 3014656 | tf_op jit(solution)/shard_map/dot_general | solution.py:15
  108.0 0.6 collective-permute-start.4
  108.6 1.7 %multiply_convert_fusion.11 = (bf16[256,192]{0,1:T(8,128)(2,1)S(1)}, bf16[256,192]{0,1:T(8,128)(2,1)S(1)}) fusion(f32[256,384]{0,1:T(8,128)S(1)} %fusion.81, bf16[256,2048]{1,0:T(8,128)(2,1)} %collective-permute-done.3, bf16[1,768,2048]{2,1,0:T(8,128)(2,1)S(1)} %copy-done, s32[]{:T(128)S(6)} %select_n.49), kind=kOutput, calls=%fused_computation.79 | convolution fusion | flops 201965568 | bytes 2424836 | tf_op jit(solution)/shard_map/dot_general | solution.py:15
  110.3 0.0 copy-start.3
  110.3 1.8 %multiply_convert_fusion.13 = (bf16[256,192]{0,1:T(8,128)(2,1)S(1)}, bf16[256,192]{0,1:T(8,128)(2,1)S(1)}) fusion(f32[256,384]{0,1:T(8,128)S(1)} %fusion.82, bf16[256,2048]{1,0:T(8,128)(2,1)} %collective-permute-done.1, bf16[1,768,2048]{2,1,0:T(8,128)(2,1)S(1)} %copy-done, s32[]{:T(128)S(6)} %select_n.49), kind=kOutput, calls=%fused_computation.83 | convolution fusion | flops 201965568 | bytes 2424836 | tf_op jit(solution)/shard_map/dot_general | solution.py:15
  112.2 1.8 %fusion.36 = f32[384,2048]{1,0:T(8,128)S(1)} fusion(bf16[256,2048]{1,0:T(8,128)(2,1)} %collective-permute-done, bf16[256,192]{0,1:T(8,128)(2,1)S(1)} %get-tuple-element.44, bf16[256,192]{0,1:T(8,128)(2,1)S(1)} %get-tuple-element.43), kind=kOutput, calls=%fused_computation.58 | convolution fusion | flops 403046400 | bytes 4390912 | tf_op jit(solution)/shard_map/dot_general | solution.py:21
  114.0 0.3 multiply_reduce_fusion
  114.3 0.7 maximum_maximum_fusion
  115.0 1.8 %fusion.40 = f32[384,2048]{1,0:T(8,128)S(1)} fusion(bf16[256,2048]{1,0:T(8,128)(2,1)} %collective-permute-done.2, bf16[256,192]{0,1:T(8,128)(2,1)S(1)} %get-tuple-element.48, bf16[256,192]{0,1:T(8,128)(2,1)S(1)} %get-tuple-element.47), kind=kOutput, calls=%fused_computation.62 | convolution fusion | flops 403046400 | bytes 4390912 | tf_op jit(solution)/shard_map/dot_general | solution.py:21
  116.8 1.6 %convolution_add_fusion.1 = f32[192,2048]{1,0:T(8,128)S(1)} fusion(f32[192,2048]{1,0:T(8,128)S(1)} %copy-done.2, bf16[256,2048]{1,0:T(8,128)(2,1)} %collective-permute-done.1, f32[256,384]{0,1:T(8,128)S(1)} %fusion.82), kind=kOutput, calls=%fused_computation.11 | convolution fusion | flops 202014720 | bytes 4587520 | tf_op jit(solution)/shard_map/dot_general | solution.py:21
  118.4 0.0 collective-permute-done.5
  118.4 0.6 fusion.80
  119.1 0.5 multiply_convert_fusion.9
  119.6 0.4 fusion.58
  120.0 2.7 %fusion.13 = bf16[1,192,2048]{2,1,0:T(8,128)(2,1)} fusion(f32[192,2048]{1,0:T(8,128)S(1)} %fusion.58, f32[192,2048]{1,0:T(8,128)S(1)} %convolution_add_fusion.1, bf16[256,2048]{1,0:T(8,128)(2,1)} %collective-permute-done.3, f32[256,384]{0,1:T(8,128)S(1)} %fusion.81), kind=kOutput, calls=%fused_computation.18 | convolution fusion | flops 202801152 | bytes 5373952 | tf_op jit(solution)/shard_map/dot_general | solution.py:21
  122.7 0.6 add_convert_fusion
  123.3 1.2 slice_bitcast_fusion
  124.5 2.1 %all-to-all-done.3 = bf16[8,32,2048]{2,1,0:T(8,128)(2,1)} async-done(((bf16[8,32,2048]{2,1,0:T(8,128)(2,1)}), bf16[8,32,2048]{2,1,0:T(8,128)(2,1)}, u32[]{:S(2)}, u32[]{:S(2)}) %all-to-all-start.3) | async-done | bytes 1048608 | tf_op jit(solution)/shard_map/all_to_all | solution.py:112
  126.6 4.7 %gather_fusion = bf16[256,2048]{1,0:T(8,128)(2,1)} fusion(bf16[256,2048]{1,0:T(8,128)(2,1)} %bitcast.14, s32[1024]{0:T(1024)S(1)} %pad_clamp_fusion), kind=kCustom, calls=%fused_computation | custom fusion | bytes 2098176 | tf_op jit(solution)/shard_map/jit(_take)/gather | solution.py:179
  131.3 2.3 %broadcast_select_fusion = bf16[256,2048]{1,0:T(8,128)(2,1)} fusion(bf16[256,2048]{1,0:T(8,128)(2,1)} %gather_fusion, pred[256]{0:T(512)(128)(4,1)S(1)} %get-tuple-element.34), kind=kLoop, calls=%fused_computation.24 | loop fusion | flops 524288 | bytes 2097408 | tf_op jit(solution)/shard_map/jit(_take)/select_n | solution.py:179
  (22 shorter events, 0.1 us)
Async XLA Ops:
  0.6 51.8 %copy-start = (bf16[1,768,2048]{2,1,0:T(8,128)(2,1)S(1)}, bf16[1,768,2048]{2,1,0:T(8,128)(2,1)}, u32[]{:S(2)}) copy-start(bf16[1,768,2048]{2,1,0:T(8,128)(2,1)} %param.12) | copy-start | bytes 9437188
  4.4 33.1 %all-to-all-start = ((bf16[8,32,2048]{2,1,0:T(8,128)(2,1)}), bf16[8,32,2048]{2,1,0:T(8,128)(2,1)}, u32[]{:S(2)}, u32[]{:S(2)}) async-start(bf16[8,32,2048]{2,1,0:T(8,128)(2,1)} %bitcast.75), calls=%async_computation | async-start | bytes 2097152 | tf_op jit(solution)/shard_map/all_to_all | solution.py:58
  37.5 29.9 %all-to-all-start.1 = ((bf16[8,32,2048]{2,1,0:T(8,128)(2,1)}), bf16[8,32,2048]{2,1,0:T(8,128)(2,1)}, u32[]{:S(2)}, u32[]{:S(2)}) async-start(bf16[8,32,2048]{2,1,0:T(8,128)(2,1)} %bitcast.74), calls=%async_computation.1 | async-start | bytes 2097152 | tf_op jit(solution)/shard_map/all_to_all | solution.py:58
  42.0 5.2 %copy-start.8 = (bf16[1,768,2048]{2,1,0:T(8,128)(2,1)S(1)}, bf16[1,768,2048]{2,1,0:T(8,128)(2,1)}, u32[]{:S(2)}) copy-start(bf16[1,768,2048]{2,1,0:T(8,128)(2,1)} %param.11) | copy-start | bytes 9437188
  45.7 58.6 %collective-permute-start.2 = (bf16[256,2048]{1,0:T(8,128)(2,1)}, bf16[256,2048]{1,0:T(8,128)(2,1)}, u32[]{:S(2)}, u32[]{:S(2)}) collective-permute-start(bf16[256,2048]{1,0:T(8,128)(2,1)} %bitcast.5), channel_id=1, source_target_pairs={{0,16},{8,24},{16,0},{24,8},{1,17},{9,25},{17,1},{25,9},{2,18},{10... | collective-permute-start | bytes 3145736 | tf_op jit(solution)/shard_map/ppermute | solution.py:73
  47.2 54.3 %collective-permute-start = (bf16[256,2048]{1,0:T(8,128)(2,1)}, bf16[256,2048]{1,0:T(8,128)(2,1)}, u32[]{:S(2)}, u32[]{:S(2)}) collective-permute-start(bf16[256,2048]{1,0:T(8,128)(2,1)} %bitcast.5), channel_id=1, source_target_pairs={{0,8},{8,0},{16,24},{24,16},{1,9},{9,1},{17,25},{25,17},{2,10},{10... | collective-permute-start | bytes 3145736 | tf_op jit(solution)/shard_map/ppermute | solution.py:73
  51.2 1.2 copy-start.11
  67.3 29.6 %all-to-all-start.2 = ((bf16[8,32,2048]{2,1,0:T(8,128)(2,1)}), bf16[8,32,2048]{2,1,0:T(8,128)(2,1)}, u32[]{:S(2)}, u32[]{:S(2)}) async-start(bf16[8,32,2048]{2,1,0:T(8,128)(2,1)} %bitcast.77), calls=%async_computation.2 | async-start | bytes 2097152 | tf_op jit(solution)/shard_map/all_to_all | solution.py:94
  71.6 3.1 %copy-start.9 = (bf16[1,768,2048]{2,1,0:T(8,128)(2,1)S(1)}, bf16[1,768,2048]{2,1,0:T(8,128)(2,1)}, u32[]{:S(2)}) copy-start(bf16[1,768,2048]{2,1,0:T(8,128)(2,1)} %param.11) | copy-start | bytes 9437188
  71.6 3.6 %copy-start.10 = (bf16[1,768,2048]{2,1,0:T(8,128)(2,1)S(1)}, bf16[1,768,2048]{2,1,0:T(8,128)(2,1)}, u32[]{:S(2)}) copy-start(bf16[1,768,2048]{2,1,0:T(8,128)(2,1)} %param.10) | copy-start | bytes 9437188
  75.2 4.3 %copy-start.4 = (bf16[192,2048]{1,0:T(8,128)(2,1)S(1)}, bf16[192,2048]{1,0:T(8,128)(2,1)}, u32[]{:S(2)}) copy-start(bf16[192,2048]{1,0:T(8,128)(2,1)} %get-tuple-element.51) | copy-start | bytes 2359300
  75.2 4.3 %copy-start.6 = (bf16[192,2048]{1,0:T(8,128)(2,1)S(1)}, bf16[192,2048]{1,0:T(8,128)(2,1)}, u32[]{:S(2)}) copy-start(bf16[192,2048]{1,0:T(8,128)(2,1)} %get-tuple-element.52) | copy-start | bytes 2359300
  78.1 26.2 %collective-permute-start.3 = (bf16[256,2048]{1,0:T(8,128)(2,1)}, bf16[256,2048]{1,0:T(8,128)(2,1)}, u32[]{:S(2)}, u32[]{:S(2)}) collective-permute-start(bf16[256,2048]{1,0:T(8,128)(2,1)} %bitcast.10), channel_id=1, source_target_pairs={{0,16},{8,24},{16,0},{24,8},{1,17},{9,25},{17,1},{25,9},{2,18},{10... | collective-permute-start | bytes 3145736 | tf_op jit(solution)/shard_map/ppermute | solution.py:73
  79.6 21.9 %collective-permute-start.1 = (bf16[256,2048]{1,0:T(8,128)(2,1)}, bf16[256,2048]{1,0:T(8,128)(2,1)}, u32[]{:S(2)}, u32[]{:S(2)}) collective-permute-start(bf16[256,2048]{1,0:T(8,128)(2,1)} %bitcast.10), channel_id=1, source_target_pairs={{0,8},{8,0},{16,24},{24,16},{1,9},{9,1},{17,25},{25,17},{2,10},{10... | collective-permute-start | bytes 3145736 | tf_op jit(solution)/shard_map/ppermute | solution.py:73
  97.0 29.6 %all-to-all-start.3 = ((bf16[8,32,2048]{2,1,0:T(8,128)(2,1)}), bf16[8,32,2048]{2,1,0:T(8,128)(2,1)}, u32[]{:S(2)}, u32[]{:S(2)}) async-start(bf16[8,32,2048]{2,1,0:T(8,128)(2,1)} %bitcast.76), calls=%async_computation.3 | async-start | bytes 2097152 | tf_op jit(solution)/shard_map/all_to_all | solution.py:112
  101.4 2.8 %copy-start.5 = (bf16[192,2048]{1,0:T(8,128)(2,1)S(1)}, bf16[192,2048]{1,0:T(8,128)(2,1)}, u32[]{:S(2)}) copy-start(bf16[192,2048]{1,0:T(8,128)(2,1)} %get-tuple-element.51) | copy-start | bytes 2359300
  101.4 2.8 %copy-start.7 = (bf16[192,2048]{1,0:T(8,128)(2,1)S(1)}, bf16[192,2048]{1,0:T(8,128)(2,1)}, u32[]{:S(2)}) copy-start(bf16[192,2048]{1,0:T(8,128)(2,1)} %get-tuple-element.52) | copy-start | bytes 2359300
  106.1 12.3 %collective-permute-start.5 = (bf16[256,2048]{1,0:T(8,128)(2,1)}, bf16[256,2048]{1,0:T(8,128)(2,1)S(1)}, u32[]{:S(2)}, u32[]{:S(2)}) collective-permute-start(bf16[256,2048]{1,0:T(8,128)(2,1)} %collective-permute-done.2), channel_id=1, source_target_pairs={{0,8},{8,0},{16,24},{24,16},{1,9},{9,1},{17,25},{25,17},{2,10},{10... | collective-permute-start | bytes 3145736 | tf_op jit(solution)/shard_map/ppermute | solution.py:73
  108.0 11.0 %collective-permute-start.4 = (bf16[256,2048]{1,0:T(8,128)(2,1)}, bf16[256,2048]{1,0:T(8,128)(2,1)S(1)}, u32[]{:S(2)}, u32[]{:S(2)}) collective-permute-start(bf16[256,2048]{1,0:T(8,128)(2,1)} %collective-permute-done.3), channel_id=1, source_target_pairs={{0,8},{8,0},{16,24},{24,16},{1,9},{9,1},{17,25},{25,17},{2,10},{10... | collective-permute-start | bytes 3145736 | tf_op jit(solution)/shard_map/ppermute | solution.py:73
  110.3 3.7 %copy-start.3 = (bf16[256,2048]{1,0:T(8,128)(2,1)S(1)}, bf16[256,2048]{1,0:T(8,128)(2,1)}, u32[]{:S(2)}) copy-start(bf16[256,2048]{1,0:T(8,128)(2,1)} %param.13) | copy-start | bytes 3145732
  114.0 2.8 %copy-start.2 = (f32[192,2048]{1,0:T(8,128)S(1)}, f32[192,2048]{1,0:T(8,128)}, u32[]{:S(2)}) copy-start(f32[192,2048]{1,0:T(8,128)} %fusion.57) | copy-start | bytes 4718596
  120.0 2.7 %copy-start.1 = (f32[384,2048]{1,0:T(8,128)S(1)}, f32[384,2048]{1,0:T(8,128)}, u32[]{:S(2)}) copy-start(f32[384,2048]{1,0:T(8,128)} %fusion.32) | copy-start | bytes 9437188

commit v17 on v15

--- a/solution.py
+++ b/solution.py
@@ -50,7 +50,7 @@
     hit = slot_ids[:, None] == slot_index[None, :]
     slot_gate = jnp.sum(jnp.where(hit, flat_gates[None, :], 0.0), axis=1)
     pick = jnp.any(hit.reshape(total_slots, tok_count, live_cols), axis=2).astype(jnp.bfloat16)
-    send_rows = matmul(pick, tokens).astype(jnp.bfloat16)
+    send_rows = jnp.dot(pick, tokens, preferred_element_type=jnp.bfloat16)
     grad_rows = matmul(pick, out_grad)
     scaled_grad = (slot_gate[:, None] * grad_rows).astype(jnp.bfloat16)
 
@@ -173,7 +173,7 @@
     part_back, gate_w_grad, up_w_grad, down_w_grad = lax.optimization_barrier(
         (part_back, gate_w_grad, up_w_grad, down_w_grad)
     )
-    tokens_grad = matmul(back_pick, part_back).astype(jnp.bfloat16)
+    tokens_grad = jnp.dot(back_pick, part_back, preferred_element_type=jnp.bfloat16)
     return (layer_out, tokens_grad, gates_grad, gate_w_grad, up_w_grad, down_w_grad)
 
 

time: 130 us -> 130 us (level)
    dot_general x0 -> x2, matrix products: none -> 5.35 us  [the longest x1 2.68 us: body(): jnp.dot(back_pick, part_back, preferred_element_type=jnp.bfloat16)]
    dot_general x7 -> x5, matrix products: 15.8 us -> 10.5 us  [matmul(): return jnp.dot(left, right, preferred_element_type=jnp.float32)]
where the time goes in v17:
time: 130 us; the launch traced here: 129 us
  matrix products  49.9 us (38%)
  waiting for transfers between devices  45.1 us (35%)
  starting transfers between devices  23.8 us (18%)
  local copies, waits for them, and re-layouts  7.6 us (6%)
  other arithmetic  1.95 us (2%)
    all_to_all x2, waiting for transfers between devices, exchange(): lax.all_to_all(rows.reshape(experts, per_pair, feature_width), 'ep', spli...  35.3 us
    dot_general x10, matrix products, rows_times(): lax.dot_general(left, right, (((1,), (1,)), ((), ())), preferred_element_...  19 us
    dot_general x8, matrix products, inner_rows(): lax.dot_general(left, right, (((0,), (0,)), ((), ())), preferred_element_...  15.1 us
    all_to_all x2, starting transfers between devices, exchange(): lax.all_to_all(rows.reshape(experts, per_pair, feature_width), 'ep', spli...  11.5 us
    dot_general x5, matrix products, matmul(): return jnp.dot(left, right, preferred_element_type=jnp.float32)  10.5 us
    all_to_all x1, waiting for transfers between devices, body(): lax.all_to_all(expert_out.reshape(experts, per_pair, feature_width), 'ep'...  7.61 us
    all_to_all x1, starting transfers between devices, body(): lax.all_to_all(token_part.reshape(experts, per_pair, feature_width), 'ep'...  4.41 us
    all_to_all x1, starting transfers between devices, body(): lax.all_to_all(expert_out.reshape(experts, per_pair, feature_width), 'ep'...  4.24 us
  transfers between devices with their start and end apart: 10, of which 4 were waited for; matrix products, arithmetic and copies ran while one was open for 40% of the time, Pallas kernels for 0%

profile of v17, /device:TPU:0, one launch (start us, length us, event | category | flops | bytes accessed | tf_op | source)
XLA Modules:
  0.0 129.4 jit_solution(17712426209018553223)
XLA Ops:
  0.6 0.0 copy-start
  0.7 0.9 slice.45
  1.5 0.2 fusion.14
  1.7 2.7 %fusion.15 = bf16[8,32,2048]{2,1,0:T(8,128)(2,1)} fusion(bf16[256,2048]{1,0:T(8,128)(2,1)} %param.7, s32[256]{0:T(256)S(1)} %compare_select_fusion.1, s32[8,32]{1,0:T(8,128)S(1)} %multiply_add_fusion), kind=kOutput, calls=%fused_computation.21 | convolution fusion | flops 268500992 | bytes 2099200 | tf_op jit(solution)/shard_map/dot_general | solution.py:53
  4.4 7.2 %all-to-all-start = ((bf16[8,32,2048]{2,1,0:T(8,128)(2,1)}), bf16[8,32,2048]{2,1,0:T(8,128)(2,1)}, u32[]{:S(2)}, u32[]{:S(2)}) async-start(bf16[8,32,2048]{2,1,0:T(8,128)(2,1)} %fusion.15), calls=%async_computation | async-start | bytes 2097152 | tf_op jit(solution)/shard_map/all_to_all | solution.py:58
  11.6 0.7 slice.44
  12.3 0.1 select_reduce_fusion
  12.5 2.6 %fusion.6 = bf16[256,2048]{1,0:T(8,128)(2,1)} fusion(bf16[256,2048]{1,0:T(8,128)(2,1)} %param.13, f32[256]{0:T(256)S(1)} %select_reduce_fusion, s32[256]{0:T(256)S(1)} %compare_select_fusion.1), kind=kOutput, calls=%fused_computation.11 | convolution fusion | flops 269549568 | bytes 2099200 | tf_op jit(solution)/shard_map/dot_general | solution.py:27
  15.1 22.4 %all-to-all-done = bf16[8,32,2048]{2,1,0:T(8,128)(2,1)} async-done(((bf16[8,32,2048]{2,1,0:T(8,128)(2,1)}), bf16[8,32,2048]{2,1,0:T(8,128)(2,1)}, u32[]{:S(2)}, u32[]{:S(2)}) %all-to-all-start) | async-done | bytes 1048608 | tf_op jit(solution)/shard_map/all_to_all | solution.py:58
  37.5 4.3 %all-to-all-start.1 = ((bf16[8,32,2048]{2,1,0:T(8,128)(2,1)}), bf16[8,32,2048]{2,1,0:T(8,128)(2,1)}, u32[]{:S(2)}, u32[]{:S(2)}) async-start(bf16[8,32,2048]{2,1,0:T(8,128)(2,1)} %bitcast.75), calls=%async_computation.1 | async-start | bytes 2097152 | tf_op jit(solution)/shard_map/all_to_all | solution.py:58
  41.8 0.1 pad.1.clone
  41.9 0.1 pad.3.clone
  42.0 0.1 pad.2.clone
  42.1 0.9 compare_select_fusion
  42.9 2.8 %dynamic-slice_bitcast_fusion = (bf16[192,2048]{1,0:T(8,128)(2,1)}, bf16[192,2048]{1,0:T(8,128)(2,1)}) fusion(bf16[1,768,2048]{2,1,0:T(8,128)(2,1)} %param.11, s32[]{:T(128)S(6)} %select_n.28, bf16[1,768,2048]{2,1,0:T(8,128)(2,1)} %param.10), kind=kLoop, calls=%fused_computation.37 | loop fusion | bytes 3145732 | tf_op jit(solution)/shard_map/dynamic_slice | solution.py:152
  45.7 1.5 %collective-permute-start.2 = (bf16[256,2048]{1,0:T(8,128)(2,1)}, bf16[256,2048]{1,0:T(8,128)(2,1)}, u32[]{:S(2)}, u32[]{:S(2)}) collective-permute-start(bf16[256,2048]{1,0:T(8,128)(2,1)} %bitcast.5), channel_id=1, source_target_pairs={{0,16},{8,24},{16,0},{24,8},{1,17},{9,25},{17,1},{25,9},{2,18},{10... | collective-permute-start | bytes 3145736 | tf_op jit(solution)/shard_map/ppermute | solution.py:73
  47.2 0.0 collective-permute-start
  47.2 4.0 %fusion.1 = f32[256,1536]{1,0:T(8,128)S(1)} fusion(bf16[256,2048]{1,0:T(8,128)(2,1)} %bitcast.5, bf16[768,2048]{1,0:T(8,128)(2,1)S(1)} %bitcast.78, bf16[768,2048]{1,0:T(8,128)(2,1)} %bitcast.80), kind=kOutput, calls=%fused_computation.2 | convolution fusion | flops 1623195648 | bytes 8912896 | tf_op jit(solution)/shard_map/dot_general | solution.py:15
  51.3 1.2 copy-done.11
  52.4 2.0 %fusion.9 = bf16[256,2048]{1,0:T(8,128)(2,1)} fusion(bf16[1,768,2048]{2,1,0:T(8,128)(2,1)S(1)} %copy-done, f32[256,1536]{1,0:T(8,128)S(1)} %fusion.1), kind=kOutput, calls=%fused_computation.14 | convolution fusion | flops 807010304 | bytes 5767168 | tf_op jit(solution)/shard_map/dot_general | solution.py:27
  54.5 12.9 %all-to-all-done.1 = bf16[8,32,2048]{2,1,0:T(8,128)(2,1)} async-done(((bf16[8,32,2048]{2,1,0:T(8,128)(2,1)}), bf16[8,32,2048]{2,1,0:T(8,128)(2,1)}, u32[]{:S(2)}, u32[]{:S(2)}) %all-to-all-start.1) | async-done | bytes 1048608 | tf_op jit(solution)/shard_map/all_to_all | solution.py:58
  67.4 4.2 %all-to-all-start.2 = ((bf16[8,32,2048]{2,1,0:T(8,128)(2,1)}), bf16[8,32,2048]{2,1,0:T(8,128)(2,1)}, u32[]{:S(2)}, u32[]{:S(2)}) async-start(bf16[8,32,2048]{2,1,0:T(8,128)(2,1)} %bitcast.77), calls=%async_computation.2 | async-start | bytes 2097152 | tf_op jit(solution)/shard_map/all_to_all | solution.py:94
  71.6 0.0 copy-start.9
  71.6 0.0 copy-start.10
  71.7 3.0 %multiply_convert_fusion.1 = (bf16[256,768]{1,0:T(8,128)(2,1)S(1)}, bf16[256,768]{1,0:T(8,128)(2,1)S(1)}) fusion(f32[256,1536]{1,0:T(8,128)} %copy-done.11, bf16[256,2048]{1,0:T(8,128)(2,1)} %bitcast.10, bf16[1,768,2048]{2,1,0:T(8,128)(2,1)S(1)} %copy-done), kind=kOutput, calls=%fused_computation.40 | convolution fusion | flops 807862272 | bytes 6553600 | tf_op jit(solution)/shard_map/dot_general | solution.py:15
  74.7 0.6 copy-done.10
  75.3 2.8 %fusion.7 = bf16[256,2048]{1,0:T(8,128)(2,1)} fusion(bf16[768,2048]{1,0:T(8,128)(2,1)S(1)} %bitcast.79, bf16[768,2048]{1,0:T(8,128)(2,1)S(1)} %bitcast.81, bf16[256,768]{1,0:T(8,128)(2,1)S(1)} %get-tuple-element.35, bf16[256,768]{1,0:T(8,128)(2,1)S(1)} %get-tuple-element.34), kind=kOutput, calls=%fused_computation.12 | convolution fusion | flops 1625292800 | bytes 8126464 | tf_op jit(solution)/shard_map/dot_general | solution.py:27
  78.1 1.5 %collective-permute-start.3 = (bf16[256,2048]{1,0:T(8,128)(2,1)}, bf16[256,2048]{1,0:T(8,128)(2,1)}, u32[]{:S(2)}, u32[]{:S(2)}) collective-permute-start(bf16[256,2048]{1,0:T(8,128)(2,1)} %bitcast.10), channel_id=1, source_target_pairs={{0,16},{8,24},{16,0},{24,8},{1,17},{9,25},{17,1},{25,9},{2,18},{10... | collective-permute-start | bytes 3145736 | tf_op jit(solution)/shard_map/ppermute | solution.py:73
  79.6 0.0 collective-permute-start.1
  79.6 1.8 %fusion.89 = f32[256,384]{0,1:T(8,128)S(1)} fusion(bf16[256,2048]{1,0:T(8,128)(2,1)} %bitcast.5, bf16[192,2048]{1,0:T(8,128)(2,1)S(1)} %copy-done.4, bf16[192,2048]{1,0:T(8,128)(2,1)S(1)} %copy-done.6), kind=kOutput, calls=%fused_computation.122 | convolution fusion | flops 405798912 | bytes 3014656 | tf_op jit(solution)/shard_map/dot_general | solution.py:15
  81.5 1.7 %multiply_convert_fusion.15 = (bf16[256,192]{0,1:T(8,128)(2,1)S(1)}, bf16[256,192]{0,1:T(8,128)(2,1)S(1)}) fusion(f32[256,384]{0,1:T(8,128)S(1)} %fusion.89, bf16[256,2048]{1,0:T(8,128)(2,1)} %bitcast.10, bf16[1,768,2048]{2,1,0:T(8,128)(2,1)S(1)} %copy-done, s32[]{:T(128)S(6)} %select_n.28), kind=kOutput, calls=%fused_computation.88 | convolution fusion | flops 201965568 | bytes 2424836 | tf_op jit(solution)/shard_map/dot_general | solution.py:15
  83.2 2.8 %fusion.63 = f32[192,2048]{1,0:T(8,128)} fusion(bf16[256,2048]{1,0:T(8,128)(2,1)} %bitcast.10, f32[256,384]{0,1:T(8,128)S(1)} %fusion.89), kind=kOutput, calls=%fused_computation.96 | convolution fusion | flops 201621504 | bytes 3014656 | tf_op jit(solution)/shard_map/dot_general | solution.py:21
  86.0 3.4 %fusion.36 = f32[384,2048]{1,0:T(8,128)} fusion(bf16[256,2048]{1,0:T(8,128)(2,1)} %bitcast.5, bf16[256,192]{0,1:T(8,128)(2,1)S(1)} %get-tuple-element.43, bf16[256,192]{0,1:T(8,128)(2,1)S(1)} %get-tuple-element.42), kind=kOutput, calls=%fused_computation.55 | convolution fusion | flops 403046400 | bytes 4390912 | tf_op jit(solution)/shard_map/dot_general | solution.py:21
  89.4 7.6 %all-to-all-done.2 = bf16[8,32,2048]{2,1,0:T(8,128)(2,1)} async-done(((bf16[8,32,2048]{2,1,0:T(8,128)(2,1)}), bf16[8,32,2048]{2,1,0:T(8,128)(2,1)}, u32[]{:S(2)}, u32[]{:S(2)}) %all-to-all-start.2) | async-done | bytes 1048608 | tf_op jit(solution)/shard_map/all_to_all | solution.py:94
  97.0 4.4 %all-to-all-start.3 = ((bf16[8,32,2048]{2,1,0:T(8,128)(2,1)}), bf16[8,32,2048]{2,1,0:T(8,128)(2,1)}, u32[]{:S(2)}, u32[]{:S(2)}) async-start(bf16[8,32,2048]{2,1,0:T(8,128)(2,1)} %bitcast.76), calls=%async_computation.3 | async-start | bytes 2097152 | tf_op jit(solution)/shard_map/all_to_all | solution.py:112
  101.5 0.0 copy-start.5
  101.5 0.0 copy-start.7
  101.5 0.0 collective-permute-done
  101.5 0.0 collective-permute-done.1
  101.5 2.8 %broadcast_multiply_fusion = (bf16[256,2048]{1,0:T(8,128)(2,1)}, f32[256,2048]{1,0:T(8,128)S(1)}) fusion(f32[256]{0:T(256)S(1)} %bitcast.85, bf16[256,2048]{1,0:T(8,128)(2,1)} %bitcast.12, s32[256]{0:T(256)S(1)} %bitcast.82), kind=kOutput, calls=%fused_computation.23 | convolution fusion | flops 269549568 | bytes 4196352 | tf_op jit(solution)/shard_map/dot_general | solution.py:27
  104.3 0.0 collective-permute-done.2
  104.3 0.0 collective-permute-done.3
  104.3 1.8 %fusion.87 = f32[256,384]{0,1:T(8,128)S(1)} fusion(bf16[256,2048]{1,0:T(8,128)(2,1)} %collective-permute-done.2, bf16[192,2048]{1,0:T(8,128)(2,1)S(1)} %copy-done.5, bf16[192,2048]{1,0:T(8,128)(2,1)S(1)} %copy-done.7), kind=kOutput, calls=%fused_computation.120 | convolution fusion | flops 405798912 | bytes 3014656 | tf_op jit(solution)/shard_map/dot_general | solution.py:15
  106.2 0.1 collective-permute-start.5
  106.2 1.8 %fusion.88 = f32[256,384]{0,1:T(8,128)S(1)} fusion(bf16[256,2048]{1,0:T(8,128)(2,1)} %collective-permute-done, bf16[192,2048]{1,0:T(8,128)(2,1)S(1)} %copy-done.5, bf16[192,2048]{1,0:T(8,128)(2,1)S(1)} %copy-done.7), kind=kOutput, calls=%fused_computation.121 | convolution fusion | flops 405798912 | bytes 3014656 | tf_op jit(solution)/shard_map/dot_general | solution.py:15
  108.1 0.6 collective-permute-start.4
  108.6 1.7 %multiply_convert_fusion.11 = (bf16[256,192]{0,1:T(8,128)(2,1)S(1)}, bf16[256,192]{0,1:T(8,128)(2,1)S(1)}) fusion(f32[256,384]{0,1:T(8,128)S(1)} %fusion.87, bf16[256,2048]{1,0:T(8,128)(2,1)} %collective-permute-done.3, bf16[1,768,2048]{2,1,0:T(8,128)(2,1)S(1)} %copy-done, s32[]{:T(128)S(6)} %select_n.28), kind=kOutput, calls=%fused_computation.80 | convolution fusion | flops 201965568 | bytes 2424836 | tf_op jit(solution)/shard_map/dot_general | solution.py:15
  110.4 0.0 copy-start.3
  110.4 1.8 %multiply_convert_fusion.13 = (bf16[256,192]{0,1:T(8,128)(2,1)S(1)}, bf16[256,192]{0,1:T(8,128)(2,1)S(1)}) fusion(f32[256,384]{0,1:T(8,128)S(1)} %fusion.88, bf16[256,2048]{1,0:T(8,128)(2,1)} %collective-permute-done.1, bf16[1,768,2048]{2,1,0:T(8,128)(2,1)S(1)} %copy-done, s32[]{:T(128)S(6)} %select_n.28), kind=kOutput, calls=%fused_computation.84 | convolution fusion | flops 201965568 | bytes 2424836 | tf_op jit(solution)/shard_map/dot_general | solution.py:15
  112.2 1.8 %fusion.40 = f32[384,2048]{1,0:T(8,128)S(1)} fusion(bf16[256,2048]{1,0:T(8,128)(2,1)} %collective-permute-done, bf16[256,192]{0,1:T(8,128)(2,1)S(1)} %get-tuple-element.41, bf16[256,192]{0,1:T(8,128)(2,1)S(1)} %get-tuple-element.40), kind=kOutput, calls=%fused_computation.59 | convolution fusion | flops 403046400 | bytes 4390912 | tf_op jit(solution)/shard_map/dot_general | solution.py:21
  114.0 0.3 multiply_reduce_fusion
  114.3 0.7 maximum_maximum_fusion
  115.0 1.8 %fusion.44 = f32[384,2048]{1,0:T(8,128)S(1)} fusion(bf16[256,2048]{1,0:T(8,128)(2,1)} %collective-permute-done.2, bf16[256,192]{0,1:T(8,128)(2,1)S(1)} %get-tuple-element.45, bf16[256,192]{0,1:T(8,128)(2,1)S(1)} %get-tuple-element.44), kind=kOutput, calls=%fused_computation.63 | convolution fusion | flops 403046400 | bytes 4390912 | tf_op jit(solution)/shard_map/dot_general | solution.py:21
  116.8 1.6 %convolution_add_fusion.1 = f32[192,2048]{1,0:T(8,128)S(1)} fusion(f32[192,2048]{1,0:T(8,128)S(1)} %copy-done.2, bf16[256,2048]{1,0:T(8,128)(2,1)} %collective-permute-done.1, f32[256,384]{0,1:T(8,128)S(1)} %fusion.88), kind=kOutput, calls=%fused_computation.10 | convolution fusion | flops 202014720 | bytes 4587520 | tf_op jit(solution)/shard_map/dot_general | solution.py:21
  118.5 0.0 collective-permute-done.5
  118.5 0.6 fusion.86
  119.1 0.0 collective-permute-done.4
  119.1 0.5 multiply_convert_fusion.9
  119.6 0.4 fusion.64
  120.0 2.7 %fusion.13 = bf16[1,192,2048]{2,1,0:T(8,128)(2,1)} fusion(f32[192,2048]{1,0:T(8,128)S(1)} %fusion.64, f32[192,2048]{1,0:T(8,128)S(1)} %convolution_add_fusion.1, bf16[256,2048]{1,0:T(8,128)(2,1)} %collective-permute-done.3, f32[256,384]{0,1:T(8,128)S(1)} %fusion.87), kind=kOutput, calls=%fused_computation.16 | convolution fusion | flops 202801152 | bytes 5373952 | tf_op jit(solution)/shard_map/dot_general | solution.py:21
  122.7 0.6 add_convert_fusion
  123.3 1.2 slice_bitcast_fusion
  124.6 2.1 %all-to-all-done.3 = bf16[8,32,2048]{2,1,0:T(8,128)(2,1)} async-done(((bf16[8,32,2048]{2,1,0:T(8,128)(2,1)}), bf16[8,32,2048]{2,1,0:T(8,128)(2,1)}, u32[]{:S(2)}, u32[]{:S(2)}) %all-to-all-start.3) | async-done | bytes 1048608 | tf_op jit(solution)/shard_map/all_to_all | solution.py:112
  126.7 2.7 %fusion.33 = bf16[256,2048]{1,0:T(8,128)(2,1)} fusion(bf16[256,2048]{1,0:T(8,128)(2,1)} %bitcast.14, s32[256]{0:T(256)S(1)} %bitcast.83), kind=kOutput, calls=%fused_computation.51 | convolution fusion | flops 268500992 | bytes 2098176 | tf_op jit(solution)/shard_map/dot_general | solution.py:176
  (21 shorter events, 0.1 us)
Async XLA Ops:
  0.6 51.8 %copy-start = (bf16[1,768,2048]{2,1,0:T(8,128)(2,1)S(1)}, bf16[1,768,2048]{2,1,0:T(8,128)(2,1)}, u32[]{:S(2)}) copy-start(bf16[1,768,2048]{2,1,0:T(8,128)(2,1)} %param.12) | copy-start | bytes 9437188
  4.4 33.1 %all-to-all-start = ((bf16[8,32,2048]{2,1,0:T(8,128)(2,1)}), bf16[8,32,2048]{2,1,0:T(8,128)(2,1)}, u32[]{:S(2)}, u32[]{:S(2)}) async-start(bf16[8,32,2048]{2,1,0:T(8,128)(2,1)} %fusion.15), calls=%async_computation | async-start | bytes 2097152 | tf_op jit(solution)/shard_map/all_to_all | solution.py:58
  37.5 29.9 %all-to-all-start.1 = ((bf16[8,32,2048]{2,1,0:T(8,128)(2,1)}), bf16[8,32,2048]{2,1,0:T(8,128)(2,1)}, u32[]{:S(2)}, u32[]{:S(2)}) async-start(bf16[8,32,2048]{2,1,0:T(8,128)(2,1)} %bitcast.75), calls=%async_computation.1 | async-start | bytes 2097152 | tf_op jit(solution)/shard_map/all_to_all | solution.py:58
  42.1 5.2 %copy-start.8 = (bf16[1,768,2048]{2,1,0:T(8,128)(2,1)S(1)}, bf16[1,768,2048]{2,1,0:T(8,128)(2,1)}, u32[]{:S(2)}) copy-start(bf16[1,768,2048]{2,1,0:T(8,128)(2,1)} %param.11) | copy-start | bytes 9437188
  45.7 58.6 %collective-permute-start.2 = (bf16[256,2048]{1,0:T(8,128)(2,1)}, bf16[256,2048]{1,0:T(8,128)(2,1)}, u32[]{:S(2)}, u32[]{:S(2)}) collective-permute-start(bf16[256,2048]{1,0:T(8,128)(2,1)} %bitcast.5), channel_id=1, source_target_pairs={{0,16},{8,24},{16,0},{24,8},{1,17},{9,25},{17,1},{25,9},{2,18},{10... | collective-permute-start | bytes 3145736 | tf_op jit(solution)/shard_map/ppermute | solution.py:73
  47.2 54.3 %collective-permute-start = (bf16[256,2048]{1,0:T(8,128)(2,1)}, bf16[256,2048]{1,0:T(8,128)(2,1)}, u32[]{:S(2)}, u32[]{:S(2)}) collective-permute-start(bf16[256,2048]{1,0:T(8,128)(2,1)} %bitcast.5), channel_id=1, source_target_pairs={{0,8},{8,0},{16,24},{24,16},{1,9},{9,1},{17,25},{25,17},{2,10},{10... | collective-permute-start | bytes 3145736 | tf_op jit(solution)/shard_map/ppermute | solution.py:73
  51.3 1.2 copy-start.11
  67.4 29.6 %all-to-all-start.2 = ((bf16[8,32,2048]{2,1,0:T(8,128)(2,1)}), bf16[8,32,2048]{2,1,0:T(8,128)(2,1)}, u32[]{:S(2)}, u32[]{:S(2)}) async-start(bf16[8,32,2048]{2,1,0:T(8,128)(2,1)} %bitcast.77), calls=%async_computation.2 | async-start | bytes 2097152 | tf_op jit(solution)/shard_map/all_to_all | solution.py:94
  71.6 3.1 %copy-start.9 = (bf16[1,768,2048]{2,1,0:T(8,128)(2,1)S(1)}, bf16[1,768,2048]{2,1,0:T(8,128)(2,1)}, u32[]{:S(2)}) copy-start(bf16[1,768,2048]{2,1,0:T(8,128)(2,1)} %param.11) | copy-start | bytes 9437188
  71.6 3.6 %copy-start.10 = (bf16[1,768,2048]{2,1,0:T(8,128)(2,1)S(1)}, bf16[1,768,2048]{2,1,0:T(8,128)(2,1)}, u32[]{:S(2)}) copy-start(bf16[1,768,2048]{2,1,0:T(8,128)(2,1)} %param.10) | copy-start | bytes 9437188
  75.3 4.3 %copy-start.4 = (bf16[192,2048]{1,0:T(8,128)(2,1)S(1)}, bf16[192,2048]{1,0:T(8,128)(2,1)}, u32[]{:S(2)}) copy-start(bf16[192,2048]{1,0:T(8,128)(2,1)} %get-tuple-element.48) | copy-start | bytes 2359300
  75.3 4.3 %copy-start.6 = (bf16[192,2048]{1,0:T(8,128)(2,1)S(1)}, bf16[192,2048]{1,0:T(8,128)(2,1)}, u32[]{:S(2)}) copy-start(bf16[192,2048]{1,0:T(8,128)(2,1)} %get-tuple-element.49) | copy-start | bytes 2359300
  78.1 26.2 %collective-permute-start.3 = (bf16[256,2048]{1,0:T(8,128)(2,1)}, bf16[256,2048]{1,0:T(8,128)(2,1)}, u32[]{:S(2)}, u32[]{:S(2)}) collective-permute-start(bf16[256,2048]{1,0:T(8,128)(2,1)} %bitcast.10), channel_id=1, source_target_pairs={{0,16},{8,24},{16,0},{24,8},{1,17},{9,25},{17,1},{25,9},{2,18},{10... | collective-permute-start | bytes 3145736 | tf_op jit(solution)/shard_map/ppermute | solution.py:73
  79.6 21.9 %collective-permute-start.1 = (bf16[256,2048]{1,0:T(8,128)(2,1)}, bf16[256,2048]{1,0:T(8,128)(2,1)}, u32[]{:S(2)}, u32[]{:S(2)}) collective-permute-start(bf16[256,2048]{1,0:T(8,128)(2,1)} %bitcast.10), channel_id=1, source_target_pairs={{0,8},{8,0},{16,24},{24,16},{1,9},{9,1},{17,25},{25,17},{2,10},{10... | collective-permute-start | bytes 3145736 | tf_op jit(solution)/shard_map/ppermute | solution.py:73
  97.0 29.6 %all-to-all-start.3 = ((bf16[8,32,2048]{2,1,0:T(8,128)(2,1)}), bf16[8,32,2048]{2,1,0:T(8,128)(2,1)}, u32[]{:S(2)}, u32[]{:S(2)}) async-start(bf16[8,32,2048]{2,1,0:T(8,128)(2,1)} %bitcast.76), calls=%async_computation.3 | async-start | bytes 2097152 | tf_op jit(solution)/shard_map/all_to_all | solution.py:112
  101.5 2.9 %copy-start.5 = (bf16[192,2048]{1,0:T(8,128)(2,1)S(1)}, bf16[192,2048]{1,0:T(8,128)(2,1)}, u32[]{:S(2)}) copy-start(bf16[192,2048]{1,0:T(8,128)(2,1)} %get-tuple-element.48) | copy-start | bytes 2359300
  101.5 2.8 %copy-start.7 = (bf16[192,2048]{1,0:T(8,128)(2,1)S(1)}, bf16[192,2048]{1,0:T(8,128)(2,1)}, u32[]{:S(2)}) copy-start(bf16[192,2048]{1,0:T(8,128)(2,1)} %get-tuple-element.49) | copy-start | bytes 2359300
  106.2 12.3 %collective-permute-start.5 = (bf16[256,2048]{1,0:T(8,128)(2,1)}, bf16[256,2048]{1,0:T(8,128)(2,1)S(1)}, u32[]{:S(2)}, u32[]{:S(2)}) collective-permute-start(bf16[256,2048]{1,0:T(8,128)(2,1)} %collective-permute-done.2), channel_id=1, source_target_pairs={{0,8},{8,0},{16,24},{24,16},{1,9},{9,1},{17,25},{25,17},{2,10},{10... | collective-permute-start | bytes 3145736 | tf_op jit(solution)/shard_map/ppermute | solution.py:73
  108.1 11.0 %collective-permute-start.4 = (bf16[256,2048]{1,0:T(8,128)(2,1)}, bf16[256,2048]{1,0:T(8,128)(2,1)S(1)}, u32[]{:S(2)}, u32[]{:S(2)}) collective-permute-start(bf16[256,2048]{1,0:T(8,128)(2,1)} %collective-permute-done.3), channel_id=1, source_target_pairs={{0,8},{8,0},{16,24},{24,16},{1,9},{9,1},{17,25},{25,17},{2,10},{10... | collective-permute-start | bytes 3145736 | tf_op jit(solution)/shard_map/ppermute | solution.py:73
  110.4 3.7 %copy-start.3 = (bf16[256,2048]{1,0:T(8,128)(2,1)S(1)}, bf16[256,2048]{1,0:T(8,128)(2,1)}, u32[]{:S(2)}) copy-start(bf16[256,2048]{1,0:T(8,128)(2,1)} %param.13) | copy-start | bytes 3145732
  114.0 2.8 %copy-start.2 = (f32[192,2048]{1,0:T(8,128)S(1)}, f32[192,2048]{1,0:T(8,128)}, u32[]{:S(2)}) copy-start(f32[192,2048]{1,0:T(8,128)} %fusion.63) | copy-start | bytes 4718596
  120.0 2.7 %copy-start.1 = (f32[384,2048]{1,0:T(8,128)S(1)}, f32[384,2048]{1,0:T(8,128)}, u32[]{:S(2)}) copy-start(f32[384,2048]{1,0:T(8,128)} %fusion.36) | copy-start | bytes 9437188
